TPU v7x, 256 devices: a whole 4x4x8 slice. The times are simulated.
256 devices in a mesh: ctx: 16 (over x, y_hi, core), tp: 16 (over z, y_lo).
Axes of the slice: x: 4, y: 4 (y_hi: 2, y_lo: 2; y = y_hi * 2 + y_lo), z: 8, core: 2. Of those that a mesh axis runs over, the one named last changes fastest.
Arguments:
- tokens: bfloat16 [2048, 4096], P('ctx', 'tp'), may hold values from -6 to 6
- gate_tiles: bfloat16 [1024, 128, 128], P('tp'), may hold values from -0.25 to 0.25
- up_tiles: bfloat16 [1024, 128, 128], P('tp'), may hold values from -0.25 to 0.25
- down_tiles: bfloat16 [1024, 128, 128], P('tp'), may hold values from -0.125 to 0.125
- gu_blocks: int32 [2, 1024], P(None, 'tp'), may hold values from 0 to 31, as said below
- down_blocks: int32 [2, 1024], P(None, 'tp'), may hold values from 0 to 31, as said below
- counts: int32 [2, 16], P(None, 'tp'), may hold values from 1 to 64, as said below
Outputs:
- mixed: bfloat16 [128, 16, 4096], P('tp', None, 'ctx')
Inputs may be any that keep to these rules, and one draw needn't show every extreme that they name: `gu_blocks`: within one shard's 64 slots the pairs (row 0, row 1) are all different; row 0 is below 32, row 1 below 8. `down_blocks`: within one shard's 64 slots the pairs (row 0, row 1) are all different; row 0 is below 8, row 1 below 32. In each row some shard has exactly 64 live slots; only the first counts slots of a shard are live.
All inputs are finite; a program needn't handle non-finite values.
Results may differ from a plain program's by a relative error of at most 0.0052.
Values may be sent and summed in bfloat16 or wider, within the bound.
No kernel may reach another device: no remote copies, remote signals or barrier semaphores. Data moves between devices by JAX's collectives and lax.ppermute only.
A program may use at most 64 MiB of HBM per device.

v0:
```python
import jax
import jax.numpy as jnp
from jax import lax
from jax.sharding import PartitionSpec as P

FF = 16384


def per_device(tokens, gate_tiles, up_tiles, down_tiles, gu_blocks, down_blocks, counts):
    gathered = lax.all_gather(tokens, "tp", axis=1, tiled=True)
    tok_rows, feat_width = gathered.shape
    slot_count = gate_tiles.shape[0]
    tile_size = gate_tiles.shape[1]
    in_blocks = feat_width // tile_size
    tp_count = lax.axis_size("tp")
    hid_blocks = FF // tp_count // tile_size
    widened = gathered.astype(jnp.float32)
    squares = jnp.mean(widened * widened, axis=1, keepdims=True)
    normed = (widened * lax.rsqrt(squares + 1e-05)).astype(jnp.bfloat16)
    slot_ids = jnp.arange(slot_count)
    valid_in = (slot_ids < counts[0, 0]).astype(jnp.float32)
    valid_out = (slot_ids < counts[1, 0]).astype(jnp.float32)
    pick_hidden = (gu_blocks[1][:, None] == jnp.arange(hid_blocks)[None, :]).astype(
        jnp.float32
    ) * valid_in[:, None]
    pick_out = (down_blocks[1][:, None] == jnp.arange(in_blocks)[None, :]).astype(
        jnp.float32
    ) * valid_out[:, None]
    block_rows = min(tok_rows, 512)

    def hidden_block(row_block):
        row_tiles = row_block.reshape(block_rows, in_blocks, tile_size)
        chosen = jnp.take(row_tiles, gu_blocks[0], axis=1)
        gate_part = jnp.einsum(
            "tmk,mkn->tmn", chosen, gate_tiles, preferred_element_type=jnp.float32
        )
        up_part = jnp.einsum("tmk,mkn->tmn", chosen, up_tiles, preferred_element_type=jnp.float32)
        gate_sum = jnp.einsum(
            "tmn,mh->thn", gate_part, pick_hidden, precision=lax.Precision.HIGHEST
        )
        up_sum = jnp.einsum("tmn,mh->thn", up_part, pick_hidden, precision=lax.Precision.HIGHEST)
        return (jax.nn.silu(gate_sum) * up_sum).astype(jnp.bfloat16)

    hidden = lax.map(hidden_block, normed.reshape(tok_rows // block_rows, block_rows, feat_width))
    hidden = hidden.reshape(tok_rows, hid_blocks, tile_size)
    first_shard = jnp.where(lax.axis_index("tp") == 0, 1.0, 0.0).astype(jnp.float32)
    chosen_hidden = jnp.take(hidden, down_blocks[0], axis=1)
    products = jnp.einsum(
        "tmk,mkn->tmn", chosen_hidden, down_tiles, preferred_element_type=jnp.float32
    )
    summed = jnp.einsum("tmn,mo->ton", products, pick_out, precision=lax.Precision.HIGHEST)
    partial_term = summed.reshape(tok_rows, feat_width) + first_shard * widened
    arrived = lax.all_to_all(
        partial_term.reshape(tok_rows, 1, feat_width),
        "ctx",
        split_axis=2,
        concat_axis=1,
        tiled=True,
    )
    finished = lax.psum_scatter(arrived, "tp", scatter_dimension=0, tiled=True)
    return finished.astype(jnp.bfloat16)


def solution(mesh):
    return jax.shard_map(
        per_device,
        mesh=mesh,
        in_specs=(
            P("ctx", "tp"),
            P("tp", None, None),
            P("tp", None, None),
            P("tp", None, None),
            P(None, "tp"),
            P(None, "tp"),
            P(None, "tp"),
        ),
        out_specs=P("tp", None, "ctx"),
        check_vma=False,
    )
```

profile of v0, /device:TPU:2, one launch (start us, length us, event | category | flops | bytes accessed | tf_op | source)
XLA Modules:
  0.0 236.4 jit_solution(7079399391941856147)
XLA Ops:
  6.5 1.7 copy.17
  8.3 0.0 all-gather.2.cloned.1.call-update
  8.3 0.0 reduce-scatter.2.cloned.1.call-start
  8.3 1.3 fusion.53
  9.7 0.7 compare_convert_fusion
  10.4 0.6 compare_convert_fusion.1
  10.9 0.7 fusion.45
  11.6 0.7 fusion.46
  12.3 0.7 compare_and_fusion
  13.0 0.7 slice_bitcast_fusion
  13.7 0.7 compare_and_fusion.1
  14.4 0.7 slice_bitcast_fusion.1
  15.1 65.7 %all-gather.2.cloned.1.call-done = bf16[128,4096]{0,1:T(8,128)(2,1)} async-done(((bf16[128,256]{0,1:T(8,128)(2,1)}), bf16[128,4096]{0,1:T(8,128)(2,1)}) %all-gather.2.cloned.1.call-update) | async-done | bytes 1048592 | tf_op jit(solution)/shard_map/all_gather | solution.py:10
  80.8 1.8 fusion.6
  82.6 2.4 %fusion.7 = bf16[128,4096]{0,1:T(8,128)(2,1)} fusion(bf16[128,4096]{0,1:T(8,128)(2,1)} %all-gather.2.cloned.1.call-done, f32[128]{0:T(128)S(1)} %add_rsqrt_fusion), kind=kLoop, calls=%fused_computation.15 | loop fusion | flops 1572864 | bytes 2097664 | tf_op jit(solution)/shard_map/convert_element_type | solution.py:19
  85.0 1.6 copy.18
  86.6 2.2 gather_fusion
  88.8 2.5 %convolution_bitcast_fusion.2 = f32[128,64,128]{2,0,1:T(8,128)S(1)} fusion(bf16[64,128,128]{2,1,0:T(8,128)(2,1)S(1)} %copy-done, bf16[64,128,128]{2,1,0:T(8,128)(2,1)} %gather_fusion, pred[64]{0:T(512)(128)(4,1)S(1)} %compare_and_fusion), kind=kOutput, calls=%fused_computation.13 | convolution fusion | flops 269484032 | bytes 8388672 | tf_op jit(solution)/shard_map/while/body/eval_jaxpr/tmk,mkn->tmn/dot_general | solution.py:34
  91.3 0.3 copy-done.3
  91.6 0.8 convolution_bitcast_fusion.1
  92.4 4.4 %fusion.17 = f32[128,8,128]{2,1,0:T(8,128)S(1)} fusion(f32[128,64,128]{2,0,1:T(8,128)S(1)} %convolution_bitcast_fusion.2, f32[64]{0:T(128)S(1)} %compare_convert_fusion, s32[64]{0:T(128)S(1)} %slice_bitcast_fusion), kind=kOutput, calls=%fused_computation.24 | convolution fusion | flops 100664320 | bytes 4719104 | tf_op jit(solution)/shard_map/while/body/eval_jaxpr/tmn,mh->thn/dot_general | solution.py:38
  96.8 4.4 %fusion.26 = bf16[128,8,128]{2,1,0:T(8,128)(2,1)S(1)} fusion(f32[128,64,128]{2,0,1:T(8,128)S(1)} %convolution_bitcast_fusion.1, f32[128,8,128]{2,1,0:T(8,128)S(1)} %fusion.17, f32[64]{0:T(128)S(1)} %compare_convert_fusion, s32[64]{0:T(128)S(1)} %slice_bitcast_fusion), kind=kOutput, calls=%fused_computation.27 | convolution fusion | flops 101450752 | bytes 4981248 | tf_op jit(solution)/shard_map/while/body/eval_jaxpr/tmn,mh->thn/dot_general | solution.py:41
  101.2 2.2 gather_fusion.1
  103.3 3.0 %convolution_bitcast_fusion = f32[128,64,128]{2,0,1:T(8,128)S(1)} fusion(bf16[64,128,128]{2,1,0:T(8,128)(2,1)} %param.10, bf16[64,128,128]{2,1,0:T(8,128)(2,1)} %gather_fusion.1, pred[64]{0:T(512)(128)(4,1)S(1)} %compare_and_fusion.1), kind=kOutput, calls=%fused_computation.11 | convolution fusion | flops 269484032 | bytes 8388672 | tf_op jit(solution)/shard_map/tmk,mkn->tmn/dot_general | solution.py:48
  106.3 6.0 %fusion.14 = f32[128,32,128]{2,1,0:T(8,128)} fusion(f32[128,64,128]{2,0,1:T(8,128)S(1)} %convolution_bitcast_fusion, f32[64]{0:T(128)S(1)} %compare_convert_fusion.1, s32[64]{0:T(128)S(1)} %slice_bitcast_fusion.1), kind=kOutput, calls=%fused_computation.23 | convolution fusion | flops 402657280 | bytes 6291968 | tf_op jit(solution)/shard_map/tmn,mo->ton/dot_general | solution.py:51
  112.3 3.1 %copy.26 = f32[128,32,128]{0,2,1:T(8,128)} copy(f32[128,32,128]{2,1,0:T(8,128)} %fusion.14) | data formatting | bytes 4194304 | tf_op jit(solution)/shard_map/reshape | solution.py:52
  115.4 1.8 fusion.8
  117.2 33.9 %all_to_all.12 = f32[128,1,4096]{0,1,2:T(1,128)} all-to-all(f32[128,1,4096]{0,1,2:T(1,128)S(1)} %bitcast.60), channel_id=1, replica_groups=mesh['ctx'=16,'tp'=16] {'ctx'}, dimensions={2} | all-to-all | bytes 4194304 | tf_op jit(solution)/shard_map/all_to_all | solution.py:53
  151.1 3.1 %copy.25 = f32[128,16,256]{2,1,0:T(8,128)} copy(f32[128,16,256]{0,2,1:T(8,128)} %bitcast.61) | data formatting | bytes 4194304 | tf_op jit(solution)/shard_map/all_to_all | solution.py:53
  154.2 0.0 reduce-scatter.2.cloned.1.call-update
  154.2 73.8 %reduce-scatter.2.cloned.1.call-done = f32[8,16,256]{2,1,0:T(8,128)} async-done(((f32[128,16,256]{2,1,0:T(8,128)}), f32[8,16,256]{2,1,0:T(8,128)}) %reduce-scatter.2.cloned.1.call-update) | async-done | bytes 131088 | tf_op jit(solution)/shard_map/reduce_scatter | solution.py:60
  228.0 1.5 convert_element_type.34
  (12 shorter events, 0.1 us)
Async XLA Ops:
  6.5 82.2 %copy-start = (bf16[64,128,128]{2,1,0:T(8,128)(2,1)S(1)}, bf16[64,128,128]{2,1,0:T(8,128)(2,1)}, u32[]{:S(2)}) copy-start(bf16[64,128,128]{2,1,0:T(8,128)(2,1)} %param.8) | copy-start | bytes 6291460
  6.5 74.2 %all-gather.2.cloned.1.call-start = ((), (), s32[]{:S(2)}) async-start(), calls=%async_computation.2 | async-start | bytes 1114112 | tf_op jit(solution)/shard_map/all_gather | solution.py:10
  8.3 219.7 %reduce-scatter.2.cloned.1.call-start = ((), (), s32[]{:S(2)}) async-start(), calls=%async_computation.3 | async-start | bytes 2228224 | tf_op jit(solution)/shard_map/reduce_scatter | solution.py:60
  88.8 2.5 %copy-start.1 = (bf16[64,128,128]{2,1,0:T(8,128)(2,1)S(1)}, bf16[64,128,128]{2,1,0:T(8,128)(2,1)}, u32[]{:S(2)}) copy-start(bf16[64,128,128]{2,1,0:T(8,128)(2,1)} %gather_fusion) | copy-start | bytes 6291460
  88.8 2.9 %copy-start.3 = (bf16[64,128,128]{2,1,0:T(8,128)(2,1)S(1)}, bf16[64,128,128]{2,1,0:T(8,128)(2,1)}, u32[]{:S(2)}) copy-start(bf16[64,128,128]{2,1,0:T(8,128)(2,1)} %param.9) | copy-start | bytes 6291460
  112.3 3.1 %copy-start.2 = (bf16[128,4096]{0,1:T(8,128)(2,1)S(1)}, bf16[128,4096]{0,1:T(8,128)(2,1)}, u32[]{:S(2)}) copy-start(bf16[128,4096]{0,1:T(8,128)(2,1)} %all-gather.2.cloned.1.call-done) | copy-start | bytes 3145732
Sparse Core Ops, SparseCore 0:
  9.1 71.5 all-gather.1
  154.4 73.5 reduce-scatter.1
where the time goes:
time: 237 us; the launch traced here: 236 us
  waiting for transfers between devices  140 us (59%)
  blocking collectives  33.9 us (14%)
  matrix products  21 us (9%)
  local copies, waits for them, and re-layouts  16.9 us (7%)
  between operations  13.5 us (6%)
  other arithmetic  11.5 us (5%)
    reduce_scatter x1, waiting for transfers between devices, per_device(): finished = lax.psum_scatter(arrived, 'tp', scatter_dimension=0, tiled=True)  73.8 us
    all_gather x1, waiting for transfers between devices, per_device(): gathered = lax.all_gather(tokens, 'tp', axis=1, tiled=True)  65.7 us
    all_to_all x1, blocking collectives, per_device(): lax.all_to_all(partial_term.reshape(tok_rows, 1, feat_width), 'ctx', spli...  33.9 us
    dot_general x1, matrix products, per_device(): jnp.einsum('tmn,mo->ton', products, pick_out, precision=lax.Precision.HIG...  6 us
  transfers between devices with their start and end apart: 2, of which 2 were waited for; matrix products, arithmetic and copies ran while one was open for 3% of the time, Pallas kernels for 0%

commit v1 on v0

--- a/solution.py
+++ b/solution.py
@@ -7,12 +7,16 @@
 
 
 def per_device(tokens, gate_tiles, up_tiles, down_tiles, gu_blocks, down_blocks, counts):
-    gathered = lax.all_gather(tokens, "tp", axis=1, tiled=True)
+    tp_count = lax.axis_size("tp")
+    ctx_count = lax.axis_size("ctx")
+    own_rows, own_width = tokens.shape
+    copies = jnp.broadcast_to(tokens[None], (tp_count, own_rows, own_width))
+    pieces = lax.all_to_all(copies, "tp", 0, 0, tiled=True)
+    gathered = jnp.transpose(pieces, (1, 0, 2)).reshape(own_rows, tp_count * own_width)
     tok_rows, feat_width = gathered.shape
     slot_count = gate_tiles.shape[0]
     tile_size = gate_tiles.shape[1]
     in_blocks = feat_width // tile_size
-    tp_count = lax.axis_size("tp")
     hid_blocks = FF // tp_count // tile_size
     widened = gathered.astype(jnp.float32)
     squares = jnp.mean(widened * widened, axis=1, keepdims=True)
@@ -43,22 +47,20 @@
 
     hidden = lax.map(hidden_block, normed.reshape(tok_rows // block_rows, block_rows, feat_width))
     hidden = hidden.reshape(tok_rows, hid_blocks, tile_size)
-    first_shard = jnp.where(lax.axis_index("tp") == 0, 1.0, 0.0).astype(jnp.float32)
     chosen_hidden = jnp.take(hidden, down_blocks[0], axis=1)
     products = jnp.einsum(
         "tmk,mkn->tmn", chosen_hidden, down_tiles, preferred_element_type=jnp.float32
     )
     summed = jnp.einsum("tmn,mo->ton", products, pick_out, precision=lax.Precision.HIGHEST)
-    partial_term = summed.reshape(tok_rows, feat_width) + first_shard * widened
-    arrived = lax.all_to_all(
-        partial_term.reshape(tok_rows, 1, feat_width),
-        "ctx",
-        split_axis=2,
-        concat_axis=1,
-        tiled=True,
+    share = tok_rows // tp_count
+    outgoing = summed.reshape(tp_count, share, feat_width).astype(jnp.bfloat16)
+    incoming = lax.all_to_all(outgoing, "tp", 0, 0, tiled=True)
+    total = jnp.sum(incoming.astype(jnp.float32), axis=0)
+    residual = lax.dynamic_slice_in_dim(widened, lax.axis_index("tp") * share, share, 0)
+    mixed = (total + residual).astype(jnp.bfloat16)
+    return lax.all_to_all(
+        mixed.reshape(share, ctx_count, feat_width // ctx_count), "ctx", 1, 1, tiled=True
     )
-    finished = lax.psum_scatter(arrived, "tp", scatter_dimension=0, tiled=True)
-    return finished.astype(jnp.bfloat16)
 
 
 def solution(mesh):

time: 237 us -> 121 us (0.51)
  the two profiles are of different devices: /device:TPU:2 before, /device:TPU:1 now
where the time goes in v1:
time: 121 us
  waiting for transfers between devices  42.1 us (35%)
  matrix products  19.7 us (16%)
  blocking collectives  18.6 us (15%)
  local copies, waits for them, and re-layouts  18 us (15%)
  starting transfers between devices  16.5 us (14%)
  other arithmetic  5.51 us (5%)
    all_to_all x1, waiting for transfers between devices, per_device(): pieces = lax.all_to_all(copies, 'tp', 0, 0, tiled=True)  23.3 us
    all_to_all x1, waiting for transfers between devices, per_device(): incoming = lax.all_to_all(outgoing, 'tp', 0, 0, tiled=True)  18.8 us
    all_to_all x1, blocking collectives, per_device(): lax.all_to_all(mixed.reshape(share, ctx_count, feat_width // ctx_count),...  18.6 us
    all_to_all x1, starting transfers between devices, per_device(): pieces = lax.all_to_all(copies, 'tp', 0, 0, tiled=True)  10.1 us
    all_to_all x1, starting transfers between devices, per_device(): incoming = lax.all_to_all(outgoing, 'tp', 0, 0, tiled=True)  6.36 us
    dot_general x1, matrix products, per_device(): jnp.einsum('tmn,mo->ton', products, pick_out, precision=lax.Precision.HIG...  4.52 us
    dot_general x1, matrix products, hidden_block(): jnp.einsum('tmn,mh->thn', gate_part, pick_hidden, precision=lax.Precision...  4.37 us
    dot_general x1, matrix products, hidden_block(): jnp.einsum('tmn,mh->thn', up_part, pick_hidden, precision=lax.Precision.H...  4.36 us
  transfers between devices with their start and end apart: 2, of which 2 were waited for; matrix products, arithmetic and copies ran while one was open for 6% of the time, Pallas kernels for 0%

profile of v1, /device:TPU:1, one launch (start us, length us, event | category | flops | bytes accessed | tf_op | source)
XLA Modules:
  0.0 120.6 jit_solution(1404699886127358957)
XLA Ops:
  0.0 0.0 copy-start
  0.0 0.0 copy-start.5
  0.0 1.1 copy.16
  1.1 1.2 broadcast_in_dim.38
  2.3 10.1 %all-to-all-start = ((bf16[16,128,256]{1,2,0:T(8,128)(2,1)}), bf16[16,128,256]{1,2,0:T(8,128)(2,1)S(1)}, u32[]{:S(2)}, u32[]{:S(2)}) async-start(bf16[16,128,256]{1,2,0:T(8,128)(2,1)} %broadcast_in_dim.38), calls=%async_computation | async-start | bytes 2097152 | tf_op jit(solution)/shard_map/all_to_all | solution.py:14
  12.4 0.0 copy-done.3
  12.5 0.6 fusion.53
  13.0 0.6 compare_convert_fusion
  13.7 0.7 compare_convert_fusion.1
  14.4 23.3 %all-to-all-done = bf16[16,128,256]{1,2,0:T(8,128)(2,1)S(1)} async-done(((bf16[16,128,256]{1,2,0:T(8,128)(2,1)}), bf16[16,128,256]{1,2,0:T(8,128)(2,1)S(1)}, u32[]{:S(2)}, u32[]{:S(2)}) %all-to-all-start) | async-done | bytes 1048608 | tf_op jit(solution)/shard_map/all_to_all | solution.py:14
  37.7 1.5 %convert_element_type.76 = f32[16,128,256]{1,2,0:T(8,128)} convert(bf16[16,128,256]{1,2,0:T(8,128)(2,1)S(1)} %all-to-all-done) | non-fusion elementwise | flops 524288 | bytes 3145728 | tf_op jit(solution)/shard_map/convert_element_type | solution.py:21
  39.3 2.9 %copy.17 = f32[128,32,128]{2,0,1:T(8,128)} copy(f32[128,32,128]{0,2,1:T(8,128)} %bitcast.59) | data formatting | bytes 4194304 | tf_op jit(solution)/shard_map/convert_element_type | solution.py:21
  42.2 0.6 multiply_reduce_fusion
  42.7 1.9 %multiply_convert_fusion = bf16[128,32,128]{2,0,1:T(8,128)(2,1)S(1)} fusion(f32[128,32,128]{2,0,1:T(8,128)} %copy.17, f32[128]{0:T(128)S(1)} %add_rsqrt_fusion), kind=kLoop, calls=%fused_computation.16 | loop fusion | flops 1048576 | bytes 3146240 | tf_op jit(solution)/shard_map/convert_element_type | solution.py:23
  44.7 2.1 %gather_fusion = bf16[64,128,128]{2,1,0:T(8,128)(2,1)} fusion(bf16[128,32,128]{2,0,1:T(8,128)(2,1)S(1)} %multiply_convert_fusion, s32[1024]{0:T(1024)S(1)} %pad_clamp_fusion.1), kind=kCustom, calls=%fused_computation | custom fusion | bytes 4194560 | tf_op jit(solution)/shard_map/while/body/eval_jaxpr/jit(_take)/gather | solution.py:37
  46.8 2.5 %convolution_bitcast_fusion.2 = f32[128,64,128]{2,0,1:T(8,128)S(1)} fusion(bf16[64,128,128]{2,1,0:T(8,128)(2,1)S(1)} %copy-done, bf16[64,128,128]{2,1,0:T(8,128)(2,1)} %gather_fusion, pred[64]{0:T(512)(128)(4,1)S(1)} %compare_and_fusion), kind=kOutput, calls=%fused_computation.10 | convolution fusion | flops 269484032 | bytes 8388672 | tf_op jit(solution)/shard_map/while/body/eval_jaxpr/tmk,mkn->tmn/dot_general | solution.py:38
  49.3 0.0 copy-done.1
  49.3 0.3 copy-done.2
  49.7 0.8 convolution_bitcast_fusion.1
  50.4 4.4 %fusion.17 = f32[128,8,128]{2,1,0:T(8,128)S(1)} fusion(f32[128,64,128]{2,0,1:T(8,128)S(1)} %convolution_bitcast_fusion.2, f32[64]{0:T(128)S(1)} %compare_convert_fusion, s32[64]{0:T(128)S(1)} %slice_bitcast_fusion), kind=kOutput, calls=%fused_computation.22 | convolution fusion | flops 100664320 | bytes 4719104 | tf_op jit(solution)/shard_map/while/body/eval_jaxpr/tmn,mh->thn/dot_general | solution.py:42
  54.8 4.4 %fusion.26 = bf16[128,8,128]{2,1,0:T(8,128)(2,1)S(1)} fusion(f32[128,64,128]{2,0,1:T(8,128)S(1)} %convolution_bitcast_fusion.1, f32[128,8,128]{2,1,0:T(8,128)S(1)} %fusion.17, f32[64]{0:T(128)S(1)} %compare_convert_fusion, s32[64]{0:T(128)S(1)} %slice_bitcast_fusion), kind=kOutput, calls=%fused_computation.25 | convolution fusion | flops 101450752 | bytes 4981248 | tf_op jit(solution)/shard_map/while/body/eval_jaxpr/tmn,mh->thn/dot_general | solution.py:45
  59.2 2.1 %gather_fusion.1 = bf16[64,128,128]{2,1,0:T(8,128)(2,1)} fusion(bf16[128,8,128]{2,0,1:T(8,128)(2,1)S(1)} %copy.20, s32[1024]{0:T(1024)S(1)} %pad_clamp_fusion), kind=kCustom, calls=%fused_computation.1 | custom fusion | bytes 4194560 | tf_op jit(solution)/shard_map/jit(_take)/gather | solution.py:50
  61.3 3.2 %convolution_bitcast_fusion = f32[128,64,128]{2,0,1:T(8,128)S(1)} fusion(bf16[64,128,128]{2,1,0:T(8,128)(2,1)} %param.10, bf16[64,128,128]{2,1,0:T(8,128)(2,1)} %gather_fusion.1, pred[64]{0:T(512)(128)(4,1)S(1)} %compare_and_fusion.1), kind=kOutput, calls=%fused_computation.8 | convolution fusion | flops 269484032 | bytes 8388672 | tf_op jit(solution)/shard_map/tmk,mkn->tmn/dot_general | solution.py:51
  64.5 4.5 %fusion.14 = bf16[128,32,128]{2,1,0:T(8,128)(2,1)S(1)} fusion(f32[128,64,128]{2,0,1:T(8,128)S(1)} %convolution_bitcast_fusion, f32[64]{0:T(128)S(1)} %compare_convert_fusion.1, s32[64]{0:T(128)S(1)} %slice_bitcast_fusion.1), kind=kOutput, calls=%fused_computation.21 | convolution fusion | flops 403181568 | bytes 5243392 | tf_op jit(solution)/shard_map/tmn,mo->ton/dot_general | solution.py:54
  69.0 1.3 %convert_element_type.69 = bf16[16,8,4096]{2,1,0:T(8,128)(2,1)} reshape(bf16[128,32,128]{2,1,0:T(8,128)(2,1)S(1)} %fusion.14) | data formatting | bytes 2097152 | tf_op jit(solution)/shard_map/convert_element_type | solution.py:56
  70.3 6.4 %all-to-all-start.1 = ((bf16[16,8,4096]{2,1,0:T(8,128)(2,1)}), bf16[16,8,4096]{2,1,0:T(8,128)(2,1)S(1)}, u32[]{:S(2)}, u32[]{:S(2)}) async-start(bf16[16,8,4096]{2,1,0:T(8,128)(2,1)} %convert_element_type.69), calls=%async_computation.1 | async-start | bytes 2097152 | tf_op jit(solution)/shard_map/all_to_all | solution.py:57
  76.7 3.5 %constant_dynamic-slice_fusion = f32[8,4096]{0,1:T(8,128)} fusion(f32[128,4096]{0,1:T(8,128)} %bitcast.60, s32[]{:T(128)S(6)} %select_n.50), kind=kLoop, calls=%fused_computation.60 | loop fusion | bytes 262148 | tf_op jit(solution)/shard_map/dynamic_slice | solution.py:59
  80.2 2.2 %copy.25 = f32[8,4096]{1,0:T(8,128)S(1)} copy(f32[8,4096]{0,1:T(8,128)} %constant_dynamic-slice_fusion) | data formatting | bytes 262144
  82.4 18.8 %all-to-all-done.1 = bf16[16,8,4096]{2,1,0:T(8,128)(2,1)S(1)} async-done(((bf16[16,8,4096]{2,1,0:T(8,128)(2,1)}), bf16[16,8,4096]{2,1,0:T(8,128)(2,1)S(1)}, u32[]{:S(2)}, u32[]{:S(2)}) %all-to-all-start.1) | async-done | bytes 1048608 | tf_op jit(solution)/shard_map/all_to_all | solution.py:57
  101.2 0.1 convert_reduce_fusion
  101.3 18.6 %all_to_all.15 = bf16[8,16,256]{2,0,1:T(8,128)(2,1)S(1)} all-to-all(bf16[8,16,256]{2,0,1:T(8,128)(2,1)S(1)} %bitcast.61), channel_id=1, replica_groups=mesh['ctx'=16,'tp'=16] {'ctx'}, dimensions={1} | all-to-all | bytes 131072 | tf_op jit(solution)/shard_map/all_to_all | solution.py:61
  120.0 0.6 copy.23
  (18 shorter events, 0.1 us)
Async XLA Ops:
  0.0 46.8 %copy-start = (bf16[64,128,128]{2,1,0:T(8,128)(2,1)S(1)}, bf16[64,128,128]{2,1,0:T(8,128)(2,1)}, u32[]{:S(2)}) copy-start(bf16[64,128,128]{2,1,0:T(8,128)(2,1)} %param.8) | copy-start | bytes 6291460
  0.0 12.4 %copy-start.3 = (s32[2,1]{0,1:T(1,128)S(1)}, s32[2,1]{0,1:T(1,128)}, u32[]{:S(2)}) copy-start(s32[2,1]{0,1:T(1,128)} %param.13) | copy-start | bytes 28
  0.0 14.3 %copy-start.4 = (s32[2,64]{1,0:T(2,128)S(1)}, s32[2,64]{1,0:T(2,128)}, u32[]{:S(2)}) copy-start(s32[2,64]{1,0:T(2,128)} %param.11) | copy-start | bytes 1540
  0.0 14.4 %copy-start.5 = (s32[2,64]{1,0:T(2,128)S(1)}, s32[2,64]{1,0:T(2,128)}, u32[]{:S(2)}) copy-start(s32[2,64]{1,0:T(2,128)} %param.12) | copy-start | bytes 1540
  2.3 35.4 %all-to-all-start = ((bf16[16,128,256]{1,2,0:T(8,128)(2,1)}), bf16[16,128,256]{1,2,0:T(8,128)(2,1)S(1)}, u32[]{:S(2)}, u32[]{:S(2)}) async-start(bf16[16,128,256]{1,2,0:T(8,128)(2,1)} %broadcast_in_dim.38), calls=%async_computation | async-start | bytes 2097152 | tf_op jit(solution)/shard_map/all_to_all | solution.py:14
  46.8 2.5 %copy-start.1 = (bf16[64,128,128]{2,1,0:T(8,128)(2,1)S(1)}, bf16[64,128,128]{2,1,0:T(8,128)(2,1)}, u32[]{:S(2)}) copy-start(bf16[64,128,128]{2,1,0:T(8,128)(2,1)} %gather_fusion) | copy-start | bytes 6291460
  46.8 2.9 %copy-start.2 = (bf16[64,128,128]{2,1,0:T(8,128)(2,1)S(1)}, bf16[64,128,128]{2,1,0:T(8,128)(2,1)}, u32[]{:S(2)}) copy-start(bf16[64,128,128]{2,1,0:T(8,128)(2,1)} %param.9) | copy-start | bytes 6291460
  70.3 30.8 %all-to-all-start.1 = ((bf16[16,8,4096]{2,1,0:T(8,128)(2,1)}), bf16[16,8,4096]{2,1,0:T(8,128)(2,1)S(1)}, u32[]{:S(2)}, u32[]{:S(2)}) async-start(bf16[16,8,4096]{2,1,0:T(8,128)(2,1)} %convert_element_type.69), calls=%async_computation.1 | async-start | bytes 2097152 | tf_op jit(solution)/shard_map/all_to_all | solution.py:57

commit v2 on v1

v2 whole, which is shorter than its diff:
```python
import jax
import jax.numpy as jnp
from jax import lax
from jax.experimental import pallas as pl
from jax.experimental.pallas import tpu as pltpu
from jax.sharding import PartitionSpec as P

FF = 16384


def ffn_kernel(cnt_ref, gu_ref, dn_ref, pieces_ref, g_ref, u_ref, d_ref, out_ref,
               normed_s, accg_s, accu_s, hid_s, acco_s):
    n_src, rows, width = pieces_ref.shape
    tile = g_ref.shape[1]
    per_src = width // tile
    feat = n_src * width
    ss = jnp.zeros((rows, 1), jnp.float32)
    for s in range(n_src):
        x = pieces_ref[s].astype(jnp.float32)
        ss = ss + jnp.sum(x * x, axis=1, keepdims=True)
    scale = lax.rsqrt(ss / feat + 1e-05)
    for s in range(n_src):
        for h in range(per_src):
            x = pieces_ref[s, :, h * tile:(h + 1) * tile].astype(jnp.float32)
            normed_s[s * per_src + h] = (x * scale).astype(jnp.bfloat16)
    accg_s[...] = jnp.zeros(accg_s.shape, jnp.float32)
    accu_s[...] = jnp.zeros(accu_s.shape, jnp.float32)

    def gu_body(m, carry):
        x = normed_s[gu_ref[0, m]]
        h = gu_ref[1, m]
        accg_s[h] += jnp.dot(x, g_ref[m], preferred_element_type=jnp.float32)
        accu_s[h] += jnp.dot(x, u_ref[m], preferred_element_type=jnp.float32)
        return carry

    lax.fori_loop(0, cnt_ref[0], gu_body, 0)
    g = accg_s[...]
    hid_s[...] = (g / (1.0 + jnp.exp(-g)) * accu_s[...]).astype(jnp.bfloat16)
    acco_s[...] = jnp.zeros(acco_s.shape, jnp.float32)

    def dn_body(m, carry):
        o = dn_ref[1, m]
        acco_s[o] += jnp.dot(hid_s[dn_ref[0, m]], d_ref[m], preferred_element_type=jnp.float32)
        return carry

    lax.fori_loop(0, cnt_ref[1], dn_body, 0)
    out_ref[...] = acco_s[...].astype(out_ref.dtype)


def ffn(counts, gu_blocks, down_blocks, pieces, gate_tiles, up_tiles, down_tiles, hid_blocks, out_dtype):
    n_src, rows, width = pieces.shape
    tile = gate_tiles.shape[1]
    in_blocks = n_src * width // tile
    smem = pl.BlockSpec(memory_space=pltpu.SMEM)
    vmem = pl.BlockSpec(memory_space=pltpu.VMEM)
    return pl.pallas_call(
        ffn_kernel,
        out_shape=jax.ShapeDtypeStruct((in_blocks, rows, tile), out_dtype),
        in_specs=[smem, smem, smem, vmem, vmem, vmem, vmem],
        out_specs=vmem,
        scratch_shapes=[
            pltpu.VMEM((in_blocks, rows, tile), jnp.bfloat16),
            pltpu.VMEM((hid_blocks, rows, tile), jnp.float32),
            pltpu.VMEM((hid_blocks, rows, tile), jnp.float32),
            pltpu.VMEM((hid_blocks, rows, tile), jnp.bfloat16),
            pltpu.VMEM((in_blocks, rows, tile), jnp.float32),
        ],
    )(counts.reshape(-1), gu_blocks, down_blocks, pieces, gate_tiles, up_tiles, down_tiles)


def per_device(tokens, gate_tiles, up_tiles, down_tiles, gu_blocks, down_blocks, counts):
    tp_count = lax.axis_size("tp")
    ctx_count = lax.axis_size("ctx")
    own_rows, own_width = tokens.shape
    copies = jnp.broadcast_to(tokens[None], (tp_count, own_rows, own_width))
    pieces = lax.all_to_all(copies, "tp", 0, 0, tiled=True)
    tile = gate_tiles.shape[1]
    feat_width = tp_count * own_width
    in_blocks = feat_width // tile
    hid_blocks = FF // tp_count // tile
    partial = ffn(counts, gu_blocks, down_blocks, pieces, gate_tiles, up_tiles, down_tiles,
                  hid_blocks, jnp.bfloat16)
    share = own_rows // tp_count
    outgoing = partial.reshape(in_blocks, tp_count, share, tile).transpose(1, 2, 0, 3)
    incoming = lax.all_to_all(outgoing.reshape(tp_count, share, feat_width), "tp", 0, 0, tiled=True)
    total = jnp.sum(incoming.astype(jnp.float32), axis=0)
    own = lax.dynamic_slice_in_dim(pieces, lax.axis_index("tp") * share, share, 1)
    residual = jnp.transpose(own, (1, 0, 2)).reshape(share, feat_width).astype(jnp.float32)
    mixed = (total + residual).astype(jnp.bfloat16)
    return lax.all_to_all(
        mixed.reshape(share, ctx_count, feat_width // ctx_count), "ctx", 1, 1, tiled=True
    )


def solution(mesh):
    return jax.shard_map(
        per_device,
        mesh=mesh,
        in_specs=(
            P("ctx", "tp"),
            P("tp", None, None),
            P("tp", None, None),
            P("tp", None, None),
            P(None, "tp"),
            P(None, "tp"),
            P(None, "tp"),
        ),
        out_specs=P("tp", None, "ctx"),
        check_vma=False,
    )
```

time: 121 us -> 113 us (0.934)
  blocking collectives: 18.6 us -> 55.5 us
  matrix products: 19.7 us -> 0 us
  Pallas kernels: 0 us -> 18.1 us
  waiting for transfers between devices: 42.1 us -> 24.5 us
  local copies, waits for them, and re-layouts: 18 us -> 4.77 us
  starting transfers between devices: 16.5 us -> 9.9 us
  other arithmetic: 5.51 us -> 1 us
    all_to_all x0 -> x1, blocking collectives: none -> 36.9 us  [per_device(): pieces = lax.all_to_all(copies, 'tp', 0, 0, tiled=True)]
    dot_general x6 -> x0, matrix products: 19.7 us -> none  [the longest x1 4.52 us: per_device(): jnp.einsum('tmn,mo->ton', products, pick_out, precision=lax.Precision.HIG...]
    pallas_call x0 -> x1, Pallas kernels: none -> 18.1 us  [ffn(): pl.pallas_call(ffn_kernel, out_shape=jax.ShapeDtypeStruct((in_blocks, row...]
    all_to_all x2 -> x1, waiting for transfers between devices: 42.1 us -> 24.5 us  [per_device(): lax.all_to_all(outgoing.reshape(tp_count, share, feat_width), 'tp', 0, 0,...]
    all_to_all x2 -> x1, starting transfers between devices: 16.5 us -> 9.9 us  [per_device(): lax.all_to_all(outgoing.reshape(tp_count, share, feat_width), 'tp', 0, 0,...]
    convert_element_type x4 -> x0, other arithmetic: 4.75 us -> none  [the longest x1 1.93 us: per_device(): normed = (widened * lax.rsqrt(squares + 1e-05)).astype(jnp.bfloat16)]
    gather x2 -> x0, local copies, waits for them, and re-layouts: 4.23 us -> none  [the longest x1 2.12 us: hidden_block(): chosen = jnp.take(row_tiles, gu_blocks[0], axis=1)]
    convert_element_type x3 -> x0, local copies, waits for them, and re-layouts: 4.21 us -> none  [the longest x1 2.89 us: per_device(): widened = gathered.astype(jnp.float32)]
  transfers between devices with their start and end apart: 2 -> 1, of which waited for: 2 -> 1; matrix products, arithmetic and copies ran while one was open for 6% -> 0% of each run, Pallas kernels for 0% -> 0%
where the time goes in v2:
time: 113 us; the launch traced here: 114 us
  blocking collectives  55.5 us (49%)
  waiting for transfers between devices  24.5 us (22%)
  Pallas kernels  18.1 us (16%)
  starting transfers between devices  9.9 us (9%)
  local copies, waits for them, and re-layouts  4.77 us (4%)
    all_to_all x1, blocking collectives, per_device(): pieces = lax.all_to_all(copies, 'tp', 0, 0, tiled=True)  36.9 us
    all_to_all x1, waiting for transfers between devices, per_device(): lax.all_to_all(outgoing.reshape(tp_count, share, feat_width), 'tp', 0, 0,...  24.5 us
    all_to_all x1, blocking collectives, per_device(): lax.all_to_all(mixed.reshape(share, ctx_count, feat_width // ctx_count),...  18.6 us
    pallas_call x1, Pallas kernels, ffn(): pl.pallas_call(ffn_kernel, out_shape=jax.ShapeDtypeStruct((in_blocks, row...  18.1 us
    all_to_all x1, starting transfers between devices, per_device(): lax.all_to_all(outgoing.reshape(tp_count, share, feat_width), 'tp', 0, 0,...  9.9 us
  transfers between devices with their start and end apart: 1, of which 1 were waited for; matrix products, arithmetic and copies ran while one was open for 0% of the time, Pallas kernels for 0%

profile of v2, /device:TPU:1, one launch (start us, length us, event | category | flops | bytes accessed | tf_op | source)
XLA Modules:
  0.0 113.8 jit_solution(13636039651847488587)
XLA Ops:
  0.0 0.9 broadcast_in_dim.2
  0.9 36.9 %all_to_all.15.pieces_ref = bf16[16,128,256]{2,1,0:T(8,128)(2,1)} all-to-all(bf16[16,128,256]{2,1,0:T(8,128)(2,1)S(1)} %broadcast_in_dim.2), channel_id=1, replica_groups=mesh['ctx'=16,'tp'=16] {'tp'}, dimensions={0} | all-to-all | bytes 2097152 | tf_op jit(solution)/shard_map/all_to_all | solution.py:76
  37.8 18.1 %shard_map.73 = bf16[32,128,128]{2,1,0:T(8,128)(2,1)} custom-call(s32[2]{0:T(128)} %bitcast.15, s32[2,64]{1,0:T(2,128)} %gu_ref.1, s32[2,64]{1,0:T(2,128)} %dn_ref.1, bf16[16,128,256]{2,1,0:T(8,128)(2,1)} %all_to_all.15.pieces_ref, bf16[64,128,128]{2,1,0:T(8,128)(2,1)} %g_ref.1, bf16[64,128,128]{2,1,0:T(8,128)(2,1)} %u_ref.1, bf16[64,128,128]{2,1,0:T(8,128)(2,1)} %d_ref.1), custom_call_target="tpu_custom_call" | custom-call | tf_op jit(solution)/shard_map/pallas_call | solution.py:56
  56.0 1.9 %copy.12 = bf16[32,16,8,128]{3,0,2,1:T(8,128)(2,1)S(1)} copy(bf16[32,16,8,128]{3,2,1,0:T(8,128)(2,1)} %bitcast.12) | data formatting | bytes 2097152 | tf_op jit(solution)/shard_map/reshape | solution.py:84
  57.9 1.3 %reshape.15 = bf16[16,8,4096]{2,1,0:T(8,128)(2,1)} reshape(bf16[16,8,32,128]{3,2,1,0:T(8,128)(2,1)S(1)} %bitcast.13) | data formatting | bytes 2097152 | tf_op jit(solution)/shard_map/reshape | solution.py:85
  59.2 9.9 %all-to-all-start.1 = ((bf16[16,8,4096]{2,1,0:T(8,128)(2,1)}), bf16[16,8,4096]{2,1,0:T(8,128)(2,1)S(1)}, u32[]{:S(2)}, u32[]{:S(2)}) async-start(bf16[16,8,4096]{2,1,0:T(8,128)(2,1)} %reshape.15), calls=%async_computation.1 | async-start | bytes 2097152 | tf_op jit(solution)/shard_map/all_to_all | solution.py:85
  69.1 24.5 %all-to-all-done.1 = bf16[16,8,4096]{2,1,0:T(8,128)(2,1)S(1)} async-done(((bf16[16,8,4096]{2,1,0:T(8,128)(2,1)}), bf16[16,8,4096]{2,1,0:T(8,128)(2,1)S(1)}, u32[]{:S(2)}, u32[]{:S(2)}) %all-to-all-start.1) | async-done | bytes 1048608 | tf_op jit(solution)/shard_map/all_to_all | solution.py:85
  93.5 0.1 convert_reduce_fusion
  93.7 0.9 fusion
  94.5 18.6 %all_to_all.16 = bf16[8,16,256]{2,0,1:T(8,128)(2,1)S(1)} all-to-all(bf16[8,16,256]{2,0,1:T(8,128)(2,1)S(1)} %fusion), channel_id=1, replica_groups=mesh['ctx'=16,'tp'=16] {'ctx'}, dimensions={1} | all-to-all | bytes 131072 | tf_op jit(solution)/shard_map/all_to_all | solution.py:90
  113.2 0.6 copy.10
Async XLA Ops:
  59.2 34.4 %all-to-all-start.1 = ((bf16[16,8,4096]{2,1,0:T(8,128)(2,1)}), bf16[16,8,4096]{2,1,0:T(8,128)(2,1)S(1)}, u32[]{:S(2)}, u32[]{:S(2)}) async-start(bf16[16,8,4096]{2,1,0:T(8,128)(2,1)} %reshape.15), calls=%async_computation.1 | async-start | bytes 2097152 | tf_op jit(solution)/shard_map/all_to_all | solution.py:85

commit v3 on v2

--- a/solution.py
+++ b/solution.py
@@ -6,6 +6,7 @@
 from jax.sharding import PartitionSpec as P
 
 FF = 16384
+Y_LO = 2
 
 
 def ffn_kernel(cnt_ref, gu_ref, dn_ref, pieces_ref, g_ref, u_ref, d_ref, out_ref,
@@ -68,29 +69,53 @@
     )(counts.reshape(-1), gu_blocks, down_blocks, pieces, gate_tiles, up_tiles, down_tiles)
 
 
+def ring_pairs(count, step):
+    return [(i, ((i // Y_LO + step) % count) * Y_LO + i % Y_LO) for i in range(count * Y_LO)]
+
+
 def per_device(tokens, gate_tiles, up_tiles, down_tiles, gu_blocks, down_blocks, counts):
     tp_count = lax.axis_size("tp")
     ctx_count = lax.axis_size("ctx")
+    z_count = tp_count // Y_LO
     own_rows, own_width = tokens.shape
-    copies = jnp.broadcast_to(tokens[None], (tp_count, own_rows, own_width))
-    pieces = lax.all_to_all(copies, "tp", 0, 0, tiled=True)
     tile = gate_tiles.shape[1]
+    per_src = own_width // tile
+    me = lax.axis_index("tp")
+    my_z = me // Y_LO
+    my_y = me % Y_LO
+    partner = lax.ppermute(tokens, "tp", [(i, i ^ 1) for i in range(tp_count)])
+    both = jnp.where(my_y == 0, jnp.stack([tokens, partner]), jnp.stack([partner, tokens]))
+    ahead, behind = [], []
+    fwd = bwd = both
+    for k in range(1, z_count // 2 + 1):
+        fwd = lax.ppermute(fwd, "tp", ring_pairs(z_count, 1))
+        ahead.append(fwd)
+        if k < z_count - z_count // 2:
+            bwd = lax.ppermute(bwd, "tp", ring_pairs(z_count, -1))
+            behind.append(bwd)
+    pieces = jnp.concatenate([both] + ahead + behind)
+    src_ids = jnp.arange(tp_count)
+    dz = (src_ids // Y_LO - my_z) % z_count
+    slot_of_z = jnp.where(dz == 0, 0, jnp.where(dz >= z_count // 2, z_count - dz, z_count // 2 + dz))
+    position = slot_of_z * Y_LO + src_ids % Y_LO
+    in_tile = gu_blocks[0]
+    moved = position[in_tile // per_src] * per_src + in_tile % per_src
+    gu_local = jnp.stack([moved, gu_blocks[1]])
     feat_width = tp_count * own_width
     in_blocks = feat_width // tile
     hid_blocks = FF // tp_count // tile
-    partial = ffn(counts, gu_blocks, down_blocks, pieces, gate_tiles, up_tiles, down_tiles,
+    partial = ffn(counts, gu_local, down_blocks, pieces, gate_tiles, up_tiles, down_tiles,
                   hid_blocks, jnp.bfloat16)
     share = own_rows // tp_count
     outgoing = partial.reshape(in_blocks, tp_count, share, tile).transpose(1, 2, 0, 3)
     incoming = lax.all_to_all(outgoing.reshape(tp_count, share, feat_width), "tp", 0, 0, tiled=True)
     total = jnp.sum(incoming.astype(jnp.float32), axis=0)
-    own = lax.dynamic_slice_in_dim(pieces, lax.axis_index("tp") * share, share, 1)
+    own = jnp.take(lax.dynamic_slice_in_dim(pieces, me * share, share, 1), position, axis=0)
     residual = jnp.transpose(own, (1, 0, 2)).reshape(share, feat_width).astype(jnp.float32)
     mixed = (total + residual).astype(jnp.bfloat16)
     return lax.all_to_all(
         mixed.reshape(share, ctx_count, feat_width // ctx_count), "ctx", 1, 1, tiled=True
     )
-
 
 def solution(mesh):
     return jax.shard_map(

time: 113 us -> 103 us (0.912); the launches traced: 114 us -> 102 us
  blocking collectives: 55.5 us -> 22.7 us
  starting transfers between devices: 9.9 us -> 22.7 us
  waiting for transfers between devices: 24.5 us -> 29.7 us
  local copies, waits for them, and re-layouts: 4.77 us -> 7.05 us
  other arithmetic: 1 us -> 3.27 us
  Pallas kernels: 18.1 us -> 16.6 us
    all_to_all x1 -> x0, blocking collectives: 36.9 us -> none  [per_device(): pieces = lax.all_to_all(copies, 'tp', 0, 0, tiled=True)]
    ppermute x0 -> x8, starting transfers between devices: none -> 13.8 us  [the longest x3 9.77 us: per_device(): bwd = lax.ppermute(bwd, 'tp', ring_pairs(z_count, -1))]
    ppermute x0 -> x8, waiting for transfers between devices: none -> 11.3 us  [the longest x4 10.1 us: per_device(): fwd = lax.ppermute(fwd, 'tp', ring_pairs(z_count, 1))]
    all_to_all x1, waiting for transfers between devices: 24.5 us -> 18.5 us  [per_device(): lax.all_to_all(outgoing.reshape(tp_count, share, feat_width), 'tp', 0, 0,...]
    all_to_all x1, blocking collectives: 18.6 us -> 22.7 us  [per_device(): lax.all_to_all(mixed.reshape(share, ctx_count, feat_width // ctx_count),...]
    pallas_call x1, Pallas kernels: 18.1 us -> 16.6 us  [ffn(): pl.pallas_call(ffn_kernel, out_shape=jax.ShapeDtypeStruct((in_blocks, row...]
    gather x0 -> x2, local copies, waits for them, and re-layouts: none -> 1.33 us  [the longest x1 0.78 us: per_device(): moved = position[in_tile // per_src] * per_src + in_tile % per_src]
  transfers between devices with their start and end apart: 1 -> 9, of which waited for: 1 -> 6; matrix products, arithmetic and copies ran while one was open for 0% -> 4% of each run, Pallas kernels for 0% -> 0%
where the time goes in v3:
time: 103 us; the launch traced here: 102 us
  waiting for transfers between devices  29.7 us (29%)
  starting transfers between devices  22.7 us (22%)
  blocking collectives  22.7 us (22%)
  Pallas kernels  16.6 us (16%)
  local copies, waits for them, and re-layouts  7.05 us (7%)
  other arithmetic  3.27 us (3%)
    all_to_all x1, blocking collectives, per_device(): lax.all_to_all(mixed.reshape(share, ctx_count, feat_width // ctx_count),...  22.7 us
    all_to_all x1, waiting for transfers between devices, per_device(): lax.all_to_all(outgoing.reshape(tp_count, share, feat_width), 'tp', 0, 0,...  18.5 us
    pallas_call x1, Pallas kernels, ffn(): pl.pallas_call(ffn_kernel, out_shape=jax.ShapeDtypeStruct((in_blocks, row...  16.6 us
    ppermute x4, waiting for transfers between devices, per_device(): fwd = lax.ppermute(fwd, 'tp', ring_pairs(z_count, 1))  10.1 us
    ppermute x3, starting transfers between devices, per_device(): bwd = lax.ppermute(bwd, 'tp', ring_pairs(z_count, -1))  9.77 us
    all_to_all x1, starting transfers between devices, per_device(): lax.all_to_all(outgoing.reshape(tp_count, share, feat_width), 'tp', 0, 0,...  8.96 us
    ppermute x1, starting transfers between devices, per_device(): partner = lax.ppermute(tokens, 'tp', [(i, i ^ 1) for i in range(tp_count)])  2.13 us
  transfers between devices with their start and end apart: 9, of which 6 were waited for; matrix products, arithmetic and copies ran while one was open for 4% of the time, Pallas kernels for 0%

profile of v3, /device:TPU:1, one launch (start us, length us, event | category | flops | bytes accessed | tf_op | source)
XLA Modules:
  0.0 102.2 jit_solution(8310500218460840330)
XLA Ops:
  0.0 2.1 %collective-permute-start = (bf16[128,256]{1,0:T(8,128)(2,1)}, bf16[128,256]{1,0:T(8,128)(2,1)S(1)}, u32[]{:S(2)}, u32[]{:S(2)}) collective-permute-start(bf16[128,256]{1,0:T(8,128)(2,1)} %param.7), channel_id=1, source_target_pairs={{0,1},{1,0},{2,3},{3,2},{4,5},{5,4},{6,7},{7,6},{8,9},{9,8},{10,11... | collective-permute-start | bytes 196616 | tf_op jit(solution)/shard_map/ppermute | solution.py:86
  2.1 0.7 fusion.11
  2.8 1.2 %collective-permute-done = bf16[128,256]{1,0:T(8,128)(2,1)S(1)} collective-permute-done((bf16[128,256]{1,0:T(8,128)(2,1)}, bf16[128,256]{1,0:T(8,128)(2,1)S(1)}, u32[]{:S(2)}, u32[]{:S(2)}) %collective-permute-start) | collective-permute-done | bytes 65568 | tf_op jit(solution)/shard_map/ppermute | solution.py:86
  4.0 0.9 constant_dynamic-update-slice_fusion.7
  4.9 1.9 %collective-permute-start.1 = (bf16[2,128,256]{2,1,0:T(8,128)(2,1)S(1)}, bf16[2,128,256]{2,1,0:T(8,128)(2,1)S(1)}, u32[]{:S(2)}, u32[]{:S(2)}) collective-permute-start(bf16[2,128,256]{2,1,0:T(8,128)(2,1)S(1)} %get-tuple-element.6), channel_id=1, source_target_pairs={{0,2},{1,3},{2,4},{3,5},{4,6},{5,7},{6,8},{7,9},{8,10},{9,11},{10,... | collective-permute-start | bytes 393224 | tf_op jit(solution)/shard_map/ppermute | solution.py:91
  6.8 0.8 gather_fusion
  7.6 4.0 %collective-permute-start.5 = (bf16[2,128,256]{2,1,0:T(8,128)(2,1)S(1)}, bf16[2,128,256]{2,1,0:T(8,128)(2,1)S(1)}, u32[]{:S(2)}, u32[]{:S(2)}) collective-permute-start(bf16[2,128,256]{2,1,0:T(8,128)(2,1)S(1)} %get-tuple-element.6), channel_id=1, source_target_pairs={{0,14},{1,15},{2,0},{3,1},{4,2},{5,3},{6,4},{7,5},{8,6},{9,7},{10,... | collective-permute-start | bytes 393224 | tf_op jit(solution)/shard_map/ppermute | solution.py:94
  11.6 1.5 %collective-permute-done.1 = bf16[2,128,256]{2,1,0:T(8,128)(2,1)S(1)} collective-permute-done((bf16[2,128,256]{2,1,0:T(8,128)(2,1)S(1)}, bf16[2,128,256]{2,1,0:T(8,128)(2,1)S(1)}, u32[]{:S(2)}, u32[]{:S(2)}) %collective-permute-start.1) | collective-permute-done | bytes 131104 | tf_op jit(solution)/shard_map/ppermute | solution.py:91
  13.1 0.0 collective-permute-start.2
  13.1 0.8 fusion.3
  13.9 0.0 collective-permute-done.5
  13.9 2.8 %collective-permute-start.6 = (bf16[2,128,256]{2,1,0:T(8,128)(2,1)S(1)}, bf16[2,128,256]{2,1,0:T(8,128)(2,1)S(1)}, u32[]{:S(2)}, u32[]{:S(2)}) collective-permute-start(bf16[2,128,256]{2,1,0:T(8,128)(2,1)S(1)} %collective-permute-done.5), channel_id=1, source_target_pairs={{0,14},{1,15},{2,0},{3,1},{4,2},{5,3},{6,4},{7,5},{8,6},{9,7},{10,... | collective-permute-start | bytes 393224 | tf_op jit(solution)/shard_map/ppermute | solution.py:94
  16.7 1.5 %collective-permute-done.2 = bf16[2,128,256]{2,1,0:T(8,128)(2,1)S(1)} collective-permute-done((bf16[2,128,256]{2,1,0:T(8,128)(2,1)S(1)}, bf16[2,128,256]{2,1,0:T(8,128)(2,1)S(1)}, u32[]{:S(2)}, u32[]{:S(2)}) %collective-permute-start.2) | collective-permute-done | bytes 131104 | tf_op jit(solution)/shard_map/ppermute | solution.py:91
  18.1 0.0 collective-permute-start.3
  18.2 0.6 pad_add_fusion.gu_ref
  18.7 0.0 collective-permute-done.6
  18.7 3.0 %collective-permute-start.7 = (bf16[2,128,256]{2,1,0:T(8,128)(2,1)S(1)}, bf16[2,128,256]{2,1,0:T(8,128)(2,1)S(1)}, u32[]{:S(2)}, u32[]{:S(2)}) collective-permute-start(bf16[2,128,256]{2,1,0:T(8,128)(2,1)S(1)} %collective-permute-done.6), channel_id=1, source_target_pairs={{0,14},{1,15},{2,0},{3,1},{4,2},{5,3},{6,4},{7,5},{8,6},{9,7},{10,... | collective-permute-start | bytes 393224 | tf_op jit(solution)/shard_map/ppermute | solution.py:94
  21.7 1.5 %collective-permute-done.3 = bf16[2,128,256]{2,1,0:T(8,128)(2,1)S(1)} collective-permute-done((bf16[2,128,256]{2,1,0:T(8,128)(2,1)S(1)}, bf16[2,128,256]{2,1,0:T(8,128)(2,1)S(1)}, u32[]{:S(2)}, u32[]{:S(2)}) %collective-permute-start.3) | collective-permute-done | bytes 131104 | tf_op jit(solution)/shard_map/ppermute | solution.py:91
  23.2 0.0 collective-permute-start.4
  23.2 5.7 %collective-permute-done.4 = bf16[2,128,256]{2,1,0:T(8,128)(2,1)S(1)} collective-permute-done((bf16[2,128,256]{2,1,0:T(8,128)(2,1)S(1)}, bf16[2,128,256]{2,1,0:T(8,128)(2,1)S(1)}, u32[]{:S(2)}, u32[]{:S(2)}) %collective-permute-start.4) | collective-permute-done | bytes 131104 | tf_op jit(solution)/shard_map/ppermute | solution.py:91
  29.0 1.0 copy-done
  29.9 16.6 %shard_map.73 = bf16[32,128,128]{2,1,0:T(8,128)(2,1)} custom-call(s32[2]{0:T(128)} %bitcast.35, s32[2,64]{1,0:T(2,128)} %pad_add_fusion.gu_ref, s32[2,64]{1,0:T(2,128)} %dn_ref.1, bf16[16,128,256]{2,1,0:T(8,128)(2,1)} %copy-done, bf16[64,128,128]{2,1,0:T(8,128)(2,1)} %g_ref.1, bf16[64,128,128]{2,1,0:T(8,128)(2,1)} %u_ref.1, bf16[64,128,128]{2,1,0:T(8,128)(2,1)} %d_ref.1), custom_call_target="tpu_custom_call" | custom-call | tf_op jit(solution)/shard_map/pallas_call | solution.py:57
  46.6 1.9 %copy.12 = bf16[32,16,8,128]{3,0,2,1:T(8,128)(2,1)S(1)} copy(bf16[32,16,8,128]{3,2,1,0:T(8,128)(2,1)} %bitcast.30) | data formatting | bytes 2097152 | tf_op jit(solution)/shard_map/reshape | solution.py:110
  48.5 1.3 %reshape.225 = bf16[16,8,4096]{2,1,0:T(8,128)(2,1)} reshape(bf16[16,8,32,128]{3,2,1,0:T(8,128)(2,1)S(1)} %bitcast.31) | data formatting | bytes 2097152 | tf_op jit(solution)/shard_map/reshape | solution.py:111
  49.7 9.0 %all-to-all-start = ((bf16[16,8,4096]{2,1,0:T(8,128)(2,1)}), bf16[16,8,4096]{2,1,0:T(8,128)(2,1)S(1)}, u32[]{:S(2)}, u32[]{:S(2)}) async-start(bf16[16,8,4096]{2,1,0:T(8,128)(2,1)} %reshape.225), calls=%async_computation | async-start | bytes 2097152 | tf_op jit(solution)/shard_map/all_to_all | solution.py:111
  58.8 0.9 constant_dynamic-slice_fusion
  59.6 0.6 gather_fusion.1
  60.2 18.5 %all-to-all-done = bf16[16,8,4096]{2,1,0:T(8,128)(2,1)S(1)} async-done(((bf16[16,8,4096]{2,1,0:T(8,128)(2,1)}), bf16[16,8,4096]{2,1,0:T(8,128)(2,1)S(1)}, u32[]{:S(2)}, u32[]{:S(2)}) %all-to-all-start) | async-done | bytes 1048608 | tf_op jit(solution)/shard_map/all_to_all | solution.py:111
  78.7 0.1 convert_reduce_fusion
  78.8 0.1 fusion
  78.9 22.7 %all_to_all.10 = bf16[8,16,256]{2,0,1:T(8,128)(2,1)S(1)} all-to-all(bf16[8,16,256]{2,0,1:T(8,128)(2,1)S(1)} %fusion), channel_id=1, replica_groups=mesh['ctx'=16,'tp'=16] {'ctx'}, dimensions={1} | all-to-all | bytes 131072 | tf_op jit(solution)/shard_map/all_to_all | solution.py:116
  101.6 0.6 copy.10
  (14 shorter events, 0.1 us)
Async XLA Ops:
  0.0 4.0 %collective-permute-start = (bf16[128,256]{1,0:T(8,128)(2,1)}, bf16[128,256]{1,0:T(8,128)(2,1)S(1)}, u32[]{:S(2)}, u32[]{:S(2)}) collective-permute-start(bf16[128,256]{1,0:T(8,128)(2,1)} %param.7), channel_id=1, source_target_pairs={{0,1},{1,0},{2,3},{3,2},{4,5},{5,4},{6,7},{7,6},{8,9},{9,8},{10,11... | collective-permute-start | bytes 196616 | tf_op jit(solution)/shard_map/ppermute | solution.py:86
  4.9 8.2 %collective-permute-start.1 = (bf16[2,128,256]{2,1,0:T(8,128)(2,1)S(1)}, bf16[2,128,256]{2,1,0:T(8,128)(2,1)S(1)}, u32[]{:S(2)}, u32[]{:S(2)}) collective-permute-start(bf16[2,128,256]{2,1,0:T(8,128)(2,1)S(1)} %get-tuple-element.6), channel_id=1, source_target_pairs={{0,2},{1,3},{2,4},{3,5},{4,6},{5,7},{6,8},{7,9},{8,10},{9,11},{10,... | collective-permute-start | bytes 393224 | tf_op jit(solution)/shard_map/ppermute | solution.py:91
  7.6 6.3 %collective-permute-start.5 = (bf16[2,128,256]{2,1,0:T(8,128)(2,1)S(1)}, bf16[2,128,256]{2,1,0:T(8,128)(2,1)S(1)}, u32[]{:S(2)}, u32[]{:S(2)}) collective-permute-start(bf16[2,128,256]{2,1,0:T(8,128)(2,1)S(1)} %get-tuple-element.6), channel_id=1, source_target_pairs={{0,14},{1,15},{2,0},{3,1},{4,2},{5,3},{6,4},{7,5},{8,6},{9,7},{10,... | collective-permute-start | bytes 393224 | tf_op jit(solution)/shard_map/ppermute | solution.py:94
  13.1 5.0 %collective-permute-start.2 = (bf16[2,128,256]{2,1,0:T(8,128)(2,1)S(1)}, bf16[2,128,256]{2,1,0:T(8,128)(2,1)S(1)}, u32[]{:S(2)}, u32[]{:S(2)}) collective-permute-start(bf16[2,128,256]{2,1,0:T(8,128)(2,1)S(1)} %collective-permute-done.1), channel_id=1, source_target_pairs={{0,2},{1,3},{2,4},{3,5},{4,6},{5,7},{6,8},{7,9},{8,10},{9,11},{10,... | collective-permute-start | bytes 393224 | tf_op jit(solution)/shard_map/ppermute | solution.py:91
  13.9 4.8 %collective-permute-start.6 = (bf16[2,128,256]{2,1,0:T(8,128)(2,1)S(1)}, bf16[2,128,256]{2,1,0:T(8,128)(2,1)S(1)}, u32[]{:S(2)}, u32[]{:S(2)}) collective-permute-start(bf16[2,128,256]{2,1,0:T(8,128)(2,1)S(1)} %collective-permute-done.5), channel_id=1, source_target_pairs={{0,14},{1,15},{2,0},{3,1},{4,2},{5,3},{6,4},{7,5},{8,6},{9,7},{10,... | collective-permute-start | bytes 393224 | tf_op jit(solution)/shard_map/ppermute | solution.py:94
  18.1 5.0 %collective-permute-start.3 = (bf16[2,128,256]{2,1,0:T(8,128)(2,1)S(1)}, bf16[2,128,256]{2,1,0:T(8,128)(2,1)S(1)}, u32[]{:S(2)}, u32[]{:S(2)}) collective-permute-start(bf16[2,128,256]{2,1,0:T(8,128)(2,1)S(1)} %collective-permute-done.2), channel_id=1, source_target_pairs={{0,2},{1,3},{2,4},{3,5},{4,6},{5,7},{6,8},{7,9},{8,10},{9,11},{10,... | collective-permute-start | bytes 393224 | tf_op jit(solution)/shard_map/ppermute | solution.py:91
  18.7 10.2 %collective-permute-start.7 = (bf16[2,128,256]{2,1,0:T(8,128)(2,1)S(1)}, bf16[2,128,256]{2,1,0:T(8,128)(2,1)S(1)}, u32[]{:S(2)}, u32[]{:S(2)}) collective-permute-start(bf16[2,128,256]{2,1,0:T(8,128)(2,1)S(1)} %collective-permute-done.6), channel_id=1, source_target_pairs={{0,14},{1,15},{2,0},{3,1},{4,2},{5,3},{6,4},{7,5},{8,6},{9,7},{10,... | collective-permute-start | bytes 393224 | tf_op jit(solution)/shard_map/ppermute | solution.py:94
  23.2 5.7 %collective-permute-start.4 = (bf16[2,128,256]{2,1,0:T(8,128)(2,1)S(1)}, bf16[2,128,256]{2,1,0:T(8,128)(2,1)S(1)}, u32[]{:S(2)}, u32[]{:S(2)}) collective-permute-start(bf16[2,128,256]{2,1,0:T(8,128)(2,1)S(1)} %collective-permute-done.3), channel_id=1, source_target_pairs={{0,2},{1,3},{2,4},{3,5},{4,6},{5,7},{6,8},{7,9},{8,10},{9,11},{10,... | collective-permute-start | bytes 393224 | tf_op jit(solution)/shard_map/ppermute | solution.py:91
  29.0 1.0 copy-start
  49.7 28.9 %all-to-all-start = ((bf16[16,8,4096]{2,1,0:T(8,128)(2,1)}), bf16[16,8,4096]{2,1,0:T(8,128)(2,1)S(1)}, u32[]{:S(2)}, u32[]{:S(2)}) async-start(bf16[16,8,4096]{2,1,0:T(8,128)(2,1)} %reshape.225), calls=%async_computation | async-start | bytes 2097152 | tf_op jit(solution)/shard_map/all_to_all | solution.py:111

commit v4 on v3

--- a/solution.py
+++ b/solution.py
@@ -7,6 +7,7 @@
 
 FF = 16384
 Y_LO = 2
+UNROLL = 8
 
 
 def ffn_kernel(cnt_ref, gu_ref, dn_ref, pieces_ref, g_ref, u_ref, d_ref, out_ref,
@@ -30,21 +31,23 @@
     def gu_body(m, carry):
         x = normed_s[gu_ref[0, m]]
         h = gu_ref[1, m]
-        accg_s[h] += jnp.dot(x, g_ref[m], preferred_element_type=jnp.float32)
-        accu_s[h] += jnp.dot(x, u_ref[m], preferred_element_type=jnp.float32)
+        live = (m < cnt_ref[0]).astype(jnp.float32)
+        accg_s[h] += jnp.dot(x, g_ref[m], preferred_element_type=jnp.float32) * live
+        accu_s[h] += jnp.dot(x, u_ref[m], preferred_element_type=jnp.float32) * live
         return carry
 
-    lax.fori_loop(0, cnt_ref[0], gu_body, 0)
+    lax.fori_loop(0, g_ref.shape[0], gu_body, 0, unroll=UNROLL)
     g = accg_s[...]
     hid_s[...] = (g / (1.0 + jnp.exp(-g)) * accu_s[...]).astype(jnp.bfloat16)
     acco_s[...] = jnp.zeros(acco_s.shape, jnp.float32)
 
     def dn_body(m, carry):
         o = dn_ref[1, m]
-        acco_s[o] += jnp.dot(hid_s[dn_ref[0, m]], d_ref[m], preferred_element_type=jnp.float32)
+        live = (m < cnt_ref[1]).astype(jnp.float32)
+        acco_s[o] += jnp.dot(hid_s[dn_ref[0, m]], d_ref[m], preferred_element_type=jnp.float32) * live
         return carry
 
-    lax.fori_loop(0, cnt_ref[1], dn_body, 0)
+    lax.fori_loop(0, d_ref.shape[0], dn_body, 0, unroll=UNROLL)
     out_ref[...] = acco_s[...].astype(out_ref.dtype)
 
 

time: 103 us -> 93.2 us (0.905)
  Pallas kernels: 16.6 us -> 9.43 us
  starting transfers between devices: 22.7 us -> 20.5 us
    pallas_call x1, Pallas kernels: 16.6 us -> 9.43 us  [ffn(): pl.pallas_call(ffn_kernel, out_shape=jax.ShapeDtypeStruct((in_blocks, row...]
    all_to_all x1, starting transfers between devices: 8.96 us -> 6.68 us  [per_device(): lax.all_to_all(outgoing.reshape(tp_count, share, feat_width), 'tp', 0, 0,...]
  transfers between devices with their start and end apart: 9 -> 9, of which waited for: 6 -> 6; matrix products, arithmetic and copies ran while one was open for 4% -> 5% of each run, Pallas kernels for 0% -> 0%
where the time goes in v4:
time: 93.2 us; the launch traced here: 92.8 us
  waiting for transfers between devices  29.6 us (32%)
  blocking collectives  22.9 us (25%)
  starting transfers between devices  20.5 us (22%)
  Pallas kernels  9.43 us (10%)
  local copies, waits for them, and re-layouts  7.05 us (8%)
  other arithmetic  3.27 us (4%)
    all_to_all x1, blocking collectives, per_device(): lax.all_to_all(mixed.reshape(share, ctx_count, feat_width // ctx_count),...  22.9 us
    all_to_all x1, waiting for transfers between devices, per_device(): lax.all_to_all(outgoing.reshape(tp_count, share, feat_width), 'tp', 0, 0,...  18.4 us
    ppermute x4, waiting for transfers between devices, per_device(): fwd = lax.ppermute(fwd, 'tp', ring_pairs(z_count, 1))  10.1 us
    ppermute x3, starting transfers between devices, per_device(): bwd = lax.ppermute(bwd, 'tp', ring_pairs(z_count, -1))  9.77 us
    pallas_call x1, Pallas kernels, ffn(): pl.pallas_call(ffn_kernel, out_shape=jax.ShapeDtypeStruct((in_blocks, row...  9.43 us
    all_to_all x1, starting transfers between devices, per_device(): lax.all_to_all(outgoing.reshape(tp_count, share, feat_width), 'tp', 0, 0,...  6.68 us
    ppermute x1, starting transfers between devices, per_device(): partner = lax.ppermute(tokens, 'tp', [(i, i ^ 1) for i in range(tp_count)])  2.13 us
    reshape x1, local copies, waits for them, and re-layouts, per_device(): partial.reshape(in_blocks, tp_count, share, tile).transpose(1, 2, 0, 3)  1.9 us
  transfers between devices with their start and end apart: 9, of which 6 were waited for; matrix products, arithmetic and copies ran while one was open for 5% of the time, Pallas kernels for 0%

profile of v4, /device:TPU:1, one launch (start us, length us, event | category | flops | bytes accessed | tf_op | source)
XLA Modules:
  0.0 92.8 jit_solution(4820720071902063732)
XLA Ops:
  0.0 2.1 %collective-permute-start = (bf16[128,256]{1,0:T(8,128)(2,1)}, bf16[128,256]{1,0:T(8,128)(2,1)S(1)}, u32[]{:S(2)}, u32[]{:S(2)}) collective-permute-start(bf16[128,256]{1,0:T(8,128)(2,1)} %param.7), channel_id=1, source_target_pairs={{0,1},{1,0},{2,3},{3,2},{4,5},{5,4},{6,7},{7,6},{8,9},{9,8},{10,11... | collective-permute-start | bytes 196616 | tf_op jit(solution)/shard_map/ppermute | solution.py:89
  2.1 0.7 fusion.11
  2.8 1.2 %collective-permute-done = bf16[128,256]{1,0:T(8,128)(2,1)S(1)} collective-permute-done((bf16[128,256]{1,0:T(8,128)(2,1)}, bf16[128,256]{1,0:T(8,128)(2,1)S(1)}, u32[]{:S(2)}, u32[]{:S(2)}) %collective-permute-start) | collective-permute-done | bytes 65568 | tf_op jit(solution)/shard_map/ppermute | solution.py:89
  4.0 0.9 %constant_dynamic-update-slice_fusion.7 = (bf16[16,128,256]{2,1,0:T(8,128)(2,1)S(1)}, bf16[2,128,256]{2,1,0:T(8,128)(2,1)S(1)}) fusion(bf16[1,128,256]{2,1,0:T(8,128)(2,1)} %bitcast.33, bf16[1,128,256]{2,1,0:T(8,128)(2,1)S(1)} %bitcast.34, pred[]{:T(512)S(6)} %eq.25), kind=kLoop, calls=%fused_computation.14 | loop fusion | flops 589823 | bytes 393217
  4.9 1.9 %collective-permute-start.1 = (bf16[2,128,256]{2,1,0:T(8,128)(2,1)S(1)}, bf16[2,128,256]{2,1,0:T(8,128)(2,1)S(1)}, u32[]{:S(2)}, u32[]{:S(2)}) collective-permute-start(bf16[2,128,256]{2,1,0:T(8,128)(2,1)S(1)} %get-tuple-element.6), channel_id=1, source_target_pairs={{0,2},{1,3},{2,4},{3,5},{4,6},{5,7},{6,8},{7,9},{8,10},{9,11},{10,... | collective-permute-start | bytes 393224 | tf_op jit(solution)/shard_map/ppermute | solution.py:94
  6.8 0.8 gather_fusion
  7.6 4.0 %collective-permute-start.5 = (bf16[2,128,256]{2,1,0:T(8,128)(2,1)S(1)}, bf16[2,128,256]{2,1,0:T(8,128)(2,1)S(1)}, u32[]{:S(2)}, u32[]{:S(2)}) collective-permute-start(bf16[2,128,256]{2,1,0:T(8,128)(2,1)S(1)} %get-tuple-element.6), channel_id=1, source_target_pairs={{0,14},{1,15},{2,0},{3,1},{4,2},{5,3},{6,4},{7,5},{8,6},{9,7},{10,... | collective-permute-start | bytes 393224 | tf_op jit(solution)/shard_map/ppermute | solution.py:97
  11.6 1.5 %collective-permute-done.1 = bf16[2,128,256]{2,1,0:T(8,128)(2,1)S(1)} collective-permute-done((bf16[2,128,256]{2,1,0:T(8,128)(2,1)S(1)}, bf16[2,128,256]{2,1,0:T(8,128)(2,1)S(1)}, u32[]{:S(2)}, u32[]{:S(2)}) %collective-permute-start.1) | collective-permute-done | bytes 131104 | tf_op jit(solution)/shard_map/ppermute | solution.py:94
  13.1 0.0 collective-permute-start.2
  13.1 0.8 fusion.3
  13.9 0.0 collective-permute-done.5
  13.9 2.8 %collective-permute-start.6 = (bf16[2,128,256]{2,1,0:T(8,128)(2,1)S(1)}, bf16[2,128,256]{2,1,0:T(8,128)(2,1)S(1)}, u32[]{:S(2)}, u32[]{:S(2)}) collective-permute-start(bf16[2,128,256]{2,1,0:T(8,128)(2,1)S(1)} %collective-permute-done.5), channel_id=1, source_target_pairs={{0,14},{1,15},{2,0},{3,1},{4,2},{5,3},{6,4},{7,5},{8,6},{9,7},{10,... | collective-permute-start | bytes 393224 | tf_op jit(solution)/shard_map/ppermute | solution.py:97
  16.7 1.5 %collective-permute-done.2 = bf16[2,128,256]{2,1,0:T(8,128)(2,1)S(1)} collective-permute-done((bf16[2,128,256]{2,1,0:T(8,128)(2,1)S(1)}, bf16[2,128,256]{2,1,0:T(8,128)(2,1)S(1)}, u32[]{:S(2)}, u32[]{:S(2)}) %collective-permute-start.2) | collective-permute-done | bytes 131104 | tf_op jit(solution)/shard_map/ppermute | solution.py:94
  18.1 0.0 collective-permute-start.3
  18.2 0.6 pad_add_fusion.gu_ref
  18.7 0.0 collective-permute-done.6
  18.7 3.0 %collective-permute-start.7 = (bf16[2,128,256]{2,1,0:T(8,128)(2,1)S(1)}, bf16[2,128,256]{2,1,0:T(8,128)(2,1)S(1)}, u32[]{:S(2)}, u32[]{:S(2)}) collective-permute-start(bf16[2,128,256]{2,1,0:T(8,128)(2,1)S(1)} %collective-permute-done.6), channel_id=1, source_target_pairs={{0,14},{1,15},{2,0},{3,1},{4,2},{5,3},{6,4},{7,5},{8,6},{9,7},{10,... | collective-permute-start | bytes 393224 | tf_op jit(solution)/shard_map/ppermute | solution.py:97
  21.7 1.5 %collective-permute-done.3 = bf16[2,128,256]{2,1,0:T(8,128)(2,1)S(1)} collective-permute-done((bf16[2,128,256]{2,1,0:T(8,128)(2,1)S(1)}, bf16[2,128,256]{2,1,0:T(8,128)(2,1)S(1)}, u32[]{:S(2)}, u32[]{:S(2)}) %collective-permute-start.3) | collective-permute-done | bytes 131104 | tf_op jit(solution)/shard_map/ppermute | solution.py:94
  23.2 5.7 %collective-permute-done.4 = bf16[2,128,256]{2,1,0:T(8,128)(2,1)S(1)} collective-permute-done((bf16[2,128,256]{2,1,0:T(8,128)(2,1)S(1)}, bf16[2,128,256]{2,1,0:T(8,128)(2,1)S(1)}, u32[]{:S(2)}, u32[]{:S(2)}) %collective-permute-start.4) | collective-permute-done | bytes 131104 | tf_op jit(solution)/shard_map/ppermute | solution.py:94
  28.9 0.0 collective-permute-done.7
  29.0 1.0 %copy-done = bf16[16,128,256]{2,1,0:T(8,128)(2,1)} copy-done((bf16[16,128,256]{2,1,0:T(8,128)(2,1)}, bf16[16,128,256]{2,1,0:T(8,128)(2,1)S(1)}, u32[]{:S(2)}) %copy-start) | copy-done | bytes 1048600
  29.9 9.4 %shard_map.73 = bf16[32,128,128]{2,1,0:T(8,128)(2,1)} custom-call(s32[2]{0:T(128)} %bitcast.35, s32[2,64]{1,0:T(2,128)} %pad_add_fusion.gu_ref, s32[2,64]{1,0:T(2,128)} %dn_ref.1, bf16[16,128,256]{2,1,0:T(8,128)(2,1)} %copy-done, bf16[64,128,128]{2,1,0:T(8,128)(2,1)} %g_ref.1, bf16[64,128,128]{2,1,0:T(8,128)(2,1)} %u_ref.1, bf16[64,128,128]{2,1,0:T(8,128)(2,1)} %d_ref.1), custom_call_target="tpu_custom_call" | custom-call | tf_op jit(solution)/shard_map/pallas_call | solution.py:60
  39.4 1.9 %copy.12 = bf16[32,16,8,128]{3,0,2,1:T(8,128)(2,1)S(1)} copy(bf16[32,16,8,128]{3,2,1,0:T(8,128)(2,1)} %bitcast.30) | data formatting | bytes 2097152 | tf_op jit(solution)/shard_map/reshape | solution.py:113
  41.3 1.3 %reshape.225 = bf16[16,8,4096]{2,1,0:T(8,128)(2,1)} reshape(bf16[16,8,32,128]{3,2,1,0:T(8,128)(2,1)S(1)} %bitcast.31) | data formatting | bytes 2097152 | tf_op jit(solution)/shard_map/reshape | solution.py:114
  42.6 6.7 %all-to-all-start = ((bf16[16,8,4096]{2,1,0:T(8,128)(2,1)}), bf16[16,8,4096]{2,1,0:T(8,128)(2,1)S(1)}, u32[]{:S(2)}, u32[]{:S(2)}) async-start(bf16[16,8,4096]{2,1,0:T(8,128)(2,1)} %reshape.225), calls=%async_computation | async-start | bytes 2097152 | tf_op jit(solution)/shard_map/all_to_all | solution.py:114
  49.3 0.9 constant_dynamic-slice_fusion
  50.2 0.6 gather_fusion.1
  50.7 18.4 %all-to-all-done = bf16[16,8,4096]{2,1,0:T(8,128)(2,1)S(1)} async-done(((bf16[16,8,4096]{2,1,0:T(8,128)(2,1)}), bf16[16,8,4096]{2,1,0:T(8,128)(2,1)S(1)}, u32[]{:S(2)}, u32[]{:S(2)}) %all-to-all-start) | async-done | bytes 1048608 | tf_op jit(solution)/shard_map/all_to_all | solution.py:114
  69.1 0.1 convert_reduce_fusion
  69.2 0.1 fusion
  69.3 22.9 %all_to_all.10 = bf16[8,16,256]{2,0,1:T(8,128)(2,1)S(1)} all-to-all(bf16[8,16,256]{2,0,1:T(8,128)(2,1)S(1)} %fusion), channel_id=1, replica_groups=mesh['ctx'=16,'tp'=16] {'ctx'}, dimensions={1} | all-to-all | bytes 131072 | tf_op jit(solution)/shard_map/all_to_all | solution.py:119
  92.2 0.6 copy.10
  (14 shorter events, 0.1 us)
Async XLA Ops:
  0.0 4.0 %collective-permute-start = (bf16[128,256]{1,0:T(8,128)(2,1)}, bf16[128,256]{1,0:T(8,128)(2,1)S(1)}, u32[]{:S(2)}, u32[]{:S(2)}) collective-permute-start(bf16[128,256]{1,0:T(8,128)(2,1)} %param.7), channel_id=1, source_target_pairs={{0,1},{1,0},{2,3},{3,2},{4,5},{5,4},{6,7},{7,6},{8,9},{9,8},{10,11... | collective-permute-start | bytes 196616 | tf_op jit(solution)/shard_map/ppermute | solution.py:89
  4.9 8.2 %collective-permute-start.1 = (bf16[2,128,256]{2,1,0:T(8,128)(2,1)S(1)}, bf16[2,128,256]{2,1,0:T(8,128)(2,1)S(1)}, u32[]{:S(2)}, u32[]{:S(2)}) collective-permute-start(bf16[2,128,256]{2,1,0:T(8,128)(2,1)S(1)} %get-tuple-element.6), channel_id=1, source_target_pairs={{0,2},{1,3},{2,4},{3,5},{4,6},{5,7},{6,8},{7,9},{8,10},{9,11},{10,... | collective-permute-start | bytes 393224 | tf_op jit(solution)/shard_map/ppermute | solution.py:94
  7.6 6.3 %collective-permute-start.5 = (bf16[2,128,256]{2,1,0:T(8,128)(2,1)S(1)}, bf16[2,128,256]{2,1,0:T(8,128)(2,1)S(1)}, u32[]{:S(2)}, u32[]{:S(2)}) collective-permute-start(bf16[2,128,256]{2,1,0:T(8,128)(2,1)S(1)} %get-tuple-element.6), channel_id=1, source_target_pairs={{0,14},{1,15},{2,0},{3,1},{4,2},{5,3},{6,4},{7,5},{8,6},{9,7},{10,... | collective-permute-start | bytes 393224 | tf_op jit(solution)/shard_map/ppermute | solution.py:97
  13.1 5.0 %collective-permute-start.2 = (bf16[2,128,256]{2,1,0:T(8,128)(2,1)S(1)}, bf16[2,128,256]{2,1,0:T(8,128)(2,1)S(1)}, u32[]{:S(2)}, u32[]{:S(2)}) collective-permute-start(bf16[2,128,256]{2,1,0:T(8,128)(2,1)S(1)} %collective-permute-done.1), channel_id=1, source_target_pairs={{0,2},{1,3},{2,4},{3,5},{4,6},{5,7},{6,8},{7,9},{8,10},{9,11},{10,... | collective-permute-start | bytes 393224 | tf_op jit(solution)/shard_map/ppermute | solution.py:94
  13.9 4.8 %collective-permute-start.6 = (bf16[2,128,256]{2,1,0:T(8,128)(2,1)S(1)}, bf16[2,128,256]{2,1,0:T(8,128)(2,1)S(1)}, u32[]{:S(2)}, u32[]{:S(2)}) collective-permute-start(bf16[2,128,256]{2,1,0:T(8,128)(2,1)S(1)} %collective-permute-done.5), channel_id=1, source_target_pairs={{0,14},{1,15},{2,0},{3,1},{4,2},{5,3},{6,4},{7,5},{8,6},{9,7},{10,... | collective-permute-start | bytes 393224 | tf_op jit(solution)/shard_map/ppermute | solution.py:97
  18.1 5.0 %collective-permute-start.3 = (bf16[2,128,256]{2,1,0:T(8,128)(2,1)S(1)}, bf16[2,128,256]{2,1,0:T(8,128)(2,1)S(1)}, u32[]{:S(2)}, u32[]{:S(2)}) collective-permute-start(bf16[2,128,256]{2,1,0:T(8,128)(2,1)S(1)} %collective-permute-done.2), channel_id=1, source_target_pairs={{0,2},{1,3},{2,4},{3,5},{4,6},{5,7},{6,8},{7,9},{8,10},{9,11},{10,... | collective-permute-start | bytes 393224 | tf_op jit(solution)/shard_map/ppermute | solution.py:94
  18.7 10.2 %collective-permute-start.7 = (bf16[2,128,256]{2,1,0:T(8,128)(2,1)S(1)}, bf16[2,128,256]{2,1,0:T(8,128)(2,1)S(1)}, u32[]{:S(2)}, u32[]{:S(2)}) collective-permute-start(bf16[2,128,256]{2,1,0:T(8,128)(2,1)S(1)} %collective-permute-done.6), channel_id=1, source_target_pairs={{0,14},{1,15},{2,0},{3,1},{4,2},{5,3},{6,4},{7,5},{8,6},{9,7},{10,... | collective-permute-start | bytes 393224 | tf_op jit(solution)/shard_map/ppermute | solution.py:97
  23.2 5.7 %collective-permute-start.4 = (bf16[2,128,256]{2,1,0:T(8,128)(2,1)S(1)}, bf16[2,128,256]{2,1,0:T(8,128)(2,1)S(1)}, u32[]{:S(2)}, u32[]{:S(2)}) collective-permute-start(bf16[2,128,256]{2,1,0:T(8,128)(2,1)S(1)} %collective-permute-done.3), channel_id=1, source_target_pairs={{0,2},{1,3},{2,4},{3,5},{4,6},{5,7},{6,8},{7,9},{8,10},{9,11},{10,... | collective-permute-start | bytes 393224 | tf_op jit(solution)/shard_map/ppermute | solution.py:94
  29.0 1.0 %copy-start = (bf16[16,128,256]{2,1,0:T(8,128)(2,1)}, bf16[16,128,256]{2,1,0:T(8,128)(2,1)S(1)}, u32[]{:S(2)}) copy-start(bf16[16,128,256]{2,1,0:T(8,128)(2,1)S(1)} %constant_dynamic-update-slice_fusion.pieces_ref) | copy-start | bytes 3145732
  42.6 26.5 %all-to-all-start = ((bf16[16,8,4096]{2,1,0:T(8,128)(2,1)}), bf16[16,8,4096]{2,1,0:T(8,128)(2,1)S(1)}, u32[]{:S(2)}, u32[]{:S(2)}) async-start(bf16[16,8,4096]{2,1,0:T(8,128)(2,1)} %reshape.225), calls=%async_computation | async-start | bytes 2097152 | tf_op jit(solution)/shard_map/all_to_all | solution.py:114

commit v5 on v4

--- a/solution.py
+++ b/solution.py
@@ -10,7 +10,7 @@
 UNROLL = 8
 
 
-def ffn_kernel(cnt_ref, gu_ref, dn_ref, pieces_ref, g_ref, u_ref, d_ref, out_ref,
+def ffn_kernel(cnt_ref, gu_ref, dn_ref, me_ref, pieces_ref, g_ref, u_ref, d_ref, res_ref, out_ref,
                normed_s, accg_s, accu_s, hid_s, acco_s):
     n_src, rows, width = pieces_ref.shape
     tile = g_ref.shape[1]
@@ -48,19 +48,29 @@
         return carry
 
     lax.fori_loop(0, d_ref.shape[0], dn_body, 0, unroll=UNROLL)
-    out_ref[...] = acco_s[...].astype(out_ref.dtype)
+    groups, dests, share, group_width = out_ref.shape
+    rows = pl.ds(pl.multiple_of(me_ref[0] * share, share), share)
+    per_group = group_width // tile
+    for o in range(acco_s.shape[0]):
+        acco_s[o, rows, :] += res_ref[:, o * tile:(o + 1) * tile]
+        block = acco_s[o].reshape(dests, share, tile).astype(out_ref.dtype)
+        group, half = divmod(o, per_group)
+        out_ref[group, :, :, half * tile:(half + 1) * tile] = block
 
 
-def ffn(counts, gu_blocks, down_blocks, pieces, gate_tiles, up_tiles, down_tiles, hid_blocks, out_dtype):
+def ffn(counts, gu_blocks, down_blocks, me, pieces, gate_tiles, up_tiles, down_tiles, residual,
+        hid_blocks, groups):
     n_src, rows, width = pieces.shape
     tile = gate_tiles.shape[1]
     in_blocks = n_src * width // tile
+    share = residual.shape[0]
     smem = pl.BlockSpec(memory_space=pltpu.SMEM)
     vmem = pl.BlockSpec(memory_space=pltpu.VMEM)
     return pl.pallas_call(
         ffn_kernel,
-        out_shape=jax.ShapeDtypeStruct((in_blocks, rows, tile), out_dtype),
-        in_specs=[smem, smem, smem, vmem, vmem, vmem, vmem],
+        out_shape=jax.ShapeDtypeStruct((groups, rows // share, share, in_blocks * tile // groups),
+                                       jnp.bfloat16),
+        in_specs=[smem, smem, smem, smem, vmem, vmem, vmem, vmem, vmem],
         out_specs=vmem,
         scratch_shapes=[
             pltpu.VMEM((in_blocks, rows, tile), jnp.bfloat16),
@@ -69,8 +79,8 @@
             pltpu.VMEM((hid_blocks, rows, tile), jnp.bfloat16),
             pltpu.VMEM((in_blocks, rows, tile), jnp.float32),
         ],
-    )(counts.reshape(-1), gu_blocks, down_blocks, pieces, gate_tiles, up_tiles, down_tiles)
-
+    )(counts.reshape(-1), gu_blocks, down_blocks, me.reshape(1), pieces, gate_tiles, up_tiles,
+      down_tiles, residual)
 
 def ring_pairs(count, step):
     return [(i, ((i // Y_LO + step) % count) * Y_LO + i % Y_LO) for i in range(count * Y_LO)]
@@ -107,18 +117,19 @@
     feat_width = tp_count * own_width
     in_blocks = feat_width // tile
     hid_blocks = FF // tp_count // tile
-    partial = ffn(counts, gu_local, down_blocks, pieces, gate_tiles, up_tiles, down_tiles,
-                  hid_blocks, jnp.bfloat16)
     share = own_rows // tp_count
-    outgoing = partial.reshape(in_blocks, tp_count, share, tile).transpose(1, 2, 0, 3)
-    incoming = lax.all_to_all(outgoing.reshape(tp_count, share, feat_width), "tp", 0, 0, tiled=True)
-    total = jnp.sum(incoming.astype(jnp.float32), axis=0)
     own = jnp.take(lax.dynamic_slice_in_dim(pieces, me * share, share, 1), position, axis=0)
     residual = jnp.transpose(own, (1, 0, 2)).reshape(share, feat_width).astype(jnp.float32)
-    mixed = (total + residual).astype(jnp.bfloat16)
-    return lax.all_to_all(
-        mixed.reshape(share, ctx_count, feat_width // ctx_count), "ctx", 1, 1, tiled=True
+    outgoing = ffn(counts, gu_local, down_blocks, me.astype(jnp.int32), pieces, gate_tiles,
+                   up_tiles, down_tiles, residual, hid_blocks, ctx_count)
+    incoming = lax.all_to_all(
+        outgoing.reshape(ctx_count * tp_count, share, feat_width // ctx_count),
+        ("ctx", "tp"), 0, 0, tiled=True,
     )
+    total = jnp.sum(
+        incoming.reshape(ctx_count, tp_count, share, -1).astype(jnp.float32), axis=1
+    )
+    return jnp.transpose(total, (1, 0, 2)).astype(jnp.bfloat16)
 
 def solution(mesh):
     return jax.shard_map(

time: 93.2 us -> 91.4 us (0.981)
  blocking collectives: 22.9 us -> 50.5 us
  waiting for transfers between devices: 29.6 us -> 12.8 us
  starting transfers between devices: 20.5 us -> 12.2 us
  local copies, waits for them, and re-layouts: 7.05 us -> 2.07 us
    all_to_all x1, blocking collectives: 22.9 us -> 50.5 us  [per_device(): lax.all_to_all(outgoing.reshape(ctx_count * tp_count, share, feat_width /...]
    all_to_all x1 -> x0, waiting for transfers between devices: 18.4 us -> none  [per_device(): lax.all_to_all(outgoing.reshape(tp_count, share, feat_width), 'tp', 0, 0,...]
    all_to_all x1 -> x0, starting transfers between devices: 6.68 us -> none  [per_device(): lax.all_to_all(outgoing.reshape(tp_count, share, feat_width), 'tp', 0, 0,...]
    reshape x2 -> x0, local copies, waits for them, and re-layouts: 3.18 us -> none  [the longest x1 1.9 us: per_device(): partial.reshape(in_blocks, tp_count, share, tile).transpose(1, 2, 0, 3)]
    ppermute x4, waiting for transfers between devices: 10.1 us -> 12.4 us  [per_device(): fwd = lax.ppermute(fwd, 'tp', ring_pairs(z_count, 1))]
    ppermute x3, starting transfers between devices: 9.77 us -> 8.17 us  [per_device(): bwd = lax.ppermute(bwd, 'tp', ring_pairs(z_count, -1))]
    unnamed x8, local copies, waits for them, and re-layouts: 1.03 us -> 0.06 us
  transfers between devices with their start and end apart: 9 -> 8, of which waited for: 6 -> 5; matrix products, arithmetic and copies ran while one was open for 5% -> 3% of each run, Pallas kernels for 0% -> 0%
where the time goes in v5:
time: 91.4 us; the launch traced here: 91.2 us
  blocking collectives  50.5 us (55%)
  waiting for transfers between devices  12.8 us (14%)
  starting transfers between devices  12.2 us (13%)
  Pallas kernels  9.63 us (11%)
  other arithmetic  3.92 us (4%)
  local copies, waits for them, and re-layouts  2.07 us (2%)
    all_to_all x1, blocking collectives, per_device(): lax.all_to_all(outgoing.reshape(ctx_count * tp_count, share, feat_width /...  50.5 us
    ppermute x4, waiting for transfers between devices, per_device(): fwd = lax.ppermute(fwd, 'tp', ring_pairs(z_count, 1))  12.4 us
    pallas_call x1, Pallas kernels, ffn(): pl.pallas_call(ffn_kernel, out_shape=jax.ShapeDtypeStruct((groups, rows /...  9.63 us
    ppermute x3, starting transfers between devices, per_device(): bwd = lax.ppermute(bwd, 'tp', ring_pairs(z_count, -1))  8.17 us
    ppermute x1, starting transfers between devices, per_device(): partner = lax.ppermute(tokens, 'tp', [(i, i ^ 1) for i in range(tp_count)])  2.13 us
    ppermute x4, starting transfers between devices, per_device(): fwd = lax.ppermute(fwd, 'tp', ring_pairs(z_count, 1))  1.89 us
  transfers between devices with their start and end apart: 8, of which 5 were waited for; matrix products, arithmetic and copies ran while one was open for 3% of the time, Pallas kernels for 0%

profile of v5, /device:TPU:1, one launch (start us, length us, event | category | flops | bytes accessed | tf_op | source)
XLA Modules:
  0.0 91.2 jit_solution(10681883105633883228)
XLA Ops:
  0.0 2.1 %collective-permute-start = (bf16[128,256]{1,0:T(8,128)(2,1)}, bf16[128,256]{1,0:T(8,128)(2,1)S(1)}, u32[]{:S(2)}, u32[]{:S(2)}) collective-permute-start(bf16[128,256]{1,0:T(8,128)(2,1)} %param.7), channel_id=1, source_target_pairs={{0,1},{1,0},{2,3},{3,2},{4,5},{5,4},{6,7},{7,6},{8,9},{9,8},{10,11... | collective-permute-start | bytes 196616 | tf_op jit(solution)/shard_map/ppermute | solution.py:99
  2.1 0.7 fusion.10
  2.9 0.8 gather_fusion
  3.6 0.4 collective-permute-done
  4.0 0.9 %constant_dynamic-update-slice_fusion.7 = (bf16[16,128,256]{2,1,0:T(8,128)(2,1)S(1)}, bf16[2,128,256]{2,1,0:T(8,128)(2,1)S(1)}) fusion(bf16[1,128,256]{2,1,0:T(8,128)(2,1)} %bitcast.30, bf16[1,128,256]{2,1,0:T(8,128)(2,1)S(1)} %bitcast.31, pred[]{:T(512)S(6)} %eq.25), kind=kLoop, calls=%fused_computation.12 | loop fusion | flops 589823 | bytes 393217
  4.9 1.9 %collective-permute-start.1 = (bf16[2,128,256]{2,1,0:T(8,128)(2,1)S(1)}, bf16[2,128,256]{2,1,0:T(8,128)(2,1)S(1)}, u32[]{:S(2)}, u32[]{:S(2)}) collective-permute-start(bf16[2,128,256]{2,1,0:T(8,128)(2,1)S(1)} %get-tuple-element.6), channel_id=1, source_target_pairs={{0,2},{1,3},{2,4},{3,5},{4,6},{5,7},{6,8},{7,9},{8,10},{9,11},{10,... | collective-permute-start | bytes 393224 | tf_op jit(solution)/shard_map/ppermute | solution.py:104
  6.8 0.8 fusion.2
  7.6 5.5 %collective-permute-done.1 = bf16[2,128,256]{2,1,0:T(8,128)(2,1)S(1)} collective-permute-done((bf16[2,128,256]{2,1,0:T(8,128)(2,1)S(1)}, bf16[2,128,256]{2,1,0:T(8,128)(2,1)S(1)}, u32[]{:S(2)}, u32[]{:S(2)}) %collective-permute-start.1) | collective-permute-done | bytes 131104 | tf_op jit(solution)/shard_map/ppermute | solution.py:104
  13.1 0.0 collective-permute-start.2
  13.1 2.7 %collective-permute-start.5 = (bf16[2,128,256]{2,1,0:T(8,128)(2,1)S(1)}, bf16[2,128,256]{2,1,0:T(8,128)(2,1)S(1)}, u32[]{:S(2)}, u32[]{:S(2)}) collective-permute-start(bf16[2,128,256]{2,1,0:T(8,128)(2,1)S(1)} %get-tuple-element.6), channel_id=1, source_target_pairs={{0,14},{1,15},{2,0},{3,1},{4,2},{5,3},{6,4},{7,5},{8,6},{9,7},{10,... | collective-permute-start | bytes 393224 | tf_op jit(solution)/shard_map/ppermute | solution.py:107
  15.8 0.6 pad_add_fusion.gu_ref
  16.4 1.8 %collective-permute-done.2 = bf16[2,128,256]{2,1,0:T(8,128)(2,1)S(1)} collective-permute-done((bf16[2,128,256]{2,1,0:T(8,128)(2,1)S(1)}, bf16[2,128,256]{2,1,0:T(8,128)(2,1)S(1)}, u32[]{:S(2)}, u32[]{:S(2)}) %collective-permute-start.2) | collective-permute-done | bytes 131104 | tf_op jit(solution)/shard_map/ppermute | solution.py:104
  18.1 0.0 collective-permute-start.3
  18.2 0.0 collective-permute-done.5
  18.2 2.7 %collective-permute-start.6 = (bf16[2,128,256]{2,1,0:T(8,128)(2,1)S(1)}, bf16[2,128,256]{2,1,0:T(8,128)(2,1)S(1)}, u32[]{:S(2)}, u32[]{:S(2)}) collective-permute-start(bf16[2,128,256]{2,1,0:T(8,128)(2,1)S(1)} %collective-permute-done.5), channel_id=1, source_target_pairs={{0,14},{1,15},{2,0},{3,1},{4,2},{5,3},{6,4},{7,5},{8,6},{9,7},{10,... | collective-permute-start | bytes 393224 | tf_op jit(solution)/shard_map/ppermute | solution.py:107
  20.9 2.2 %collective-permute-done.3 = bf16[2,128,256]{2,1,0:T(8,128)(2,1)S(1)} collective-permute-done((bf16[2,128,256]{2,1,0:T(8,128)(2,1)S(1)}, bf16[2,128,256]{2,1,0:T(8,128)(2,1)S(1)}, u32[]{:S(2)}, u32[]{:S(2)}) %collective-permute-start.3) | collective-permute-done | bytes 131104 | tf_op jit(solution)/shard_map/ppermute | solution.py:104
  23.2 0.0 collective-permute-start.4
  23.2 0.0 collective-permute-done.6
  23.2 2.8 %collective-permute-start.7 = (bf16[2,128,256]{2,1,0:T(8,128)(2,1)S(1)}, bf16[2,128,256]{2,1,0:T(8,128)(2,1)S(1)}, u32[]{:S(2)}, u32[]{:S(2)}) collective-permute-start(bf16[2,128,256]{2,1,0:T(8,128)(2,1)S(1)} %collective-permute-done.6), channel_id=1, source_target_pairs={{0,14},{1,15},{2,0},{3,1},{4,2},{5,3},{6,4},{7,5},{8,6},{9,7},{10,... | collective-permute-start | bytes 393224 | tf_op jit(solution)/shard_map/ppermute | solution.py:107
  26.0 2.9 %collective-permute-done.4 = bf16[2,128,256]{2,1,0:T(8,128)(2,1)S(1)} collective-permute-done((bf16[2,128,256]{2,1,0:T(8,128)(2,1)S(1)}, bf16[2,128,256]{2,1,0:T(8,128)(2,1)S(1)}, u32[]{:S(2)}, u32[]{:S(2)}) %collective-permute-start.4) | collective-permute-done | bytes 131104 | tf_op jit(solution)/shard_map/ppermute | solution.py:104
  28.9 0.0 collective-permute-done.7
  29.0 0.0 copy-start
  29.0 0.6 gather_fusion.1
  29.6 0.7 select_convert_fusion
  30.3 0.0 copy-done
  30.3 9.6 %shard_map.73 = bf16[16,16,8,256]{3,2,1,0:T(8,128)(2,1)} custom-call(s32[2]{0:T(128)} %bitcast.32, s32[2,64]{1,0:T(2,128)} %pad_add_fusion.gu_ref, s32[2,64]{1,0:T(2,128)} %dn_ref.1, s32[1]{0:T(128)} %bitcast.4.me_ref, bf16[16,128,256]{2,1,0:T(8,128)(2,1)} %copy-done, bf16[64,128,128]{2,1,0:T(8,128)(2,1)} %g_ref.1, bf16[64,128,128]{2,1,0:T(8,128)(2,1)} %u_ref.1, ...), custom_call_target="tpu_custom_call" | custom-call | tf_op jit(solution)/shard_map/pallas_call | solution.py:69
  39.9 50.5 %all_to_all.5 = bf16[256,8,256]{2,1,0:T(8,128)(2,1)S(1)} all-to-all(bf16[256,8,256]{2,1,0:T(8,128)(2,1)} %bitcast.27), channel_id=1, replica_groups=mesh['ctx'=16,'tp'=16] {'ctx','tp'}, dimensions={0} | all-to-all | bytes 2097152 | tf_op jit(solution)/shard_map/all_to_all | solution.py:125
  90.4 0.1 bitcast_reduce_fusion
  90.6 0.6 copy.8
  (13 shorter events, 0.2 us)
Async XLA Ops:
  0.0 4.0 %collective-permute-start = (bf16[128,256]{1,0:T(8,128)(2,1)}, bf16[128,256]{1,0:T(8,128)(2,1)S(1)}, u32[]{:S(2)}, u32[]{:S(2)}) collective-permute-start(bf16[128,256]{1,0:T(8,128)(2,1)} %param.7), channel_id=1, source_target_pairs={{0,1},{1,0},{2,3},{3,2},{4,5},{5,4},{6,7},{7,6},{8,9},{9,8},{10,11... | collective-permute-start | bytes 196616 | tf_op jit(solution)/shard_map/ppermute | solution.py:99
  4.9 8.2 %collective-permute-start.1 = (bf16[2,128,256]{2,1,0:T(8,128)(2,1)S(1)}, bf16[2,128,256]{2,1,0:T(8,128)(2,1)S(1)}, u32[]{:S(2)}, u32[]{:S(2)}) collective-permute-start(bf16[2,128,256]{2,1,0:T(8,128)(2,1)S(1)} %get-tuple-element.6), channel_id=1, source_target_pairs={{0,2},{1,3},{2,4},{3,5},{4,6},{5,7},{6,8},{7,9},{8,10},{9,11},{10,... | collective-permute-start | bytes 393224 | tf_op jit(solution)/shard_map/ppermute | solution.py:104
  13.1 5.0 %collective-permute-start.2 = (bf16[2,128,256]{2,1,0:T(8,128)(2,1)S(1)}, bf16[2,128,256]{2,1,0:T(8,128)(2,1)S(1)}, u32[]{:S(2)}, u32[]{:S(2)}) collective-permute-start(bf16[2,128,256]{2,1,0:T(8,128)(2,1)S(1)} %collective-permute-done.1), channel_id=1, source_target_pairs={{0,2},{1,3},{2,4},{3,5},{4,6},{5,7},{6,8},{7,9},{8,10},{9,11},{10,... | collective-permute-start | bytes 393224 | tf_op jit(solution)/shard_map/ppermute | solution.py:104
  13.1 5.0 %collective-permute-start.5 = (bf16[2,128,256]{2,1,0:T(8,128)(2,1)S(1)}, bf16[2,128,256]{2,1,0:T(8,128)(2,1)S(1)}, u32[]{:S(2)}, u32[]{:S(2)}) collective-permute-start(bf16[2,128,256]{2,1,0:T(8,128)(2,1)S(1)} %get-tuple-element.6), channel_id=1, source_target_pairs={{0,14},{1,15},{2,0},{3,1},{4,2},{5,3},{6,4},{7,5},{8,6},{9,7},{10,... | collective-permute-start | bytes 393224 | tf_op jit(solution)/shard_map/ppermute | solution.py:107
  18.1 5.0 %collective-permute-start.3 = (bf16[2,128,256]{2,1,0:T(8,128)(2,1)S(1)}, bf16[2,128,256]{2,1,0:T(8,128)(2,1)S(1)}, u32[]{:S(2)}, u32[]{:S(2)}) collective-permute-start(bf16[2,128,256]{2,1,0:T(8,128)(2,1)S(1)} %collective-permute-done.2), channel_id=1, source_target_pairs={{0,2},{1,3},{2,4},{3,5},{4,6},{5,7},{6,8},{7,9},{8,10},{9,11},{10,... | collective-permute-start | bytes 393224 | tf_op jit(solution)/shard_map/ppermute | solution.py:104
  18.2 5.0 %collective-permute-start.6 = (bf16[2,128,256]{2,1,0:T(8,128)(2,1)S(1)}, bf16[2,128,256]{2,1,0:T(8,128)(2,1)S(1)}, u32[]{:S(2)}, u32[]{:S(2)}) collective-permute-start(bf16[2,128,256]{2,1,0:T(8,128)(2,1)S(1)} %collective-permute-done.5), channel_id=1, source_target_pairs={{0,14},{1,15},{2,0},{3,1},{4,2},{5,3},{6,4},{7,5},{8,6},{9,7},{10,... | collective-permute-start | bytes 393224 | tf_op jit(solution)/shard_map/ppermute | solution.py:107
  23.2 5.7 %collective-permute-start.4 = (bf16[2,128,256]{2,1,0:T(8,128)(2,1)S(1)}, bf16[2,128,256]{2,1,0:T(8,128)(2,1)S(1)}, u32[]{:S(2)}, u32[]{:S(2)}) collective-permute-start(bf16[2,128,256]{2,1,0:T(8,128)(2,1)S(1)} %collective-permute-done.3), channel_id=1, source_target_pairs={{0,2},{1,3},{2,4},{3,5},{4,6},{5,7},{6,8},{7,9},{8,10},{9,11},{10,... | collective-permute-start | bytes 393224 | tf_op jit(solution)/shard_map/ppermute | solution.py:104
  23.2 5.7 %collective-permute-start.7 = (bf16[2,128,256]{2,1,0:T(8,128)(2,1)S(1)}, bf16[2,128,256]{2,1,0:T(8,128)(2,1)S(1)}, u32[]{:S(2)}, u32[]{:S(2)}) collective-permute-start(bf16[2,128,256]{2,1,0:T(8,128)(2,1)S(1)} %collective-permute-done.6), channel_id=1, source_target_pairs={{0,14},{1,15},{2,0},{3,1},{4,2},{5,3},{6,4},{7,5},{8,6},{9,7},{10,... | collective-permute-start | bytes 393224 | tf_op jit(solution)/shard_map/ppermute | solution.py:107
  29.0 1.3 %copy-start = (bf16[16,128,256]{2,1,0:T(8,128)(2,1)}, bf16[16,128,256]{2,1,0:T(8,128)(2,1)S(1)}, u32[]{:S(2)}) copy-start(bf16[16,128,256]{2,1,0:T(8,128)(2,1)S(1)} %constant_dynamic-update-slice_fusion.pieces_ref) | copy-start | bytes 3145732

commit v6 on v5

--- a/solution.py
+++ b/solution.py
@@ -10,10 +10,16 @@
 UNROLL = 8
 
 
-def ffn_kernel(cnt_ref, gu_ref, dn_ref, me_ref, pieces_ref, g_ref, u_ref, d_ref, res_ref, out_ref,
-               normed_s, accg_s, accu_s, hid_s, acco_s):
+def ffn_kernel(cnt_ref, gu_ref, dn_ref, me_ref, pieces_ref, g_hbm, u_hbm, d_hbm, res_ref, out_ref,
+               normed_s, accg_s, accu_s, hid_s, acco_s, gu_v, d_v, sems):
     n_src, rows, width = pieces_ref.shape
-    tile = g_ref.shape[1]
+    tile = g_hbm.shape[1]
+    gate_copy = pltpu.make_async_copy(g_hbm, gu_v.at[:, :, 0:tile], sems.at[0])
+    up_copy = pltpu.make_async_copy(u_hbm, gu_v.at[:, :, tile:2 * tile], sems.at[1])
+    down_copy = pltpu.make_async_copy(d_hbm, d_v, sems.at[2])
+    gate_copy.start()
+    up_copy.start()
+    down_copy.start()
     per_src = width // tile
     feat = n_src * width
     ss = jnp.zeros((rows, 1), jnp.float32)
@@ -27,27 +33,31 @@
             normed_s[s * per_src + h] = (x * scale).astype(jnp.bfloat16)
     accg_s[...] = jnp.zeros(accg_s.shape, jnp.float32)
     accu_s[...] = jnp.zeros(accu_s.shape, jnp.float32)
+    gate_copy.wait()
+    up_copy.wait()
 
     def gu_body(m, carry):
         x = normed_s[gu_ref[0, m]]
         h = gu_ref[1, m]
         live = (m < cnt_ref[0]).astype(jnp.float32)
-        accg_s[h] += jnp.dot(x, g_ref[m], preferred_element_type=jnp.float32) * live
-        accu_s[h] += jnp.dot(x, u_ref[m], preferred_element_type=jnp.float32) * live
+        both = jnp.dot(x, gu_v[m], preferred_element_type=jnp.float32) * live
+        accg_s[h] += both[:, :tile]
+        accu_s[h] += both[:, tile:]
         return carry
 
-    lax.fori_loop(0, g_ref.shape[0], gu_body, 0, unroll=UNROLL)
+    lax.fori_loop(0, gu_v.shape[0], gu_body, 0, unroll=UNROLL)
     g = accg_s[...]
     hid_s[...] = (g / (1.0 + jnp.exp(-g)) * accu_s[...]).astype(jnp.bfloat16)
     acco_s[...] = jnp.zeros(acco_s.shape, jnp.float32)
+    down_copy.wait()
 
     def dn_body(m, carry):
         o = dn_ref[1, m]
         live = (m < cnt_ref[1]).astype(jnp.float32)
-        acco_s[o] += jnp.dot(hid_s[dn_ref[0, m]], d_ref[m], preferred_element_type=jnp.float32) * live
+        acco_s[o] += jnp.dot(hid_s[dn_ref[0, m]], d_v[m], preferred_element_type=jnp.float32) * live
         return carry
 
-    lax.fori_loop(0, d_ref.shape[0], dn_body, 0, unroll=UNROLL)
+    lax.fori_loop(0, d_v.shape[0], dn_body, 0, unroll=UNROLL)
     groups, dests, share, group_width = out_ref.shape
     rows = pl.ds(pl.multiple_of(me_ref[0] * share, share), share)
     per_group = group_width // tile
@@ -66,11 +76,13 @@
     share = residual.shape[0]
     smem = pl.BlockSpec(memory_space=pltpu.SMEM)
     vmem = pl.BlockSpec(memory_space=pltpu.VMEM)
+    hbm = pl.BlockSpec(memory_space=pl.ANY)
+    slots = gate_tiles.shape[0]
     return pl.pallas_call(
         ffn_kernel,
         out_shape=jax.ShapeDtypeStruct((groups, rows // share, share, in_blocks * tile // groups),
                                        jnp.bfloat16),
-        in_specs=[smem, smem, smem, smem, vmem, vmem, vmem, vmem, vmem],
+        in_specs=[smem, smem, smem, smem, vmem, hbm, hbm, hbm, vmem],
         out_specs=vmem,
         scratch_shapes=[
             pltpu.VMEM((in_blocks, rows, tile), jnp.bfloat16),
@@ -78,6 +90,9 @@
             pltpu.VMEM((hid_blocks, rows, tile), jnp.float32),
             pltpu.VMEM((hid_blocks, rows, tile), jnp.bfloat16),
             pltpu.VMEM((in_blocks, rows, tile), jnp.float32),
+            pltpu.VMEM((slots, tile, 2 * tile), jnp.bfloat16),
+            pltpu.VMEM((slots, tile, tile), jnp.bfloat16),
+            pltpu.SemaphoreType.DMA((3,)),
         ],
     )(counts.reshape(-1), gu_blocks, down_blocks, me.reshape(1), pieces, gate_tiles, up_tiles,
       down_tiles, residual)

time: 91.4 us -> 91.1 us (level)
  no operation moved by 1% of the time
where the time goes in v6:
time: 91.1 us; the launch traced here: 90.9 us
  blocking collectives  50.4 us (55%)
  waiting for transfers between devices  12.8 us (14%)
  starting transfers between devices  12.2 us (13%)
  Pallas kernels  9.36 us (10%)
  other arithmetic  3.92 us (4%)
  local copies, waits for them, and re-layouts  2.07 us (2%)
    all_to_all x1, blocking collectives, per_device(): lax.all_to_all(outgoing.reshape(ctx_count * tp_count, share, feat_width /...  50.4 us
    ppermute x4, waiting for transfers between devices, per_device(): fwd = lax.ppermute(fwd, 'tp', ring_pairs(z_count, 1))  12.4 us
    pallas_call x1, Pallas kernels, ffn(): pl.pallas_call(ffn_kernel, out_shape=jax.ShapeDtypeStruct((groups, rows /...  9.36 us
    ppermute x3, starting transfers between devices, per_device(): bwd = lax.ppermute(bwd, 'tp', ring_pairs(z_count, -1))  8.17 us
    ppermute x1, starting transfers between devices, per_device(): partner = lax.ppermute(tokens, 'tp', [(i, i ^ 1) for i in range(tp_count)])  2.13 us
    ppermute x4, starting transfers between devices, per_device(): fwd = lax.ppermute(fwd, 'tp', ring_pairs(z_count, 1))  1.89 us
  transfers between devices with their start and end apart: 8, of which 5 were waited for; matrix products, arithmetic and copies ran while one was open for 3% of the time, Pallas kernels for 0%

profile of v6, /device:TPU:1, one launch (start us, length us, event | category | flops | bytes accessed | tf_op | source)
XLA Modules:
  0.0 90.9 jit_solution(1593970482020707439)
XLA Ops:
  0.0 2.1 %collective-permute-start = (bf16[128,256]{1,0:T(8,128)(2,1)}, bf16[128,256]{1,0:T(8,128)(2,1)S(1)}, u32[]{:S(2)}, u32[]{:S(2)}) collective-permute-start(bf16[128,256]{1,0:T(8,128)(2,1)} %param.7), channel_id=1, source_target_pairs={{0,1},{1,0},{2,3},{3,2},{4,5},{5,4},{6,7},{7,6},{8,9},{9,8},{10,11... | collective-permute-start | bytes 196616 | tf_op jit(solution)/shard_map/ppermute | solution.py:114
  2.1 0.7 fusion.10
  2.9 0.8 gather_fusion
  3.6 0.4 collective-permute-done
  4.0 0.9 %constant_dynamic-update-slice_fusion.7 = (bf16[16,128,256]{2,1,0:T(8,128)(2,1)S(1)}, bf16[2,128,256]{2,1,0:T(8,128)(2,1)S(1)}) fusion(bf16[1,128,256]{2,1,0:T(8,128)(2,1)} %bitcast.30, bf16[1,128,256]{2,1,0:T(8,128)(2,1)S(1)} %bitcast.31, pred[]{:T(512)S(6)} %eq.25), kind=kLoop, calls=%fused_computation.12 | loop fusion | flops 589823 | bytes 393217
  4.9 1.9 %collective-permute-start.1 = (bf16[2,128,256]{2,1,0:T(8,128)(2,1)S(1)}, bf16[2,128,256]{2,1,0:T(8,128)(2,1)S(1)}, u32[]{:S(2)}, u32[]{:S(2)}) collective-permute-start(bf16[2,128,256]{2,1,0:T(8,128)(2,1)S(1)} %get-tuple-element.6), channel_id=1, source_target_pairs={{0,2},{1,3},{2,4},{3,5},{4,6},{5,7},{6,8},{7,9},{8,10},{9,11},{10,... | collective-permute-start | bytes 393224 | tf_op jit(solution)/shard_map/ppermute | solution.py:119
  6.8 0.8 fusion.2
  7.6 5.5 %collective-permute-done.1 = bf16[2,128,256]{2,1,0:T(8,128)(2,1)S(1)} collective-permute-done((bf16[2,128,256]{2,1,0:T(8,128)(2,1)S(1)}, bf16[2,128,256]{2,1,0:T(8,128)(2,1)S(1)}, u32[]{:S(2)}, u32[]{:S(2)}) %collective-permute-start.1) | collective-permute-done | bytes 131104 | tf_op jit(solution)/shard_map/ppermute | solution.py:119
  13.1 0.0 collective-permute-start.2
  13.1 2.7 %collective-permute-start.5 = (bf16[2,128,256]{2,1,0:T(8,128)(2,1)S(1)}, bf16[2,128,256]{2,1,0:T(8,128)(2,1)S(1)}, u32[]{:S(2)}, u32[]{:S(2)}) collective-permute-start(bf16[2,128,256]{2,1,0:T(8,128)(2,1)S(1)} %get-tuple-element.6), channel_id=1, source_target_pairs={{0,14},{1,15},{2,0},{3,1},{4,2},{5,3},{6,4},{7,5},{8,6},{9,7},{10,... | collective-permute-start | bytes 393224 | tf_op jit(solution)/shard_map/ppermute | solution.py:122
  15.8 0.6 pad_add_fusion.gu_ref
  16.4 1.8 %collective-permute-done.2 = bf16[2,128,256]{2,1,0:T(8,128)(2,1)S(1)} collective-permute-done((bf16[2,128,256]{2,1,0:T(8,128)(2,1)S(1)}, bf16[2,128,256]{2,1,0:T(8,128)(2,1)S(1)}, u32[]{:S(2)}, u32[]{:S(2)}) %collective-permute-start.2) | collective-permute-done | bytes 131104 | tf_op jit(solution)/shard_map/ppermute | solution.py:119
  18.1 0.0 collective-permute-start.3
  18.2 0.0 collective-permute-done.5
  18.2 2.7 %collective-permute-start.6 = (bf16[2,128,256]{2,1,0:T(8,128)(2,1)S(1)}, bf16[2,128,256]{2,1,0:T(8,128)(2,1)S(1)}, u32[]{:S(2)}, u32[]{:S(2)}) collective-permute-start(bf16[2,128,256]{2,1,0:T(8,128)(2,1)S(1)} %collective-permute-done.5), channel_id=1, source_target_pairs={{0,14},{1,15},{2,0},{3,1},{4,2},{5,3},{6,4},{7,5},{8,6},{9,7},{10,... | collective-permute-start | bytes 393224 | tf_op jit(solution)/shard_map/ppermute | solution.py:122
  20.9 2.2 %collective-permute-done.3 = bf16[2,128,256]{2,1,0:T(8,128)(2,1)S(1)} collective-permute-done((bf16[2,128,256]{2,1,0:T(8,128)(2,1)S(1)}, bf16[2,128,256]{2,1,0:T(8,128)(2,1)S(1)}, u32[]{:S(2)}, u32[]{:S(2)}) %collective-permute-start.3) | collective-permute-done | bytes 131104 | tf_op jit(solution)/shard_map/ppermute | solution.py:119
  23.2 0.0 collective-permute-start.4
  23.2 0.0 collective-permute-done.6
  23.2 2.8 %collective-permute-start.7 = (bf16[2,128,256]{2,1,0:T(8,128)(2,1)S(1)}, bf16[2,128,256]{2,1,0:T(8,128)(2,1)S(1)}, u32[]{:S(2)}, u32[]{:S(2)}) collective-permute-start(bf16[2,128,256]{2,1,0:T(8,128)(2,1)S(1)} %collective-permute-done.6), channel_id=1, source_target_pairs={{0,14},{1,15},{2,0},{3,1},{4,2},{5,3},{6,4},{7,5},{8,6},{9,7},{10,... | collective-permute-start | bytes 393224 | tf_op jit(solution)/shard_map/ppermute | solution.py:122
  26.0 2.9 %collective-permute-done.4 = bf16[2,128,256]{2,1,0:T(8,128)(2,1)S(1)} collective-permute-done((bf16[2,128,256]{2,1,0:T(8,128)(2,1)S(1)}, bf16[2,128,256]{2,1,0:T(8,128)(2,1)S(1)}, u32[]{:S(2)}, u32[]{:S(2)}) %collective-permute-start.4) | collective-permute-done | bytes 131104 | tf_op jit(solution)/shard_map/ppermute | solution.py:119
  28.9 0.0 collective-permute-done.7
  29.0 0.0 copy-start
  29.0 0.6 gather_fusion.1
  29.6 0.7 select_convert_fusion
  30.3 0.0 copy-done
  30.3 9.4 %shard_map.73 = bf16[16,16,8,256]{3,2,1,0:T(8,128)(2,1)} custom-call(s32[2]{0:T(128)} %bitcast.32, s32[2,64]{1,0:T(2,128)} %pad_add_fusion.gu_ref, s32[2,64]{1,0:T(2,128)} %dn_ref.1, s32[1]{0:T(128)} %bitcast.4.me_ref, bf16[16,128,256]{2,1,0:T(8,128)(2,1)} %copy-done, bf16[64,128,128]{2,1,0:T(8,128)(2,1)} %g_hbm.1, bf16[64,128,128]{2,1,0:T(8,128)(2,1)} %u_hbm.1, ...), custom_call_target="tpu_custom_call" | custom-call | tf_op jit(solution)/shard_map/pallas_call | solution.py:81
  39.7 50.4 %all_to_all.5 = bf16[256,8,256]{2,1,0:T(8,128)(2,1)S(1)} all-to-all(bf16[256,8,256]{2,1,0:T(8,128)(2,1)} %bitcast.27), channel_id=1, replica_groups=mesh['ctx'=16,'tp'=16] {'ctx','tp'}, dimensions={0} | all-to-all | bytes 2097152 | tf_op jit(solution)/shard_map/all_to_all | solution.py:140
  90.1 0.1 bitcast_reduce_fusion
  90.2 0.6 copy.8
  (13 shorter events, 0.2 us)
Async XLA Ops:
  0.0 4.0 %collective-permute-start = (bf16[128,256]{1,0:T(8,128)(2,1)}, bf16[128,256]{1,0:T(8,128)(2,1)S(1)}, u32[]{:S(2)}, u32[]{:S(2)}) collective-permute-start(bf16[128,256]{1,0:T(8,128)(2,1)} %param.7), channel_id=1, source_target_pairs={{0,1},{1,0},{2,3},{3,2},{4,5},{5,4},{6,7},{7,6},{8,9},{9,8},{10,11... | collective-permute-start | bytes 196616 | tf_op jit(solution)/shard_map/ppermute | solution.py:114
  4.9 8.2 %collective-permute-start.1 = (bf16[2,128,256]{2,1,0:T(8,128)(2,1)S(1)}, bf16[2,128,256]{2,1,0:T(8,128)(2,1)S(1)}, u32[]{:S(2)}, u32[]{:S(2)}) collective-permute-start(bf16[2,128,256]{2,1,0:T(8,128)(2,1)S(1)} %get-tuple-element.6), channel_id=1, source_target_pairs={{0,2},{1,3},{2,4},{3,5},{4,6},{5,7},{6,8},{7,9},{8,10},{9,11},{10,... | collective-permute-start | bytes 393224 | tf_op jit(solution)/shard_map/ppermute | solution.py:119
  13.1 5.0 %collective-permute-start.2 = (bf16[2,128,256]{2,1,0:T(8,128)(2,1)S(1)}, bf16[2,128,256]{2,1,0:T(8,128)(2,1)S(1)}, u32[]{:S(2)}, u32[]{:S(2)}) collective-permute-start(bf16[2,128,256]{2,1,0:T(8,128)(2,1)S(1)} %collective-permute-done.1), channel_id=1, source_target_pairs={{0,2},{1,3},{2,4},{3,5},{4,6},{5,7},{6,8},{7,9},{8,10},{9,11},{10,... | collective-permute-start | bytes 393224 | tf_op jit(solution)/shard_map/ppermute | solution.py:119
  13.1 5.0 %collective-permute-start.5 = (bf16[2,128,256]{2,1,0:T(8,128)(2,1)S(1)}, bf16[2,128,256]{2,1,0:T(8,128)(2,1)S(1)}, u32[]{:S(2)}, u32[]{:S(2)}) collective-permute-start(bf16[2,128,256]{2,1,0:T(8,128)(2,1)S(1)} %get-tuple-element.6), channel_id=1, source_target_pairs={{0,14},{1,15},{2,0},{3,1},{4,2},{5,3},{6,4},{7,5},{8,6},{9,7},{10,... | collective-permute-start | bytes 393224 | tf_op jit(solution)/shard_map/ppermute | solution.py:122
  18.1 5.0 %collective-permute-start.3 = (bf16[2,128,256]{2,1,0:T(8,128)(2,1)S(1)}, bf16[2,128,256]{2,1,0:T(8,128)(2,1)S(1)}, u32[]{:S(2)}, u32[]{:S(2)}) collective-permute-start(bf16[2,128,256]{2,1,0:T(8,128)(2,1)S(1)} %collective-permute-done.2), channel_id=1, source_target_pairs={{0,2},{1,3},{2,4},{3,5},{4,6},{5,7},{6,8},{7,9},{8,10},{9,11},{10,... | collective-permute-start | bytes 393224 | tf_op jit(solution)/shard_map/ppermute | solution.py:119
  18.2 5.0 %collective-permute-start.6 = (bf16[2,128,256]{2,1,0:T(8,128)(2,1)S(1)}, bf16[2,128,256]{2,1,0:T(8,128)(2,1)S(1)}, u32[]{:S(2)}, u32[]{:S(2)}) collective-permute-start(bf16[2,128,256]{2,1,0:T(8,128)(2,1)S(1)} %collective-permute-done.5), channel_id=1, source_target_pairs={{0,14},{1,15},{2,0},{3,1},{4,2},{5,3},{6,4},{7,5},{8,6},{9,7},{10,... | collective-permute-start | bytes 393224 | tf_op jit(solution)/shard_map/ppermute | solution.py:122
  23.2 5.7 %collective-permute-start.4 = (bf16[2,128,256]{2,1,0:T(8,128)(2,1)S(1)}, bf16[2,128,256]{2,1,0:T(8,128)(2,1)S(1)}, u32[]{:S(2)}, u32[]{:S(2)}) collective-permute-start(bf16[2,128,256]{2,1,0:T(8,128)(2,1)S(1)} %collective-permute-done.3), channel_id=1, source_target_pairs={{0,2},{1,3},{2,4},{3,5},{4,6},{5,7},{6,8},{7,9},{8,10},{9,11},{10,... | collective-permute-start | bytes 393224 | tf_op jit(solution)/shard_map/ppermute | solution.py:119
  23.2 5.7 %collective-permute-start.7 = (bf16[2,128,256]{2,1,0:T(8,128)(2,1)S(1)}, bf16[2,128,256]{2,1,0:T(8,128)(2,1)S(1)}, u32[]{:S(2)}, u32[]{:S(2)}) collective-permute-start(bf16[2,128,256]{2,1,0:T(8,128)(2,1)S(1)} %collective-permute-done.6), channel_id=1, source_target_pairs={{0,14},{1,15},{2,0},{3,1},{4,2},{5,3},{6,4},{7,5},{8,6},{9,7},{10,... | collective-permute-start | bytes 393224 | tf_op jit(solution)/shard_map/ppermute | solution.py:122
  29.0 1.3 %copy-start = (bf16[16,128,256]{2,1,0:T(8,128)(2,1)}, bf16[16,128,256]{2,1,0:T(8,128)(2,1)S(1)}, u32[]{:S(2)}) copy-start(bf16[16,128,256]{2,1,0:T(8,128)(2,1)S(1)} %constant_dynamic-update-slice_fusion.pieces_ref) | copy-start | bytes 3145732

commit v7 on v6

--- a/solution.py
+++ b/solution.py
@@ -7,19 +7,32 @@
 
 FF = 16384
 Y_LO = 2
-UNROLL = 8
+CHUNKS = 8
 
 
 def ffn_kernel(cnt_ref, gu_ref, dn_ref, me_ref, pieces_ref, g_hbm, u_hbm, d_hbm, res_ref, out_ref,
                normed_s, accg_s, accu_s, hid_s, acco_s, gu_v, d_v, sems):
     n_src, rows, width = pieces_ref.shape
     tile = g_hbm.shape[1]
-    gate_copy = pltpu.make_async_copy(g_hbm, gu_v.at[:, :, 0:tile], sems.at[0])
-    up_copy = pltpu.make_async_copy(u_hbm, gu_v.at[:, :, tile:2 * tile], sems.at[1])
-    down_copy = pltpu.make_async_copy(d_hbm, d_v, sems.at[2])
-    gate_copy.start()
-    up_copy.start()
-    down_copy.start()
+    slots = g_hbm.shape[0]
+    step = slots // CHUNKS
+    copies = []
+    for k in range(CHUNKS):
+        part = pl.ds(k * step, step)
+        copies.append((
+            pltpu.make_async_copy(g_hbm.at[part], gu_v.at[part, :, 0:tile], sems.at[0, k]),
+            pltpu.make_async_copy(u_hbm.at[part], gu_v.at[part, :, tile:2 * tile], sems.at[1, k]),
+        ))
+    down_copies = [
+        pltpu.make_async_copy(d_hbm.at[pl.ds(k * step, step)], d_v.at[pl.ds(k * step, step)],
+                              sems.at[2, k])
+        for k in range(CHUNKS)
+    ]
+    for gate_copy, up_copy in copies:
+        gate_copy.start()
+        up_copy.start()
+    for down_copy in down_copies:
+        down_copy.start()
     per_src = width // tile
     feat = n_src * width
     ss = jnp.zeros((rows, 1), jnp.float32)
@@ -33,8 +46,6 @@
             normed_s[s * per_src + h] = (x * scale).astype(jnp.bfloat16)
     accg_s[...] = jnp.zeros(accg_s.shape, jnp.float32)
     accu_s[...] = jnp.zeros(accu_s.shape, jnp.float32)
-    gate_copy.wait()
-    up_copy.wait()
 
     def gu_body(m, carry):
         x = normed_s[gu_ref[0, m]]
@@ -45,11 +56,13 @@
         accu_s[h] += both[:, tile:]
         return carry
 
-    lax.fori_loop(0, gu_v.shape[0], gu_body, 0, unroll=UNROLL)
+    for k, (gate_copy, up_copy) in enumerate(copies):
+        gate_copy.wait()
+        up_copy.wait()
+        lax.fori_loop(k * step, (k + 1) * step, gu_body, 0, unroll=True)
     g = accg_s[...]
     hid_s[...] = (g / (1.0 + jnp.exp(-g)) * accu_s[...]).astype(jnp.bfloat16)
     acco_s[...] = jnp.zeros(acco_s.shape, jnp.float32)
-    down_copy.wait()
 
     def dn_body(m, carry):
         o = dn_ref[1, m]
@@ -57,7 +70,9 @@
         acco_s[o] += jnp.dot(hid_s[dn_ref[0, m]], d_v[m], preferred_element_type=jnp.float32) * live
         return carry
 
-    lax.fori_loop(0, d_v.shape[0], dn_body, 0, unroll=UNROLL)
+    for k, down_copy in enumerate(down_copies):
+        down_copy.wait()
+        lax.fori_loop(k * step, (k + 1) * step, dn_body, 0, unroll=True)
     groups, dests, share, group_width = out_ref.shape
     rows = pl.ds(pl.multiple_of(me_ref[0] * share, share), share)
     per_group = group_width // tile
@@ -92,7 +107,7 @@
             pltpu.VMEM((in_blocks, rows, tile), jnp.float32),
             pltpu.VMEM((slots, tile, 2 * tile), jnp.bfloat16),
             pltpu.VMEM((slots, tile, tile), jnp.bfloat16),
-            pltpu.SemaphoreType.DMA((3,)),
+            pltpu.SemaphoreType.DMA((3, CHUNKS)),
         ],
     )(counts.reshape(-1), gu_blocks, down_blocks, me.reshape(1), pieces, gate_tiles, up_tiles,
       down_tiles, residual)
@@ -111,21 +126,32 @@
     me = lax.axis_index("tp")
     my_z = me // Y_LO
     my_y = me % Y_LO
-    partner = lax.ppermute(tokens, "tp", [(i, i ^ 1) for i in range(tp_count)])
-    both = jnp.where(my_y == 0, jnp.stack([tokens, partner]), jnp.stack([partner, tokens]))
-    ahead, behind = [], []
-    fwd = bwd = both
-    for k in range(1, z_count // 2 + 1):
+    swap = [(i, i ^ 1) for i in range(tp_count)]
+    half = z_count // 2
+    arrays = [tokens[None], lax.ppermute(tokens, "tp", swap)[None]]
+    origins = [(0, 0), (0, 1)]
+    fwd = bwd = tokens
+    for k in range(1, half + 1):
         fwd = lax.ppermute(fwd, "tp", ring_pairs(z_count, 1))
-        ahead.append(fwd)
-        if k < z_count - z_count // 2:
+        arrays.append(fwd[None])
+        origins.append((-k % z_count, 0))
+        if k < z_count - half:
             bwd = lax.ppermute(bwd, "tp", ring_pairs(z_count, -1))
-            behind.append(bwd)
-    pieces = jnp.concatenate([both] + ahead + behind)
+            arrays.append(bwd[None])
+            origins.append((k, 0))
+            arrays.append(lax.ppermute(jnp.stack([fwd, bwd]), "tp", swap))
+            origins += [(-k % z_count, 1), (k, 1)]
+        else:
+            arrays.append(lax.ppermute(fwd, "tp", swap)[None])
+            origins.append((-k % z_count, 1))
+    pieces = jnp.concatenate(arrays)
+    table = [[0] * Y_LO for _ in range(z_count)]
+    for index, (dz, dy) in enumerate(origins):
+        table[dz][dy] = index
     src_ids = jnp.arange(tp_count)
     dz = (src_ids // Y_LO - my_z) % z_count
-    slot_of_z = jnp.where(dz == 0, 0, jnp.where(dz >= z_count // 2, z_count - dz, z_count // 2 + dz))
-    position = slot_of_z * Y_LO + src_ids % Y_LO
+    dy = (src_ids % Y_LO != my_y).astype(jnp.int32)
+    position = jnp.array(table, jnp.int32)[dz, dy]
     in_tile = gu_blocks[0]
     moved = position[in_tile // per_src] * per_src + in_tile % per_src
     gu_local = jnp.stack([moved, gu_blocks[1]])
@@ -146,6 +172,7 @@
     )
     return jnp.transpose(total, (1, 0, 2)).astype(jnp.bfloat16)
 
+
 def solution(mesh):
     return jax.shard_map(
         per_device,

time: 91.1 us -> 90.6 us (level)
  starting transfers between devices: 12.2 us -> 16.3 us
  waiting for transfers between devices: 12.8 us -> 9.08 us
  local copies, waits for them, and re-layouts: 2.07 us -> 4.33 us
  blocking collectives: 50.4 us -> 49.2 us
  Pallas kernels: 9.36 us -> 8.31 us
  other arithmetic: 3.92 us -> 3 us
    ppermute x4, waiting for transfers between devices: 12.4 us -> 5.29 us  [per_device(): fwd = lax.ppermute(fwd, 'tp', ring_pairs(z_count, 1))]
    ppermute x1 -> x5, waiting for transfers between devices: 0.36 us -> 3.78 us  [the longest x1 2.95 us: per_device(): arrays.append(lax.ppermute(fwd, 'tp', swap)[None])]
    ppermute x1 -> x5, starting transfers between devices: 2.13 us -> 5.32 us  [the longest x3 3.02 us: per_device(): arrays.append(lax.ppermute(jnp.stack([fwd, bwd]), 'tp', swap))]
    gather x0 -> x1, local copies, waits for them, and re-layouts: none -> 1.36 us  [per_device(): position = jnp.array(table, jnp.int32)[dz, dy]]
    all_to_all x1, blocking collectives: 50.4 us -> 49.2 us  [per_device(): lax.all_to_all(outgoing.reshape(ctx_count * tp_count, share, feat_width /...]
    ppermute x3, starting transfers between devices: 8.17 us -> 9.29 us  [per_device(): bwd = lax.ppermute(bwd, 'tp', ring_pairs(z_count, -1))]
    pallas_call x1, Pallas kernels: 9.36 us -> 8.31 us  [ffn(): pl.pallas_call(ffn_kernel, out_shape=jax.ShapeDtypeStruct((groups, rows /...]
    unnamed x1 -> x0, other arithmetic: 0.95 us -> none
  transfers between devices with their start and end apart: 8 -> 12, of which waited for: 5 -> 5; matrix products, arithmetic and copies ran while one was open for 3% -> 6% of each run, Pallas kernels for 0% -> 0%
where the time goes in v7:
time: 90.6 us; the launch traced here: 90.3 us
  blocking collectives  49.2 us (54%)
  starting transfers between devices  16.3 us (18%)
  waiting for transfers between devices  9.08 us (10%)
  Pallas kernels  8.31 us (9%)
  local copies, waits for them, and re-layouts  4.33 us (5%)
  other arithmetic  3 us (3%)
    all_to_all x1, blocking collectives, per_device(): lax.all_to_all(outgoing.reshape(ctx_count * tp_count, share, feat_width /...  49.2 us
    ppermute x3, starting transfers between devices, per_device(): bwd = lax.ppermute(bwd, 'tp', ring_pairs(z_count, -1))  9.29 us
    pallas_call x1, Pallas kernels, ffn(): pl.pallas_call(ffn_kernel, out_shape=jax.ShapeDtypeStruct((groups, rows /...  8.31 us
    ppermute x4, waiting for transfers between devices, per_device(): fwd = lax.ppermute(fwd, 'tp', ring_pairs(z_count, 1))  5.29 us
    ppermute x3, starting transfers between devices, per_device(): arrays.append(lax.ppermute(jnp.stack([fwd, bwd]), 'tp', swap))  3.02 us
    ppermute x1, waiting for transfers between devices, per_device(): arrays.append(lax.ppermute(fwd, 'tp', swap)[None])  2.95 us
    ppermute x1, starting transfers between devices, per_device(): arrays = [tokens[None], lax.ppermute(tokens, 'tp', swap)[None]]  2.13 us
  transfers between devices with their start and end apart: 12, of which 5 were waited for; matrix products, arithmetic and copies ran while one was open for 6% of the time, Pallas kernels for 0%

profile of v7, /device:TPU:1, one launch (start us, length us, event | category | flops | bytes accessed | tf_op | source)
XLA Modules:
  0.0 90.3 jit_solution(16956474868877139450)
XLA Ops:
  0.0 2.1 %collective-permute-start = (bf16[128,256]{1,0:T(8,128)(2,1)}, bf16[128,256]{1,0:T(8,128)(2,1)S(1)}, u32[]{:S(2)}, u32[]{:S(2)}) collective-permute-start(bf16[128,256]{1,0:T(8,128)(2,1)} %param.8), channel_id=1, source_target_pairs={{0,1},{1,0},{2,3},{3,2},{4,5},{5,4},{6,7},{7,6},{8,9},{9,8},{10,11... | collective-permute-start | bytes 196616 | tf_op jit(solution)/shard_map/ppermute | solution.py:131
  2.1 1.6 %collective-permute-start.1 = (bf16[128,256]{1,0:T(8,128)(2,1)}, bf16[128,256]{1,0:T(8,128)(2,1)S(1)}, u32[]{:S(2)}, u32[]{:S(2)}) collective-permute-start(bf16[128,256]{1,0:T(8,128)(2,1)} %param.8), channel_id=1, source_target_pairs={{0,2},{1,3},{2,4},{3,5},{4,6},{5,7},{6,8},{7,9},{8,10},{9,11},{10,... | collective-permute-start | bytes 196616 | tf_op jit(solution)/shard_map/ppermute | solution.py:135
  3.8 3.9 %collective-permute-start.2 = (bf16[128,256]{1,0:T(8,128)(2,1)}, bf16[128,256]{1,0:T(8,128)(2,1)S(1)}, u32[]{:S(2)}, u32[]{:S(2)}) collective-permute-start(bf16[128,256]{1,0:T(8,128)(2,1)} %param.8), channel_id=1, source_target_pairs={{0,14},{1,15},{2,0},{3,1},{4,2},{5,3},{6,4},{7,5},{8,6},{9,7},{10,... | collective-permute-start | bytes 196616 | tf_op jit(solution)/shard_map/ppermute | solution.py:139
  7.7 0.9 bitcast_dynamic-update-slice_fusion.3
  8.6 1.4 %gather_fusion = s32[16]{0:T(128)S(1)} fusion(s32[8,2]{1,0:T(8,128)} %constant.104.clone, s32[16]{0:T(128)S(1)} %fusion.4), kind=kCustom, calls=%fused_computation | custom fusion | bytes 256 | tf_op jit(solution)/shard_map/gather | solution.py:154
  10.0 0.7 fusion.10
  10.7 0.8 gather_fusion.1
  11.5 0.8 fusion
  12.2 0.6 pad_add_fusion.gu_ref
  12.8 0.3 collective-permute-start.3
  13.1 0.0 collective-permute-start.4
  13.1 2.7 %collective-permute-start.5 = (bf16[128,256]{1,0:T(8,128)(2,1)S(1)}, bf16[128,256]{1,0:T(8,128)(2,1)S(1)}, u32[]{:S(2)}, u32[]{:S(2)}) collective-permute-start(bf16[128,256]{1,0:T(8,128)(2,1)S(1)} %collective-permute-done.2), channel_id=1, source_target_pairs={{0,14},{1,15},{2,0},{3,1},{4,2},{5,3},{6,4},{7,5},{8,6},{9,7},{10,... | collective-permute-start | bytes 196616 | tf_op jit(solution)/shard_map/ppermute | solution.py:139
  15.8 0.0 collective-permute-done
  15.8 1.6 %collective-permute-done.4 = bf16[128,256]{1,0:T(8,128)(2,1)S(1)} collective-permute-done((bf16[128,256]{1,0:T(8,128)(2,1)S(1)}, bf16[128,256]{1,0:T(8,128)(2,1)S(1)}, u32[]{:S(2)}, u32[]{:S(2)}) %collective-permute-start.4) | collective-permute-done | bytes 65568 | tf_op jit(solution)/shard_map/ppermute | solution.py:135
  17.4 0.0 collective-permute-start.7
  17.4 0.0 collective-permute-done.5
  17.4 2.7 %collective-permute-start.8 = (bf16[128,256]{1,0:T(8,128)(2,1)S(1)}, bf16[128,256]{1,0:T(8,128)(2,1)S(1)}, u32[]{:S(2)}, u32[]{:S(2)}) collective-permute-start(bf16[128,256]{1,0:T(8,128)(2,1)S(1)} %collective-permute-done.5), channel_id=1, source_target_pairs={{0,14},{1,15},{2,0},{3,1},{4,2},{5,3},{6,4},{7,5},{8,6},{9,7},{10,... | collective-permute-start | bytes 196616 | tf_op jit(solution)/shard_map/ppermute | solution.py:139
  20.1 1.4 %collective-permute-start.6 = (bf16[2,128,256]{2,1,0:T(8,128)(2,1)S(1)}, bf16[2,128,256]{2,1,0:T(8,128)(2,1)S(1)}, u32[]{:S(2)}, u32[]{:S(2)}) collective-permute-start(bf16[2,128,256]{2,1,0:T(8,128)(2,1)S(1)} %pad_maximum_fusion.1), channel_id=1, source_target_pairs={{0,1},{1,0},{2,3},{3,2},{4,5},{5,4},{6,7},{7,6},{8,9},{9,8},{10,11... | collective-permute-start | bytes 393224 | tf_op jit(solution)/shard_map/ppermute | solution.py:142
  21.5 0.2 collective-permute-done.7
  21.8 1.4 %collective-permute-start.9 = (bf16[2,128,256]{2,1,0:T(8,128)(2,1)S(1)}, bf16[2,128,256]{2,1,0:T(8,128)(2,1)S(1)}, u32[]{:S(2)}, u32[]{:S(2)}) collective-permute-start(bf16[2,128,256]{2,1,0:T(8,128)(2,1)S(1)} %pad_maximum_fusion.2), channel_id=1, source_target_pairs={{0,1},{1,0},{2,3},{3,2},{4,5},{5,4},{6,7},{7,6},{8,9},{9,8},{10,11... | collective-permute-start | bytes 393224 | tf_op jit(solution)/shard_map/ppermute | solution.py:142
  23.2 0.0 collective-permute-start.10
  23.2 0.8 collective-permute-done.6
  24.0 3.4 %collective-permute-done.10 = bf16[128,256]{1,0:T(8,128)(2,1)S(1)} collective-permute-done((bf16[128,256]{1,0:T(8,128)(2,1)S(1)}, bf16[128,256]{1,0:T(8,128)(2,1)S(1)}, u32[]{:S(2)}, u32[]{:S(2)}) %collective-permute-start.10) | collective-permute-done | bytes 65568 | tf_op jit(solution)/shard_map/ppermute | solution.py:135
  27.5 0.2 collective-permute-start.11
  27.7 0.0 collective-permute-done.9
  27.7 3.0 %collective-permute-done.11 = bf16[128,256]{1,0:T(8,128)(2,1)S(1)} collective-permute-done((bf16[128,256]{1,0:T(8,128)(2,1)S(1)}, bf16[128,256]{1,0:T(8,128)(2,1)S(1)}, u32[]{:S(2)}, u32[]{:S(2)}) %collective-permute-start.11) | collective-permute-done | bytes 65568 | tf_op jit(solution)/shard_map/ppermute | solution.py:145
  30.7 0.6 gather_fusion.2
  31.3 0.7 select_convert_fusion
  32.0 8.3 %shard_map.82 = bf16[16,16,8,256]{3,2,1,0:T(8,128)(2,1)} custom-call(s32[2]{0:T(128)} %bitcast.58, s32[2,64]{1,0:T(2,128)} %pad_add_fusion.gu_ref, s32[2,64]{1,0:T(2,128)} %dn_ref.1, s32[1]{0:T(128)} %bitcast.5.me_ref, bf16[16,128,256]{2,1,0:T(8,128)(2,1)} %copy-done, bf16[64,128,128]{2,1,0:T(8,128)(2,1)} %g_hbm.1, bf16[64,128,128]{2,1,0:T(8,128)(2,1)} %u_hbm.1, ...), custom_call_target="tpu_custom_call" | custom-call | tf_op jit(solution)/shard_map/pallas_call | solution.py:96
  40.3 49.2 %all_to_all.5 = bf16[256,8,256]{2,1,0:T(8,128)(2,1)S(1)} all-to-all(bf16[256,8,256]{2,1,0:T(8,128)(2,1)} %bitcast.49), channel_id=1, replica_groups=mesh['ctx'=16,'tp'=16] {'ctx','tp'}, dimensions={0} | all-to-all | bytes 2097152 | tf_op jit(solution)/shard_map/all_to_all | solution.py:166
  89.5 0.1 bitcast_reduce_fusion
  89.7 0.6 copy.9
  (27 shorter events, 0.2 us)
Async XLA Ops:
  0.0 15.8 %collective-permute-start = (bf16[128,256]{1,0:T(8,128)(2,1)}, bf16[128,256]{1,0:T(8,128)(2,1)S(1)}, u32[]{:S(2)}, u32[]{:S(2)}) collective-permute-start(bf16[128,256]{1,0:T(8,128)(2,1)} %param.8), channel_id=1, source_target_pairs={{0,1},{1,0},{2,3},{3,2},{4,5},{5,4},{6,7},{7,6},{8,9},{9,8},{10,11... | collective-permute-start | bytes 196616 | tf_op jit(solution)/shard_map/ppermute | solution.py:131
  2.1 10.7 %collective-permute-start.1 = (bf16[128,256]{1,0:T(8,128)(2,1)}, bf16[128,256]{1,0:T(8,128)(2,1)S(1)}, u32[]{:S(2)}, u32[]{:S(2)}) collective-permute-start(bf16[128,256]{1,0:T(8,128)(2,1)} %param.8), channel_id=1, source_target_pairs={{0,2},{1,3},{2,4},{3,5},{4,6},{5,7},{6,8},{7,9},{8,10},{9,11},{10,... | collective-permute-start | bytes 196616 | tf_op jit(solution)/shard_map/ppermute | solution.py:135
  3.8 9.0 %collective-permute-start.2 = (bf16[128,256]{1,0:T(8,128)(2,1)}, bf16[128,256]{1,0:T(8,128)(2,1)S(1)}, u32[]{:S(2)}, u32[]{:S(2)}) collective-permute-start(bf16[128,256]{1,0:T(8,128)(2,1)} %param.8), channel_id=1, source_target_pairs={{0,14},{1,15},{2,0},{3,1},{4,2},{5,3},{6,4},{7,5},{8,6},{9,7},{10,... | collective-permute-start | bytes 196616 | tf_op jit(solution)/shard_map/ppermute | solution.py:139
  12.8 10.3 %collective-permute-start.3 = (bf16[2,128,256]{2,1,0:T(8,128)(2,1)S(1)}, bf16[2,128,256]{2,1,0:T(8,128)(2,1)S(1)}, u32[]{:S(2)}, u32[]{:S(2)}) collective-permute-start(bf16[2,128,256]{2,1,0:T(8,128)(2,1)S(1)} %pad_maximum_fusion), channel_id=1, source_target_pairs={{0,1},{1,0},{2,3},{3,2},{4,5},{5,4},{6,7},{7,6},{8,9},{9,8},{10,11... | collective-permute-start | bytes 393224 | tf_op jit(solution)/shard_map/ppermute | solution.py:142
  13.1 4.3 %collective-permute-start.4 = (bf16[128,256]{1,0:T(8,128)(2,1)S(1)}, bf16[128,256]{1,0:T(8,128)(2,1)S(1)}, u32[]{:S(2)}, u32[]{:S(2)}) collective-permute-start(bf16[128,256]{1,0:T(8,128)(2,1)S(1)} %collective-permute-done.1), channel_id=1, source_target_pairs={{0,2},{1,3},{2,4},{3,5},{4,6},{5,7},{6,8},{7,9},{8,10},{9,11},{10,... | collective-permute-start | bytes 196616 | tf_op jit(solution)/shard_map/ppermute | solution.py:135
  13.1 4.3 %collective-permute-start.5 = (bf16[128,256]{1,0:T(8,128)(2,1)S(1)}, bf16[128,256]{1,0:T(8,128)(2,1)S(1)}, u32[]{:S(2)}, u32[]{:S(2)}) collective-permute-start(bf16[128,256]{1,0:T(8,128)(2,1)S(1)} %collective-permute-done.2), channel_id=1, source_target_pairs={{0,14},{1,15},{2,0},{3,1},{4,2},{5,3},{6,4},{7,5},{8,6},{9,7},{10,... | collective-permute-start | bytes 196616 | tf_op jit(solution)/shard_map/ppermute | solution.py:139
  17.4 4.3 %collective-permute-start.7 = (bf16[128,256]{1,0:T(8,128)(2,1)S(1)}, bf16[128,256]{1,0:T(8,128)(2,1)S(1)}, u32[]{:S(2)}, u32[]{:S(2)}) collective-permute-start(bf16[128,256]{1,0:T(8,128)(2,1)S(1)} %collective-permute-done.4), channel_id=1, source_target_pairs={{0,2},{1,3},{2,4},{3,5},{4,6},{5,7},{6,8},{7,9},{8,10},{9,11},{10,... | collective-permute-start | bytes 196616 | tf_op jit(solution)/shard_map/ppermute | solution.py:135
  17.4 4.3 %collective-permute-start.8 = (bf16[128,256]{1,0:T(8,128)(2,1)S(1)}, bf16[128,256]{1,0:T(8,128)(2,1)S(1)}, u32[]{:S(2)}, u32[]{:S(2)}) collective-permute-start(bf16[128,256]{1,0:T(8,128)(2,1)S(1)} %collective-permute-done.5), channel_id=1, source_target_pairs={{0,14},{1,15},{2,0},{3,1},{4,2},{5,3},{6,4},{7,5},{8,6},{9,7},{10,... | collective-permute-start | bytes 196616 | tf_op jit(solution)/shard_map/ppermute | solution.py:139
  20.1 3.9 %collective-permute-start.6 = (bf16[2,128,256]{2,1,0:T(8,128)(2,1)S(1)}, bf16[2,128,256]{2,1,0:T(8,128)(2,1)S(1)}, u32[]{:S(2)}, u32[]{:S(2)}) collective-permute-start(bf16[2,128,256]{2,1,0:T(8,128)(2,1)S(1)} %pad_maximum_fusion.1), channel_id=1, source_target_pairs={{0,1},{1,0},{2,3},{3,2},{4,5},{5,4},{6,7},{7,6},{8,9},{9,8},{10,11... | collective-permute-start | bytes 393224 | tf_op jit(solution)/shard_map/ppermute | solution.py:142
  21.8 5.9 %collective-permute-start.9 = (bf16[2,128,256]{2,1,0:T(8,128)(2,1)S(1)}, bf16[2,128,256]{2,1,0:T(8,128)(2,1)S(1)}, u32[]{:S(2)}, u32[]{:S(2)}) collective-permute-start(bf16[2,128,256]{2,1,0:T(8,128)(2,1)S(1)} %pad_maximum_fusion.2), channel_id=1, source_target_pairs={{0,1},{1,0},{2,3},{3,2},{4,5},{5,4},{6,7},{7,6},{8,9},{9,8},{10,11... | collective-permute-start | bytes 393224 | tf_op jit(solution)/shard_map/ppermute | solution.py:142
  23.2 4.3 %collective-permute-start.10 = (bf16[128,256]{1,0:T(8,128)(2,1)S(1)}, bf16[128,256]{1,0:T(8,128)(2,1)S(1)}, u32[]{:S(2)}, u32[]{:S(2)}) collective-permute-start(bf16[128,256]{1,0:T(8,128)(2,1)S(1)} %collective-permute-done.7), channel_id=1, source_target_pairs={{0,2},{1,3},{2,4},{3,5},{4,6},{5,7},{6,8},{7,9},{8,10},{9,11},{10,... | collective-permute-start | bytes 196616 | tf_op jit(solution)/shard_map/ppermute | solution.py:135
  27.5 3.2 %collective-permute-start.11 = (bf16[128,256]{1,0:T(8,128)(2,1)S(1)}, bf16[128,256]{1,0:T(8,128)(2,1)S(1)}, u32[]{:S(2)}, u32[]{:S(2)}) collective-permute-start(bf16[128,256]{1,0:T(8,128)(2,1)S(1)} %collective-permute-done.10), channel_id=1, source_target_pairs={{0,1},{1,0},{2,3},{3,2},{4,5},{5,4},{6,7},{7,6},{8,9},{9,8},{10,11... | collective-permute-start | bytes 196616 | tf_op jit(solution)/shard_map/ppermute | solution.py:145
  30.7 1.3 %copy-start = (bf16[16,128,256]{2,1,0:T(8,128)(2,1)}, bf16[16,128,256]{2,1,0:T(8,128)(2,1)S(1)}, u32[]{:S(2)}) copy-start(bf16[16,128,256]{2,1,0:T(8,128)(2,1)S(1)} %bitcast_dynamic-update-slice_fusion.pieces_ref) | copy-start | bytes 3145732

commit v8 on v7

--- a/solution.py
+++ b/solution.py
@@ -10,7 +10,7 @@
 CHUNKS = 8
 
 
-def ffn_kernel(cnt_ref, gu_ref, dn_ref, me_ref, pieces_ref, g_hbm, u_hbm, d_hbm, res_ref, out_ref,
+def ffn_kernel(cnt_ref, gu_ref, dn_ref, me_ref, table_ref, pieces_ref, g_hbm, u_hbm, d_hbm, out_ref,
                normed_s, accg_s, accu_s, hid_s, acco_s, gu_v, d_v, sems):
     n_src, rows, width = pieces_ref.shape
     tile = g_hbm.shape[1]
@@ -47,8 +47,16 @@
     accg_s[...] = jnp.zeros(accg_s.shape, jnp.float32)
     accu_s[...] = jnp.zeros(accu_s.shape, jnp.float32)
 
+    z_count = n_src // Y_LO
+    my_z = me_ref[0] // Y_LO
+    my_y = me_ref[0] % Y_LO
+
     def gu_body(m, carry):
-        x = normed_s[gu_ref[0, m]]
+        in_tile = gu_ref[0, m]
+        source = in_tile // per_src
+        dz = (source // Y_LO - my_z + z_count) % z_count
+        dy = jnp.where(source % Y_LO == my_y, 0, 1)
+        x = normed_s[table_ref[dz * Y_LO + dy] * per_src + in_tile % per_src]
         h = gu_ref[1, m]
         live = (m < cnt_ref[0]).astype(jnp.float32)
         both = jnp.dot(x, gu_v[m], preferred_element_type=jnp.float32) * live
@@ -74,21 +82,20 @@
         down_copy.wait()
         lax.fori_loop(k * step, (k + 1) * step, dn_body, 0, unroll=True)
     groups, dests, share, group_width = out_ref.shape
-    rows = pl.ds(pl.multiple_of(me_ref[0] * share, share), share)
+    for h in range(per_src):
+        acco_s[me_ref[0] * per_src + h] += pieces_ref[0, :, h * tile:(h + 1) * tile].astype(jnp.float32)
     per_group = group_width // tile
     for o in range(acco_s.shape[0]):
-        acco_s[o, rows, :] += res_ref[:, o * tile:(o + 1) * tile]
         block = acco_s[o].reshape(dests, share, tile).astype(out_ref.dtype)
         group, half = divmod(o, per_group)
         out_ref[group, :, :, half * tile:(half + 1) * tile] = block
 
 
-def ffn(counts, gu_blocks, down_blocks, me, pieces, gate_tiles, up_tiles, down_tiles, residual,
-        hid_blocks, groups):
+def ffn(counts, gu_blocks, down_blocks, me, table, pieces, gate_tiles, up_tiles, down_tiles,
+        hid_blocks, groups, share):
     n_src, rows, width = pieces.shape
     tile = gate_tiles.shape[1]
     in_blocks = n_src * width // tile
-    share = residual.shape[0]
     smem = pl.BlockSpec(memory_space=pltpu.SMEM)
     vmem = pl.BlockSpec(memory_space=pltpu.VMEM)
     hbm = pl.BlockSpec(memory_space=pl.ANY)
@@ -97,7 +104,7 @@
         ffn_kernel,
         out_shape=jax.ShapeDtypeStruct((groups, rows // share, share, in_blocks * tile // groups),
                                        jnp.bfloat16),
-        in_specs=[smem, smem, smem, smem, vmem, hbm, hbm, hbm, vmem],
+        in_specs=[smem, smem, smem, smem, smem, vmem, hbm, hbm, hbm],
         out_specs=vmem,
         scratch_shapes=[
             pltpu.VMEM((in_blocks, rows, tile), jnp.bfloat16),
@@ -109,8 +116,8 @@
             pltpu.VMEM((slots, tile, tile), jnp.bfloat16),
             pltpu.SemaphoreType.DMA((3, CHUNKS)),
         ],
-    )(counts.reshape(-1), gu_blocks, down_blocks, me.reshape(1), pieces, gate_tiles, up_tiles,
-      down_tiles, residual)
+    )(counts.reshape(-1), gu_blocks, down_blocks, me.reshape(1), table, pieces, gate_tiles,
+      up_tiles, down_tiles)
 
 def ring_pairs(count, step):
     return [(i, ((i // Y_LO + step) % count) * Y_LO + i % Y_LO) for i in range(count * Y_LO)]
@@ -148,21 +155,12 @@
     table = [[0] * Y_LO for _ in range(z_count)]
     for index, (dz, dy) in enumerate(origins):
         table[dz][dy] = index
-    src_ids = jnp.arange(tp_count)
-    dz = (src_ids // Y_LO - my_z) % z_count
-    dy = (src_ids % Y_LO != my_y).astype(jnp.int32)
-    position = jnp.array(table, jnp.int32)[dz, dy]
-    in_tile = gu_blocks[0]
-    moved = position[in_tile // per_src] * per_src + in_tile % per_src
-    gu_local = jnp.stack([moved, gu_blocks[1]])
     feat_width = tp_count * own_width
-    in_blocks = feat_width // tile
     hid_blocks = FF // tp_count // tile
     share = own_rows // tp_count
-    own = jnp.take(lax.dynamic_slice_in_dim(pieces, me * share, share, 1), position, axis=0)
-    residual = jnp.transpose(own, (1, 0, 2)).reshape(share, feat_width).astype(jnp.float32)
-    outgoing = ffn(counts, gu_local, down_blocks, me.astype(jnp.int32), pieces, gate_tiles,
-                   up_tiles, down_tiles, residual, hid_blocks, ctx_count)
+    outgoing = ffn(counts, gu_blocks, down_blocks, me.astype(jnp.int32),
+                   jnp.array(table, jnp.int32).reshape(-1), pieces, gate_tiles, up_tiles,
+                   down_tiles, hid_blocks, ctx_count, share)
     incoming = lax.all_to_all(
         outgoing.reshape(ctx_count * tp_count, share, feat_width // ctx_count),
         ("ctx", "tp"), 0, 0, tiled=True,

time: 90.6 us -> 87.5 us (0.966)
  other arithmetic: 3 us -> 0.18 us
  starting transfers between devices: 16.3 us -> 18.5 us
  local copies, waits for them, and re-layouts: 4.33 us -> 2.58 us
    ppermute x4, starting transfers between devices: 1.65 us -> 4.47 us  [per_device(): fwd = lax.ppermute(fwd, 'tp', ring_pairs(z_count, 1))]
    gather x3 -> x0, local copies, waits for them, and re-layouts: 2.7 us -> none  [the longest x1 1.36 us: per_device(): position = jnp.array(table, jnp.int32)[dz, dy]]
    ppermute x4, waiting for transfers between devices: 5.29 us -> 4.09 us  [per_device(): fwd = lax.ppermute(fwd, 'tp', ring_pairs(z_count, 1))]
    unnamed x14, local copies, waits for them, and re-layouts: 0.96 us -> 1.93 us
  transfers between devices with their start and end apart: 12 -> 12, of which waited for: 5 -> 5; matrix products, arithmetic and copies ran while one was open for 6% -> 1% of each run, Pallas kernels for 0% -> 0%
where the time goes in v8:
time: 87.5 us; the launch traced here: 87.3 us
  blocking collectives  49 us (56%)
  starting transfers between devices  18.5 us (21%)
  waiting for transfers between devices  8.69 us (10%)
  Pallas kernels  8.29 us (9%)
  local copies, waits for them, and re-layouts  2.58 us (3%)
    all_to_all x1, blocking collectives, per_device(): lax.all_to_all(outgoing.reshape(ctx_count * tp_count, share, feat_width /...  49 us
    ppermute x3, starting transfers between devices, per_device(): bwd = lax.ppermute(bwd, 'tp', ring_pairs(z_count, -1))  9.47 us
    pallas_call x1, Pallas kernels, ffn(): pl.pallas_call(ffn_kernel, out_shape=jax.ShapeDtypeStruct((groups, rows /...  8.29 us
    ppermute x4, starting transfers between devices, per_device(): fwd = lax.ppermute(fwd, 'tp', ring_pairs(z_count, 1))  4.47 us
    ppermute x4, waiting for transfers between devices, per_device(): fwd = lax.ppermute(fwd, 'tp', ring_pairs(z_count, 1))  4.09 us
    ppermute x1, waiting for transfers between devices, per_device(): arrays.append(lax.ppermute(fwd, 'tp', swap)[None])  3.82 us
    ppermute x3, starting transfers between devices, per_device(): arrays.append(lax.ppermute(jnp.stack([fwd, bwd]), 'tp', swap))  3.07 us
    unnamed x14, local copies, waits for them, and re-layouts  1.93 us
  transfers between devices with their start and end apart: 12, of which 5 were waited for; matrix products, arithmetic and copies ran while one was open for 1% of the time, Pallas kernels for 0%

profile of v8, /device:TPU:1, one launch (start us, length us, event | category | flops | bytes accessed | tf_op | source)
XLA Modules:
  0.0 87.3 jit_solution(10369691087832276709)
XLA Ops:
  0.0 2.5 %collective-permute-start.1 = (bf16[128,256]{1,0:T(8,128)(2,1)}, bf16[128,256]{1,0:T(8,128)(2,1)S(1)}, u32[]{:S(2)}, u32[]{:S(2)}) collective-permute-start(bf16[128,256]{1,0:T(8,128)(2,1)} %param.8), channel_id=1, source_target_pairs={{0,2},{1,3},{2,4},{3,5},{4,6},{5,7},{6,8},{7,9},{8,10},{9,11},{10,... | collective-permute-start | bytes 196616 | tf_op jit(solution)/shard_map/ppermute | solution.py:142
  2.5 1.3 %collective-permute-start = (bf16[128,256]{1,0:T(8,128)(2,1)}, bf16[128,256]{1,0:T(8,128)(2,1)S(1)}, u32[]{:S(2)}, u32[]{:S(2)}) collective-permute-start(bf16[128,256]{1,0:T(8,128)(2,1)} %param.8), channel_id=1, source_target_pairs={{0,1},{1,0},{2,3},{3,2},{4,5},{5,4},{6,7},{7,6},{8,9},{9,8},{10,11... | collective-permute-start | bytes 196616 | tf_op jit(solution)/shard_map/ppermute | solution.py:138
  3.8 3.9 %collective-permute-start.2 = (bf16[128,256]{1,0:T(8,128)(2,1)}, bf16[128,256]{1,0:T(8,128)(2,1)S(1)}, u32[]{:S(2)}, u32[]{:S(2)}) collective-permute-start(bf16[128,256]{1,0:T(8,128)(2,1)} %param.8), channel_id=1, source_target_pairs={{0,14},{1,15},{2,0},{3,1},{4,2},{5,3},{6,4},{7,5},{8,6},{9,7},{10,... | collective-permute-start | bytes 196616 | tf_op jit(solution)/shard_map/ppermute | solution.py:146
  7.7 0.9 %bitcast_dynamic-update-slice_fusion.3 = bf16[16,128,256]{2,1,0:T(8,128)(2,1)S(1)} fusion(bf16[128,256]{1,0:T(8,128)(2,1)} %param.8), kind=kLoop, calls=%fused_computation.7 | loop fusion | bytes 131072
  8.6 0.0 collective-permute-done.1
  8.6 0.8 collective-permute-done.2
  9.4 0.3 collective-permute-start.3
  9.7 0.0 collective-permute-start.4
  9.7 2.8 %collective-permute-start.5 = (bf16[128,256]{1,0:T(8,128)(2,1)S(1)}, bf16[128,256]{1,0:T(8,128)(2,1)S(1)}, u32[]{:S(2)}, u32[]{:S(2)}) collective-permute-start(bf16[128,256]{1,0:T(8,128)(2,1)S(1)} %collective-permute-done.2), channel_id=1, source_target_pairs={{0,14},{1,15},{2,0},{3,1},{4,2},{5,3},{6,4},{7,5},{8,6},{9,7},{10,... | collective-permute-start | bytes 196616 | tf_op jit(solution)/shard_map/ppermute | solution.py:146
  12.5 0.0 collective-permute-done
  12.6 1.6 %collective-permute-done.4 = bf16[128,256]{1,0:T(8,128)(2,1)S(1)} collective-permute-done((bf16[128,256]{1,0:T(8,128)(2,1)S(1)}, bf16[128,256]{1,0:T(8,128)(2,1)S(1)}, u32[]{:S(2)}, u32[]{:S(2)}) %collective-permute-start.4) | collective-permute-done | bytes 65568 | tf_op jit(solution)/shard_map/ppermute | solution.py:142
  14.2 0.0 collective-permute-start.7
  14.2 0.0 collective-permute-done.5
  14.2 2.7 %collective-permute-start.8 = (bf16[128,256]{1,0:T(8,128)(2,1)S(1)}, bf16[128,256]{1,0:T(8,128)(2,1)S(1)}, u32[]{:S(2)}, u32[]{:S(2)}) collective-permute-start(bf16[128,256]{1,0:T(8,128)(2,1)S(1)} %collective-permute-done.5), channel_id=1, source_target_pairs={{0,14},{1,15},{2,0},{3,1},{4,2},{5,3},{6,4},{7,5},{8,6},{9,7},{10,... | collective-permute-start | bytes 196616 | tf_op jit(solution)/shard_map/ppermute | solution.py:146
  16.9 1.4 %collective-permute-start.6 = (bf16[2,128,256]{2,1,0:T(8,128)(2,1)S(1)}, bf16[2,128,256]{2,1,0:T(8,128)(2,1)S(1)}, u32[]{:S(2)}, u32[]{:S(2)}) collective-permute-start(bf16[2,128,256]{2,1,0:T(8,128)(2,1)S(1)} %pad_maximum_fusion.1), channel_id=1, source_target_pairs={{0,1},{1,0},{2,3},{3,2},{4,5},{5,4},{6,7},{7,6},{8,9},{9,8},{10,11... | collective-permute-start | bytes 393224 | tf_op jit(solution)/shard_map/ppermute | solution.py:149
  18.3 0.2 collective-permute-done.7
  18.5 0.0 collective-permute-done.8
  18.5 1.4 %collective-permute-start.9 = (bf16[2,128,256]{2,1,0:T(8,128)(2,1)S(1)}, bf16[2,128,256]{2,1,0:T(8,128)(2,1)S(1)}, u32[]{:S(2)}, u32[]{:S(2)}) collective-permute-start(bf16[2,128,256]{2,1,0:T(8,128)(2,1)S(1)} %pad_maximum_fusion.2), channel_id=1, source_target_pairs={{0,1},{1,0},{2,3},{3,2},{4,5},{5,4},{6,7},{7,6},{8,9},{9,8},{10,11... | collective-permute-start | bytes 393224 | tf_op jit(solution)/shard_map/ppermute | solution.py:149
  19.9 2.0 %collective-permute-start.10 = (bf16[128,256]{1,0:T(8,128)(2,1)S(1)}, bf16[128,256]{1,0:T(8,128)(2,1)S(1)}, u32[]{:S(2)}, u32[]{:S(2)}) collective-permute-start(bf16[128,256]{1,0:T(8,128)(2,1)S(1)} %collective-permute-done.7), channel_id=1, source_target_pairs={{0,2},{1,3},{2,4},{3,5},{4,6},{5,7},{6,8},{7,9},{8,10},{9,11},{10,... | collective-permute-start | bytes 196616 | tf_op jit(solution)/shard_map/ppermute | solution.py:142
  21.9 0.0 collective-permute-done.3
  21.9 0.0 collective-permute-done.6
  22.0 2.2 %collective-permute-done.10 = bf16[128,256]{1,0:T(8,128)(2,1)S(1)} collective-permute-done((bf16[128,256]{1,0:T(8,128)(2,1)S(1)}, bf16[128,256]{1,0:T(8,128)(2,1)S(1)}, u32[]{:S(2)}, u32[]{:S(2)}) %collective-permute-start.10) | collective-permute-done | bytes 65568 | tf_op jit(solution)/shard_map/ppermute | solution.py:142
  24.2 0.2 collective-permute-start.11
  24.4 0.0 collective-permute-done.9
  24.5 3.8 %collective-permute-done.11 = bf16[128,256]{1,0:T(8,128)(2,1)S(1)} collective-permute-done((bf16[128,256]{1,0:T(8,128)(2,1)S(1)}, bf16[128,256]{1,0:T(8,128)(2,1)S(1)}, u32[]{:S(2)}, u32[]{:S(2)}) %collective-permute-start.11) | collective-permute-done | bytes 65568 | tf_op jit(solution)/shard_map/ppermute | solution.py:152
  28.3 0.0 copy-start
  28.3 1.0 %copy-done = bf16[16,128,256]{2,1,0:T(8,128)(2,1)} copy-done((bf16[16,128,256]{2,1,0:T(8,128)(2,1)}, bf16[16,128,256]{2,1,0:T(8,128)(2,1)S(1)}, u32[]{:S(2)}) %copy-start) | copy-done | bytes 1048600
  29.3 8.3 %shard_map.82 = bf16[16,16,8,256]{3,2,1,0:T(8,128)(2,1)} custom-call(s32[2]{0:T(128)} %bitcast.34, s32[2,64]{1,0:T(2,128)} %gu_ref.1, s32[2,64]{1,0:T(2,128)} %dn_ref.1, s32[1]{0:T(128)} %bitcast.1.me_ref, s32[16]{0:T(128)} %constant.10.table_ref, bf16[16,128,256]{2,1,0:T(8,128)(2,1)} %copy-done, bf16[64,128,128]{2,1,0:T(8,128)(2,1)} %g_hbm.1, ...), custom_call_target="tpu_custom_call" | custom-call | tf_op jit(solution)/shard_map/pallas_call | solution.py:103
  37.6 49.0 %all_to_all.5 = bf16[256,8,256]{2,1,0:T(8,128)(2,1)S(1)} all-to-all(bf16[256,8,256]{2,1,0:T(8,128)(2,1)} %bitcast.26), channel_id=1, replica_groups=mesh['ctx'=16,'tp'=16] {'ctx','tp'}, dimensions={0} | all-to-all | bytes 2097152 | tf_op jit(solution)/shard_map/all_to_all | solution.py:164
  86.5 0.1 bitcast_reduce_fusion
  86.7 0.6 copy.9
  (15 shorter events, 0.1 us)
Async XLA Ops:
  0.0 8.6 %collective-permute-start.1 = (bf16[128,256]{1,0:T(8,128)(2,1)}, bf16[128,256]{1,0:T(8,128)(2,1)S(1)}, u32[]{:S(2)}, u32[]{:S(2)}) collective-permute-start(bf16[128,256]{1,0:T(8,128)(2,1)} %param.8), channel_id=1, source_target_pairs={{0,2},{1,3},{2,4},{3,5},{4,6},{5,7},{6,8},{7,9},{8,10},{9,11},{10,... | collective-permute-start | bytes 196616 | tf_op jit(solution)/shard_map/ppermute | solution.py:142
  2.5 10.1 %collective-permute-start = (bf16[128,256]{1,0:T(8,128)(2,1)}, bf16[128,256]{1,0:T(8,128)(2,1)S(1)}, u32[]{:S(2)}, u32[]{:S(2)}) collective-permute-start(bf16[128,256]{1,0:T(8,128)(2,1)} %param.8), channel_id=1, source_target_pairs={{0,1},{1,0},{2,3},{3,2},{4,5},{5,4},{6,7},{7,6},{8,9},{9,8},{10,11... | collective-permute-start | bytes 196616 | tf_op jit(solution)/shard_map/ppermute | solution.py:138
  3.8 5.6 %collective-permute-start.2 = (bf16[128,256]{1,0:T(8,128)(2,1)}, bf16[128,256]{1,0:T(8,128)(2,1)S(1)}, u32[]{:S(2)}, u32[]{:S(2)}) collective-permute-start(bf16[128,256]{1,0:T(8,128)(2,1)} %param.8), channel_id=1, source_target_pairs={{0,14},{1,15},{2,0},{3,1},{4,2},{5,3},{6,4},{7,5},{8,6},{9,7},{10,... | collective-permute-start | bytes 196616 | tf_op jit(solution)/shard_map/ppermute | solution.py:146
  9.4 12.5 %collective-permute-start.3 = (bf16[2,128,256]{2,1,0:T(8,128)(2,1)S(1)}, bf16[2,128,256]{2,1,0:T(8,128)(2,1)S(1)}, u32[]{:S(2)}, u32[]{:S(2)}) collective-permute-start(bf16[2,128,256]{2,1,0:T(8,128)(2,1)S(1)} %pad_maximum_fusion), channel_id=1, source_target_pairs={{0,1},{1,0},{2,3},{3,2},{4,5},{5,4},{6,7},{7,6},{8,9},{9,8},{10,11... | collective-permute-start | bytes 393224 | tf_op jit(solution)/shard_map/ppermute | solution.py:149
  9.7 4.5 %collective-permute-start.4 = (bf16[128,256]{1,0:T(8,128)(2,1)S(1)}, bf16[128,256]{1,0:T(8,128)(2,1)S(1)}, u32[]{:S(2)}, u32[]{:S(2)}) collective-permute-start(bf16[128,256]{1,0:T(8,128)(2,1)S(1)} %collective-permute-done.1), channel_id=1, source_target_pairs={{0,2},{1,3},{2,4},{3,5},{4,6},{5,7},{6,8},{7,9},{8,10},{9,11},{10,... | collective-permute-start | bytes 196616 | tf_op jit(solution)/shard_map/ppermute | solution.py:142
  9.7 4.5 %collective-permute-start.5 = (bf16[128,256]{1,0:T(8,128)(2,1)S(1)}, bf16[128,256]{1,0:T(8,128)(2,1)S(1)}, u32[]{:S(2)}, u32[]{:S(2)}) collective-permute-start(bf16[128,256]{1,0:T(8,128)(2,1)S(1)} %collective-permute-done.2), channel_id=1, source_target_pairs={{0,14},{1,15},{2,0},{3,1},{4,2},{5,3},{6,4},{7,5},{8,6},{9,7},{10,... | collective-permute-start | bytes 196616 | tf_op jit(solution)/shard_map/ppermute | solution.py:146
  14.2 4.3 %collective-permute-start.7 = (bf16[128,256]{1,0:T(8,128)(2,1)S(1)}, bf16[128,256]{1,0:T(8,128)(2,1)S(1)}, u32[]{:S(2)}, u32[]{:S(2)}) collective-permute-start(bf16[128,256]{1,0:T(8,128)(2,1)S(1)} %collective-permute-done.4), channel_id=1, source_target_pairs={{0,2},{1,3},{2,4},{3,5},{4,6},{5,7},{6,8},{7,9},{8,10},{9,11},{10,... | collective-permute-start | bytes 196616 | tf_op jit(solution)/shard_map/ppermute | solution.py:142
  14.2 4.3 %collective-permute-start.8 = (bf16[128,256]{1,0:T(8,128)(2,1)S(1)}, bf16[128,256]{1,0:T(8,128)(2,1)S(1)}, u32[]{:S(2)}, u32[]{:S(2)}) collective-permute-start(bf16[128,256]{1,0:T(8,128)(2,1)S(1)} %collective-permute-done.5), channel_id=1, source_target_pairs={{0,14},{1,15},{2,0},{3,1},{4,2},{5,3},{6,4},{7,5},{8,6},{9,7},{10,... | collective-permute-start | bytes 196616 | tf_op jit(solution)/shard_map/ppermute | solution.py:146
  16.9 5.1 %collective-permute-start.6 = (bf16[2,128,256]{2,1,0:T(8,128)(2,1)S(1)}, bf16[2,128,256]{2,1,0:T(8,128)(2,1)S(1)}, u32[]{:S(2)}, u32[]{:S(2)}) collective-permute-start(bf16[2,128,256]{2,1,0:T(8,128)(2,1)S(1)} %pad_maximum_fusion.1), channel_id=1, source_target_pairs={{0,1},{1,0},{2,3},{3,2},{4,5},{5,4},{6,7},{7,6},{8,9},{9,8},{10,11... | collective-permute-start | bytes 393224 | tf_op jit(solution)/shard_map/ppermute | solution.py:149
  18.5 5.9 %collective-permute-start.9 = (bf16[2,128,256]{2,1,0:T(8,128)(2,1)S(1)}, bf16[2,128,256]{2,1,0:T(8,128)(2,1)S(1)}, u32[]{:S(2)}, u32[]{:S(2)}) collective-permute-start(bf16[2,128,256]{2,1,0:T(8,128)(2,1)S(1)} %pad_maximum_fusion.2), channel_id=1, source_target_pairs={{0,1},{1,0},{2,3},{3,2},{4,5},{5,4},{6,7},{7,6},{8,9},{9,8},{10,11... | collective-permute-start | bytes 393224 | tf_op jit(solution)/shard_map/ppermute | solution.py:149
  19.9 4.3 %collective-permute-start.10 = (bf16[128,256]{1,0:T(8,128)(2,1)S(1)}, bf16[128,256]{1,0:T(8,128)(2,1)S(1)}, u32[]{:S(2)}, u32[]{:S(2)}) collective-permute-start(bf16[128,256]{1,0:T(8,128)(2,1)S(1)} %collective-permute-done.7), channel_id=1, source_target_pairs={{0,2},{1,3},{2,4},{3,5},{4,6},{5,7},{6,8},{7,9},{8,10},{9,11},{10,... | collective-permute-start | bytes 196616 | tf_op jit(solution)/shard_map/ppermute | solution.py:142
  24.2 4.1 %collective-permute-start.11 = (bf16[128,256]{1,0:T(8,128)(2,1)S(1)}, bf16[128,256]{1,0:T(8,128)(2,1)S(1)}, u32[]{:S(2)}, u32[]{:S(2)}) collective-permute-start(bf16[128,256]{1,0:T(8,128)(2,1)S(1)} %collective-permute-done.10), channel_id=1, source_target_pairs={{0,1},{1,0},{2,3},{3,2},{4,5},{5,4},{6,7},{7,6},{8,9},{9,8},{10,11... | collective-permute-start | bytes 196616 | tf_op jit(solution)/shard_map/ppermute | solution.py:152
  28.3 1.0 %copy-start = (bf16[16,128,256]{2,1,0:T(8,128)(2,1)}, bf16[16,128,256]{2,1,0:T(8,128)(2,1)S(1)}, u32[]{:S(2)}) copy-start(bf16[16,128,256]{2,1,0:T(8,128)(2,1)S(1)} %bitcast_dynamic-update-slice_fusion.pieces_ref) | copy-start | bytes 3145732

commit v9 on v8

--- a/solution.py
+++ b/solution.py
@@ -119,8 +119,8 @@
     )(counts.reshape(-1), gu_blocks, down_blocks, me.reshape(1), table, pieces, gate_tiles,
       up_tiles, down_tiles)
 
-def ring_pairs(count, step):
-    return [(i, ((i // Y_LO + step) % count) * Y_LO + i % Y_LO) for i in range(count * Y_LO)]
+def ring_pairs(count, step, flip=0):
+    return [(i, ((i // Y_LO + step) % count) * Y_LO + (i % Y_LO ^ flip)) for i in range(count * Y_LO)]
 
 
 def per_device(tokens, gate_tiles, up_tiles, down_tiles, gu_blocks, down_blocks, counts):
@@ -139,18 +139,17 @@
     origins = [(0, 0), (0, 1)]
     fwd = bwd = tokens
     for k in range(1, half + 1):
+        arrays.append(lax.ppermute(fwd, "tp", ring_pairs(z_count, 1, 1))[None])
+        origins.append((-k % z_count, 1))
         fwd = lax.ppermute(fwd, "tp", ring_pairs(z_count, 1))
         arrays.append(fwd[None])
         origins.append((-k % z_count, 0))
         if k < z_count - half:
+            arrays.append(lax.ppermute(bwd, "tp", ring_pairs(z_count, -1, 1))[None])
+            origins.append((k, 1))
             bwd = lax.ppermute(bwd, "tp", ring_pairs(z_count, -1))
             arrays.append(bwd[None])
             origins.append((k, 0))
-            arrays.append(lax.ppermute(jnp.stack([fwd, bwd]), "tp", swap))
-            origins += [(-k % z_count, 1), (k, 1)]
-        else:
-            arrays.append(lax.ppermute(fwd, "tp", swap)[None])
-            origins.append((-k % z_count, 1))
     pieces = jnp.concatenate(arrays)
     table = [[0] * Y_LO for _ in range(z_count)]
     for index, (dz, dy) in enumerate(origins):

time: 87.5 us -> 86.2 us (0.985)
  waiting for transfers between devices: 8.69 us -> 4.63 us
  starting transfers between devices: 18.5 us -> 21.5 us
    ppermute x4 -> x7, starting transfers between devices: 3.25 us -> 11.8 us  [the longest x3 7.87 us: per_device(): arrays.append(lax.ppermute(bwd, 'tp', ring_pairs(z_count, -1, 1))[None])]
    ppermute x3, starting transfers between devices: 9.47 us -> 3.64 us  [per_device(): bwd = lax.ppermute(bwd, 'tp', ring_pairs(z_count, -1))]
    ppermute x4, waiting for transfers between devices: 4.09 us -> 0.69 us  [per_device(): fwd = lax.ppermute(fwd, 'tp', ring_pairs(z_count, 1))]
    ppermute x4 -> x7, waiting for transfers between devices: 3.82 us -> 2.79 us  [the longest x4 2.79 us: per_device(): arrays.append(lax.ppermute(fwd, 'tp', ring_pairs(z_count, 1, 1))[None])]
    unnamed x14 -> x17, local copies, waits for them, and re-layouts: 1.93 us -> 1.93 us
  transfers between devices with their start and end apart: 12 -> 15, of which waited for: 5 -> 5; matrix products, arithmetic and copies ran while one was open for 1% -> 1% of each run, Pallas kernels for 0% -> 0%
where the time goes in v9:
time: 86.2 us; the launch traced here: 86 us
  blocking collectives  48.7 us (56%)
  starting transfers between devices  21.5 us (25%)
  Pallas kernels  8.27 us (10%)
  waiting for transfers between devices  4.63 us (5%)
  local copies, waits for them, and re-layouts  2.58 us (3%)
    all_to_all x1, blocking collectives, per_device(): lax.all_to_all(outgoing.reshape(ctx_count * tp_count, share, feat_width /...  48.7 us
    pallas_call x1, Pallas kernels, ffn(): pl.pallas_call(ffn_kernel, out_shape=jax.ShapeDtypeStruct((groups, rows /...  8.27 us
    ppermute x3, starting transfers between devices, per_device(): arrays.append(lax.ppermute(bwd, 'tp', ring_pairs(z_count, -1, 1))[None])  7.87 us
    ppermute x4, starting transfers between devices, per_device(): fwd = lax.ppermute(fwd, 'tp', ring_pairs(z_count, 1))  4.86 us
    ppermute x4, starting transfers between devices, per_device(): arrays.append(lax.ppermute(fwd, 'tp', ring_pairs(z_count, 1, 1))[None])  3.89 us
    ppermute x3, starting transfers between devices, per_device(): bwd = lax.ppermute(bwd, 'tp', ring_pairs(z_count, -1))  3.64 us
    ppermute x4, waiting for transfers between devices, per_device(): arrays.append(lax.ppermute(fwd, 'tp', ring_pairs(z_count, 1, 1))[None])  2.79 us
    unnamed x17, local copies, waits for them, and re-layouts  1.93 us
  transfers between devices with their start and end apart: 15, of which 5 were waited for; matrix products, arithmetic and copies ran while one was open for 1% of the time, Pallas kernels for 0%

profile of v9, /device:TPU:1, one launch (start us, length us, event | category | flops | bytes accessed | tf_op | source)
XLA Modules:
  0.0 86.0 jit_solution(12009035009704019581)
XLA Ops:
  0.0 2.5 %collective-permute-start.2 = (bf16[128,256]{1,0:T(8,128)(2,1)}, bf16[128,256]{1,0:T(8,128)(2,1)S(1)}, u32[]{:S(2)}, u32[]{:S(2)}) collective-permute-start(bf16[128,256]{1,0:T(8,128)(2,1)} %param.8), channel_id=1, source_target_pairs={{0,2},{1,3},{2,4},{3,5},{4,6},{5,7},{6,8},{7,9},{8,10},{9,11},{10,... | collective-permute-start | bytes 196616 | tf_op jit(solution)/shard_map/ppermute | solution.py:144
  2.5 1.3 %collective-permute-start = (bf16[128,256]{1,0:T(8,128)(2,1)}, bf16[128,256]{1,0:T(8,128)(2,1)S(1)}, u32[]{:S(2)}, u32[]{:S(2)}) collective-permute-start(bf16[128,256]{1,0:T(8,128)(2,1)} %param.8), channel_id=1, source_target_pairs={{0,1},{1,0},{2,3},{3,2},{4,5},{5,4},{6,7},{7,6},{8,9},{9,8},{10,11... | collective-permute-start | bytes 196616 | tf_op jit(solution)/shard_map/ppermute | solution.py:138
  3.8 1.5 %collective-permute-start.1 = (bf16[128,256]{1,0:T(8,128)(2,1)}, bf16[128,256]{1,0:T(8,128)(2,1)S(1)}, u32[]{:S(2)}, u32[]{:S(2)}) collective-permute-start(bf16[128,256]{1,0:T(8,128)(2,1)} %param.8), channel_id=1, source_target_pairs={{0,3},{1,2},{2,5},{3,4},{4,7},{5,6},{6,9},{7,8},{8,11},{9,10},{10,... | collective-permute-start | bytes 196616 | tf_op jit(solution)/shard_map/ppermute | solution.py:142
  5.3 2.3 %collective-permute-start.3 = (bf16[128,256]{1,0:T(8,128)(2,1)}, bf16[128,256]{1,0:T(8,128)(2,1)S(1)}, u32[]{:S(2)}, u32[]{:S(2)}) collective-permute-start(bf16[128,256]{1,0:T(8,128)(2,1)} %param.8), channel_id=1, source_target_pairs={{0,15},{1,14},{2,1},{3,0},{4,3},{5,2},{6,5},{7,4},{8,7},{9,6},{10,... | collective-permute-start | bytes 196616 | tf_op jit(solution)/shard_map/ppermute | solution.py:148
  7.6 2.5 %collective-permute-start.4 = (bf16[128,256]{1,0:T(8,128)(2,1)}, bf16[128,256]{1,0:T(8,128)(2,1)S(1)}, u32[]{:S(2)}, u32[]{:S(2)}) collective-permute-start(bf16[128,256]{1,0:T(8,128)(2,1)} %param.8), channel_id=1, source_target_pairs={{0,14},{1,15},{2,0},{3,1},{4,2},{5,3},{6,4},{7,5},{8,6},{9,7},{10,... | collective-permute-start | bytes 196616 | tf_op jit(solution)/shard_map/ppermute | solution.py:150
  10.1 0.9 %bitcast_dynamic-update-slice_fusion.15 = bf16[16,128,256]{2,1,0:T(8,128)(2,1)S(1)} fusion(bf16[128,256]{1,0:T(8,128)(2,1)} %param.8), kind=kLoop, calls=%fused_computation.16 | loop fusion | bytes 131072
  11.0 0.0 collective-permute-done.2
  11.0 0.0 collective-permute-start.5
  11.0 0.0 collective-permute-done
  11.0 0.8 collective-permute-start.6
  11.7 0.0 collective-permute-done.4
  11.7 3.5 %collective-permute-start.7 = (bf16[128,256]{1,0:T(8,128)(2,1)S(1)}, bf16[128,256]{1,0:T(8,128)(2,1)S(1)}, u32[]{:S(2)}, u32[]{:S(2)}) collective-permute-start(bf16[128,256]{1,0:T(8,128)(2,1)S(1)} %collective-permute-done.4), channel_id=1, source_target_pairs={{0,15},{1,14},{2,1},{3,0},{4,3},{5,2},{6,5},{7,4},{8,7},{9,6},{10,... | collective-permute-start | bytes 196616 | tf_op jit(solution)/shard_map/ppermute | solution.py:148
  15.3 0.8 collective-permute-start.8
  16.2 1.3 %collective-permute-start.9 = (bf16[128,256]{1,0:T(8,128)(2,1)S(1)}, bf16[128,256]{1,0:T(8,128)(2,1)S(1)}, u32[]{:S(2)}, u32[]{:S(2)}) collective-permute-start(bf16[128,256]{1,0:T(8,128)(2,1)S(1)} %collective-permute-done.6), channel_id=1, source_target_pairs={{0,3},{1,2},{2,5},{3,4},{4,7},{5,6},{6,9},{7,8},{8,11},{9,10},{10,... | collective-permute-start | bytes 196616 | tf_op jit(solution)/shard_map/ppermute | solution.py:142
  17.5 0.7 collective-permute-start.10
  18.2 0.7 collective-permute-done.8
  18.9 2.0 %collective-permute-start.11 = (bf16[128,256]{1,0:T(8,128)(2,1)S(1)}, bf16[128,256]{1,0:T(8,128)(2,1)S(1)}, u32[]{:S(2)}, u32[]{:S(2)}) collective-permute-start(bf16[128,256]{1,0:T(8,128)(2,1)S(1)} %collective-permute-done.8), channel_id=1, source_target_pairs={{0,15},{1,14},{2,1},{3,0},{4,3},{5,2},{6,5},{7,4},{8,7},{9,6},{10,... | collective-permute-start | bytes 196616 | tf_op jit(solution)/shard_map/ppermute | solution.py:148
  20.9 0.0 collective-permute-done.5
  20.9 0.3 collective-permute-start.12
  21.3 0.6 collective-permute-done.10
  21.9 1.0 %collective-permute-start.13 = (bf16[128,256]{1,0:T(8,128)(2,1)S(1)}, bf16[128,256]{1,0:T(8,128)(2,1)S(1)}, u32[]{:S(2)}, u32[]{:S(2)}) collective-permute-start(bf16[128,256]{1,0:T(8,128)(2,1)S(1)} %collective-permute-done.10), channel_id=1, source_target_pairs={{0,3},{1,2},{2,5},{3,4},{4,7},{5,6},{6,9},{7,8},{8,11},{9,10},{10,... | collective-permute-start | bytes 196616 | tf_op jit(solution)/shard_map/ppermute | solution.py:142
  22.9 0.9 %collective-permute-start.14 = (bf16[128,256]{1,0:T(8,128)(2,1)S(1)}, bf16[128,256]{1,0:T(8,128)(2,1)S(1)}, u32[]{:S(2)}, u32[]{:S(2)}) collective-permute-start(bf16[128,256]{1,0:T(8,128)(2,1)S(1)} %collective-permute-done.10), channel_id=1, source_target_pairs={{0,2},{1,3},{2,4},{3,5},{4,6},{5,7},{6,8},{7,9},{8,10},{9,11},{10,... | collective-permute-start | bytes 196616 | tf_op jit(solution)/shard_map/ppermute | solution.py:144
  23.8 0.0 collective-permute-done.9
  23.8 0.0 collective-permute-done.11
  23.9 0.5 collective-permute-done.12
  24.4 2.8 %collective-permute-done.13 = bf16[128,256]{1,0:T(8,128)(2,1)S(1)} collective-permute-done((bf16[128,256]{1,0:T(8,128)(2,1)S(1)}, bf16[128,256]{1,0:T(8,128)(2,1)S(1)}, u32[]{:S(2)}, u32[]{:S(2)}) %collective-permute-start.13) | collective-permute-done | bytes 65568 | tf_op jit(solution)/shard_map/ppermute | solution.py:142
  27.1 0.1 collective-permute-done.14
  27.3 1.0 %copy-done = bf16[16,128,256]{2,1,0:T(8,128)(2,1)} copy-done((bf16[16,128,256]{2,1,0:T(8,128)(2,1)}, bf16[16,128,256]{2,1,0:T(8,128)(2,1)S(1)}, u32[]{:S(2)}) %copy-start) | copy-done | bytes 1048600
  28.2 8.3 %shard_map.82 = bf16[16,16,8,256]{3,2,1,0:T(8,128)(2,1)} custom-call(s32[2]{0:T(128)} %bitcast.40, s32[2,64]{1,0:T(2,128)} %gu_ref.1, s32[2,64]{1,0:T(2,128)} %dn_ref.1, s32[1]{0:T(128)} %bitcast.1.me_ref, s32[16]{0:T(128)} %constant.10.table_ref, bf16[16,128,256]{2,1,0:T(8,128)(2,1)} %copy-done, bf16[64,128,128]{2,1,0:T(8,128)(2,1)} %g_hbm.1, ...), custom_call_target="tpu_custom_call" | custom-call | tf_op jit(solution)/shard_map/pallas_call | solution.py:103
  36.5 48.7 %all_to_all.5 = bf16[256,8,256]{2,1,0:T(8,128)(2,1)S(1)} all-to-all(bf16[256,8,256]{2,1,0:T(8,128)(2,1)} %bitcast.38), channel_id=1, replica_groups=mesh['ctx'=16,'tp'=16] {'ctx','tp'}, dimensions={0} | all-to-all | bytes 2097152 | tf_op jit(solution)/shard_map/all_to_all | solution.py:163
  85.2 0.1 bitcast_reduce_fusion
  85.4 0.6 copy.9
  (20 shorter events, 0.1 us)
Async XLA Ops:
  0.0 11.0 %collective-permute-start.2 = (bf16[128,256]{1,0:T(8,128)(2,1)}, bf16[128,256]{1,0:T(8,128)(2,1)S(1)}, u32[]{:S(2)}, u32[]{:S(2)}) collective-permute-start(bf16[128,256]{1,0:T(8,128)(2,1)} %param.8), channel_id=1, source_target_pairs={{0,2},{1,3},{2,4},{3,5},{4,6},{5,7},{6,8},{7,9},{8,10},{9,11},{10,... | collective-permute-start | bytes 196616 | tf_op jit(solution)/shard_map/ppermute | solution.py:144
  2.5 8.5 %collective-permute-start = (bf16[128,256]{1,0:T(8,128)(2,1)}, bf16[128,256]{1,0:T(8,128)(2,1)S(1)}, u32[]{:S(2)}, u32[]{:S(2)}) collective-permute-start(bf16[128,256]{1,0:T(8,128)(2,1)} %param.8), channel_id=1, source_target_pairs={{0,1},{1,0},{2,3},{3,2},{4,5},{5,4},{6,7},{7,6},{8,9},{9,8},{10,11... | collective-permute-start | bytes 196616 | tf_op jit(solution)/shard_map/ppermute | solution.py:138
  3.8 11.5 %collective-permute-start.1 = (bf16[128,256]{1,0:T(8,128)(2,1)}, bf16[128,256]{1,0:T(8,128)(2,1)S(1)}, u32[]{:S(2)}, u32[]{:S(2)}) collective-permute-start(bf16[128,256]{1,0:T(8,128)(2,1)} %param.8), channel_id=1, source_target_pairs={{0,3},{1,2},{2,5},{3,4},{4,7},{5,6},{6,9},{7,8},{8,11},{9,10},{10,... | collective-permute-start | bytes 196616 | tf_op jit(solution)/shard_map/ppermute | solution.py:142
  5.3 10.8 %collective-permute-start.3 = (bf16[128,256]{1,0:T(8,128)(2,1)}, bf16[128,256]{1,0:T(8,128)(2,1)S(1)}, u32[]{:S(2)}, u32[]{:S(2)}) collective-permute-start(bf16[128,256]{1,0:T(8,128)(2,1)} %param.8), channel_id=1, source_target_pairs={{0,15},{1,14},{2,1},{3,0},{4,3},{5,2},{6,5},{7,4},{8,7},{9,6},{10,... | collective-permute-start | bytes 196616 | tf_op jit(solution)/shard_map/ppermute | solution.py:148
  7.6 4.2 %collective-permute-start.4 = (bf16[128,256]{1,0:T(8,128)(2,1)}, bf16[128,256]{1,0:T(8,128)(2,1)S(1)}, u32[]{:S(2)}, u32[]{:S(2)}) collective-permute-start(bf16[128,256]{1,0:T(8,128)(2,1)} %param.8), channel_id=1, source_target_pairs={{0,14},{1,15},{2,0},{3,1},{4,2},{5,3},{6,4},{7,5},{8,6},{9,7},{10,... | collective-permute-start | bytes 196616 | tf_op jit(solution)/shard_map/ppermute | solution.py:150
  11.0 10.0 %collective-permute-start.5 = (bf16[128,256]{1,0:T(8,128)(2,1)S(1)}, bf16[128,256]{1,0:T(8,128)(2,1)S(1)}, u32[]{:S(2)}, u32[]{:S(2)}) collective-permute-start(bf16[128,256]{1,0:T(8,128)(2,1)S(1)} %collective-permute-done.2), channel_id=1, source_target_pairs={{0,3},{1,2},{2,5},{3,4},{4,7},{5,6},{6,9},{7,8},{8,11},{9,10},{10,... | collective-permute-start | bytes 196616 | tf_op jit(solution)/shard_map/ppermute | solution.py:142
  11.0 5.2 %collective-permute-start.6 = (bf16[128,256]{1,0:T(8,128)(2,1)S(1)}, bf16[128,256]{1,0:T(8,128)(2,1)S(1)}, u32[]{:S(2)}, u32[]{:S(2)}) collective-permute-start(bf16[128,256]{1,0:T(8,128)(2,1)S(1)} %collective-permute-done.2), channel_id=1, source_target_pairs={{0,2},{1,3},{2,4},{3,5},{4,6},{5,7},{6,8},{7,9},{8,10},{9,11},{10,... | collective-permute-start | bytes 196616 | tf_op jit(solution)/shard_map/ppermute | solution.py:144
  11.7 9.6 %collective-permute-start.7 = (bf16[128,256]{1,0:T(8,128)(2,1)S(1)}, bf16[128,256]{1,0:T(8,128)(2,1)S(1)}, u32[]{:S(2)}, u32[]{:S(2)}) collective-permute-start(bf16[128,256]{1,0:T(8,128)(2,1)S(1)} %collective-permute-done.4), channel_id=1, source_target_pairs={{0,15},{1,14},{2,1},{3,0},{4,3},{5,2},{6,5},{7,4},{8,7},{9,6},{10,... | collective-permute-start | bytes 196616 | tf_op jit(solution)/shard_map/ppermute | solution.py:148
  15.3 3.6 %collective-permute-start.8 = (bf16[128,256]{1,0:T(8,128)(2,1)S(1)}, bf16[128,256]{1,0:T(8,128)(2,1)S(1)}, u32[]{:S(2)}, u32[]{:S(2)}) collective-permute-start(bf16[128,256]{1,0:T(8,128)(2,1)S(1)} %collective-permute-done.4), channel_id=1, source_target_pairs={{0,14},{1,15},{2,0},{3,1},{4,2},{5,3},{6,4},{7,5},{8,6},{9,7},{10,... | collective-permute-start | bytes 196616 | tf_op jit(solution)/shard_map/ppermute | solution.py:150
  16.2 7.7 %collective-permute-start.9 = (bf16[128,256]{1,0:T(8,128)(2,1)S(1)}, bf16[128,256]{1,0:T(8,128)(2,1)S(1)}, u32[]{:S(2)}, u32[]{:S(2)}) collective-permute-start(bf16[128,256]{1,0:T(8,128)(2,1)S(1)} %collective-permute-done.6), channel_id=1, source_target_pairs={{0,3},{1,2},{2,5},{3,4},{4,7},{5,6},{6,9},{7,8},{8,11},{9,10},{10,... | collective-permute-start | bytes 196616 | tf_op jit(solution)/shard_map/ppermute | solution.py:142
  17.5 4.4 %collective-permute-start.10 = (bf16[128,256]{1,0:T(8,128)(2,1)S(1)}, bf16[128,256]{1,0:T(8,128)(2,1)S(1)}, u32[]{:S(2)}, u32[]{:S(2)}) collective-permute-start(bf16[128,256]{1,0:T(8,128)(2,1)S(1)} %collective-permute-done.6), channel_id=1, source_target_pairs={{0,2},{1,3},{2,4},{3,5},{4,6},{5,7},{6,8},{7,9},{8,10},{9,11},{10,... | collective-permute-start | bytes 196616 | tf_op jit(solution)/shard_map/ppermute | solution.py:144
  18.9 5.0 %collective-permute-start.11 = (bf16[128,256]{1,0:T(8,128)(2,1)S(1)}, bf16[128,256]{1,0:T(8,128)(2,1)S(1)}, u32[]{:S(2)}, u32[]{:S(2)}) collective-permute-start(bf16[128,256]{1,0:T(8,128)(2,1)S(1)} %collective-permute-done.8), channel_id=1, source_target_pairs={{0,15},{1,14},{2,1},{3,0},{4,3},{5,2},{6,5},{7,4},{8,7},{9,6},{10,... | collective-permute-start | bytes 196616 | tf_op jit(solution)/shard_map/ppermute | solution.py:148
  20.9 3.4 %collective-permute-start.12 = (bf16[128,256]{1,0:T(8,128)(2,1)S(1)}, bf16[128,256]{1,0:T(8,128)(2,1)S(1)}, u32[]{:S(2)}, u32[]{:S(2)}) collective-permute-start(bf16[128,256]{1,0:T(8,128)(2,1)S(1)} %collective-permute-done.8), channel_id=1, source_target_pairs={{0,14},{1,15},{2,0},{3,1},{4,2},{5,3},{6,4},{7,5},{8,6},{9,7},{10,... | collective-permute-start | bytes 196616 | tf_op jit(solution)/shard_map/ppermute | solution.py:150
  21.9 5.2 %collective-permute-start.13 = (bf16[128,256]{1,0:T(8,128)(2,1)S(1)}, bf16[128,256]{1,0:T(8,128)(2,1)S(1)}, u32[]{:S(2)}, u32[]{:S(2)}) collective-permute-start(bf16[128,256]{1,0:T(8,128)(2,1)S(1)} %collective-permute-done.10), channel_id=1, source_target_pairs={{0,3},{1,2},{2,5},{3,4},{4,7},{5,6},{6,9},{7,8},{8,11},{9,10},{10,... | collective-permute-start | bytes 196616 | tf_op jit(solution)/shard_map/ppermute | solution.py:142
  22.9 4.3 %collective-permute-start.14 = (bf16[128,256]{1,0:T(8,128)(2,1)S(1)}, bf16[128,256]{1,0:T(8,128)(2,1)S(1)}, u32[]{:S(2)}, u32[]{:S(2)}) collective-permute-start(bf16[128,256]{1,0:T(8,128)(2,1)S(1)} %collective-permute-done.10), channel_id=1, source_target_pairs={{0,2},{1,3},{2,4},{3,5},{4,6},{5,7},{6,8},{7,9},{8,10},{9,11},{10,... | collective-permute-start | bytes 196616 | tf_op jit(solution)/shard_map/ppermute | solution.py:144
  27.3 1.0 %copy-start = (bf16[16,128,256]{2,1,0:T(8,128)(2,1)}, bf16[16,128,256]{2,1,0:T(8,128)(2,1)S(1)}, u32[]{:S(2)}) copy-start(bf16[16,128,256]{2,1,0:T(8,128)(2,1)S(1)} %bitcast_dynamic-update-slice_fusion.pieces_ref) | copy-start | bytes 3145732

commit v10 on v9

--- a/solution.py
+++ b/solution.py
@@ -10,9 +10,12 @@
 CHUNKS = 8
 
 
-def ffn_kernel(cnt_ref, gu_ref, dn_ref, me_ref, table_ref, pieces_ref, g_hbm, u_hbm, d_hbm, out_ref,
-               normed_s, accg_s, accu_s, hid_s, acco_s, gu_v, d_v, sems):
-    n_src, rows, width = pieces_ref.shape
+def ffn_kernel(cnt_ref, gu_ref, dn_ref, me_ref, table_ref, *refs):
+    n_src = table_ref.shape[0]
+    piece_refs = refs[:n_src]
+    (g_hbm, u_hbm, d_hbm, out_ref, normed_s, accg_s, accu_s, hid_s, acco_s, gu_v, d_v,
+     sems) = refs[n_src:]
+    rows, width = piece_refs[0].shape
     tile = g_hbm.shape[1]
     slots = g_hbm.shape[0]
     step = slots // CHUNKS
@@ -37,12 +40,12 @@
     feat = n_src * width
     ss = jnp.zeros((rows, 1), jnp.float32)
     for s in range(n_src):
-        x = pieces_ref[s].astype(jnp.float32)
+        x = piece_refs[s][...].astype(jnp.float32)
         ss = ss + jnp.sum(x * x, axis=1, keepdims=True)
     scale = lax.rsqrt(ss / feat + 1e-05)
     for s in range(n_src):
         for h in range(per_src):
-            x = pieces_ref[s, :, h * tile:(h + 1) * tile].astype(jnp.float32)
+            x = piece_refs[s][:, h * tile:(h + 1) * tile].astype(jnp.float32)
             normed_s[s * per_src + h] = (x * scale).astype(jnp.bfloat16)
     accg_s[...] = jnp.zeros(accg_s.shape, jnp.float32)
     accu_s[...] = jnp.zeros(accu_s.shape, jnp.float32)
@@ -83,7 +86,7 @@
         lax.fori_loop(k * step, (k + 1) * step, dn_body, 0, unroll=True)
     groups, dests, share, group_width = out_ref.shape
     for h in range(per_src):
-        acco_s[me_ref[0] * per_src + h] += pieces_ref[0, :, h * tile:(h + 1) * tile].astype(jnp.float32)
+        acco_s[me_ref[0] * per_src + h] += piece_refs[0][:, h * tile:(h + 1) * tile].astype(jnp.float32)
     per_group = group_width // tile
     for o in range(acco_s.shape[0]):
         block = acco_s[o].reshape(dests, share, tile).astype(out_ref.dtype)
@@ -93,7 +96,8 @@
 
 def ffn(counts, gu_blocks, down_blocks, me, table, pieces, gate_tiles, up_tiles, down_tiles,
         hid_blocks, groups, share):
-    n_src, rows, width = pieces.shape
+    n_src = len(pieces)
+    rows, width = pieces[0].shape
     tile = gate_tiles.shape[1]
     in_blocks = n_src * width // tile
     smem = pl.BlockSpec(memory_space=pltpu.SMEM)
@@ -104,7 +108,7 @@
         ffn_kernel,
         out_shape=jax.ShapeDtypeStruct((groups, rows // share, share, in_blocks * tile // groups),
                                        jnp.bfloat16),
-        in_specs=[smem, smem, smem, smem, smem, vmem, hbm, hbm, hbm],
+        in_specs=[smem] * 5 + [vmem] * n_src + [hbm] * 3,
         out_specs=vmem,
         scratch_shapes=[
             pltpu.VMEM((in_blocks, rows, tile), jnp.bfloat16),
@@ -116,7 +120,7 @@
             pltpu.VMEM((slots, tile, tile), jnp.bfloat16),
             pltpu.SemaphoreType.DMA((3, CHUNKS)),
         ],
-    )(counts.reshape(-1), gu_blocks, down_blocks, me.reshape(1), table, pieces, gate_tiles,
+    )(counts.reshape(-1), gu_blocks, down_blocks, me.reshape(1), table, *pieces, gate_tiles,
       up_tiles, down_tiles)
 
 def ring_pairs(count, step, flip=0):
@@ -135,22 +139,21 @@
     my_y = me % Y_LO
     swap = [(i, i ^ 1) for i in range(tp_count)]
     half = z_count // 2
-    arrays = [tokens[None], lax.ppermute(tokens, "tp", swap)[None]]
+    arrays = [tokens, lax.ppermute(tokens, "tp", swap)]
     origins = [(0, 0), (0, 1)]
     fwd = bwd = tokens
     for k in range(1, half + 1):
-        arrays.append(lax.ppermute(fwd, "tp", ring_pairs(z_count, 1, 1))[None])
+        arrays.append(lax.ppermute(fwd, "tp", ring_pairs(z_count, 1, 1)))
         origins.append((-k % z_count, 1))
         fwd = lax.ppermute(fwd, "tp", ring_pairs(z_count, 1))
-        arrays.append(fwd[None])
+        arrays.append(fwd)
         origins.append((-k % z_count, 0))
         if k < z_count - half:
-            arrays.append(lax.ppermute(bwd, "tp", ring_pairs(z_count, -1, 1))[None])
+            arrays.append(lax.ppermute(bwd, "tp", ring_pairs(z_count, -1, 1)))
             origins.append((k, 1))
             bwd = lax.ppermute(bwd, "tp", ring_pairs(z_count, -1))
-            arrays.append(bwd[None])
+            arrays.append(bwd)
             origins.append((k, 0))
-    pieces = jnp.concatenate(arrays)
     table = [[0] * Y_LO for _ in range(z_count)]
     for index, (dz, dy) in enumerate(origins):
         table[dz][dy] = index
@@ -158,7 +161,7 @@
     hid_blocks = FF // tp_count // tile
     share = own_rows // tp_count
     outgoing = ffn(counts, gu_blocks, down_blocks, me.astype(jnp.int32),
-                   jnp.array(table, jnp.int32).reshape(-1), pieces, gate_tiles, up_tiles,
+                   jnp.array(table, jnp.int32).reshape(-1), arrays, gate_tiles, up_tiles,
                    down_tiles, hid_blocks, ctx_count, share)
     incoming = lax.all_to_all(
         outgoing.reshape(ctx_count * tp_count, share, feat_width // ctx_count),

time: 86.2 us -> 85.6 us (level)
  local copies, waits for them, and re-layouts: 2.58 us -> 1.19 us
    ppermute x8, starting transfers between devices: 13.1 us -> 7.37 us  [the longest x3 4.54 us: per_device(): arrays.append(lax.ppermute(bwd, 'tp', ring_pairs(z_count, -1, 1)))]
    ppermute x3, starting transfers between devices: 3.64 us -> 8.62 us  [per_device(): bwd = lax.ppermute(bwd, 'tp', ring_pairs(z_count, -1))]
    unnamed x17 -> x30, local copies, waits for them, and re-layouts: 1.93 us -> 0.55 us
    ppermute x4, waiting for transfers between devices: 0.69 us -> 1.97 us  [per_device(): fwd = lax.ppermute(fwd, 'tp', ring_pairs(z_count, 1))]
    ppermute x4, starting transfers between devices: 4.86 us -> 6.06 us  [per_device(): fwd = lax.ppermute(fwd, 'tp', ring_pairs(z_count, 1))]
    ppermute x3, waiting for transfers between devices: 1.14 us -> 0.01 us  [per_device(): bwd = lax.ppermute(bwd, 'tp', ring_pairs(z_count, -1))]
  transfers between devices with their start and end apart: 15 -> 15, of which waited for: 5 -> 4; matrix products, arithmetic and copies ran while one was open for 1% -> 0% of each run, Pallas kernels for 0% -> 0%
where the time goes in v10:
time: 85.6 us; the launch traced here: 85.4 us
  blocking collectives  48.5 us (57%)
  starting transfers between devices  22.1 us (26%)
  Pallas kernels  8.29 us (10%)
  waiting for transfers between devices  5.01 us (6%)
  local copies, waits for them, and re-layouts  1.19 us (1%)
    all_to_all x1, blocking collectives, per_device(): lax.all_to_all(outgoing.reshape(ctx_count * tp_count, share, feat_width /...  48.5 us
    ppermute x3, starting transfers between devices, per_device(): bwd = lax.ppermute(bwd, 'tp', ring_pairs(z_count, -1))  8.62 us
    pallas_call x1, Pallas kernels, ffn(): pl.pallas_call(ffn_kernel, out_shape=jax.ShapeDtypeStruct((groups, rows /...  8.29 us
    ppermute x4, starting transfers between devices, per_device(): fwd = lax.ppermute(fwd, 'tp', ring_pairs(z_count, 1))  6.06 us
    ppermute x3, starting transfers between devices, per_device(): arrays.append(lax.ppermute(bwd, 'tp', ring_pairs(z_count, -1, 1)))  4.54 us
    ppermute x4, waiting for transfers between devices, per_device(): fwd = lax.ppermute(fwd, 'tp', ring_pairs(z_count, 1))  1.97 us
  transfers between devices with their start and end apart: 15, of which 4 were waited for; matrix products, arithmetic and copies ran while one was open for 0% of the time, Pallas kernels for 0%

profile of v10, /device:TPU:1, one launch (start us, length us, event | category | flops | bytes accessed | tf_op | source)
XLA Modules:
  0.0 85.4 jit_solution(14086272480536371443)
XLA Ops:
  0.0 2.5 %collective-permute-start.2 = (bf16[128,256]{1,0:T(8,128)(2,1)}, bf16[128,256]{1,0:T(8,128)(2,1)S(1)}, u32[]{:S(2)}, u32[]{:S(2)}) collective-permute-start(bf16[128,256]{1,0:T(8,128)(2,1)} %refs_0_.1), channel_id=1, source_target_pairs={{0,2},{1,3},{2,4},{3,5},{4,6},{5,7},{6,8},{7,9},{8,10},{9,11},{10,... | collective-permute-start | bytes 196616 | tf_op jit(solution)/shard_map/ppermute | solution.py:148
  2.5 3.9 %collective-permute-start.4 = (bf16[128,256]{1,0:T(8,128)(2,1)}, bf16[128,256]{1,0:T(8,128)(2,1)S(1)}, u32[]{:S(2)}, u32[]{:S(2)}) collective-permute-start(bf16[128,256]{1,0:T(8,128)(2,1)} %refs_0_.1), channel_id=1, source_target_pairs={{0,14},{1,15},{2,0},{3,1},{4,2},{5,3},{6,4},{7,5},{8,6},{9,7},{10,... | collective-permute-start | bytes 196616 | tf_op jit(solution)/shard_map/ppermute | solution.py:154
  6.4 2.5 %collective-permute-start.3 = (bf16[128,256]{1,0:T(8,128)(2,1)}, bf16[128,256]{1,0:T(8,128)(2,1)S(1)}, u32[]{:S(2)}, u32[]{:S(2)}) collective-permute-start(bf16[128,256]{1,0:T(8,128)(2,1)} %refs_0_.1), channel_id=1, source_target_pairs={{0,15},{1,14},{2,1},{3,0},{4,3},{5,2},{6,5},{7,4},{8,7},{9,6},{10,... | collective-permute-start | bytes 196616 | tf_op jit(solution)/shard_map/ppermute | solution.py:152
  8.9 0.0 collective-permute-done.2.refs_3_
  8.9 0.0 collective-permute-start.6
  8.9 0.1 collective-permute-start.1
  9.0 1.2 %collective-permute-start = (bf16[128,256]{1,0:T(8,128)(2,1)}, bf16[128,256]{1,0:T(8,128)(2,1)S(1)}, u32[]{:S(2)}, u32[]{:S(2)}) collective-permute-start(bf16[128,256]{1,0:T(8,128)(2,1)} %refs_0_.1), channel_id=1, source_target_pairs={{0,1},{1,0},{2,3},{3,2},{4,5},{5,4},{6,7},{7,6},{8,9},{9,8},{10,11... | collective-permute-start | bytes 196616 | tf_op jit(solution)/shard_map/ppermute | solution.py:142
  10.2 0.0 collective-permute-done.4.refs_5_
  10.2 2.7 %collective-permute-start.8 = (bf16[128,256]{1,0:T(8,128)(2,1)S(1)}, bf16[128,256]{1,0:T(8,128)(2,1)S(1)}, u32[]{:S(2)}, u32[]{:S(2)}) collective-permute-start(bf16[128,256]{1,0:T(8,128)(2,1)S(1)} %collective-permute-done.4.refs_5_), channel_id=1, source_target_pairs={{0,14},{1,15},{2,0},{3,1},{4,2},{5,3},{6,4},{7,5},{8,6},{9,7},{10,... | collective-permute-start | bytes 196616 | tf_op jit(solution)/shard_map/ppermute | solution.py:154
  12.8 0.0 collective-permute-done.3.refs_4_
  12.8 0.0 collective-permute-start.5
  12.9 0.4 collective-permute-done.6.refs_7_
  13.2 2.2 %collective-permute-start.10 = (bf16[128,256]{1,0:T(8,128)(2,1)S(1)}, bf16[128,256]{1,0:T(8,128)(2,1)S(1)}, u32[]{:S(2)}, u32[]{:S(2)}) collective-permute-start(bf16[128,256]{1,0:T(8,128)(2,1)S(1)} %collective-permute-done.6.refs_7_), channel_id=1, source_target_pairs={{0,2},{1,3},{2,4},{3,5},{4,6},{5,7},{6,8},{7,9},{8,10},{9,11},{10,... | collective-permute-start | bytes 196616 | tf_op jit(solution)/shard_map/ppermute | solution.py:148
  15.4 0.0 collective-permute-done.1.refs_2_
  15.4 1.4 %collective-permute-start.7 = (bf16[128,256]{1,0:T(8,128)(2,1)S(1)}, bf16[128,256]{1,0:T(8,128)(2,1)S(1)}, u32[]{:S(2)}, u32[]{:S(2)}) collective-permute-start(bf16[128,256]{1,0:T(8,128)(2,1)S(1)} %collective-permute-done.4.refs_5_), channel_id=1, source_target_pairs={{0,15},{1,14},{2,1},{3,0},{4,3},{5,2},{6,5},{7,4},{8,7},{9,6},{10,... | collective-permute-start | bytes 196616 | tf_op jit(solution)/shard_map/ppermute | solution.py:152
  16.8 0.0 collective-permute-done.refs_1_
  16.8 1.0 %collective-permute-start.9 = (bf16[128,256]{1,0:T(8,128)(2,1)S(1)}, bf16[128,256]{1,0:T(8,128)(2,1)S(1)}, u32[]{:S(2)}, u32[]{:S(2)}) collective-permute-start(bf16[128,256]{1,0:T(8,128)(2,1)S(1)} %collective-permute-done.6.refs_7_), channel_id=1, source_target_pairs={{0,3},{1,2},{2,5},{3,4},{4,7},{5,6},{6,9},{7,8},{8,11},{9,10},{10,... | collective-permute-start | bytes 196616 | tf_op jit(solution)/shard_map/ppermute | solution.py:146
  17.8 0.0 collective-permute-done.8.refs_9_
  17.8 2.0 %collective-permute-start.12 = (bf16[128,256]{1,0:T(8,128)(2,1)S(1)}, bf16[128,256]{1,0:T(8,128)(2,1)S(1)}, u32[]{:S(2)}, u32[]{:S(2)}) collective-permute-start(bf16[128,256]{1,0:T(8,128)(2,1)S(1)} %collective-permute-done.8.refs_9_), channel_id=1, source_target_pairs={{0,14},{1,15},{2,0},{3,1},{4,2},{5,3},{6,4},{7,5},{8,6},{9,7},{10,... | collective-permute-start | bytes 196616 | tf_op jit(solution)/shard_map/ppermute | solution.py:154
  19.8 0.7 collective-permute-start.11
  20.5 0.0 collective-permute-done.10.refs_11_
  20.5 1.4 %collective-permute-start.14 = (bf16[128,256]{1,0:T(8,128)(2,1)S(1)}, bf16[128,256]{1,0:T(8,128)(2,1)S(1)}, u32[]{:S(2)}, u32[]{:S(2)}) collective-permute-start(bf16[128,256]{1,0:T(8,128)(2,1)S(1)} %collective-permute-done.10.refs_11_), channel_id=1, source_target_pairs={{0,2},{1,3},{2,4},{3,5},{4,6},{5,7},{6,8},{7,9},{8,10},{9,11},{10,... | collective-permute-start | bytes 196616 | tf_op jit(solution)/shard_map/ppermute | solution.py:148
  21.9 0.0 collective-permute-done.7.refs_8_
  21.9 0.6 collective-permute-start.13
  22.5 1.3 %collective-permute-done.11.refs_12_ = bf16[128,256]{1,0:T(8,128)(2,1)S(1)} collective-permute-done((bf16[128,256]{1,0:T(8,128)(2,1)S(1)}, bf16[128,256]{1,0:T(8,128)(2,1)S(1)}, u32[]{:S(2)}, u32[]{:S(2)}) %collective-permute-start.11) | collective-permute-done | bytes 65568 | tf_op jit(solution)/shard_map/ppermute | solution.py:152
  23.9 1.6 %collective-permute-done.14.refs_15_ = bf16[128,256]{1,0:T(8,128)(2,1)S(1)} collective-permute-done((bf16[128,256]{1,0:T(8,128)(2,1)S(1)}, bf16[128,256]{1,0:T(8,128)(2,1)S(1)}, u32[]{:S(2)}, u32[]{:S(2)}) %collective-permute-start.14) | collective-permute-done | bytes 65568 | tf_op jit(solution)/shard_map/ppermute | solution.py:148
  25.5 1.7 %collective-permute-done.13.refs_14_ = bf16[128,256]{1,0:T(8,128)(2,1)S(1)} collective-permute-done((bf16[128,256]{1,0:T(8,128)(2,1)S(1)}, bf16[128,256]{1,0:T(8,128)(2,1)S(1)}, u32[]{:S(2)}, u32[]{:S(2)}) %collective-permute-start.13) | collective-permute-done | bytes 65568 | tf_op jit(solution)/shard_map/ppermute | solution.py:146
  27.3 0.5 copy-done.14
  27.7 8.3 %shard_map.82 = bf16[16,16,8,256]{3,2,1,0:T(8,128)(2,1)} custom-call(s32[2]{0:T(128)} %bitcast.8, s32[2,64]{1,0:T(2,128)} %gu_ref.1, s32[2,64]{1,0:T(2,128)} %dn_ref.1, s32[1]{0:T(128)} %bitcast.1.me_ref, s32[16]{0:T(128)} %constant.10.table_ref, bf16[128,256]{1,0:T(8,128)(2,1)} %refs_0_.1, bf16[128,256]{1,0:T(8,128)(2,1)} %copy-done.5, ...), custom_call_target="tpu_custom_call" | custom-call | tf_op jit(solution)/shard_map/pallas_call | solution.py:107
  36.0 48.5 %all_to_all.5 = bf16[256,8,256]{2,1,0:T(8,128)(2,1)S(1)} all-to-all(bf16[256,8,256]{2,1,0:T(8,128)(2,1)} %bitcast.6), channel_id=1, replica_groups=mesh['ctx'=16,'tp'=16] {'ctx','tp'}, dimensions={0} | all-to-all | bytes 2097152 | tf_op jit(solution)/shard_map/all_to_all | solution.py:166
  84.6 0.1 bitcast_reduce_fusion
  84.7 0.6 copy.9
  (32 shorter events, 0.1 us)
Async XLA Ops:
  0.0 8.9 %collective-permute-start.2 = (bf16[128,256]{1,0:T(8,128)(2,1)}, bf16[128,256]{1,0:T(8,128)(2,1)S(1)}, u32[]{:S(2)}, u32[]{:S(2)}) collective-permute-start(bf16[128,256]{1,0:T(8,128)(2,1)} %refs_0_.1), channel_id=1, source_target_pairs={{0,2},{1,3},{2,4},{3,5},{4,6},{5,7},{6,8},{7,9},{8,10},{9,11},{10,... | collective-permute-start | bytes 196616 | tf_op jit(solution)/shard_map/ppermute | solution.py:148
  2.5 7.7 %collective-permute-start.4 = (bf16[128,256]{1,0:T(8,128)(2,1)}, bf16[128,256]{1,0:T(8,128)(2,1)S(1)}, u32[]{:S(2)}, u32[]{:S(2)}) collective-permute-start(bf16[128,256]{1,0:T(8,128)(2,1)} %refs_0_.1), channel_id=1, source_target_pairs={{0,14},{1,15},{2,0},{3,1},{4,2},{5,3},{6,4},{7,5},{8,6},{9,7},{10,... | collective-permute-start | bytes 196616 | tf_op jit(solution)/shard_map/ppermute | solution.py:154
  6.4 6.4 %collective-permute-start.3 = (bf16[128,256]{1,0:T(8,128)(2,1)}, bf16[128,256]{1,0:T(8,128)(2,1)S(1)}, u32[]{:S(2)}, u32[]{:S(2)}) collective-permute-start(bf16[128,256]{1,0:T(8,128)(2,1)} %refs_0_.1), channel_id=1, source_target_pairs={{0,15},{1,14},{2,1},{3,0},{4,3},{5,2},{6,5},{7,4},{8,7},{9,6},{10,... | collective-permute-start | bytes 196616 | tf_op jit(solution)/shard_map/ppermute | solution.py:152
  8.9 18.2 %copy-start = (bf16[128,256]{1,0:T(8,128)(2,1)}, bf16[128,256]{1,0:T(8,128)(2,1)S(1)}, u32[]{:S(2)}) copy-start(bf16[128,256]{1,0:T(8,128)(2,1)S(1)} %collective-permute-done.2.refs_3_) | copy-start | bytes 196612
  8.9 4.3 %collective-permute-start.6 = (bf16[128,256]{1,0:T(8,128)(2,1)S(1)}, bf16[128,256]{1,0:T(8,128)(2,1)S(1)}, u32[]{:S(2)}, u32[]{:S(2)}) collective-permute-start(bf16[128,256]{1,0:T(8,128)(2,1)S(1)} %collective-permute-done.2.refs_3_), channel_id=1, source_target_pairs={{0,2},{1,3},{2,4},{3,5},{4,6},{5,7},{6,8},{7,9},{8,10},{9,11},{10,... | collective-permute-start | bytes 196616 | tf_op jit(solution)/shard_map/ppermute | solution.py:148
  8.9 6.5 %collective-permute-start.1 = (bf16[128,256]{1,0:T(8,128)(2,1)}, bf16[128,256]{1,0:T(8,128)(2,1)S(1)}, u32[]{:S(2)}, u32[]{:S(2)}) collective-permute-start(bf16[128,256]{1,0:T(8,128)(2,1)} %refs_0_.1), channel_id=1, source_target_pairs={{0,3},{1,2},{2,5},{3,4},{4,7},{5,6},{6,9},{7,8},{8,11},{9,10},{10,... | collective-permute-start | bytes 196616 | tf_op jit(solution)/shard_map/ppermute | solution.py:146
  9.0 7.8 %collective-permute-start = (bf16[128,256]{1,0:T(8,128)(2,1)}, bf16[128,256]{1,0:T(8,128)(2,1)S(1)}, u32[]{:S(2)}, u32[]{:S(2)}) collective-permute-start(bf16[128,256]{1,0:T(8,128)(2,1)} %refs_0_.1), channel_id=1, source_target_pairs={{0,1},{1,0},{2,3},{3,2},{4,5},{5,4},{6,7},{7,6},{8,9},{9,8},{10,11... | collective-permute-start | bytes 196616 | tf_op jit(solution)/shard_map/ppermute | solution.py:142
  10.2 17.0 %copy-start.1 = (bf16[128,256]{1,0:T(8,128)(2,1)}, bf16[128,256]{1,0:T(8,128)(2,1)S(1)}, u32[]{:S(2)}) copy-start(bf16[128,256]{1,0:T(8,128)(2,1)S(1)} %collective-permute-done.4.refs_5_) | copy-start | bytes 196612
  10.2 7.7 %collective-permute-start.8 = (bf16[128,256]{1,0:T(8,128)(2,1)S(1)}, bf16[128,256]{1,0:T(8,128)(2,1)S(1)}, u32[]{:S(2)}, u32[]{:S(2)}) collective-permute-start(bf16[128,256]{1,0:T(8,128)(2,1)S(1)} %collective-permute-done.4.refs_5_), channel_id=1, source_target_pairs={{0,14},{1,15},{2,0},{3,1},{4,2},{5,3},{6,4},{7,5},{8,6},{9,7},{10,... | collective-permute-start | bytes 196616 | tf_op jit(solution)/shard_map/ppermute | solution.py:154
  12.8 14.3 %copy-start.2 = (bf16[128,256]{1,0:T(8,128)(2,1)}, bf16[128,256]{1,0:T(8,128)(2,1)S(1)}, u32[]{:S(2)}) copy-start(bf16[128,256]{1,0:T(8,128)(2,1)S(1)} %collective-permute-done.3.refs_4_) | copy-start | bytes 196612
  12.8 7.0 %collective-permute-start.5 = (bf16[128,256]{1,0:T(8,128)(2,1)S(1)}, bf16[128,256]{1,0:T(8,128)(2,1)S(1)}, u32[]{:S(2)}, u32[]{:S(2)}) collective-permute-start(bf16[128,256]{1,0:T(8,128)(2,1)S(1)} %collective-permute-done.2.refs_3_), channel_id=1, source_target_pairs={{0,3},{1,2},{2,5},{3,4},{4,7},{5,6},{6,9},{7,8},{8,11},{9,10},{10,... | collective-permute-start | bytes 196616 | tf_op jit(solution)/shard_map/ppermute | solution.py:146
  13.2 13.9 %copy-start.3 = (bf16[128,256]{1,0:T(8,128)(2,1)}, bf16[128,256]{1,0:T(8,128)(2,1)S(1)}, u32[]{:S(2)}) copy-start(bf16[128,256]{1,0:T(8,128)(2,1)S(1)} %collective-permute-done.6.refs_7_) | copy-start | bytes 196612
  13.2 7.3 %collective-permute-start.10 = (bf16[128,256]{1,0:T(8,128)(2,1)S(1)}, bf16[128,256]{1,0:T(8,128)(2,1)S(1)}, u32[]{:S(2)}, u32[]{:S(2)}) collective-permute-start(bf16[128,256]{1,0:T(8,128)(2,1)S(1)} %collective-permute-done.6.refs_7_), channel_id=1, source_target_pairs={{0,2},{1,3},{2,4},{3,5},{4,6},{5,7},{6,8},{7,9},{8,10},{9,11},{10,... | collective-permute-start | bytes 196616 | tf_op jit(solution)/shard_map/ppermute | solution.py:148
  15.4 11.7 %copy-start.4 = (bf16[128,256]{1,0:T(8,128)(2,1)}, bf16[128,256]{1,0:T(8,128)(2,1)S(1)}, u32[]{:S(2)}) copy-start(bf16[128,256]{1,0:T(8,128)(2,1)S(1)} %collective-permute-done.1.refs_2_) | copy-start | bytes 196612
  15.4 6.5 %collective-permute-start.7 = (bf16[128,256]{1,0:T(8,128)(2,1)S(1)}, bf16[128,256]{1,0:T(8,128)(2,1)S(1)}, u32[]{:S(2)}, u32[]{:S(2)}) collective-permute-start(bf16[128,256]{1,0:T(8,128)(2,1)S(1)} %collective-permute-done.4.refs_5_), channel_id=1, source_target_pairs={{0,15},{1,14},{2,1},{3,0},{4,3},{5,2},{6,5},{7,4},{8,7},{9,6},{10,... | collective-permute-start | bytes 196616 | tf_op jit(solution)/shard_map/ppermute | solution.py:152
  16.8 10.3 %copy-start.5 = (bf16[128,256]{1,0:T(8,128)(2,1)}, bf16[128,256]{1,0:T(8,128)(2,1)S(1)}, u32[]{:S(2)}) copy-start(bf16[128,256]{1,0:T(8,128)(2,1)S(1)} %collective-permute-done.refs_1_) | copy-start | bytes 196612
  16.8 5.7 %collective-permute-start.9 = (bf16[128,256]{1,0:T(8,128)(2,1)S(1)}, bf16[128,256]{1,0:T(8,128)(2,1)S(1)}, u32[]{:S(2)}, u32[]{:S(2)}) collective-permute-start(bf16[128,256]{1,0:T(8,128)(2,1)S(1)} %collective-permute-done.6.refs_7_), channel_id=1, source_target_pairs={{0,3},{1,2},{2,5},{3,4},{4,7},{5,6},{6,9},{7,8},{8,11},{9,10},{10,... | collective-permute-start | bytes 196616 | tf_op jit(solution)/shard_map/ppermute | solution.py:146
  17.8 9.4 %copy-start.6 = (bf16[128,256]{1,0:T(8,128)(2,1)}, bf16[128,256]{1,0:T(8,128)(2,1)S(1)}, u32[]{:S(2)}) copy-start(bf16[128,256]{1,0:T(8,128)(2,1)S(1)} %collective-permute-done.8.refs_9_) | copy-start | bytes 196612
  17.8 4.7 %collective-permute-start.12 = (bf16[128,256]{1,0:T(8,128)(2,1)S(1)}, bf16[128,256]{1,0:T(8,128)(2,1)S(1)}, u32[]{:S(2)}, u32[]{:S(2)}) collective-permute-start(bf16[128,256]{1,0:T(8,128)(2,1)S(1)} %collective-permute-done.8.refs_9_), channel_id=1, source_target_pairs={{0,14},{1,15},{2,0},{3,1},{4,2},{5,3},{6,4},{7,5},{8,6},{9,7},{10,... | collective-permute-start | bytes 196616 | tf_op jit(solution)/shard_map/ppermute | solution.py:154
  19.8 7.4 %copy-start.7 = (bf16[128,256]{1,0:T(8,128)(2,1)}, bf16[128,256]{1,0:T(8,128)(2,1)S(1)}, u32[]{:S(2)}) copy-start(bf16[128,256]{1,0:T(8,128)(2,1)S(1)} %collective-permute-done.5.refs_6_) | copy-start | bytes 196612
  19.8 4.0 %collective-permute-start.11 = (bf16[128,256]{1,0:T(8,128)(2,1)S(1)}, bf16[128,256]{1,0:T(8,128)(2,1)S(1)}, u32[]{:S(2)}, u32[]{:S(2)}) collective-permute-start(bf16[128,256]{1,0:T(8,128)(2,1)S(1)} %collective-permute-done.8.refs_9_), channel_id=1, source_target_pairs={{0,15},{1,14},{2,1},{3,0},{4,3},{5,2},{6,5},{7,4},{8,7},{9,6},{10,... | collective-permute-start | bytes 196616 | tf_op jit(solution)/shard_map/ppermute | solution.py:152
  20.5 6.7 %copy-start.8 = (bf16[128,256]{1,0:T(8,128)(2,1)}, bf16[128,256]{1,0:T(8,128)(2,1)S(1)}, u32[]{:S(2)}) copy-start(bf16[128,256]{1,0:T(8,128)(2,1)S(1)} %collective-permute-done.10.refs_11_) | copy-start | bytes 196612
  20.5 4.9 %collective-permute-start.14 = (bf16[128,256]{1,0:T(8,128)(2,1)S(1)}, bf16[128,256]{1,0:T(8,128)(2,1)S(1)}, u32[]{:S(2)}, u32[]{:S(2)}) collective-permute-start(bf16[128,256]{1,0:T(8,128)(2,1)S(1)} %collective-permute-done.10.refs_11_), channel_id=1, source_target_pairs={{0,2},{1,3},{2,4},{3,5},{4,6},{5,7},{6,8},{7,9},{8,10},{9,11},{10,... | collective-permute-start | bytes 196616 | tf_op jit(solution)/shard_map/ppermute | solution.py:148
  21.9 5.3 %copy-start.9 = (bf16[128,256]{1,0:T(8,128)(2,1)}, bf16[128,256]{1,0:T(8,128)(2,1)S(1)}, u32[]{:S(2)}) copy-start(bf16[128,256]{1,0:T(8,128)(2,1)S(1)} %collective-permute-done.7.refs_8_) | copy-start | bytes 196612
  21.9 5.2 %collective-permute-start.13 = (bf16[128,256]{1,0:T(8,128)(2,1)S(1)}, bf16[128,256]{1,0:T(8,128)(2,1)S(1)}, u32[]{:S(2)}, u32[]{:S(2)}) collective-permute-start(bf16[128,256]{1,0:T(8,128)(2,1)S(1)} %collective-permute-done.10.refs_11_), channel_id=1, source_target_pairs={{0,3},{1,2},{2,5},{3,4},{4,7},{5,6},{6,9},{7,8},{8,11},{9,10},{10,... | collective-permute-start | bytes 196616 | tf_op jit(solution)/shard_map/ppermute | solution.py:146
  22.5 4.7 %copy-start.10 = (bf16[128,256]{1,0:T(8,128)(2,1)}, bf16[128,256]{1,0:T(8,128)(2,1)S(1)}, u32[]{:S(2)}) copy-start(bf16[128,256]{1,0:T(8,128)(2,1)S(1)} %collective-permute-done.9.refs_10_) | copy-start | bytes 196612
  22.5 4.7 %copy-start.11 = (bf16[128,256]{1,0:T(8,128)(2,1)}, bf16[128,256]{1,0:T(8,128)(2,1)S(1)}, u32[]{:S(2)}) copy-start(bf16[128,256]{1,0:T(8,128)(2,1)S(1)} %collective-permute-done.12.refs_13_) | copy-start | bytes 196612
  23.9 3.4 %copy-start.12 = (bf16[128,256]{1,0:T(8,128)(2,1)}, bf16[128,256]{1,0:T(8,128)(2,1)S(1)}, u32[]{:S(2)}) copy-start(bf16[128,256]{1,0:T(8,128)(2,1)S(1)} %collective-permute-done.11.refs_12_) | copy-start | bytes 196612
  25.5 1.8 %copy-start.13 = (bf16[128,256]{1,0:T(8,128)(2,1)}, bf16[128,256]{1,0:T(8,128)(2,1)S(1)}, u32[]{:S(2)}) copy-start(bf16[128,256]{1,0:T(8,128)(2,1)S(1)} %collective-permute-done.14.refs_15_) | copy-start | bytes 196612
  27.1 0.6 copy-start.14

commit v11 on v10

--- a/solution.py
+++ b/solution.py
@@ -138,22 +138,25 @@
     my_z = me // Y_LO
     my_y = me % Y_LO
     swap = [(i, i ^ 1) for i in range(tp_count)]
-    half = z_count // 2
     arrays = [tokens, lax.ppermute(tokens, "tp", swap)]
     origins = [(0, 0), (0, 1)]
-    fwd = bwd = tokens
-    for k in range(1, half + 1):
-        arrays.append(lax.ppermute(fwd, "tp", ring_pairs(z_count, 1, 1)))
-        origins.append((-k % z_count, 1))
-        fwd = lax.ppermute(fwd, "tp", ring_pairs(z_count, 1))
-        arrays.append(fwd)
-        origins.append((-k % z_count, 0))
-        if k < z_count - half:
-            arrays.append(lax.ppermute(bwd, "tp", ring_pairs(z_count, -1, 1)))
-            origins.append((k, 1))
-            bwd = lax.ppermute(bwd, "tp", ring_pairs(z_count, -1))
-            arrays.append(bwd)
-            origins.append((k, 0))
+    near = {}
+    for step in (1, -1):
+        same = lax.ppermute(tokens, "tp", ring_pairs(z_count, step))
+        other = lax.ppermute(tokens, "tp", ring_pairs(z_count, step, 1))
+        arrays += [same, other]
+        origins += [(-step % z_count, 0), (-step % z_count, 1)]
+        near[step] = jnp.stack([same, other])
+    far = {}
+    for step in (1, -1):
+        for hops in (1, 2):
+            pair = lax.ppermute(near[step], "tp", ring_pairs(z_count, step * hops))
+            arrays += [pair[0], pair[1]]
+            origins += [(-step * (hops + 1) % z_count, 0), (-step * (hops + 1) % z_count, 1)]
+            far[step, hops] = pair
+    last = lax.ppermute(far[1, 2], "tp", ring_pairs(z_count, 1))
+    arrays += [last[0], last[1]]
+    origins += [(-4 % z_count, 0), (-4 % z_count, 1)]
     table = [[0] * Y_LO for _ in range(z_count)]
     for index, (dz, dy) in enumerate(origins):
         table[dz][dy] = index

time: 85.6 us -> 81.3 us (0.950)
  starting transfers between devices: 22.1 us -> 15.4 us
  local copies, waits for them, and re-layouts: 1.19 us -> 4.55 us
  blocking collectives: 48.5 us -> 47 us
    ppermute x14 -> x9, starting transfers between devices: 20.9 us -> 15.1 us  [the longest x4 6.23 us: per_device(): pair = lax.ppermute(near[step], 'tp', ring_pairs(z_count, step * hops))]
    squeeze x0 -> x5, local copies, waits for them, and re-layouts: none -> 3.3 us  [the longest x4 2.63 us: per_device(): arrays += [pair[0], pair[1]]]
    all_to_all x1, blocking collectives: 48.5 us -> 47 us  [per_device(): lax.all_to_all(outgoing.reshape(ctx_count * tp_count, share, feat_width /...]
    ppermute x1, starting transfers between devices: 1.17 us -> 0.27 us  [per_device(): arrays = [tokens, lax.ppermute(tokens, 'tp', swap)]]
    ppermute x14 -> x9, waiting for transfers between devices: 5 us -> 5.63 us  [the longest x4 4.67 us: per_device(): pair = lax.ppermute(near[step], 'tp', ring_pairs(z_count, step * hops))]
  transfers between devices with their start and end apart: 15 -> 10, of which waited for: 4 -> 5; matrix products, arithmetic and copies ran while one was open for 0% -> 4% of each run, Pallas kernels for 0% -> 0%
where the time goes in v11:
time: 81.3 us; the launch traced here: 81.1 us
  blocking collectives  47 us (58%)
  starting transfers between devices  15.4 us (19%)
  Pallas kernels  8.27 us (10%)
  waiting for transfers between devices  5.63 us (7%)
  local copies, waits for them, and re-layouts  4.55 us (6%)
    all_to_all x1, blocking collectives, per_device(): lax.all_to_all(outgoing.reshape(ctx_count * tp_count, share, feat_width /...  47 us
    pallas_call x1, Pallas kernels, ffn(): pl.pallas_call(ffn_kernel, out_shape=jax.ShapeDtypeStruct((groups, rows /...  8.27 us
    ppermute x4, starting transfers between devices, per_device(): pair = lax.ppermute(near[step], 'tp', ring_pairs(z_count, step * hops))  6.23 us
    ppermute x2, starting transfers between devices, per_device(): other = lax.ppermute(tokens, 'tp', ring_pairs(z_count, step, 1))  5.88 us
    ppermute x4, waiting for transfers between devices, per_device(): pair = lax.ppermute(near[step], 'tp', ring_pairs(z_count, step * hops))  4.67 us
    ppermute x2, starting transfers between devices, per_device(): same = lax.ppermute(tokens, 'tp', ring_pairs(z_count, step))  3.01 us
    squeeze x4, local copies, waits for them, and re-layouts, per_device(): arrays += [pair[0], pair[1]]  2.63 us
  transfers between devices with their start and end apart: 10, of which 5 were waited for; matrix products, arithmetic and copies ran while one was open for 4% of the time, Pallas kernels for 0%

profile of v11, /device:TPU:1, one launch (start us, length us, event | category | flops | bytes accessed | tf_op | source)
XLA Modules:
  0.0 81.1 jit_solution(16272662141496873980)
XLA Ops:
  0.0 3.5 %collective-permute-start.2 = (bf16[128,256]{1,0:T(8,128)(2,1)}, bf16[128,256]{1,0:T(8,128)(2,1)S(1)}, u32[]{:S(2)}, u32[]{:S(2)}) collective-permute-start(bf16[128,256]{1,0:T(8,128)(2,1)} %refs_0_.1), channel_id=1, source_target_pairs={{0,3},{1,2},{2,5},{3,4},{4,7},{5,6},{6,9},{7,8},{8,11},{9,10},{10,... | collective-permute-start | bytes 196616 | tf_op jit(solution)/shard_map/ppermute | solution.py:146
  3.5 1.6 %collective-permute-start.1 = (bf16[128,256]{1,0:T(8,128)(2,1)}, bf16[128,256]{1,0:T(8,128)(2,1)S(1)}, u32[]{:S(2)}, u32[]{:S(2)}) collective-permute-start(bf16[128,256]{1,0:T(8,128)(2,1)} %refs_0_.1), channel_id=1, source_target_pairs={{0,2},{1,3},{2,4},{3,5},{4,6},{5,7},{6,8},{7,9},{8,10},{9,11},{10,... | collective-permute-start | bytes 196616 | tf_op jit(solution)/shard_map/ppermute | solution.py:145
  5.1 1.4 %collective-permute-start.3 = (bf16[128,256]{1,0:T(8,128)(2,1)}, bf16[128,256]{1,0:T(8,128)(2,1)S(1)}, u32[]{:S(2)}, u32[]{:S(2)}) collective-permute-start(bf16[128,256]{1,0:T(8,128)(2,1)} %refs_0_.1), channel_id=1, source_target_pairs={{0,14},{1,15},{2,0},{3,1},{4,2},{5,3},{6,4},{7,5},{8,6},{9,7},{10,... | collective-permute-start | bytes 196616 | tf_op jit(solution)/shard_map/ppermute | solution.py:145
  6.5 2.4 %collective-permute-start.4 = (bf16[128,256]{1,0:T(8,128)(2,1)}, bf16[128,256]{1,0:T(8,128)(2,1)S(1)}, u32[]{:S(2)}, u32[]{:S(2)}) collective-permute-start(bf16[128,256]{1,0:T(8,128)(2,1)} %refs_0_.1), channel_id=1, source_target_pairs={{0,15},{1,14},{2,1},{3,0},{4,3},{5,2},{6,5},{7,4},{8,7},{9,6},{10,... | collective-permute-start | bytes 196616 | tf_op jit(solution)/shard_map/ppermute | solution.py:146
  8.9 0.4 collective-permute-done.2.refs_3_
  9.3 0.6 collective-permute-done.1.refs_2_
  9.9 1.2 %collective-permute-start.6 = (bf16[2,128,256]{2,1,0:T(8,128)(2,1)S(1)}, bf16[2,128,256]{2,1,0:T(8,128)(2,1)S(1)}, u32[]{:S(2)}, u32[]{:S(2)}) collective-permute-start(bf16[2,128,256]{2,1,0:T(8,128)(2,1)S(1)} %pad_maximum_fusion), channel_id=1, source_target_pairs={{0,4},{1,5},{2,6},{3,7},{4,8},{5,9},{6,10},{7,11},{8,12},{9,13},{1... | collective-permute-start | bytes 393224 | tf_op jit(solution)/shard_map/ppermute | solution.py:153
  11.1 0.3 collective-permute-start
  11.3 1.6 %collective-permute-start.5 = (bf16[2,128,256]{2,1,0:T(8,128)(2,1)S(1)}, bf16[2,128,256]{2,1,0:T(8,128)(2,1)S(1)}, u32[]{:S(2)}, u32[]{:S(2)}) collective-permute-start(bf16[2,128,256]{2,1,0:T(8,128)(2,1)S(1)} %pad_maximum_fusion), channel_id=1, source_target_pairs={{0,2},{1,3},{2,4},{3,5},{4,6},{5,7},{6,8},{7,9},{8,10},{9,11},{10,... | collective-permute-start | bytes 393224 | tf_op jit(solution)/shard_map/ppermute | solution.py:153
  12.9 0.0 collective-permute-done.3.refs_4_
  12.9 0.0 collective-permute-done.4.refs_5_
  12.9 0.0 copy-start.3
  13.0 2.0 %collective-permute-start.8 = (bf16[2,128,256]{2,1,0:T(8,128)(2,1)S(1)}, bf16[2,128,256]{2,1,0:T(8,128)(2,1)S(1)}, u32[]{:S(2)}, u32[]{:S(2)}) collective-permute-start(bf16[2,128,256]{2,1,0:T(8,128)(2,1)S(1)} %pad_maximum_fusion.1), channel_id=1, source_target_pairs={{0,12},{1,13},{2,14},{3,15},{4,0},{5,1},{6,2},{7,3},{8,4},{9,5},{1... | collective-permute-start | bytes 393224 | tf_op jit(solution)/shard_map/ppermute | solution.py:153
  14.9 1.5 %collective-permute-start.7 = (bf16[2,128,256]{2,1,0:T(8,128)(2,1)S(1)}, bf16[2,128,256]{2,1,0:T(8,128)(2,1)S(1)}, u32[]{:S(2)}, u32[]{:S(2)}) collective-permute-start(bf16[2,128,256]{2,1,0:T(8,128)(2,1)S(1)} %pad_maximum_fusion.1), channel_id=1, source_target_pairs={{0,14},{1,15},{2,0},{3,1},{4,2},{5,3},{6,4},{7,5},{8,6},{9,7},{10,... | collective-permute-start | bytes 393224 | tf_op jit(solution)/shard_map/ppermute | solution.py:153
  16.4 0.2 collective-permute-done.6
  16.6 0.0 collective-permute-start.9
  16.6 0.7 slice_bitcast_fusion.6
  17.3 2.0 %collective-permute-done.5 = bf16[2,128,256]{2,1,0:T(8,128)(2,1)S(1)} collective-permute-done((bf16[2,128,256]{2,1,0:T(8,128)(2,1)S(1)}, bf16[2,128,256]{2,1,0:T(8,128)(2,1)S(1)}, u32[]{:S(2)}, u32[]{:S(2)}) %collective-permute-start.5) | collective-permute-done | bytes 131104 | tf_op jit(solution)/shard_map/ppermute | solution.py:153
  19.3 0.7 slice_bitcast_fusion.8
  19.9 0.0 collective-permute-done.8
  19.9 0.6 slice_bitcast_fusion.2
  20.6 2.5 %collective-permute-done.7 = bf16[2,128,256]{2,1,0:T(8,128)(2,1)S(1)} collective-permute-done((bf16[2,128,256]{2,1,0:T(8,128)(2,1)S(1)}, bf16[2,128,256]{2,1,0:T(8,128)(2,1)S(1)}, u32[]{:S(2)}, u32[]{:S(2)}) %collective-permute-start.7) | collective-permute-done | bytes 131104 | tf_op jit(solution)/shard_map/ppermute | solution.py:153
  23.1 0.7 slice_bitcast_fusion.4
  23.7 0.0 collective-permute-done.9
  23.7 0.7 slice_bitcast_fusion
  24.4 0.0 collective-permute-done.refs_1_
  24.4 0.0 copy-done
  24.4 0.6 copy-done.4
  25.0 8.3 %shard_map.82 = bf16[16,16,8,256]{3,2,1,0:T(8,128)(2,1)} custom-call(s32[2]{0:T(128)} %bitcast.36, s32[2,64]{1,0:T(2,128)} %gu_ref.1, s32[2,64]{1,0:T(2,128)} %dn_ref.1, s32[1]{0:T(128)} %bitcast.1.me_ref, s32[16]{0:T(128)} %constant.10.table_ref, bf16[128,256]{1,0:T(8,128)(2,1)} %refs_0_.1, bf16[128,256]{1,0:T(8,128)(2,1)} %copy-done.4, ...), custom_call_target="tpu_custom_call" | custom-call | tf_op jit(solution)/shard_map/pallas_call | solution.py:107
  33.3 47.0 %all_to_all.5 = bf16[256,8,256]{2,1,0:T(8,128)(2,1)S(1)} all-to-all(bf16[256,8,256]{2,1,0:T(8,128)(2,1)} %bitcast.30), channel_id=1, replica_groups=mesh['ctx'=16,'tp'=16] {'ctx','tp'}, dimensions={0} | all-to-all | bytes 2097152 | tf_op jit(solution)/shard_map/all_to_all | solution.py:169
  80.3 0.1 bitcast_reduce_fusion
  80.5 0.6 copy.9
  (9 shorter events, 0.0 us)
Async XLA Ops:
  0.0 9.3 %collective-permute-start.2 = (bf16[128,256]{1,0:T(8,128)(2,1)}, bf16[128,256]{1,0:T(8,128)(2,1)S(1)}, u32[]{:S(2)}, u32[]{:S(2)}) collective-permute-start(bf16[128,256]{1,0:T(8,128)(2,1)} %refs_0_.1), channel_id=1, source_target_pairs={{0,3},{1,2},{2,5},{3,4},{4,7},{5,6},{6,9},{7,8},{8,11},{9,10},{10,... | collective-permute-start | bytes 196616 | tf_op jit(solution)/shard_map/ppermute | solution.py:146
  3.5 6.4 %collective-permute-start.1 = (bf16[128,256]{1,0:T(8,128)(2,1)}, bf16[128,256]{1,0:T(8,128)(2,1)S(1)}, u32[]{:S(2)}, u32[]{:S(2)}) collective-permute-start(bf16[128,256]{1,0:T(8,128)(2,1)} %refs_0_.1), channel_id=1, source_target_pairs={{0,2},{1,3},{2,4},{3,5},{4,6},{5,7},{6,8},{7,9},{8,10},{9,11},{10,... | collective-permute-start | bytes 196616 | tf_op jit(solution)/shard_map/ppermute | solution.py:145
  5.1 7.8 %collective-permute-start.3 = (bf16[128,256]{1,0:T(8,128)(2,1)}, bf16[128,256]{1,0:T(8,128)(2,1)S(1)}, u32[]{:S(2)}, u32[]{:S(2)}) collective-permute-start(bf16[128,256]{1,0:T(8,128)(2,1)} %refs_0_.1), channel_id=1, source_target_pairs={{0,14},{1,15},{2,0},{3,1},{4,2},{5,3},{6,4},{7,5},{8,6},{9,7},{10,... | collective-permute-start | bytes 196616 | tf_op jit(solution)/shard_map/ppermute | solution.py:145
  6.5 6.4 %collective-permute-start.4 = (bf16[128,256]{1,0:T(8,128)(2,1)}, bf16[128,256]{1,0:T(8,128)(2,1)S(1)}, u32[]{:S(2)}, u32[]{:S(2)}) collective-permute-start(bf16[128,256]{1,0:T(8,128)(2,1)} %refs_0_.1), channel_id=1, source_target_pairs={{0,15},{1,14},{2,1},{3,0},{4,3},{5,2},{6,5},{7,4},{8,7},{9,6},{10,... | collective-permute-start | bytes 196616 | tf_op jit(solution)/shard_map/ppermute | solution.py:146
  9.3 15.1 %copy-start = (bf16[128,256]{1,0:T(8,128)(2,1)}, bf16[128,256]{1,0:T(8,128)(2,1)S(1)}, u32[]{:S(2)}) copy-start(bf16[128,256]{1,0:T(8,128)(2,1)S(1)} %collective-permute-done.2.refs_3_) | copy-start | bytes 196612
  9.8 14.6 %copy-start.1 = (bf16[128,256]{1,0:T(8,128)(2,1)}, bf16[128,256]{1,0:T(8,128)(2,1)S(1)}, u32[]{:S(2)}) copy-start(bf16[128,256]{1,0:T(8,128)(2,1)S(1)} %collective-permute-done.1.refs_2_) | copy-start | bytes 196612
  9.9 6.8 %collective-permute-start.6 = (bf16[2,128,256]{2,1,0:T(8,128)(2,1)S(1)}, bf16[2,128,256]{2,1,0:T(8,128)(2,1)S(1)}, u32[]{:S(2)}, u32[]{:S(2)}) collective-permute-start(bf16[2,128,256]{2,1,0:T(8,128)(2,1)S(1)} %pad_maximum_fusion), channel_id=1, source_target_pairs={{0,4},{1,5},{2,6},{3,7},{4,8},{5,9},{6,10},{7,11},{8,12},{9,13},{1... | collective-permute-start | bytes 393224 | tf_op jit(solution)/shard_map/ppermute | solution.py:153
  11.1 13.3 %collective-permute-start = (bf16[128,256]{1,0:T(8,128)(2,1)}, bf16[128,256]{1,0:T(8,128)(2,1)S(1)}, u32[]{:S(2)}, u32[]{:S(2)}) collective-permute-start(bf16[128,256]{1,0:T(8,128)(2,1)} %refs_0_.1), channel_id=1, source_target_pairs={{0,1},{1,0},{2,3},{3,2},{4,5},{5,4},{6,7},{7,6},{8,9},{9,8},{10,11... | collective-permute-start | bytes 196616 | tf_op jit(solution)/shard_map/ppermute | solution.py:141
  11.3 8.0 %collective-permute-start.5 = (bf16[2,128,256]{2,1,0:T(8,128)(2,1)S(1)}, bf16[2,128,256]{2,1,0:T(8,128)(2,1)S(1)}, u32[]{:S(2)}, u32[]{:S(2)}) collective-permute-start(bf16[2,128,256]{2,1,0:T(8,128)(2,1)S(1)} %pad_maximum_fusion), channel_id=1, source_target_pairs={{0,2},{1,3},{2,4},{3,5},{4,6},{5,7},{6,8},{7,9},{8,10},{9,11},{10,... | collective-permute-start | bytes 393224 | tf_op jit(solution)/shard_map/ppermute | solution.py:153
  12.9 11.5 %copy-start.2 = (bf16[128,256]{1,0:T(8,128)(2,1)}, bf16[128,256]{1,0:T(8,128)(2,1)S(1)}, u32[]{:S(2)}) copy-start(bf16[128,256]{1,0:T(8,128)(2,1)S(1)} %collective-permute-done.3.refs_4_) | copy-start | bytes 196612
  12.9 11.5 %copy-start.3 = (bf16[128,256]{1,0:T(8,128)(2,1)}, bf16[128,256]{1,0:T(8,128)(2,1)S(1)}, u32[]{:S(2)}) copy-start(bf16[128,256]{1,0:T(8,128)(2,1)S(1)} %collective-permute-done.4.refs_5_) | copy-start | bytes 196612
  13.0 7.0 %collective-permute-start.8 = (bf16[2,128,256]{2,1,0:T(8,128)(2,1)S(1)}, bf16[2,128,256]{2,1,0:T(8,128)(2,1)S(1)}, u32[]{:S(2)}, u32[]{:S(2)}) collective-permute-start(bf16[2,128,256]{2,1,0:T(8,128)(2,1)S(1)} %pad_maximum_fusion.1), channel_id=1, source_target_pairs={{0,12},{1,13},{2,14},{3,15},{4,0},{5,1},{6,2},{7,3},{8,4},{9,5},{1... | collective-permute-start | bytes 393224 | tf_op jit(solution)/shard_map/ppermute | solution.py:153
  14.9 8.1 %collective-permute-start.7 = (bf16[2,128,256]{2,1,0:T(8,128)(2,1)S(1)}, bf16[2,128,256]{2,1,0:T(8,128)(2,1)S(1)}, u32[]{:S(2)}, u32[]{:S(2)}) collective-permute-start(bf16[2,128,256]{2,1,0:T(8,128)(2,1)S(1)} %pad_maximum_fusion.1), channel_id=1, source_target_pairs={{0,14},{1,15},{2,0},{3,1},{4,2},{5,3},{6,4},{7,5},{8,6},{9,7},{10,... | collective-permute-start | bytes 393224 | tf_op jit(solution)/shard_map/ppermute | solution.py:153
  16.6 7.1 %collective-permute-start.9 = (bf16[2,128,256]{2,1,0:T(8,128)(2,1)S(1)}, bf16[2,128,256]{2,1,0:T(8,128)(2,1)S(1)}, u32[]{:S(2)}, u32[]{:S(2)}) collective-permute-start(bf16[2,128,256]{2,1,0:T(8,128)(2,1)S(1)} %collective-permute-done.6), channel_id=1, source_target_pairs={{0,2},{1,3},{2,4},{3,5},{4,6},{5,7},{6,8},{7,9},{8,10},{9,11},{10,... | collective-permute-start | bytes 393224 | tf_op jit(solution)/shard_map/ppermute | solution.py:157
  24.4 0.6 copy-start.4

commit v12 on v11

--- a/solution.py
+++ b/solution.py
@@ -1,3 +1,5 @@
+import functools
+
 import jax
 import jax.numpy as jnp
 from jax import lax
@@ -10,12 +12,18 @@
 CHUNKS = 8
 
 
-def ffn_kernel(cnt_ref, gu_ref, dn_ref, me_ref, table_ref, *refs):
-    n_src = table_ref.shape[0]
-    piece_refs = refs[:n_src]
+def ffn_kernel(layout, cnt_ref, gu_ref, dn_ref, me_ref, table_ref, *refs):
+    n_src = len(layout)
+    n_ops = len(refs) - 12
+    piece_refs = refs[:n_ops]
     (g_hbm, u_hbm, d_hbm, out_ref, normed_s, accg_s, accu_s, hid_s, acco_s, gu_v, d_v,
-     sems) = refs[n_src:]
+     sems) = refs[n_ops:]
     rows, width = piece_refs[0].shape
+
+    def piece(s, cols):
+        ref = piece_refs[layout[s][0]]
+        return ref[:, cols] if layout[s][1] < 0 else ref[layout[s][1], :, cols]
+
     tile = g_hbm.shape[1]
     slots = g_hbm.shape[0]
     step = slots // CHUNKS
@@ -40,12 +48,12 @@
     feat = n_src * width
     ss = jnp.zeros((rows, 1), jnp.float32)
     for s in range(n_src):
-        x = piece_refs[s][...].astype(jnp.float32)
+        x = piece(s, slice(None)).astype(jnp.float32)
         ss = ss + jnp.sum(x * x, axis=1, keepdims=True)
     scale = lax.rsqrt(ss / feat + 1e-05)
     for s in range(n_src):
         for h in range(per_src):
-            x = piece_refs[s][:, h * tile:(h + 1) * tile].astype(jnp.float32)
+            x = piece(s, slice(h * tile, (h + 1) * tile)).astype(jnp.float32)
             normed_s[s * per_src + h] = (x * scale).astype(jnp.bfloat16)
     accg_s[...] = jnp.zeros(accg_s.shape, jnp.float32)
     accu_s[...] = jnp.zeros(accu_s.shape, jnp.float32)
@@ -86,7 +94,7 @@
         lax.fori_loop(k * step, (k + 1) * step, dn_body, 0, unroll=True)
     groups, dests, share, group_width = out_ref.shape
     for h in range(per_src):
-        acco_s[me_ref[0] * per_src + h] += piece_refs[0][:, h * tile:(h + 1) * tile].astype(jnp.float32)
+        acco_s[me_ref[0] * per_src + h] += piece(0, slice(h * tile, (h + 1) * tile)).astype(jnp.float32)
     per_group = group_width // tile
     for o in range(acco_s.shape[0]):
         block = acco_s[o].reshape(dests, share, tile).astype(out_ref.dtype)
@@ -96,7 +104,10 @@
 
 def ffn(counts, gu_blocks, down_blocks, me, table, pieces, gate_tiles, up_tiles, down_tiles,
         hid_blocks, groups, share):
-    n_src = len(pieces)
+    layout = []
+    for index, array in enumerate(pieces):
+        layout += [(index, -1)] if array.ndim == 2 else [(index, sub) for sub in range(array.shape[0])]
+    n_src = len(layout)
     rows, width = pieces[0].shape
     tile = gate_tiles.shape[1]
     in_blocks = n_src * width // tile
@@ -105,10 +116,10 @@
     hbm = pl.BlockSpec(memory_space=pl.ANY)
     slots = gate_tiles.shape[0]
     return pl.pallas_call(
-        ffn_kernel,
+        functools.partial(ffn_kernel, tuple(layout)),
         out_shape=jax.ShapeDtypeStruct((groups, rows // share, share, in_blocks * tile // groups),
                                        jnp.bfloat16),
-        in_specs=[smem] * 5 + [vmem] * n_src + [hbm] * 3,
+        in_specs=[smem] * 5 + [vmem] * len(pieces) + [hbm] * 3,
         out_specs=vmem,
         scratch_shapes=[
             pltpu.VMEM((in_blocks, rows, tile), jnp.bfloat16),
@@ -151,11 +162,11 @@
     for step in (1, -1):
         for hops in (1, 2):
             pair = lax.ppermute(near[step], "tp", ring_pairs(z_count, step * hops))
-            arrays += [pair[0], pair[1]]
+            arrays.append(pair)
             origins += [(-step * (hops + 1) % z_count, 0), (-step * (hops + 1) % z_count, 1)]
             far[step, hops] = pair
     last = lax.ppermute(far[1, 2], "tp", ring_pairs(z_count, 1))
-    arrays += [last[0], last[1]]
+    arrays.append(last)
     origins += [(-4 % z_count, 0), (-4 % z_count, 1)]
     table = [[0] * Y_LO for _ in range(z_count)]
     for index, (dz, dy) in enumerate(origins):

time: 81.3 us -> 80.7 us (level)
  local copies, waits for them, and re-layouts: 4.55 us -> 1.3 us
  waiting for transfers between devices: 5.63 us -> 7.39 us
    squeeze x5 -> x0, local copies, waits for them, and re-layouts: 3.3 us -> none  [the longest x4 2.63 us: per_device(): arrays += [pair[0], pair[1]]]
    ppermute x1, waiting for transfers between devices: 0.01 us -> 2.97 us  [per_device(): arrays = [tokens, lax.ppermute(tokens, 'tp', swap)]]
    ppermute x4, waiting for transfers between devices: 4.67 us -> 3.47 us  [per_device(): pair = lax.ppermute(near[step], 'tp', ring_pairs(z_count, step * hops))]
  transfers between devices with their start and end apart: 10 -> 10, of which waited for: 5 -> 5; matrix products, arithmetic and copies ran while one was open for 4% -> 0% of each run, Pallas kernels for 0% -> 0%
where the time goes in v12:
time: 80.7 us; the launch traced here: 80.5 us
  blocking collectives  47.8 us (59%)
  starting transfers between devices  15.4 us (19%)
  Pallas kernels  8.32 us (10%)
  waiting for transfers between devices  7.39 us (9%)
  local copies, waits for them, and re-layouts  1.3 us (2%)
    all_to_all x1, blocking collectives, per_device(): lax.all_to_all(outgoing.reshape(ctx_count * tp_count, share, feat_width /...  47.8 us
    pallas_call x1, Pallas kernels, ffn(): pl.pallas_call(functools.partial(ffn_kernel, tuple(layout)), out_shape=ja...  8.32 us
    ppermute x2, starting transfers between devices, per_device(): other = lax.ppermute(tokens, 'tp', ring_pairs(z_count, step, 1))  5.88 us
    ppermute x4, starting transfers between devices, per_device(): pair = lax.ppermute(near[step], 'tp', ring_pairs(z_count, step * hops))  5.87 us
    ppermute x4, waiting for transfers between devices, per_device(): pair = lax.ppermute(near[step], 'tp', ring_pairs(z_count, step * hops))  3.47 us
    ppermute x2, starting transfers between devices, per_device(): same = lax.ppermute(tokens, 'tp', ring_pairs(z_count, step))  3.01 us
    ppermute x1, waiting for transfers between devices, per_device(): arrays = [tokens, lax.ppermute(tokens, 'tp', swap)]  2.97 us
  transfers between devices with their start and end apart: 10, of which 5 were waited for; matrix products, arithmetic and copies ran while one was open for 0% of the time, Pallas kernels for 0%

profile of v12, /device:TPU:1, one launch (start us, length us, event | category | flops | bytes accessed | tf_op | source)
XLA Modules:
  0.0 80.5 jit_solution(16654457457243025290)
XLA Ops:
  0.0 3.5 %collective-permute-start.2 = (bf16[128,256]{1,0:T(8,128)(2,1)}, bf16[128,256]{1,0:T(8,128)(2,1)S(1)}, u32[]{:S(2)}, u32[]{:S(2)}) collective-permute-start(bf16[128,256]{1,0:T(8,128)(2,1)} %refs_0_.1), channel_id=1, source_target_pairs={{0,3},{1,2},{2,5},{3,4},{4,7},{5,6},{6,9},{7,8},{8,11},{9,10},{10,... | collective-permute-start | bytes 196616 | tf_op jit(solution)/shard_map/ppermute | solution.py:157
  3.5 1.6 %collective-permute-start.1 = (bf16[128,256]{1,0:T(8,128)(2,1)}, bf16[128,256]{1,0:T(8,128)(2,1)S(1)}, u32[]{:S(2)}, u32[]{:S(2)}) collective-permute-start(bf16[128,256]{1,0:T(8,128)(2,1)} %refs_0_.1), channel_id=1, source_target_pairs={{0,2},{1,3},{2,4},{3,5},{4,6},{5,7},{6,8},{7,9},{8,10},{9,11},{10,... | collective-permute-start | bytes 196616 | tf_op jit(solution)/shard_map/ppermute | solution.py:156
  5.1 1.4 %collective-permute-start.3 = (bf16[128,256]{1,0:T(8,128)(2,1)}, bf16[128,256]{1,0:T(8,128)(2,1)S(1)}, u32[]{:S(2)}, u32[]{:S(2)}) collective-permute-start(bf16[128,256]{1,0:T(8,128)(2,1)} %refs_0_.1), channel_id=1, source_target_pairs={{0,14},{1,15},{2,0},{3,1},{4,2},{5,3},{6,4},{7,5},{8,6},{9,7},{10,... | collective-permute-start | bytes 196616 | tf_op jit(solution)/shard_map/ppermute | solution.py:156
  6.5 2.4 %collective-permute-start.4 = (bf16[128,256]{1,0:T(8,128)(2,1)}, bf16[128,256]{1,0:T(8,128)(2,1)S(1)}, u32[]{:S(2)}, u32[]{:S(2)}) collective-permute-start(bf16[128,256]{1,0:T(8,128)(2,1)} %refs_0_.1), channel_id=1, source_target_pairs={{0,15},{1,14},{2,1},{3,0},{4,3},{5,2},{6,5},{7,4},{8,7},{9,6},{10,... | collective-permute-start | bytes 196616 | tf_op jit(solution)/shard_map/ppermute | solution.py:157
  8.9 0.4 collective-permute-done.2.refs_3_
  9.3 0.6 collective-permute-done.1.refs_2_
  9.9 1.2 %collective-permute-start.6 = (bf16[2,128,256]{2,1,0:T(8,128)(2,1)S(1)}, bf16[2,128,256]{2,1,0:T(8,128)(2,1)S(1)}, u32[]{:S(2)}, u32[]{:S(2)}) collective-permute-start(bf16[2,128,256]{2,1,0:T(8,128)(2,1)S(1)} %pad_maximum_fusion), channel_id=1, source_target_pairs={{0,4},{1,5},{2,6},{3,7},{4,8},{5,9},{6,10},{7,11},{8,12},{9,13},{1... | collective-permute-start | bytes 393224 | tf_op jit(solution)/shard_map/ppermute | solution.py:164
  11.1 1.7 %collective-permute-start.5 = (bf16[2,128,256]{2,1,0:T(8,128)(2,1)S(1)}, bf16[2,128,256]{2,1,0:T(8,128)(2,1)S(1)}, u32[]{:S(2)}, u32[]{:S(2)}) collective-permute-start(bf16[2,128,256]{2,1,0:T(8,128)(2,1)S(1)} %pad_maximum_fusion), channel_id=1, source_target_pairs={{0,2},{1,3},{2,4},{3,5},{4,6},{5,7},{6,8},{7,9},{8,10},{9,11},{10,... | collective-permute-start | bytes 393224 | tf_op jit(solution)/shard_map/ppermute | solution.py:164
  12.7 0.0 collective-permute-done.3.refs_4_
  12.7 0.0 collective-permute-done.4.refs_5_
  12.8 0.0 copy-start.3
  12.8 1.6 %collective-permute-start.8 = (bf16[2,128,256]{2,1,0:T(8,128)(2,1)S(1)}, bf16[2,128,256]{2,1,0:T(8,128)(2,1)S(1)}, u32[]{:S(2)}, u32[]{:S(2)}) collective-permute-start(bf16[2,128,256]{2,1,0:T(8,128)(2,1)S(1)} %pad_maximum_fusion.1), channel_id=1, source_target_pairs={{0,12},{1,13},{2,14},{3,15},{4,0},{5,1},{6,2},{7,3},{8,4},{9,5},{1... | collective-permute-start | bytes 393224 | tf_op jit(solution)/shard_map/ppermute | solution.py:164
  14.4 1.4 %collective-permute-start.7 = (bf16[2,128,256]{2,1,0:T(8,128)(2,1)S(1)}, bf16[2,128,256]{2,1,0:T(8,128)(2,1)S(1)}, u32[]{:S(2)}, u32[]{:S(2)}) collective-permute-start(bf16[2,128,256]{2,1,0:T(8,128)(2,1)S(1)} %pad_maximum_fusion.1), channel_id=1, source_target_pairs={{0,14},{1,15},{2,0},{3,1},{4,2},{5,3},{6,4},{7,5},{8,6},{9,7},{10,... | collective-permute-start | bytes 393224 | tf_op jit(solution)/shard_map/ppermute | solution.py:164
  15.8 0.8 %collective-permute-done.6.refs_7_ = bf16[2,128,256]{2,1,0:T(8,128)(2,1)S(1)} collective-permute-done((bf16[2,128,256]{2,1,0:T(8,128)(2,1)S(1)}, bf16[2,128,256]{2,1,0:T(8,128)(2,1)S(1)}, u32[]{:S(2)}, u32[]{:S(2)}) %collective-permute-start.6) | collective-permute-done | bytes 131104 | tf_op jit(solution)/shard_map/ppermute | solution.py:164
  16.6 0.0 collective-permute-start.9
  16.6 0.7 collective-permute-start
  17.3 3.0 %collective-permute-done.refs_1_ = bf16[128,256]{1,0:T(8,128)(2,1)S(1)} collective-permute-done((bf16[128,256]{1,0:T(8,128)(2,1)}, bf16[128,256]{1,0:T(8,128)(2,1)S(1)}, u32[]{:S(2)}, u32[]{:S(2)}) %collective-permute-start) | collective-permute-done | bytes 65568 | tf_op jit(solution)/shard_map/ppermute | solution.py:152
  20.2 0.0 collective-permute-done.5.refs_6_
  20.2 0.0 collective-permute-done.8.refs_9_
  20.3 0.0 copy-start.6
  20.3 2.6 %collective-permute-done.7.refs_8_ = bf16[2,128,256]{2,1,0:T(8,128)(2,1)S(1)} collective-permute-done((bf16[2,128,256]{2,1,0:T(8,128)(2,1)S(1)}, bf16[2,128,256]{2,1,0:T(8,128)(2,1)S(1)}, u32[]{:S(2)}, u32[]{:S(2)}) %collective-permute-start.7) | collective-permute-done | bytes 131104 | tf_op jit(solution)/shard_map/ppermute | solution.py:164
  22.9 0.0 collective-permute-done.9.refs_10_
  22.9 0.0 copy-done
  22.9 0.0 copy-done.1
  22.9 0.0 copy-done.2
  22.9 0.0 copy-done.3
  23.0 0.6 copy-done.7
  23.5 0.1 copy-done.8
  23.6 8.3 %shard_map.82 = bf16[16,16,8,256]{3,2,1,0:T(8,128)(2,1)} custom-call(s32[2]{0:T(128)} %bitcast.16, s32[2,64]{1,0:T(2,128)} %gu_ref.1, s32[2,64]{1,0:T(2,128)} %dn_ref.1, s32[1]{0:T(128)} %bitcast.1.me_ref, s32[16]{0:T(128)} %constant.10.table_ref, bf16[128,256]{1,0:T(8,128)(2,1)} %refs_0_.1, bf16[128,256]{1,0:T(8,128)(2,1)} %copy-done.9, ...), custom_call_target="tpu_custom_call" | custom-call | tf_op jit(solution)/shard_map/pallas_call | solution.py:118
  31.9 47.8 %all_to_all.5 = bf16[256,8,256]{2,1,0:T(8,128)(2,1)S(1)} all-to-all(bf16[256,8,256]{2,1,0:T(8,128)(2,1)} %bitcast.10), channel_id=1, replica_groups=mesh['ctx'=16,'tp'=16] {'ctx','tp'}, dimensions={0} | all-to-all | bytes 2097152 | tf_op jit(solution)/shard_map/all_to_all | solution.py:180
  79.7 0.1 bitcast_reduce_fusion
  79.9 0.6 copy.9
  (14 shorter events, 0.1 us)
Async XLA Ops:
  0.0 9.3 %collective-permute-start.2 = (bf16[128,256]{1,0:T(8,128)(2,1)}, bf16[128,256]{1,0:T(8,128)(2,1)S(1)}, u32[]{:S(2)}, u32[]{:S(2)}) collective-permute-start(bf16[128,256]{1,0:T(8,128)(2,1)} %refs_0_.1), channel_id=1, source_target_pairs={{0,3},{1,2},{2,5},{3,4},{4,7},{5,6},{6,9},{7,8},{8,11},{9,10},{10,... | collective-permute-start | bytes 196616 | tf_op jit(solution)/shard_map/ppermute | solution.py:157
  3.5 6.4 %collective-permute-start.1 = (bf16[128,256]{1,0:T(8,128)(2,1)}, bf16[128,256]{1,0:T(8,128)(2,1)S(1)}, u32[]{:S(2)}, u32[]{:S(2)}) collective-permute-start(bf16[128,256]{1,0:T(8,128)(2,1)} %refs_0_.1), channel_id=1, source_target_pairs={{0,2},{1,3},{2,4},{3,5},{4,6},{5,7},{6,8},{7,9},{8,10},{9,11},{10,... | collective-permute-start | bytes 196616 | tf_op jit(solution)/shard_map/ppermute | solution.py:156
  5.1 7.6 %collective-permute-start.3 = (bf16[128,256]{1,0:T(8,128)(2,1)}, bf16[128,256]{1,0:T(8,128)(2,1)S(1)}, u32[]{:S(2)}, u32[]{:S(2)}) collective-permute-start(bf16[128,256]{1,0:T(8,128)(2,1)} %refs_0_.1), channel_id=1, source_target_pairs={{0,14},{1,15},{2,0},{3,1},{4,2},{5,3},{6,4},{7,5},{8,6},{9,7},{10,... | collective-permute-start | bytes 196616 | tf_op jit(solution)/shard_map/ppermute | solution.py:156
  6.5 6.3 %collective-permute-start.4 = (bf16[128,256]{1,0:T(8,128)(2,1)}, bf16[128,256]{1,0:T(8,128)(2,1)S(1)}, u32[]{:S(2)}, u32[]{:S(2)}) collective-permute-start(bf16[128,256]{1,0:T(8,128)(2,1)} %refs_0_.1), channel_id=1, source_target_pairs={{0,15},{1,14},{2,1},{3,0},{4,3},{5,2},{6,5},{7,4},{8,7},{9,6},{10,... | collective-permute-start | bytes 196616 | tf_op jit(solution)/shard_map/ppermute | solution.py:157
  9.3 13.6 %copy-start = (bf16[128,256]{1,0:T(8,128)(2,1)}, bf16[128,256]{1,0:T(8,128)(2,1)S(1)}, u32[]{:S(2)}) copy-start(bf16[128,256]{1,0:T(8,128)(2,1)S(1)} %collective-permute-done.2.refs_3_) | copy-start | bytes 196612
  9.8 13.1 %copy-start.1 = (bf16[128,256]{1,0:T(8,128)(2,1)}, bf16[128,256]{1,0:T(8,128)(2,1)S(1)}, u32[]{:S(2)}) copy-start(bf16[128,256]{1,0:T(8,128)(2,1)S(1)} %collective-permute-done.1.refs_2_) | copy-start | bytes 196612
  9.9 6.8 %collective-permute-start.6 = (bf16[2,128,256]{2,1,0:T(8,128)(2,1)S(1)}, bf16[2,128,256]{2,1,0:T(8,128)(2,1)S(1)}, u32[]{:S(2)}, u32[]{:S(2)}) collective-permute-start(bf16[2,128,256]{2,1,0:T(8,128)(2,1)S(1)} %pad_maximum_fusion), channel_id=1, source_target_pairs={{0,4},{1,5},{2,6},{3,7},{4,8},{5,9},{6,10},{7,11},{8,12},{9,13},{1... | collective-permute-start | bytes 393224 | tf_op jit(solution)/shard_map/ppermute | solution.py:164
  11.1 9.2 %collective-permute-start.5 = (bf16[2,128,256]{2,1,0:T(8,128)(2,1)S(1)}, bf16[2,128,256]{2,1,0:T(8,128)(2,1)S(1)}, u32[]{:S(2)}, u32[]{:S(2)}) collective-permute-start(bf16[2,128,256]{2,1,0:T(8,128)(2,1)S(1)} %pad_maximum_fusion), channel_id=1, source_target_pairs={{0,2},{1,3},{2,4},{3,5},{4,6},{5,7},{6,8},{7,9},{8,10},{9,11},{10,... | collective-permute-start | bytes 393224 | tf_op jit(solution)/shard_map/ppermute | solution.py:164
  12.7 10.2 %copy-start.2 = (bf16[128,256]{1,0:T(8,128)(2,1)}, bf16[128,256]{1,0:T(8,128)(2,1)S(1)}, u32[]{:S(2)}) copy-start(bf16[128,256]{1,0:T(8,128)(2,1)S(1)} %collective-permute-done.3.refs_4_) | copy-start | bytes 196612
  12.8 10.2 %copy-start.3 = (bf16[128,256]{1,0:T(8,128)(2,1)}, bf16[128,256]{1,0:T(8,128)(2,1)S(1)}, u32[]{:S(2)}) copy-start(bf16[128,256]{1,0:T(8,128)(2,1)S(1)} %collective-permute-done.4.refs_5_) | copy-start | bytes 196612
  12.8 7.5 %collective-permute-start.8 = (bf16[2,128,256]{2,1,0:T(8,128)(2,1)S(1)}, bf16[2,128,256]{2,1,0:T(8,128)(2,1)S(1)}, u32[]{:S(2)}, u32[]{:S(2)}) collective-permute-start(bf16[2,128,256]{2,1,0:T(8,128)(2,1)S(1)} %pad_maximum_fusion.1), channel_id=1, source_target_pairs={{0,12},{1,13},{2,14},{3,15},{4,0},{5,1},{6,2},{7,3},{8,4},{9,5},{1... | collective-permute-start | bytes 393224 | tf_op jit(solution)/shard_map/ppermute | solution.py:164
  14.4 8.5 %collective-permute-start.7 = (bf16[2,128,256]{2,1,0:T(8,128)(2,1)S(1)}, bf16[2,128,256]{2,1,0:T(8,128)(2,1)S(1)}, u32[]{:S(2)}, u32[]{:S(2)}) collective-permute-start(bf16[2,128,256]{2,1,0:T(8,128)(2,1)S(1)} %pad_maximum_fusion.1), channel_id=1, source_target_pairs={{0,14},{1,15},{2,0},{3,1},{4,2},{5,3},{6,4},{7,5},{8,6},{9,7},{10,... | collective-permute-start | bytes 393224 | tf_op jit(solution)/shard_map/ppermute | solution.py:164
  16.6 6.3 %copy-start.4 = (bf16[2,128,256]{2,1,0:T(8,128)(2,1)}, bf16[2,128,256]{2,1,0:T(8,128)(2,1)S(1)}, u32[]{:S(2)}) copy-start(bf16[2,128,256]{2,1,0:T(8,128)(2,1)S(1)} %collective-permute-done.6.refs_7_) | copy-start | bytes 393220
  16.6 6.3 %collective-permute-start.9 = (bf16[2,128,256]{2,1,0:T(8,128)(2,1)S(1)}, bf16[2,128,256]{2,1,0:T(8,128)(2,1)S(1)}, u32[]{:S(2)}, u32[]{:S(2)}) collective-permute-start(bf16[2,128,256]{2,1,0:T(8,128)(2,1)S(1)} %collective-permute-done.6.refs_7_), channel_id=1, source_target_pairs={{0,2},{1,3},{2,4},{3,5},{4,6},{5,7},{6,8},{7,9},{8,10},{9,11},{10,... | collective-permute-start | bytes 393224 | tf_op jit(solution)/shard_map/ppermute | solution.py:168
  16.6 3.6 %collective-permute-start = (bf16[128,256]{1,0:T(8,128)(2,1)}, bf16[128,256]{1,0:T(8,128)(2,1)S(1)}, u32[]{:S(2)}, u32[]{:S(2)}) collective-permute-start(bf16[128,256]{1,0:T(8,128)(2,1)} %refs_0_.1), channel_id=1, source_target_pairs={{0,1},{1,0},{2,3},{3,2},{4,5},{5,4},{6,7},{7,6},{8,9},{9,8},{10,11... | collective-permute-start | bytes 196616 | tf_op jit(solution)/shard_map/ppermute | solution.py:152
  20.2 2.7 %copy-start.9 = (bf16[128,256]{1,0:T(8,128)(2,1)}, bf16[128,256]{1,0:T(8,128)(2,1)S(1)}, u32[]{:S(2)}) copy-start(bf16[128,256]{1,0:T(8,128)(2,1)S(1)} %collective-permute-done.refs_1_) | copy-start | bytes 196612
  20.2 2.7 %copy-start.5 = (bf16[2,128,256]{2,1,0:T(8,128)(2,1)}, bf16[2,128,256]{2,1,0:T(8,128)(2,1)S(1)}, u32[]{:S(2)}) copy-start(bf16[2,128,256]{2,1,0:T(8,128)(2,1)S(1)} %collective-permute-done.5.refs_6_) | copy-start | bytes 393220
  20.3 2.7 %copy-start.6 = (bf16[2,128,256]{2,1,0:T(8,128)(2,1)}, bf16[2,128,256]{2,1,0:T(8,128)(2,1)S(1)}, u32[]{:S(2)}) copy-start(bf16[2,128,256]{2,1,0:T(8,128)(2,1)S(1)} %collective-permute-done.8.refs_9_) | copy-start | bytes 393220
  22.9 0.7 copy-start.7
  22.9 0.7 copy-start.8

commit v13 on v12

--- a/solution.py
+++ b/solution.py
@@ -149,12 +149,17 @@
     my_z = me // Y_LO
     my_y = me % Y_LO
     swap = [(i, i ^ 1) for i in range(tp_count)]
-    arrays = [tokens, lax.ppermute(tokens, "tp", swap)]
+    partner = lax.ppermute(tokens, "tp", swap)
+    first = {}
+    for step in (1, -1):
+        first[step] = (lax.ppermute(tokens, "tp", ring_pairs(z_count, step)),
+                       lax.ppermute(tokens, "tp", ring_pairs(z_count, step, 1)))
+    partner, first = lax.optimization_barrier((partner, first))
+    arrays = [tokens, partner]
     origins = [(0, 0), (0, 1)]
     near = {}
     for step in (1, -1):
-        same = lax.ppermute(tokens, "tp", ring_pairs(z_count, step))
-        other = lax.ppermute(tokens, "tp", ring_pairs(z_count, step, 1))
+        same, other = first[step]
         arrays += [same, other]
         origins += [(-step % z_count, 0), (-step % z_count, 1)]
         near[step] = jnp.stack([same, other])

time: 80.7 us -> 84 us (1.041)
  waiting for transfers between devices: 7.39 us -> 11.9 us
  blocking collectives: 47.8 us -> 46.7 us
    ppermute x1, waiting for transfers between devices: 0.01 us -> 3.1 us  [per_device(): last = lax.ppermute(far[1, 2], 'tp', ring_pairs(z_count, 1))]
    all_to_all x1, blocking collectives: 47.8 us -> 46.7 us  [per_device(): lax.all_to_all(outgoing.reshape(ctx_count * tp_count, share, feat_width /...]
    ppermute x4, waiting for transfers between devices: 3.47 us -> 4.32 us  [per_device(): pair = lax.ppermute(near[step], 'tp', ring_pairs(z_count, step * hops))]
  transfers between devices with their start and end apart: 10 -> 10, of which waited for: 5 -> 6; matrix products, arithmetic and copies ran while one was open for 0% -> 0% of each run, Pallas kernels for 0% -> 0%
where the time goes in v13:
time: 84 us; the launch traced here: 83.8 us
  blocking collectives  46.7 us (56%)
  starting transfers between devices  15.3 us (18%)
  waiting for transfers between devices  11.9 us (14%)
  Pallas kernels  8.32 us (10%)
  local copies, waits for them, and re-layouts  1.25 us (1%)
    all_to_all x1, blocking collectives, per_device(): lax.all_to_all(outgoing.reshape(ctx_count * tp_count, share, feat_width /...  46.7 us
    pallas_call x1, Pallas kernels, ffn(): pl.pallas_call(functools.partial(ffn_kernel, tuple(layout)), out_shape=ja...  8.32 us
    ppermute x2, starting transfers between devices, per_device(): lax.ppermute(tokens, 'tp', ring_pairs(z_count, step, 1))  5.97 us
    ppermute x4, starting transfers between devices, per_device(): pair = lax.ppermute(near[step], 'tp', ring_pairs(z_count, step * hops))  5.19 us
    ppermute x4, waiting for transfers between devices, per_device(): pair = lax.ppermute(near[step], 'tp', ring_pairs(z_count, step * hops))  4.32 us
    ppermute x2, starting transfers between devices, per_device(): lax.ppermute(tokens, 'tp', ring_pairs(z_count, step))  3.93 us
    ppermute x1, waiting for transfers between devices, per_device(): last = lax.ppermute(far[1, 2], 'tp', ring_pairs(z_count, 1))  3.1 us
    ppermute x2, waiting for transfers between devices, per_device(): lax.ppermute(tokens, 'tp', ring_pairs(z_count, step, 1))  2.14 us
  transfers between devices with their start and end apart: 10, of which 6 were waited for; matrix products, arithmetic and copies ran while one was open for 0% of the time, Pallas kernels for 0%

profile of v13, /device:TPU:1, one launch (start us, length us, event | category | flops | bytes accessed | tf_op | source)
XLA Modules:
  0.0 83.8 jit_solution(10724302124520581207)
XLA Ops:
  0.0 2.5 %collective-permute-start.3 = (bf16[128,256]{1,0:T(8,128)(2,1)}, bf16[128,256]{1,0:T(8,128)(2,1)S(1)}, u32[]{:S(2)}, u32[]{:S(2)}) collective-permute-start(bf16[128,256]{1,0:T(8,128)(2,1)} %refs_0_.1), channel_id=1, source_target_pairs={{0,2},{1,3},{2,4},{3,5},{4,6},{5,7},{6,8},{7,9},{8,10},{9,11},{10,... | collective-permute-start | bytes 196616 | tf_op jit(solution)/shard_map/ppermute | solution.py:155
  2.5 5.0 %collective-permute-start.2 = (bf16[128,256]{1,0:T(8,128)(2,1)}, bf16[128,256]{1,0:T(8,128)(2,1)S(1)}, u32[]{:S(2)}, u32[]{:S(2)}) collective-permute-start(bf16[128,256]{1,0:T(8,128)(2,1)} %refs_0_.1), channel_id=1, source_target_pairs={{0,15},{1,14},{2,1},{3,0},{4,3},{5,2},{6,5},{7,4},{8,7},{9,6},{10,... | collective-permute-start | bytes 196616 | tf_op jit(solution)/shard_map/ppermute | solution.py:156
  7.4 1.5 %collective-permute-start.1 = (bf16[128,256]{1,0:T(8,128)(2,1)}, bf16[128,256]{1,0:T(8,128)(2,1)S(1)}, u32[]{:S(2)}, u32[]{:S(2)}) collective-permute-start(bf16[128,256]{1,0:T(8,128)(2,1)} %refs_0_.1), channel_id=1, source_target_pairs={{0,14},{1,15},{2,0},{3,1},{4,2},{5,3},{6,4},{7,5},{8,6},{9,7},{10,... | collective-permute-start | bytes 196616 | tf_op jit(solution)/shard_map/ppermute | solution.py:155
  8.9 0.2 collective-permute-start
  9.1 1.0 %collective-permute-start.4 = (bf16[128,256]{1,0:T(8,128)(2,1)}, bf16[128,256]{1,0:T(8,128)(2,1)S(1)}, u32[]{:S(2)}, u32[]{:S(2)}) collective-permute-start(bf16[128,256]{1,0:T(8,128)(2,1)} %refs_0_.1), channel_id=1, source_target_pairs={{0,3},{1,2},{2,5},{3,4},{4,7},{5,6},{6,9},{7,8},{8,11},{9,10},{10,... | collective-permute-start | bytes 196616 | tf_op jit(solution)/shard_map/ppermute | solution.py:156
  10.1 0.0 collective-permute-done.3.refs_2_
  10.1 0.0 collective-permute-done.2.refs_5_
  10.1 0.0 copy-start.1
  10.1 0.7 collective-permute-done.1.refs_4_
  10.8 1.7 %collective-permute-done.refs_1_ = bf16[128,256]{1,0:T(8,128)(2,1)S(1)} collective-permute-done((bf16[128,256]{1,0:T(8,128)(2,1)}, bf16[128,256]{1,0:T(8,128)(2,1)S(1)}, u32[]{:S(2)}, u32[]{:S(2)}) %collective-permute-start) | collective-permute-done | bytes 65568 | tf_op jit(solution)/shard_map/ppermute | solution.py:152
  12.5 2.1 %collective-permute-done.4.refs_3_ = bf16[128,256]{1,0:T(8,128)(2,1)S(1)} collective-permute-done((bf16[128,256]{1,0:T(8,128)(2,1)}, bf16[128,256]{1,0:T(8,128)(2,1)S(1)}, u32[]{:S(2)}, u32[]{:S(2)}) %collective-permute-start.4) | collective-permute-done | bytes 65568 | tf_op jit(solution)/shard_map/ppermute | solution.py:156
  14.6 0.1 collective-permute-start.6
  14.7 0.3 collective-permute-start.5
  15.0 3.4 %collective-permute-start.8 = (bf16[2,128,256]{2,1,0:T(8,128)(2,1)S(1)}, bf16[2,128,256]{2,1,0:T(8,128)(2,1)S(1)}, u32[]{:S(2)}, u32[]{:S(2)}) collective-permute-start(bf16[2,128,256]{2,1,0:T(8,128)(2,1)S(1)} %pad_maximum_fusion.1), channel_id=1, source_target_pairs={{0,12},{1,13},{2,14},{3,15},{4,0},{5,1},{6,2},{7,3},{8,4},{9,5},{1... | collective-permute-start | bytes 393224 | tf_op jit(solution)/shard_map/ppermute | solution.py:169
  18.4 1.5 %collective-permute-start.7 = (bf16[2,128,256]{2,1,0:T(8,128)(2,1)S(1)}, bf16[2,128,256]{2,1,0:T(8,128)(2,1)S(1)}, u32[]{:S(2)}, u32[]{:S(2)}) collective-permute-start(bf16[2,128,256]{2,1,0:T(8,128)(2,1)S(1)} %pad_maximum_fusion.1), channel_id=1, source_target_pairs={{0,14},{1,15},{2,0},{3,1},{4,2},{5,3},{6,4},{7,5},{8,6},{9,7},{10,... | collective-permute-start | bytes 393224 | tf_op jit(solution)/shard_map/ppermute | solution.py:169
  19.8 2.3 %collective-permute-done.6.refs_7_ = bf16[2,128,256]{2,1,0:T(8,128)(2,1)S(1)} collective-permute-done((bf16[2,128,256]{2,1,0:T(8,128)(2,1)S(1)}, bf16[2,128,256]{2,1,0:T(8,128)(2,1)S(1)}, u32[]{:S(2)}, u32[]{:S(2)}) %collective-permute-start.6) | collective-permute-done | bytes 131104 | tf_op jit(solution)/shard_map/ppermute | solution.py:169
  22.2 0.0 collective-permute-start.9
  22.2 0.0 collective-permute-done.5.refs_6_
  22.2 0.0 copy-start.5
  22.2 0.0 collective-permute-done.8.refs_9_
  22.2 0.0 copy-start.6
  22.2 2.0 %collective-permute-done.7.refs_8_ = bf16[2,128,256]{2,1,0:T(8,128)(2,1)S(1)} collective-permute-done((bf16[2,128,256]{2,1,0:T(8,128)(2,1)S(1)}, bf16[2,128,256]{2,1,0:T(8,128)(2,1)S(1)}, u32[]{:S(2)}, u32[]{:S(2)}) %collective-permute-start.7) | collective-permute-done | bytes 131104 | tf_op jit(solution)/shard_map/ppermute | solution.py:169
  24.2 3.1 %collective-permute-done.9.refs_10_ = bf16[2,128,256]{2,1,0:T(8,128)(2,1)S(1)} collective-permute-done((bf16[2,128,256]{2,1,0:T(8,128)(2,1)S(1)}, bf16[2,128,256]{2,1,0:T(8,128)(2,1)S(1)}, u32[]{:S(2)}, u32[]{:S(2)}) %collective-permute-start.9) | collective-permute-done | bytes 131104 | tf_op jit(solution)/shard_map/ppermute | solution.py:173
  27.3 0.0 copy-done
  27.3 0.0 copy-done.1
  27.3 0.0 copy-done.2
  27.3 0.0 copy-done.9
  27.4 0.6 copy-done.8
  27.9 8.3 %shard_map.82 = bf16[16,16,8,256]{3,2,1,0:T(8,128)(2,1)} custom-call(s32[2]{0:T(128)} %bitcast.16, s32[2,64]{1,0:T(2,128)} %gu_ref.1, s32[2,64]{1,0:T(2,128)} %dn_ref.1, s32[1]{0:T(128)} %bitcast.1.me_ref, s32[16]{0:T(128)} %constant.10.table_ref, bf16[128,256]{1,0:T(8,128)(2,1)} %refs_0_.1, bf16[128,256]{1,0:T(8,128)(2,1)} %copy-done.9, ...), custom_call_target="tpu_custom_call" | custom-call | tf_op jit(solution)/shard_map/pallas_call | solution.py:118
  36.3 46.7 %all_to_all.5 = bf16[256,8,256]{2,1,0:T(8,128)(2,1)S(1)} all-to-all(bf16[256,8,256]{2,1,0:T(8,128)(2,1)} %bitcast.10), channel_id=1, replica_groups=mesh['ctx'=16,'tp'=16] {'ctx','tp'}, dimensions={0} | all-to-all | bytes 2097152 | tf_op jit(solution)/shard_map/all_to_all | solution.py:185
  83.0 0.1 bitcast_reduce_fusion
  83.2 0.6 copy.9
  (14 shorter events, 0.0 us)
Async XLA Ops:
  0.0 10.1 %collective-permute-start.3 = (bf16[128,256]{1,0:T(8,128)(2,1)}, bf16[128,256]{1,0:T(8,128)(2,1)S(1)}, u32[]{:S(2)}, u32[]{:S(2)}) collective-permute-start(bf16[128,256]{1,0:T(8,128)(2,1)} %refs_0_.1), channel_id=1, source_target_pairs={{0,2},{1,3},{2,4},{3,5},{4,6},{5,7},{6,8},{7,9},{8,10},{9,11},{10,... | collective-permute-start | bytes 196616 | tf_op jit(solution)/shard_map/ppermute | solution.py:155
  2.5 7.6 %collective-permute-start.2 = (bf16[128,256]{1,0:T(8,128)(2,1)}, bf16[128,256]{1,0:T(8,128)(2,1)S(1)}, u32[]{:S(2)}, u32[]{:S(2)}) collective-permute-start(bf16[128,256]{1,0:T(8,128)(2,1)} %refs_0_.1), channel_id=1, source_target_pairs={{0,15},{1,14},{2,1},{3,0},{4,3},{5,2},{6,5},{7,4},{8,7},{9,6},{10,... | collective-permute-start | bytes 196616 | tf_op jit(solution)/shard_map/ppermute | solution.py:156
  7.4 3.4 %collective-permute-start.1 = (bf16[128,256]{1,0:T(8,128)(2,1)}, bf16[128,256]{1,0:T(8,128)(2,1)S(1)}, u32[]{:S(2)}, u32[]{:S(2)}) collective-permute-start(bf16[128,256]{1,0:T(8,128)(2,1)} %refs_0_.1), channel_id=1, source_target_pairs={{0,14},{1,15},{2,0},{3,1},{4,2},{5,3},{6,4},{7,5},{8,6},{9,7},{10,... | collective-permute-start | bytes 196616 | tf_op jit(solution)/shard_map/ppermute | solution.py:155
  8.9 3.6 %collective-permute-start = (bf16[128,256]{1,0:T(8,128)(2,1)}, bf16[128,256]{1,0:T(8,128)(2,1)S(1)}, u32[]{:S(2)}, u32[]{:S(2)}) collective-permute-start(bf16[128,256]{1,0:T(8,128)(2,1)} %refs_0_.1), channel_id=1, source_target_pairs={{0,1},{1,0},{2,3},{3,2},{4,5},{5,4},{6,7},{7,6},{8,9},{9,8},{10,11... | collective-permute-start | bytes 196616 | tf_op jit(solution)/shard_map/ppermute | solution.py:152
  9.1 5.5 %collective-permute-start.4 = (bf16[128,256]{1,0:T(8,128)(2,1)}, bf16[128,256]{1,0:T(8,128)(2,1)S(1)}, u32[]{:S(2)}, u32[]{:S(2)}) collective-permute-start(bf16[128,256]{1,0:T(8,128)(2,1)} %refs_0_.1), channel_id=1, source_target_pairs={{0,3},{1,2},{2,5},{3,4},{4,7},{5,6},{6,9},{7,8},{8,11},{9,10},{10,... | collective-permute-start | bytes 196616 | tf_op jit(solution)/shard_map/ppermute | solution.py:156
  10.1 17.2 %copy-start = (bf16[128,256]{1,0:T(8,128)(2,1)}, bf16[128,256]{1,0:T(8,128)(2,1)S(1)}, u32[]{:S(2)}) copy-start(bf16[128,256]{1,0:T(8,128)(2,1)S(1)} %collective-permute-done.3.refs_2_) | copy-start | bytes 196612
  10.1 17.2 %copy-start.1 = (bf16[128,256]{1,0:T(8,128)(2,1)}, bf16[128,256]{1,0:T(8,128)(2,1)S(1)}, u32[]{:S(2)}) copy-start(bf16[128,256]{1,0:T(8,128)(2,1)S(1)} %collective-permute-done.2.refs_5_) | copy-start | bytes 196612
  10.8 16.5 %copy-start.2 = (bf16[128,256]{1,0:T(8,128)(2,1)}, bf16[128,256]{1,0:T(8,128)(2,1)S(1)}, u32[]{:S(2)}) copy-start(bf16[128,256]{1,0:T(8,128)(2,1)S(1)} %collective-permute-done.1.refs_4_) | copy-start | bytes 196612
  12.5 14.9 %copy-start.9 = (bf16[128,256]{1,0:T(8,128)(2,1)}, bf16[128,256]{1,0:T(8,128)(2,1)S(1)}, u32[]{:S(2)}) copy-start(bf16[128,256]{1,0:T(8,128)(2,1)S(1)} %collective-permute-done.refs_1_) | copy-start | bytes 196612
  14.6 12.7 %copy-start.3 = (bf16[128,256]{1,0:T(8,128)(2,1)}, bf16[128,256]{1,0:T(8,128)(2,1)S(1)}, u32[]{:S(2)}) copy-start(bf16[128,256]{1,0:T(8,128)(2,1)S(1)} %collective-permute-done.4.refs_3_) | copy-start | bytes 196612
  14.6 7.5 %collective-permute-start.6 = (bf16[2,128,256]{2,1,0:T(8,128)(2,1)S(1)}, bf16[2,128,256]{2,1,0:T(8,128)(2,1)S(1)}, u32[]{:S(2)}, u32[]{:S(2)}) collective-permute-start(bf16[2,128,256]{2,1,0:T(8,128)(2,1)S(1)} %pad_maximum_fusion), channel_id=1, source_target_pairs={{0,4},{1,5},{2,6},{3,7},{4,8},{5,9},{6,10},{7,11},{8,12},{9,13},{1... | collective-permute-start | bytes 393224 | tf_op jit(solution)/shard_map/ppermute | solution.py:169
  14.7 7.5 %collective-permute-start.5 = (bf16[2,128,256]{2,1,0:T(8,128)(2,1)S(1)}, bf16[2,128,256]{2,1,0:T(8,128)(2,1)S(1)}, u32[]{:S(2)}, u32[]{:S(2)}) collective-permute-start(bf16[2,128,256]{2,1,0:T(8,128)(2,1)S(1)} %pad_maximum_fusion), channel_id=1, source_target_pairs={{0,2},{1,3},{2,4},{3,5},{4,6},{5,7},{6,8},{7,9},{8,10},{9,11},{10,... | collective-permute-start | bytes 393224 | tf_op jit(solution)/shard_map/ppermute | solution.py:169
  15.0 7.2 %collective-permute-start.8 = (bf16[2,128,256]{2,1,0:T(8,128)(2,1)S(1)}, bf16[2,128,256]{2,1,0:T(8,128)(2,1)S(1)}, u32[]{:S(2)}, u32[]{:S(2)}) collective-permute-start(bf16[2,128,256]{2,1,0:T(8,128)(2,1)S(1)} %pad_maximum_fusion.1), channel_id=1, source_target_pairs={{0,12},{1,13},{2,14},{3,15},{4,0},{5,1},{6,2},{7,3},{8,4},{9,5},{1... | collective-permute-start | bytes 393224 | tf_op jit(solution)/shard_map/ppermute | solution.py:169
  18.4 5.8 %collective-permute-start.7 = (bf16[2,128,256]{2,1,0:T(8,128)(2,1)S(1)}, bf16[2,128,256]{2,1,0:T(8,128)(2,1)S(1)}, u32[]{:S(2)}, u32[]{:S(2)}) collective-permute-start(bf16[2,128,256]{2,1,0:T(8,128)(2,1)S(1)} %pad_maximum_fusion.1), channel_id=1, source_target_pairs={{0,14},{1,15},{2,0},{3,1},{4,2},{5,3},{6,4},{7,5},{8,6},{9,7},{10,... | collective-permute-start | bytes 393224 | tf_op jit(solution)/shard_map/ppermute | solution.py:169
  22.2 5.2 %copy-start.4 = (bf16[2,128,256]{2,1,0:T(8,128)(2,1)}, bf16[2,128,256]{2,1,0:T(8,128)(2,1)S(1)}, u32[]{:S(2)}) copy-start(bf16[2,128,256]{2,1,0:T(8,128)(2,1)S(1)} %collective-permute-done.6.refs_7_) | copy-start | bytes 393220
  22.2 5.1 %collective-permute-start.9 = (bf16[2,128,256]{2,1,0:T(8,128)(2,1)S(1)}, bf16[2,128,256]{2,1,0:T(8,128)(2,1)S(1)}, u32[]{:S(2)}, u32[]{:S(2)}) collective-permute-start(bf16[2,128,256]{2,1,0:T(8,128)(2,1)S(1)} %collective-permute-done.6.refs_7_), channel_id=1, source_target_pairs={{0,2},{1,3},{2,4},{3,5},{4,6},{5,7},{6,8},{7,9},{8,10},{9,11},{10,... | collective-permute-start | bytes 393224 | tf_op jit(solution)/shard_map/ppermute | solution.py:173
  22.2 5.2 %copy-start.5 = (bf16[2,128,256]{2,1,0:T(8,128)(2,1)}, bf16[2,128,256]{2,1,0:T(8,128)(2,1)S(1)}, u32[]{:S(2)}) copy-start(bf16[2,128,256]{2,1,0:T(8,128)(2,1)S(1)} %collective-permute-done.5.refs_6_) | copy-start | bytes 393220
  22.2 5.2 %copy-start.6 = (bf16[2,128,256]{2,1,0:T(8,128)(2,1)}, bf16[2,128,256]{2,1,0:T(8,128)(2,1)S(1)}, u32[]{:S(2)}) copy-start(bf16[2,128,256]{2,1,0:T(8,128)(2,1)S(1)} %collective-permute-done.8.refs_9_) | copy-start | bytes 393220
  24.2 3.2 %copy-start.7 = (bf16[2,128,256]{2,1,0:T(8,128)(2,1)}, bf16[2,128,256]{2,1,0:T(8,128)(2,1)S(1)}, u32[]{:S(2)}) copy-start(bf16[2,128,256]{2,1,0:T(8,128)(2,1)S(1)} %collective-permute-done.7.refs_8_) | copy-start | bytes 393220
  27.3 0.6 copy-start.8

commit v14 on v12

--- a/solution.py
+++ b/solution.py
@@ -92,14 +92,14 @@
     for k, down_copy in enumerate(down_copies):
         down_copy.wait()
         lax.fori_loop(k * step, (k + 1) * step, dn_body, 0, unroll=True)
-    groups, dests, share, group_width = out_ref.shape
+    dests, groups, share, group_width = out_ref.shape
     for h in range(per_src):
         acco_s[me_ref[0] * per_src + h] += piece(0, slice(h * tile, (h + 1) * tile)).astype(jnp.float32)
     per_group = group_width // tile
     for o in range(acco_s.shape[0]):
         block = acco_s[o].reshape(dests, share, tile).astype(out_ref.dtype)
         group, half = divmod(o, per_group)
-        out_ref[group, :, :, half * tile:(half + 1) * tile] = block
+        out_ref[:, group, :, half * tile:(half + 1) * tile] = block
 
 
 def ffn(counts, gu_blocks, down_blocks, me, table, pieces, gate_tiles, up_tiles, down_tiles,
@@ -117,7 +117,7 @@
     slots = gate_tiles.shape[0]
     return pl.pallas_call(
         functools.partial(ffn_kernel, tuple(layout)),
-        out_shape=jax.ShapeDtypeStruct((groups, rows // share, share, in_blocks * tile // groups),
+        out_shape=jax.ShapeDtypeStruct((rows // share, groups, share, in_blocks * tile // groups),
                                        jnp.bfloat16),
         in_specs=[smem] * 5 + [vmem] * len(pieces) + [hbm] * 3,
         out_specs=vmem,
@@ -179,10 +179,10 @@
                    down_tiles, hid_blocks, ctx_count, share)
     incoming = lax.all_to_all(
         outgoing.reshape(ctx_count * tp_count, share, feat_width // ctx_count),
-        ("ctx", "tp"), 0, 0, tiled=True,
+        ("tp", "ctx"), 0, 0, tiled=True,
     )
     total = jnp.sum(
-        incoming.reshape(ctx_count, tp_count, share, -1).astype(jnp.float32), axis=1
+        incoming.reshape(tp_count, ctx_count, share, -1).astype(jnp.float32), axis=0
     )
     return jnp.transpose(total, (1, 0, 2)).astype(jnp.bfloat16)
 

time: 80.7 us -> 81.7 us (1.012)
  blocking collectives: 47.8 us -> 48.7 us
    all_to_all x1, blocking collectives: 47.8 us -> 48.7 us  [per_device(): lax.all_to_all(outgoing.reshape(ctx_count * tp_count, share, feat_width /...]
where the time goes in v14:
time: 81.7 us; the launch traced here: 81.5 us
  blocking collectives  48.7 us (60%)
  starting transfers between devices  15.4 us (19%)
  Pallas kernels  8.4 us (10%)
  waiting for transfers between devices  7.39 us (9%)
  local copies, waits for them, and re-layouts  1.3 us (2%)
    all_to_all x1, blocking collectives, per_device(): lax.all_to_all(outgoing.reshape(ctx_count * tp_count, share, feat_width /...  48.7 us
    pallas_call x1, Pallas kernels, ffn(): pl.pallas_call(functools.partial(ffn_kernel, tuple(layout)), out_shape=ja...  8.4 us
    ppermute x2, starting transfers between devices, per_device(): other = lax.ppermute(tokens, 'tp', ring_pairs(z_count, step, 1))  5.88 us
    ppermute x4, starting transfers between devices, per_device(): pair = lax.ppermute(near[step], 'tp', ring_pairs(z_count, step * hops))  5.87 us
    ppermute x4, waiting for transfers between devices, per_device(): pair = lax.ppermute(near[step], 'tp', ring_pairs(z_count, step * hops))  3.47 us
    ppermute x2, starting transfers between devices, per_device(): same = lax.ppermute(tokens, 'tp', ring_pairs(z_count, step))  3.01 us
    ppermute x1, waiting for transfers between devices, per_device(): arrays = [tokens, lax.ppermute(tokens, 'tp', swap)]  2.97 us
  transfers between devices with their start and end apart: 10, of which 5 were waited for; matrix products, arithmetic and copies ran while one was open for 0% of the time, Pallas kernels for 0%

profile of v14, /device:TPU:1, one launch (start us, length us, event | category | flops | bytes accessed | tf_op | source)
XLA Modules:
  0.0 81.5 jit_solution(4778034980613606963)
XLA Ops:
  0.0 3.5 %collective-permute-start.2 = (bf16[128,256]{1,0:T(8,128)(2,1)}, bf16[128,256]{1,0:T(8,128)(2,1)S(1)}, u32[]{:S(2)}, u32[]{:S(2)}) collective-permute-start(bf16[128,256]{1,0:T(8,128)(2,1)} %refs_0_.1), channel_id=1, source_target_pairs={{0,3},{1,2},{2,5},{3,4},{4,7},{5,6},{6,9},{7,8},{8,11},{9,10},{10,... | collective-permute-start | bytes 196616 | tf_op jit(solution)/shard_map/ppermute | solution.py:157
  3.5 1.6 %collective-permute-start.1 = (bf16[128,256]{1,0:T(8,128)(2,1)}, bf16[128,256]{1,0:T(8,128)(2,1)S(1)}, u32[]{:S(2)}, u32[]{:S(2)}) collective-permute-start(bf16[128,256]{1,0:T(8,128)(2,1)} %refs_0_.1), channel_id=1, source_target_pairs={{0,2},{1,3},{2,4},{3,5},{4,6},{5,7},{6,8},{7,9},{8,10},{9,11},{10,... | collective-permute-start | bytes 196616 | tf_op jit(solution)/shard_map/ppermute | solution.py:156
  5.1 1.4 %collective-permute-start.3 = (bf16[128,256]{1,0:T(8,128)(2,1)}, bf16[128,256]{1,0:T(8,128)(2,1)S(1)}, u32[]{:S(2)}, u32[]{:S(2)}) collective-permute-start(bf16[128,256]{1,0:T(8,128)(2,1)} %refs_0_.1), channel_id=1, source_target_pairs={{0,14},{1,15},{2,0},{3,1},{4,2},{5,3},{6,4},{7,5},{8,6},{9,7},{10,... | collective-permute-start | bytes 196616 | tf_op jit(solution)/shard_map/ppermute | solution.py:156
  6.5 2.4 %collective-permute-start.4 = (bf16[128,256]{1,0:T(8,128)(2,1)}, bf16[128,256]{1,0:T(8,128)(2,1)S(1)}, u32[]{:S(2)}, u32[]{:S(2)}) collective-permute-start(bf16[128,256]{1,0:T(8,128)(2,1)} %refs_0_.1), channel_id=1, source_target_pairs={{0,15},{1,14},{2,1},{3,0},{4,3},{5,2},{6,5},{7,4},{8,7},{9,6},{10,... | collective-permute-start | bytes 196616 | tf_op jit(solution)/shard_map/ppermute | solution.py:157
  8.9 0.4 collective-permute-done.2.refs_3_
  9.3 0.6 collective-permute-done.1.refs_2_
  9.9 1.2 %collective-permute-start.6 = (bf16[2,128,256]{2,1,0:T(8,128)(2,1)S(1)}, bf16[2,128,256]{2,1,0:T(8,128)(2,1)S(1)}, u32[]{:S(2)}, u32[]{:S(2)}) collective-permute-start(bf16[2,128,256]{2,1,0:T(8,128)(2,1)S(1)} %pad_maximum_fusion), channel_id=1, source_target_pairs={{0,4},{1,5},{2,6},{3,7},{4,8},{5,9},{6,10},{7,11},{8,12},{9,13},{1... | collective-permute-start | bytes 393224 | tf_op jit(solution)/shard_map/ppermute | solution.py:164
  11.1 1.7 %collective-permute-start.5 = (bf16[2,128,256]{2,1,0:T(8,128)(2,1)S(1)}, bf16[2,128,256]{2,1,0:T(8,128)(2,1)S(1)}, u32[]{:S(2)}, u32[]{:S(2)}) collective-permute-start(bf16[2,128,256]{2,1,0:T(8,128)(2,1)S(1)} %pad_maximum_fusion), channel_id=1, source_target_pairs={{0,2},{1,3},{2,4},{3,5},{4,6},{5,7},{6,8},{7,9},{8,10},{9,11},{10,... | collective-permute-start | bytes 393224 | tf_op jit(solution)/shard_map/ppermute | solution.py:164
  12.7 0.0 collective-permute-done.3.refs_4_
  12.7 0.0 collective-permute-done.4.refs_5_
  12.8 1.6 %collective-permute-start.8 = (bf16[2,128,256]{2,1,0:T(8,128)(2,1)S(1)}, bf16[2,128,256]{2,1,0:T(8,128)(2,1)S(1)}, u32[]{:S(2)}, u32[]{:S(2)}) collective-permute-start(bf16[2,128,256]{2,1,0:T(8,128)(2,1)S(1)} %pad_maximum_fusion.1), channel_id=1, source_target_pairs={{0,12},{1,13},{2,14},{3,15},{4,0},{5,1},{6,2},{7,3},{8,4},{9,5},{1... | collective-permute-start | bytes 393224 | tf_op jit(solution)/shard_map/ppermute | solution.py:164
  14.4 1.4 %collective-permute-start.7 = (bf16[2,128,256]{2,1,0:T(8,128)(2,1)S(1)}, bf16[2,128,256]{2,1,0:T(8,128)(2,1)S(1)}, u32[]{:S(2)}, u32[]{:S(2)}) collective-permute-start(bf16[2,128,256]{2,1,0:T(8,128)(2,1)S(1)} %pad_maximum_fusion.1), channel_id=1, source_target_pairs={{0,14},{1,15},{2,0},{3,1},{4,2},{5,3},{6,4},{7,5},{8,6},{9,7},{10,... | collective-permute-start | bytes 393224 | tf_op jit(solution)/shard_map/ppermute | solution.py:164
  15.8 0.8 %collective-permute-done.6.refs_7_ = bf16[2,128,256]{2,1,0:T(8,128)(2,1)S(1)} collective-permute-done((bf16[2,128,256]{2,1,0:T(8,128)(2,1)S(1)}, bf16[2,128,256]{2,1,0:T(8,128)(2,1)S(1)}, u32[]{:S(2)}, u32[]{:S(2)}) %collective-permute-start.6) | collective-permute-done | bytes 131104 | tf_op jit(solution)/shard_map/ppermute | solution.py:164
  16.6 0.0 collective-permute-start.9
  16.6 0.7 collective-permute-start
  17.3 3.0 %collective-permute-done.refs_1_ = bf16[128,256]{1,0:T(8,128)(2,1)S(1)} collective-permute-done((bf16[128,256]{1,0:T(8,128)(2,1)}, bf16[128,256]{1,0:T(8,128)(2,1)S(1)}, u32[]{:S(2)}, u32[]{:S(2)}) %collective-permute-start) | collective-permute-done | bytes 65568 | tf_op jit(solution)/shard_map/ppermute | solution.py:152
  20.2 0.0 collective-permute-done.5.refs_6_
  20.2 0.0 collective-permute-done.8.refs_9_
  20.3 0.0 copy-start.6
  20.3 2.6 %collective-permute-done.7.refs_8_ = bf16[2,128,256]{2,1,0:T(8,128)(2,1)S(1)} collective-permute-done((bf16[2,128,256]{2,1,0:T(8,128)(2,1)S(1)}, bf16[2,128,256]{2,1,0:T(8,128)(2,1)S(1)}, u32[]{:S(2)}, u32[]{:S(2)}) %collective-permute-start.7) | collective-permute-done | bytes 131104 | tf_op jit(solution)/shard_map/ppermute | solution.py:164
  22.9 0.0 collective-permute-done.9.refs_10_
  22.9 0.0 copy-done.1
  22.9 0.0 copy-done.2
  22.9 0.0 copy-done.3
  22.9 0.0 copy-done.4
  22.9 0.0 copy-done.9
  23.0 0.6 copy-done.7
  23.5 0.1 copy-done.8
  23.6 8.4 %shard_map.82 = bf16[16,16,8,256]{3,2,1,0:T(8,128)(2,1)} custom-call(s32[2]{0:T(128)} %bitcast.16, s32[2,64]{1,0:T(2,128)} %gu_ref.1, s32[2,64]{1,0:T(2,128)} %dn_ref.1, s32[1]{0:T(128)} %bitcast.1.me_ref, s32[16]{0:T(128)} %constant.10.table_ref, bf16[128,256]{1,0:T(8,128)(2,1)} %refs_0_.1, bf16[128,256]{1,0:T(8,128)(2,1)} %copy-done.9, ...), custom_call_target="tpu_custom_call" | custom-call | tf_op jit(solution)/shard_map/pallas_call | solution.py:118
  32.0 48.7 %all_to_all.5 = bf16[256,8,256]{2,1,0:T(8,128)(2,1)S(1)} all-to-all(bf16[256,8,256]{2,1,0:T(8,128)(2,1)} %bitcast.9), channel_id=1, replica_groups=mesh['ctx'=16,'tp'=16] {'tp','ctx'}, dimensions={0} | all-to-all | bytes 2097152 | tf_op jit(solution)/shard_map/all_to_all | solution.py:180
  80.7 0.1 reduce
  80.9 0.6 copy.9
  (14 shorter events, 0.1 us)
Async XLA Ops:
  0.0 9.3 %collective-permute-start.2 = (bf16[128,256]{1,0:T(8,128)(2,1)}, bf16[128,256]{1,0:T(8,128)(2,1)S(1)}, u32[]{:S(2)}, u32[]{:S(2)}) collective-permute-start(bf16[128,256]{1,0:T(8,128)(2,1)} %refs_0_.1), channel_id=1, source_target_pairs={{0,3},{1,2},{2,5},{3,4},{4,7},{5,6},{6,9},{7,8},{8,11},{9,10},{10,... | collective-permute-start | bytes 196616 | tf_op jit(solution)/shard_map/ppermute | solution.py:157
  3.5 6.4 %collective-permute-start.1 = (bf16[128,256]{1,0:T(8,128)(2,1)}, bf16[128,256]{1,0:T(8,128)(2,1)S(1)}, u32[]{:S(2)}, u32[]{:S(2)}) collective-permute-start(bf16[128,256]{1,0:T(8,128)(2,1)} %refs_0_.1), channel_id=1, source_target_pairs={{0,2},{1,3},{2,4},{3,5},{4,6},{5,7},{6,8},{7,9},{8,10},{9,11},{10,... | collective-permute-start | bytes 196616 | tf_op jit(solution)/shard_map/ppermute | solution.py:156
  5.1 7.6 %collective-permute-start.3 = (bf16[128,256]{1,0:T(8,128)(2,1)}, bf16[128,256]{1,0:T(8,128)(2,1)S(1)}, u32[]{:S(2)}, u32[]{:S(2)}) collective-permute-start(bf16[128,256]{1,0:T(8,128)(2,1)} %refs_0_.1), channel_id=1, source_target_pairs={{0,14},{1,15},{2,0},{3,1},{4,2},{5,3},{6,4},{7,5},{8,6},{9,7},{10,... | collective-permute-start | bytes 196616 | tf_op jit(solution)/shard_map/ppermute | solution.py:156
  6.5 6.3 %collective-permute-start.4 = (bf16[128,256]{1,0:T(8,128)(2,1)}, bf16[128,256]{1,0:T(8,128)(2,1)S(1)}, u32[]{:S(2)}, u32[]{:S(2)}) collective-permute-start(bf16[128,256]{1,0:T(8,128)(2,1)} %refs_0_.1), channel_id=1, source_target_pairs={{0,15},{1,14},{2,1},{3,0},{4,3},{5,2},{6,5},{7,4},{8,7},{9,6},{10,... | collective-permute-start | bytes 196616 | tf_op jit(solution)/shard_map/ppermute | solution.py:157
  9.3 13.6 %copy-start = (bf16[128,256]{1,0:T(8,128)(2,1)}, bf16[128,256]{1,0:T(8,128)(2,1)S(1)}, u32[]{:S(2)}) copy-start(bf16[128,256]{1,0:T(8,128)(2,1)S(1)} %collective-permute-done.2.refs_3_) | copy-start | bytes 196612
  9.8 13.1 %copy-start.1 = (bf16[128,256]{1,0:T(8,128)(2,1)}, bf16[128,256]{1,0:T(8,128)(2,1)S(1)}, u32[]{:S(2)}) copy-start(bf16[128,256]{1,0:T(8,128)(2,1)S(1)} %collective-permute-done.1.refs_2_) | copy-start | bytes 196612
  9.9 6.8 %collective-permute-start.6 = (bf16[2,128,256]{2,1,0:T(8,128)(2,1)S(1)}, bf16[2,128,256]{2,1,0:T(8,128)(2,1)S(1)}, u32[]{:S(2)}, u32[]{:S(2)}) collective-permute-start(bf16[2,128,256]{2,1,0:T(8,128)(2,1)S(1)} %pad_maximum_fusion), channel_id=1, source_target_pairs={{0,4},{1,5},{2,6},{3,7},{4,8},{5,9},{6,10},{7,11},{8,12},{9,13},{1... | collective-permute-start | bytes 393224 | tf_op jit(solution)/shard_map/ppermute | solution.py:164
  11.1 9.2 %collective-permute-start.5 = (bf16[2,128,256]{2,1,0:T(8,128)(2,1)S(1)}, bf16[2,128,256]{2,1,0:T(8,128)(2,1)S(1)}, u32[]{:S(2)}, u32[]{:S(2)}) collective-permute-start(bf16[2,128,256]{2,1,0:T(8,128)(2,1)S(1)} %pad_maximum_fusion), channel_id=1, source_target_pairs={{0,2},{1,3},{2,4},{3,5},{4,6},{5,7},{6,8},{7,9},{8,10},{9,11},{10,... | collective-permute-start | bytes 393224 | tf_op jit(solution)/shard_map/ppermute | solution.py:164
  12.7 10.2 %copy-start.2 = (bf16[128,256]{1,0:T(8,128)(2,1)}, bf16[128,256]{1,0:T(8,128)(2,1)S(1)}, u32[]{:S(2)}) copy-start(bf16[128,256]{1,0:T(8,128)(2,1)S(1)} %collective-permute-done.3.refs_4_) | copy-start | bytes 196612
  12.8 10.2 %copy-start.3 = (bf16[128,256]{1,0:T(8,128)(2,1)}, bf16[128,256]{1,0:T(8,128)(2,1)S(1)}, u32[]{:S(2)}) copy-start(bf16[128,256]{1,0:T(8,128)(2,1)S(1)} %collective-permute-done.4.refs_5_) | copy-start | bytes 196612
  12.8 7.5 %collective-permute-start.8 = (bf16[2,128,256]{2,1,0:T(8,128)(2,1)S(1)}, bf16[2,128,256]{2,1,0:T(8,128)(2,1)S(1)}, u32[]{:S(2)}, u32[]{:S(2)}) collective-permute-start(bf16[2,128,256]{2,1,0:T(8,128)(2,1)S(1)} %pad_maximum_fusion.1), channel_id=1, source_target_pairs={{0,12},{1,13},{2,14},{3,15},{4,0},{5,1},{6,2},{7,3},{8,4},{9,5},{1... | collective-permute-start | bytes 393224 | tf_op jit(solution)/shard_map/ppermute | solution.py:164
  14.4 8.5 %collective-permute-start.7 = (bf16[2,128,256]{2,1,0:T(8,128)(2,1)S(1)}, bf16[2,128,256]{2,1,0:T(8,128)(2,1)S(1)}, u32[]{:S(2)}, u32[]{:S(2)}) collective-permute-start(bf16[2,128,256]{2,1,0:T(8,128)(2,1)S(1)} %pad_maximum_fusion.1), channel_id=1, source_target_pairs={{0,14},{1,15},{2,0},{3,1},{4,2},{5,3},{6,4},{7,5},{8,6},{9,7},{10,... | collective-permute-start | bytes 393224 | tf_op jit(solution)/shard_map/ppermute | solution.py:164
  16.6 6.3 %copy-start.4 = (bf16[2,128,256]{2,1,0:T(8,128)(2,1)}, bf16[2,128,256]{2,1,0:T(8,128)(2,1)S(1)}, u32[]{:S(2)}) copy-start(bf16[2,128,256]{2,1,0:T(8,128)(2,1)S(1)} %collective-permute-done.6.refs_7_) | copy-start | bytes 393220
  16.6 6.3 %collective-permute-start.9 = (bf16[2,128,256]{2,1,0:T(8,128)(2,1)S(1)}, bf16[2,128,256]{2,1,0:T(8,128)(2,1)S(1)}, u32[]{:S(2)}, u32[]{:S(2)}) collective-permute-start(bf16[2,128,256]{2,1,0:T(8,128)(2,1)S(1)} %collective-permute-done.6.refs_7_), channel_id=1, source_target_pairs={{0,2},{1,3},{2,4},{3,5},{4,6},{5,7},{6,8},{7,9},{8,10},{9,11},{10,... | collective-permute-start | bytes 393224 | tf_op jit(solution)/shard_map/ppermute | solution.py:168
  16.6 3.6 %collective-permute-start = (bf16[128,256]{1,0:T(8,128)(2,1)}, bf16[128,256]{1,0:T(8,128)(2,1)S(1)}, u32[]{:S(2)}, u32[]{:S(2)}) collective-permute-start(bf16[128,256]{1,0:T(8,128)(2,1)} %refs_0_.1), channel_id=1, source_target_pairs={{0,1},{1,0},{2,3},{3,2},{4,5},{5,4},{6,7},{7,6},{8,9},{9,8},{10,11... | collective-permute-start | bytes 196616 | tf_op jit(solution)/shard_map/ppermute | solution.py:152
  20.2 2.7 %copy-start.9 = (bf16[128,256]{1,0:T(8,128)(2,1)}, bf16[128,256]{1,0:T(8,128)(2,1)S(1)}, u32[]{:S(2)}) copy-start(bf16[128,256]{1,0:T(8,128)(2,1)S(1)} %collective-permute-done.refs_1_) | copy-start | bytes 196612
  20.2 2.7 %copy-start.5 = (bf16[2,128,256]{2,1,0:T(8,128)(2,1)}, bf16[2,128,256]{2,1,0:T(8,128)(2,1)S(1)}, u32[]{:S(2)}) copy-start(bf16[2,128,256]{2,1,0:T(8,128)(2,1)S(1)} %collective-permute-done.5.refs_6_) | copy-start | bytes 393220
  20.3 2.7 %copy-start.6 = (bf16[2,128,256]{2,1,0:T(8,128)(2,1)}, bf16[2,128,256]{2,1,0:T(8,128)(2,1)S(1)}, u32[]{:S(2)}) copy-start(bf16[2,128,256]{2,1,0:T(8,128)(2,1)S(1)} %collective-permute-done.8.refs_9_) | copy-start | bytes 393220
  22.9 0.7 copy-start.7
  22.9 0.7 copy-start.8

commit v15 on v12

--- a/solution.py
+++ b/solution.py
@@ -148,22 +148,26 @@
     me = lax.axis_index("tp")
     my_z = me // Y_LO
     my_y = me % Y_LO
-    swap = [(i, i ^ 1) for i in range(tp_count)]
-    arrays = [tokens, lax.ppermute(tokens, "tp", swap)]
-    origins = [(0, 0), (0, 1)]
+    arrays = [tokens]
+    origins = [(0, 0)]
     near = {}
     for step in (1, -1):
         same = lax.ppermute(tokens, "tp", ring_pairs(z_count, step))
         other = lax.ppermute(tokens, "tp", ring_pairs(z_count, step, 1))
         arrays += [same, other]
         origins += [(-step % z_count, 0), (-step % z_count, 1)]
-        near[step] = jnp.stack([same, other])
+        near[step] = (same, other)
     far = {}
     for step in (1, -1):
         for hops in (1, 2):
-            pair = lax.ppermute(near[step], "tp", ring_pairs(z_count, step * hops))
+            carried = list(near[step])
+            if step == 1 and hops == 1:
+                carried.append(near[-1][1])
+            pair = lax.ppermute(jnp.stack(carried), "tp", ring_pairs(z_count, step * hops))
             arrays.append(pair)
             origins += [(-step * (hops + 1) % z_count, 0), (-step * (hops + 1) % z_count, 1)]
+            if step == 1 and hops == 1:
+                origins.append((0, 1))
             far[step, hops] = pair
     last = lax.ppermute(far[1, 2], "tp", ring_pairs(z_count, 1))
     arrays.append(last)

time: 80.7 us -> 80.6 us (level)
  blocking collectives: 47.8 us -> 46.3 us
  waiting for transfers between devices: 7.39 us -> 8.87 us
    ppermute x1, waiting for transfers between devices: 0.01 us -> 1.9 us  [per_device(): last = lax.ppermute(far[1, 2], 'tp', ring_pairs(z_count, 1))]
    all_to_all x1, blocking collectives: 47.8 us -> 46.3 us  [per_device(): lax.all_to_all(outgoing.reshape(ctx_count * tp_count, share, feat_width /...]
    ppermute x5 -> x4, starting transfers between devices: 6.53 us -> 6 us  [per_device(): lax.ppermute(jnp.stack(carried), 'tp', ring_pairs(z_count, step * hops))]
    ppermute x5 -> x4, waiting for transfers between devices: 6.44 us -> 5.97 us  [per_device(): lax.ppermute(jnp.stack(carried), 'tp', ring_pairs(z_count, step * hops))]
  transfers between devices with their start and end apart: 10 -> 9, of which waited for: 5 -> 7; matrix products, arithmetic and copies ran while one was open for 0% -> 0% of each run, Pallas kernels for 0% -> 0%
where the time goes in v15:
time: 80.6 us; the launch traced here: 80.5 us
  blocking collectives  46.3 us (57%)
  starting transfers between devices  15.5 us (19%)
  waiting for transfers between devices  8.87 us (11%)
  Pallas kernels  8.31 us (10%)
  local copies, waits for them, and re-layouts  1.26 us (2%)
    all_to_all x1, blocking collectives, per_device(): lax.all_to_all(outgoing.reshape(ctx_count * tp_count, share, feat_width /...  46.3 us
    pallas_call x1, Pallas kernels, ffn(): pl.pallas_call(functools.partial(ffn_kernel, tuple(layout)), out_shape=ja...  8.31 us
    ppermute x4, starting transfers between devices, per_device(): lax.ppermute(jnp.stack(carried), 'tp', ring_pairs(z_count, step * hops))  6 us
    ppermute x4, waiting for transfers between devices, per_device(): lax.ppermute(jnp.stack(carried), 'tp', ring_pairs(z_count, step * hops))  5.97 us
    ppermute x2, starting transfers between devices, per_device(): other = lax.ppermute(tokens, 'tp', ring_pairs(z_count, step, 1))  5.88 us
    ppermute x2, starting transfers between devices, per_device(): same = lax.ppermute(tokens, 'tp', ring_pairs(z_count, step))  3.01 us
    ppermute x1, waiting for transfers between devices, per_device(): last = lax.ppermute(far[1, 2], 'tp', ring_pairs(z_count, 1))  1.9 us
  transfers between devices with their start and end apart: 9, of which 7 were waited for; matrix products, arithmetic and copies ran while one was open for 0% of the time, Pallas kernels for 0%

profile of v15, /device:TPU:1, one launch (start us, length us, event | category | flops | bytes accessed | tf_op | source)
XLA Modules:
  0.0 80.5 jit_solution(1383875070941575523)
XLA Ops:
  0.0 3.5 %collective-permute-start.1 = (bf16[128,256]{1,0:T(8,128)(2,1)}, bf16[128,256]{1,0:T(8,128)(2,1)S(1)}, u32[]{:S(2)}, u32[]{:S(2)}) collective-permute-start(bf16[128,256]{1,0:T(8,128)(2,1)} %refs_0_.1), channel_id=1, source_target_pairs={{0,3},{1,2},{2,5},{3,4},{4,7},{5,6},{6,9},{7,8},{8,11},{9,10},{10,... | collective-permute-start | bytes 196616 | tf_op jit(solution)/shard_map/ppermute | solution.py:156
  3.5 1.6 %collective-permute-start = (bf16[128,256]{1,0:T(8,128)(2,1)}, bf16[128,256]{1,0:T(8,128)(2,1)S(1)}, u32[]{:S(2)}, u32[]{:S(2)}) collective-permute-start(bf16[128,256]{1,0:T(8,128)(2,1)} %refs_0_.1), channel_id=1, source_target_pairs={{0,2},{1,3},{2,4},{3,5},{4,6},{5,7},{6,8},{7,9},{8,10},{9,11},{10,... | collective-permute-start | bytes 196616 | tf_op jit(solution)/shard_map/ppermute | solution.py:155
  5.1 1.4 %collective-permute-start.2 = (bf16[128,256]{1,0:T(8,128)(2,1)}, bf16[128,256]{1,0:T(8,128)(2,1)S(1)}, u32[]{:S(2)}, u32[]{:S(2)}) collective-permute-start(bf16[128,256]{1,0:T(8,128)(2,1)} %refs_0_.1), channel_id=1, source_target_pairs={{0,14},{1,15},{2,0},{3,1},{4,2},{5,3},{6,4},{7,5},{8,6},{9,7},{10,... | collective-permute-start | bytes 196616 | tf_op jit(solution)/shard_map/ppermute | solution.py:155
  6.5 2.4 %collective-permute-start.3 = (bf16[128,256]{1,0:T(8,128)(2,1)}, bf16[128,256]{1,0:T(8,128)(2,1)S(1)}, u32[]{:S(2)}, u32[]{:S(2)}) collective-permute-start(bf16[128,256]{1,0:T(8,128)(2,1)} %refs_0_.1), channel_id=1, source_target_pairs={{0,15},{1,14},{2,1},{3,0},{4,3},{5,2},{6,5},{7,4},{8,7},{9,6},{10,... | collective-permute-start | bytes 196616 | tf_op jit(solution)/shard_map/ppermute | solution.py:156
  8.9 0.4 collective-permute-done.1.refs_2_
  9.3 0.0 copy-start
  9.3 0.6 collective-permute-done.refs_1_
  9.9 1.2 %collective-permute-start.5 = (bf16[2,128,256]{2,1,0:T(8,128)(2,1)S(1)}, bf16[2,128,256]{2,1,0:T(8,128)(2,1)S(1)}, u32[]{:S(2)}, u32[]{:S(2)}) collective-permute-start(bf16[2,128,256]{2,1,0:T(8,128)(2,1)S(1)} %pad_maximum_fusion.1), channel_id=1, source_target_pairs={{0,4},{1,5},{2,6},{3,7},{4,8},{5,9},{6,10},{7,11},{8,12},{9,13},{1... | collective-permute-start | bytes 393224 | tf_op jit(solution)/shard_map/ppermute | solution.py:166
  11.1 0.1 collective-permute-done.3.refs_4_
  11.1 1.7 %collective-permute-start.4 = (bf16[3,128,256]{2,1,0:T(8,128)(2,1)S(1)}, bf16[3,128,256]{2,1,0:T(8,128)(2,1)S(1)}, u32[]{:S(2)}, u32[]{:S(2)}) collective-permute-start(bf16[3,128,256]{2,1,0:T(8,128)(2,1)S(1)} %pad_maximum_fusion), channel_id=1, source_target_pairs={{0,2},{1,3},{2,4},{3,5},{4,6},{5,7},{6,8},{7,9},{8,10},{9,11},{10,... | collective-permute-start | bytes 589832 | tf_op jit(solution)/shard_map/ppermute | solution.py:166
  12.9 0.0 collective-permute-done.2.refs_3_
  12.9 2.8 %collective-permute-start.7 = (bf16[2,128,256]{2,1,0:T(8,128)(2,1)S(1)}, bf16[2,128,256]{2,1,0:T(8,128)(2,1)S(1)}, u32[]{:S(2)}, u32[]{:S(2)}) collective-permute-start(bf16[2,128,256]{2,1,0:T(8,128)(2,1)S(1)} %pad_maximum_fusion.2), channel_id=1, source_target_pairs={{0,12},{1,13},{2,14},{3,15},{4,0},{5,1},{6,2},{7,3},{8,4},{9,5},{1... | collective-permute-start | bytes 393224 | tf_op jit(solution)/shard_map/ppermute | solution.py:166
  15.7 0.3 collective-permute-start.6
  16.0 0.6 collective-permute-done.5.refs_6_
  16.6 0.6 collective-permute-start.8
  17.2 4.3 %collective-permute-done.7.refs_8_ = bf16[2,128,256]{2,1,0:T(8,128)(2,1)S(1)} collective-permute-done((bf16[2,128,256]{2,1,0:T(8,128)(2,1)S(1)}, bf16[2,128,256]{2,1,0:T(8,128)(2,1)S(1)}, u32[]{:S(2)}, u32[]{:S(2)}) %collective-permute-start.7) | collective-permute-done | bytes 131104 | tf_op jit(solution)/shard_map/ppermute | solution.py:166
  21.5 1.0 %collective-permute-done.6.refs_7_ = bf16[2,128,256]{2,1,0:T(8,128)(2,1)S(1)} collective-permute-done((bf16[2,128,256]{2,1,0:T(8,128)(2,1)S(1)}, bf16[2,128,256]{2,1,0:T(8,128)(2,1)S(1)}, u32[]{:S(2)}, u32[]{:S(2)}) %collective-permute-start.6) | collective-permute-done | bytes 131104 | tf_op jit(solution)/shard_map/ppermute | solution.py:166
  22.5 0.0 collective-permute-done.4.refs_5_
  22.5 1.9 %collective-permute-done.8.refs_9_ = bf16[2,128,256]{2,1,0:T(8,128)(2,1)S(1)} collective-permute-done((bf16[2,128,256]{2,1,0:T(8,128)(2,1)S(1)}, bf16[2,128,256]{2,1,0:T(8,128)(2,1)S(1)}, u32[]{:S(2)}, u32[]{:S(2)}) %collective-permute-start.8) | collective-permute-done | bytes 131104 | tf_op jit(solution)/shard_map/ppermute | solution.py:172
  24.4 0.0 copy-done
  24.4 0.0 copy-done.1
  24.4 0.0 copy-done.2
  24.4 0.0 copy-done.3
  24.5 0.0 copy-done.5
  24.5 0.0 copy-done.6
  24.5 0.0 copy-done.7
  24.5 0.0 copy-done.4
  24.5 0.6 copy-done.8
  25.1 8.3 %shard_map.82 = bf16[16,16,8,256]{3,2,1,0:T(8,128)(2,1)} custom-call(s32[2]{0:T(128)} %bitcast.19, s32[2,64]{1,0:T(2,128)} %gu_ref.1, s32[2,64]{1,0:T(2,128)} %dn_ref.1, s32[1]{0:T(128)} %bitcast.1.me_ref, s32[16]{0:T(128)} %constant.10.table_ref, bf16[128,256]{1,0:T(8,128)(2,1)} %refs_0_.1, bf16[128,256]{1,0:T(8,128)(2,1)} %copy-done.1, ...), custom_call_target="tpu_custom_call" | custom-call | tf_op jit(solution)/shard_map/pallas_call | solution.py:118
  33.4 46.3 %all_to_all.5 = bf16[256,8,256]{2,1,0:T(8,128)(2,1)S(1)} all-to-all(bf16[256,8,256]{2,1,0:T(8,128)(2,1)} %bitcast.10), channel_id=1, replica_groups=mesh['ctx'=16,'tp'=16] {'ctx','tp'}, dimensions={0} | all-to-all | bytes 2097152 | tf_op jit(solution)/shard_map/all_to_all | solution.py:184
  79.7 0.1 bitcast_reduce_fusion
  79.8 0.6 copy.9
  (11 shorter events, 0.1 us)
Async XLA Ops:
  0.0 9.3 %collective-permute-start.1 = (bf16[128,256]{1,0:T(8,128)(2,1)}, bf16[128,256]{1,0:T(8,128)(2,1)S(1)}, u32[]{:S(2)}, u32[]{:S(2)}) collective-permute-start(bf16[128,256]{1,0:T(8,128)(2,1)} %refs_0_.1), channel_id=1, source_target_pairs={{0,3},{1,2},{2,5},{3,4},{4,7},{5,6},{6,9},{7,8},{8,11},{9,10},{10,... | collective-permute-start | bytes 196616 | tf_op jit(solution)/shard_map/ppermute | solution.py:156
  3.5 6.4 %collective-permute-start = (bf16[128,256]{1,0:T(8,128)(2,1)}, bf16[128,256]{1,0:T(8,128)(2,1)S(1)}, u32[]{:S(2)}, u32[]{:S(2)}) collective-permute-start(bf16[128,256]{1,0:T(8,128)(2,1)} %refs_0_.1), channel_id=1, source_target_pairs={{0,2},{1,3},{2,4},{3,5},{4,6},{5,7},{6,8},{7,9},{8,10},{9,11},{10,... | collective-permute-start | bytes 196616 | tf_op jit(solution)/shard_map/ppermute | solution.py:155
  5.1 7.7 %collective-permute-start.2 = (bf16[128,256]{1,0:T(8,128)(2,1)}, bf16[128,256]{1,0:T(8,128)(2,1)S(1)}, u32[]{:S(2)}, u32[]{:S(2)}) collective-permute-start(bf16[128,256]{1,0:T(8,128)(2,1)} %refs_0_.1), channel_id=1, source_target_pairs={{0,14},{1,15},{2,0},{3,1},{4,2},{5,3},{6,4},{7,5},{8,6},{9,7},{10,... | collective-permute-start | bytes 196616 | tf_op jit(solution)/shard_map/ppermute | solution.py:155
  6.5 4.6 %collective-permute-start.3 = (bf16[128,256]{1,0:T(8,128)(2,1)}, bf16[128,256]{1,0:T(8,128)(2,1)S(1)}, u32[]{:S(2)}, u32[]{:S(2)}) collective-permute-start(bf16[128,256]{1,0:T(8,128)(2,1)} %refs_0_.1), channel_id=1, source_target_pairs={{0,15},{1,14},{2,1},{3,0},{4,3},{5,2},{6,5},{7,4},{8,7},{9,6},{10,... | collective-permute-start | bytes 196616 | tf_op jit(solution)/shard_map/ppermute | solution.py:156
  9.3 15.2 %copy-start = (bf16[128,256]{1,0:T(8,128)(2,1)}, bf16[128,256]{1,0:T(8,128)(2,1)S(1)}, u32[]{:S(2)}) copy-start(bf16[128,256]{1,0:T(8,128)(2,1)S(1)} %collective-permute-done.1.refs_2_) | copy-start | bytes 196612
  9.8 14.6 %copy-start.1 = (bf16[128,256]{1,0:T(8,128)(2,1)}, bf16[128,256]{1,0:T(8,128)(2,1)S(1)}, u32[]{:S(2)}) copy-start(bf16[128,256]{1,0:T(8,128)(2,1)S(1)} %collective-permute-done.refs_1_) | copy-start | bytes 196612
  9.9 6.8 %collective-permute-start.5 = (bf16[2,128,256]{2,1,0:T(8,128)(2,1)S(1)}, bf16[2,128,256]{2,1,0:T(8,128)(2,1)S(1)}, u32[]{:S(2)}, u32[]{:S(2)}) collective-permute-start(bf16[2,128,256]{2,1,0:T(8,128)(2,1)S(1)} %pad_maximum_fusion.1), channel_id=1, source_target_pairs={{0,4},{1,5},{2,6},{3,7},{4,8},{5,9},{6,10},{7,11},{8,12},{9,13},{1... | collective-permute-start | bytes 393224 | tf_op jit(solution)/shard_map/ppermute | solution.py:166
  11.1 13.3 %copy-start.2 = (bf16[128,256]{1,0:T(8,128)(2,1)}, bf16[128,256]{1,0:T(8,128)(2,1)S(1)}, u32[]{:S(2)}) copy-start(bf16[128,256]{1,0:T(8,128)(2,1)S(1)} %collective-permute-done.3.refs_4_) | copy-start | bytes 196612
  11.1 11.4 %collective-permute-start.4 = (bf16[3,128,256]{2,1,0:T(8,128)(2,1)S(1)}, bf16[3,128,256]{2,1,0:T(8,128)(2,1)S(1)}, u32[]{:S(2)}, u32[]{:S(2)}) collective-permute-start(bf16[3,128,256]{2,1,0:T(8,128)(2,1)S(1)} %pad_maximum_fusion), channel_id=1, source_target_pairs={{0,2},{1,3},{2,4},{3,5},{4,6},{5,7},{6,8},{7,9},{8,10},{9,11},{10,... | collective-permute-start | bytes 589832 | tf_op jit(solution)/shard_map/ppermute | solution.py:166
  12.9 11.6 %copy-start.3 = (bf16[128,256]{1,0:T(8,128)(2,1)}, bf16[128,256]{1,0:T(8,128)(2,1)S(1)}, u32[]{:S(2)}) copy-start(bf16[128,256]{1,0:T(8,128)(2,1)S(1)} %collective-permute-done.2.refs_3_) | copy-start | bytes 196612
  12.9 8.6 %collective-permute-start.7 = (bf16[2,128,256]{2,1,0:T(8,128)(2,1)S(1)}, bf16[2,128,256]{2,1,0:T(8,128)(2,1)S(1)}, u32[]{:S(2)}, u32[]{:S(2)}) collective-permute-start(bf16[2,128,256]{2,1,0:T(8,128)(2,1)S(1)} %pad_maximum_fusion.2), channel_id=1, source_target_pairs={{0,12},{1,13},{2,14},{3,15},{4,0},{5,1},{6,2},{7,3},{8,4},{9,5},{1... | collective-permute-start | bytes 393224 | tf_op jit(solution)/shard_map/ppermute | solution.py:166
  15.7 6.8 %collective-permute-start.6 = (bf16[2,128,256]{2,1,0:T(8,128)(2,1)S(1)}, bf16[2,128,256]{2,1,0:T(8,128)(2,1)S(1)}, u32[]{:S(2)}, u32[]{:S(2)}) collective-permute-start(bf16[2,128,256]{2,1,0:T(8,128)(2,1)S(1)} %pad_maximum_fusion.2), channel_id=1, source_target_pairs={{0,14},{1,15},{2,0},{3,1},{4,2},{5,3},{6,4},{7,5},{8,6},{9,7},{10,... | collective-permute-start | bytes 393224 | tf_op jit(solution)/shard_map/ppermute | solution.py:166
  16.6 7.8 %copy-start.5 = (bf16[2,128,256]{2,1,0:T(8,128)(2,1)}, bf16[2,128,256]{2,1,0:T(8,128)(2,1)S(1)}, u32[]{:S(2)}) copy-start(bf16[2,128,256]{2,1,0:T(8,128)(2,1)S(1)} %collective-permute-done.5.refs_6_) | copy-start | bytes 393220
  16.6 7.8 %collective-permute-start.8 = (bf16[2,128,256]{2,1,0:T(8,128)(2,1)S(1)}, bf16[2,128,256]{2,1,0:T(8,128)(2,1)S(1)}, u32[]{:S(2)}, u32[]{:S(2)}) collective-permute-start(bf16[2,128,256]{2,1,0:T(8,128)(2,1)S(1)} %collective-permute-done.5.refs_6_), channel_id=1, source_target_pairs={{0,2},{1,3},{2,4},{3,5},{4,6},{5,7},{6,8},{7,9},{8,10},{9,11},{10,... | collective-permute-start | bytes 393224 | tf_op jit(solution)/shard_map/ppermute | solution.py:172
  21.5 3.0 %copy-start.6 = (bf16[2,128,256]{2,1,0:T(8,128)(2,1)}, bf16[2,128,256]{2,1,0:T(8,128)(2,1)S(1)}, u32[]{:S(2)}) copy-start(bf16[2,128,256]{2,1,0:T(8,128)(2,1)S(1)} %collective-permute-done.7.refs_8_) | copy-start | bytes 393220
  22.5 2.0 %copy-start.7 = (bf16[2,128,256]{2,1,0:T(8,128)(2,1)}, bf16[2,128,256]{2,1,0:T(8,128)(2,1)S(1)}, u32[]{:S(2)}) copy-start(bf16[2,128,256]{2,1,0:T(8,128)(2,1)S(1)} %collective-permute-done.6.refs_7_) | copy-start | bytes 393220
  22.5 2.0 %copy-start.4 = (bf16[3,128,256]{2,1,0:T(8,128)(2,1)}, bf16[3,128,256]{2,1,0:T(8,128)(2,1)S(1)}, u32[]{:S(2)}) copy-start(bf16[3,128,256]{2,1,0:T(8,128)(2,1)S(1)} %collective-permute-done.4.refs_5_) | copy-start | bytes 589828
  24.4 0.7 copy-start.8

commit v16 on v12

--- a/solution.py
+++ b/solution.py
@@ -14,15 +14,22 @@
 
 def ffn_kernel(layout, cnt_ref, gu_ref, dn_ref, me_ref, table_ref, *refs):
     n_src = len(layout)
-    n_ops = len(refs) - 12
+    n_ops = len(refs) - 14
     piece_refs = refs[:n_ops]
     (g_hbm, u_hbm, d_hbm, out_ref, normed_s, accg_s, accu_s, hid_s, acco_s, gu_v, d_v,
-     sems) = refs[n_ops:]
-    rows, width = piece_refs[0].shape
+     sems, pieces_v, piece_sems) = refs[n_ops:]
+    rows, width = pieces_v.shape[1:]
+    arrivals = []
+    for index, ref in enumerate(piece_refs):
+        first = [s for s in range(n_src) if layout[s][0] == index][0]
+        count = 1 if len(ref.shape) == 2 else ref.shape[0]
+        target = pieces_v.at[first] if len(ref.shape) == 2 else pieces_v.at[pl.ds(first, count)]
+        arrivals.append(pltpu.make_async_copy(ref, target, piece_sems.at[index]))
+    for arrival in arrivals:
+        arrival.start()
 
     def piece(s, cols):
-        ref = piece_refs[layout[s][0]]
-        return ref[:, cols] if layout[s][1] < 0 else ref[layout[s][1], :, cols]
+        return pieces_v[s, :, cols]
 
     tile = g_hbm.shape[1]
     slots = g_hbm.shape[0]
@@ -46,6 +53,8 @@
         down_copy.start()
     per_src = width // tile
     feat = n_src * width
+    for arrival in arrivals:
+        arrival.wait()
     ss = jnp.zeros((rows, 1), jnp.float32)
     for s in range(n_src):
         x = piece(s, slice(None)).astype(jnp.float32)
@@ -119,7 +128,7 @@
         functools.partial(ffn_kernel, tuple(layout)),
         out_shape=jax.ShapeDtypeStruct((groups, rows // share, share, in_blocks * tile // groups),
                                        jnp.bfloat16),
-        in_specs=[smem] * 5 + [vmem] * len(pieces) + [hbm] * 3,
+        in_specs=[smem] * 5 + [hbm] * len(pieces) + [hbm] * 3,
         out_specs=vmem,
         scratch_shapes=[
             pltpu.VMEM((in_blocks, rows, tile), jnp.bfloat16),
@@ -130,6 +139,8 @@
             pltpu.VMEM((slots, tile, 2 * tile), jnp.bfloat16),
             pltpu.VMEM((slots, tile, tile), jnp.bfloat16),
             pltpu.SemaphoreType.DMA((3, CHUNKS)),
+            pltpu.VMEM((n_src, rows, width), jnp.bfloat16),
+            pltpu.SemaphoreType.DMA((len(pieces),)),
         ],
     )(counts.reshape(-1), gu_blocks, down_blocks, me.reshape(1), table, *pieces, gate_tiles,
       up_tiles, down_tiles)

time: 80.7 us -> 82.8 us (1.026)
  Pallas kernels: 8.32 us -> 10.4 us
    pallas_call x1, Pallas kernels: 8.32 us -> 10.4 us  [ffn(): pl.pallas_call(functools.partial(ffn_kernel, tuple(layout)), out_shape=ja...]
where the time goes in v16:
time: 82.8 us; the launch traced here: 82.6 us
  blocking collectives  47.8 us (58%)
  starting transfers between devices  15.4 us (19%)
  Pallas kernels  10.4 us (13%)
  waiting for transfers between devices  7.39 us (9%)
  local copies, waits for them, and re-layouts  1.3 us (2%)
    all_to_all x1, blocking collectives, per_device(): lax.all_to_all(outgoing.reshape(ctx_count * tp_count, share, feat_width /...  47.8 us
    pallas_call x1, Pallas kernels, ffn(): pl.pallas_call(functools.partial(ffn_kernel, tuple(layout)), out_shape=ja...  10.4 us
    ppermute x2, starting transfers between devices, per_device(): other = lax.ppermute(tokens, 'tp', ring_pairs(z_count, step, 1))  5.88 us
    ppermute x4, starting transfers between devices, per_device(): pair = lax.ppermute(near[step], 'tp', ring_pairs(z_count, step * hops))  5.87 us
    ppermute x4, waiting for transfers between devices, per_device(): pair = lax.ppermute(near[step], 'tp', ring_pairs(z_count, step * hops))  3.47 us
    ppermute x2, starting transfers between devices, per_device(): same = lax.ppermute(tokens, 'tp', ring_pairs(z_count, step))  3.01 us
    ppermute x1, waiting for transfers between devices, per_device(): arrays = [tokens, lax.ppermute(tokens, 'tp', swap)]  2.97 us
  transfers between devices with their start and end apart: 10, of which 5 were waited for; matrix products, arithmetic and copies ran while one was open for 0% of the time, Pallas kernels for 0%

profile of v16, /device:TPU:1, one launch (start us, length us, event | category | flops | bytes accessed | tf_op | source)
XLA Modules:
  0.0 82.6 jit_solution(4363056445108600100)
XLA Ops:
  0.0 3.5 %collective-permute-start.2 = (bf16[128,256]{1,0:T(8,128)(2,1)}, bf16[128,256]{1,0:T(8,128)(2,1)S(1)}, u32[]{:S(2)}, u32[]{:S(2)}) collective-permute-start(bf16[128,256]{1,0:T(8,128)(2,1)} %refs_0_.1), channel_id=1, source_target_pairs={{0,3},{1,2},{2,5},{3,4},{4,7},{5,6},{6,9},{7,8},{8,11},{9,10},{10,... | collective-permute-start | bytes 196616 | tf_op jit(solution)/shard_map/ppermute | solution.py:168
  3.5 1.6 %collective-permute-start.1 = (bf16[128,256]{1,0:T(8,128)(2,1)}, bf16[128,256]{1,0:T(8,128)(2,1)S(1)}, u32[]{:S(2)}, u32[]{:S(2)}) collective-permute-start(bf16[128,256]{1,0:T(8,128)(2,1)} %refs_0_.1), channel_id=1, source_target_pairs={{0,2},{1,3},{2,4},{3,5},{4,6},{5,7},{6,8},{7,9},{8,10},{9,11},{10,... | collective-permute-start | bytes 196616 | tf_op jit(solution)/shard_map/ppermute | solution.py:167
  5.1 1.4 %collective-permute-start.3 = (bf16[128,256]{1,0:T(8,128)(2,1)}, bf16[128,256]{1,0:T(8,128)(2,1)S(1)}, u32[]{:S(2)}, u32[]{:S(2)}) collective-permute-start(bf16[128,256]{1,0:T(8,128)(2,1)} %refs_0_.1), channel_id=1, source_target_pairs={{0,14},{1,15},{2,0},{3,1},{4,2},{5,3},{6,4},{7,5},{8,6},{9,7},{10,... | collective-permute-start | bytes 196616 | tf_op jit(solution)/shard_map/ppermute | solution.py:167
  6.5 2.4 %collective-permute-start.4 = (bf16[128,256]{1,0:T(8,128)(2,1)}, bf16[128,256]{1,0:T(8,128)(2,1)S(1)}, u32[]{:S(2)}, u32[]{:S(2)}) collective-permute-start(bf16[128,256]{1,0:T(8,128)(2,1)} %refs_0_.1), channel_id=1, source_target_pairs={{0,15},{1,14},{2,1},{3,0},{4,3},{5,2},{6,5},{7,4},{8,7},{9,6},{10,... | collective-permute-start | bytes 196616 | tf_op jit(solution)/shard_map/ppermute | solution.py:168
  8.9 0.4 collective-permute-done.2.refs_3_
  9.3 0.6 collective-permute-done.1.refs_2_
  9.9 1.2 %collective-permute-start.6 = (bf16[2,128,256]{2,1,0:T(8,128)(2,1)S(1)}, bf16[2,128,256]{2,1,0:T(8,128)(2,1)S(1)}, u32[]{:S(2)}, u32[]{:S(2)}) collective-permute-start(bf16[2,128,256]{2,1,0:T(8,128)(2,1)S(1)} %pad_maximum_fusion), channel_id=1, source_target_pairs={{0,4},{1,5},{2,6},{3,7},{4,8},{5,9},{6,10},{7,11},{8,12},{9,13},{1... | collective-permute-start | bytes 393224 | tf_op jit(solution)/shard_map/ppermute | solution.py:175
  11.1 1.7 %collective-permute-start.5 = (bf16[2,128,256]{2,1,0:T(8,128)(2,1)S(1)}, bf16[2,128,256]{2,1,0:T(8,128)(2,1)S(1)}, u32[]{:S(2)}, u32[]{:S(2)}) collective-permute-start(bf16[2,128,256]{2,1,0:T(8,128)(2,1)S(1)} %pad_maximum_fusion), channel_id=1, source_target_pairs={{0,2},{1,3},{2,4},{3,5},{4,6},{5,7},{6,8},{7,9},{8,10},{9,11},{10,... | collective-permute-start | bytes 393224 | tf_op jit(solution)/shard_map/ppermute | solution.py:175
  12.7 0.0 collective-permute-done.3.refs_4_
  12.7 0.0 collective-permute-done.4.refs_5_
  12.8 0.0 copy-start.3
  12.8 1.6 %collective-permute-start.8 = (bf16[2,128,256]{2,1,0:T(8,128)(2,1)S(1)}, bf16[2,128,256]{2,1,0:T(8,128)(2,1)S(1)}, u32[]{:S(2)}, u32[]{:S(2)}) collective-permute-start(bf16[2,128,256]{2,1,0:T(8,128)(2,1)S(1)} %pad_maximum_fusion.1), channel_id=1, source_target_pairs={{0,12},{1,13},{2,14},{3,15},{4,0},{5,1},{6,2},{7,3},{8,4},{9,5},{1... | collective-permute-start | bytes 393224 | tf_op jit(solution)/shard_map/ppermute | solution.py:175
  14.4 1.4 %collective-permute-start.7 = (bf16[2,128,256]{2,1,0:T(8,128)(2,1)S(1)}, bf16[2,128,256]{2,1,0:T(8,128)(2,1)S(1)}, u32[]{:S(2)}, u32[]{:S(2)}) collective-permute-start(bf16[2,128,256]{2,1,0:T(8,128)(2,1)S(1)} %pad_maximum_fusion.1), channel_id=1, source_target_pairs={{0,14},{1,15},{2,0},{3,1},{4,2},{5,3},{6,4},{7,5},{8,6},{9,7},{10,... | collective-permute-start | bytes 393224 | tf_op jit(solution)/shard_map/ppermute | solution.py:175
  15.8 0.8 %collective-permute-done.6.refs_7_ = bf16[2,128,256]{2,1,0:T(8,128)(2,1)S(1)} collective-permute-done((bf16[2,128,256]{2,1,0:T(8,128)(2,1)S(1)}, bf16[2,128,256]{2,1,0:T(8,128)(2,1)S(1)}, u32[]{:S(2)}, u32[]{:S(2)}) %collective-permute-start.6) | collective-permute-done | bytes 131104 | tf_op jit(solution)/shard_map/ppermute | solution.py:175
  16.6 0.0 collective-permute-start.9
  16.6 0.7 collective-permute-start
  17.3 3.0 %collective-permute-done.refs_1_ = bf16[128,256]{1,0:T(8,128)(2,1)S(1)} collective-permute-done((bf16[128,256]{1,0:T(8,128)(2,1)}, bf16[128,256]{1,0:T(8,128)(2,1)S(1)}, u32[]{:S(2)}, u32[]{:S(2)}) %collective-permute-start) | collective-permute-done | bytes 65568 | tf_op jit(solution)/shard_map/ppermute | solution.py:163
  20.2 0.0 collective-permute-done.5.refs_6_
  20.2 0.0 collective-permute-done.8.refs_9_
  20.3 0.0 copy-start.6
  20.3 2.6 %collective-permute-done.7.refs_8_ = bf16[2,128,256]{2,1,0:T(8,128)(2,1)S(1)} collective-permute-done((bf16[2,128,256]{2,1,0:T(8,128)(2,1)S(1)}, bf16[2,128,256]{2,1,0:T(8,128)(2,1)S(1)}, u32[]{:S(2)}, u32[]{:S(2)}) %collective-permute-start.7) | collective-permute-done | bytes 131104 | tf_op jit(solution)/shard_map/ppermute | solution.py:175
  22.9 0.0 collective-permute-done.9.refs_10_
  22.9 0.0 copy-done
  22.9 0.0 copy-done.1
  22.9 0.0 copy-done.2
  22.9 0.0 copy-done.3
  23.0 0.6 copy-done.7
  23.5 0.1 copy-done.8
  23.6 10.4 %shard_map.82 = bf16[16,16,8,256]{3,2,1,0:T(8,128)(2,1)} custom-call(s32[2]{0:T(128)} %bitcast.16, s32[2,64]{1,0:T(2,128)} %gu_ref.1, s32[2,64]{1,0:T(2,128)} %dn_ref.1, s32[1]{0:T(128)} %bitcast.1.me_ref, s32[16]{0:T(128)} %constant.10.table_ref, bf16[128,256]{1,0:T(8,128)(2,1)} %refs_0_.1, bf16[128,256]{1,0:T(8,128)(2,1)} %copy-done.9, ...), custom_call_target="tpu_custom_call" | custom-call | tf_op jit(solution)/shard_map/pallas_call | solution.py:127
  34.0 47.8 %all_to_all.5 = bf16[256,8,256]{2,1,0:T(8,128)(2,1)S(1)} all-to-all(bf16[256,8,256]{2,1,0:T(8,128)(2,1)} %bitcast.10), channel_id=1, replica_groups=mesh['ctx'=16,'tp'=16] {'ctx','tp'}, dimensions={0} | all-to-all | bytes 2097152 | tf_op jit(solution)/shard_map/all_to_all | solution.py:191
  81.9 0.1 bitcast_reduce_fusion
  82.0 0.6 copy.9
  (14 shorter events, 0.1 us)
Async XLA Ops:
  0.0 9.3 %collective-permute-start.2 = (bf16[128,256]{1,0:T(8,128)(2,1)}, bf16[128,256]{1,0:T(8,128)(2,1)S(1)}, u32[]{:S(2)}, u32[]{:S(2)}) collective-permute-start(bf16[128,256]{1,0:T(8,128)(2,1)} %refs_0_.1), channel_id=1, source_target_pairs={{0,3},{1,2},{2,5},{3,4},{4,7},{5,6},{6,9},{7,8},{8,11},{9,10},{10,... | collective-permute-start | bytes 196616 | tf_op jit(solution)/shard_map/ppermute | solution.py:168
  3.5 6.4 %collective-permute-start.1 = (bf16[128,256]{1,0:T(8,128)(2,1)}, bf16[128,256]{1,0:T(8,128)(2,1)S(1)}, u32[]{:S(2)}, u32[]{:S(2)}) collective-permute-start(bf16[128,256]{1,0:T(8,128)(2,1)} %refs_0_.1), channel_id=1, source_target_pairs={{0,2},{1,3},{2,4},{3,5},{4,6},{5,7},{6,8},{7,9},{8,10},{9,11},{10,... | collective-permute-start | bytes 196616 | tf_op jit(solution)/shard_map/ppermute | solution.py:167
  5.1 7.6 %collective-permute-start.3 = (bf16[128,256]{1,0:T(8,128)(2,1)}, bf16[128,256]{1,0:T(8,128)(2,1)S(1)}, u32[]{:S(2)}, u32[]{:S(2)}) collective-permute-start(bf16[128,256]{1,0:T(8,128)(2,1)} %refs_0_.1), channel_id=1, source_target_pairs={{0,14},{1,15},{2,0},{3,1},{4,2},{5,3},{6,4},{7,5},{8,6},{9,7},{10,... | collective-permute-start | bytes 196616 | tf_op jit(solution)/shard_map/ppermute | solution.py:167
  6.5 6.3 %collective-permute-start.4 = (bf16[128,256]{1,0:T(8,128)(2,1)}, bf16[128,256]{1,0:T(8,128)(2,1)S(1)}, u32[]{:S(2)}, u32[]{:S(2)}) collective-permute-start(bf16[128,256]{1,0:T(8,128)(2,1)} %refs_0_.1), channel_id=1, source_target_pairs={{0,15},{1,14},{2,1},{3,0},{4,3},{5,2},{6,5},{7,4},{8,7},{9,6},{10,... | collective-permute-start | bytes 196616 | tf_op jit(solution)/shard_map/ppermute | solution.py:168
  9.3 13.6 %copy-start = (bf16[128,256]{1,0:T(8,128)(2,1)}, bf16[128,256]{1,0:T(8,128)(2,1)S(1)}, u32[]{:S(2)}) copy-start(bf16[128,256]{1,0:T(8,128)(2,1)S(1)} %collective-permute-done.2.refs_3_) | copy-start | bytes 196612
  9.8 13.1 %copy-start.1 = (bf16[128,256]{1,0:T(8,128)(2,1)}, bf16[128,256]{1,0:T(8,128)(2,1)S(1)}, u32[]{:S(2)}) copy-start(bf16[128,256]{1,0:T(8,128)(2,1)S(1)} %collective-permute-done.1.refs_2_) | copy-start | bytes 196612
  9.9 6.8 %collective-permute-start.6 = (bf16[2,128,256]{2,1,0:T(8,128)(2,1)S(1)}, bf16[2,128,256]{2,1,0:T(8,128)(2,1)S(1)}, u32[]{:S(2)}, u32[]{:S(2)}) collective-permute-start(bf16[2,128,256]{2,1,0:T(8,128)(2,1)S(1)} %pad_maximum_fusion), channel_id=1, source_target_pairs={{0,4},{1,5},{2,6},{3,7},{4,8},{5,9},{6,10},{7,11},{8,12},{9,13},{1... | collective-permute-start | bytes 393224 | tf_op jit(solution)/shard_map/ppermute | solution.py:175
  11.1 9.2 %collective-permute-start.5 = (bf16[2,128,256]{2,1,0:T(8,128)(2,1)S(1)}, bf16[2,128,256]{2,1,0:T(8,128)(2,1)S(1)}, u32[]{:S(2)}, u32[]{:S(2)}) collective-permute-start(bf16[2,128,256]{2,1,0:T(8,128)(2,1)S(1)} %pad_maximum_fusion), channel_id=1, source_target_pairs={{0,2},{1,3},{2,4},{3,5},{4,6},{5,7},{6,8},{7,9},{8,10},{9,11},{10,... | collective-permute-start | bytes 393224 | tf_op jit(solution)/shard_map/ppermute | solution.py:175
  12.7 10.2 %copy-start.2 = (bf16[128,256]{1,0:T(8,128)(2,1)}, bf16[128,256]{1,0:T(8,128)(2,1)S(1)}, u32[]{:S(2)}) copy-start(bf16[128,256]{1,0:T(8,128)(2,1)S(1)} %collective-permute-done.3.refs_4_) | copy-start | bytes 196612
  12.8 10.2 %copy-start.3 = (bf16[128,256]{1,0:T(8,128)(2,1)}, bf16[128,256]{1,0:T(8,128)(2,1)S(1)}, u32[]{:S(2)}) copy-start(bf16[128,256]{1,0:T(8,128)(2,1)S(1)} %collective-permute-done.4.refs_5_) | copy-start | bytes 196612
  12.8 7.5 %collective-permute-start.8 = (bf16[2,128,256]{2,1,0:T(8,128)(2,1)S(1)}, bf16[2,128,256]{2,1,0:T(8,128)(2,1)S(1)}, u32[]{:S(2)}, u32[]{:S(2)}) collective-permute-start(bf16[2,128,256]{2,1,0:T(8,128)(2,1)S(1)} %pad_maximum_fusion.1), channel_id=1, source_target_pairs={{0,12},{1,13},{2,14},{3,15},{4,0},{5,1},{6,2},{7,3},{8,4},{9,5},{1... | collective-permute-start | bytes 393224 | tf_op jit(solution)/shard_map/ppermute | solution.py:175
  14.4 8.5 %collective-permute-start.7 = (bf16[2,128,256]{2,1,0:T(8,128)(2,1)S(1)}, bf16[2,128,256]{2,1,0:T(8,128)(2,1)S(1)}, u32[]{:S(2)}, u32[]{:S(2)}) collective-permute-start(bf16[2,128,256]{2,1,0:T(8,128)(2,1)S(1)} %pad_maximum_fusion.1), channel_id=1, source_target_pairs={{0,14},{1,15},{2,0},{3,1},{4,2},{5,3},{6,4},{7,5},{8,6},{9,7},{10,... | collective-permute-start | bytes 393224 | tf_op jit(solution)/shard_map/ppermute | solution.py:175
  16.6 6.3 %copy-start.4 = (bf16[2,128,256]{2,1,0:T(8,128)(2,1)}, bf16[2,128,256]{2,1,0:T(8,128)(2,1)S(1)}, u32[]{:S(2)}) copy-start(bf16[2,128,256]{2,1,0:T(8,128)(2,1)S(1)} %collective-permute-done.6.refs_7_) | copy-start | bytes 393220
  16.6 6.3 %collective-permute-start.9 = (bf16[2,128,256]{2,1,0:T(8,128)(2,1)S(1)}, bf16[2,128,256]{2,1,0:T(8,128)(2,1)S(1)}, u32[]{:S(2)}, u32[]{:S(2)}) collective-permute-start(bf16[2,128,256]{2,1,0:T(8,128)(2,1)S(1)} %collective-permute-done.6.refs_7_), channel_id=1, source_target_pairs={{0,2},{1,3},{2,4},{3,5},{4,6},{5,7},{6,8},{7,9},{8,10},{9,11},{10,... | collective-permute-start | bytes 393224 | tf_op jit(solution)/shard_map/ppermute | solution.py:179
  16.6 3.6 %collective-permute-start = (bf16[128,256]{1,0:T(8,128)(2,1)}, bf16[128,256]{1,0:T(8,128)(2,1)S(1)}, u32[]{:S(2)}, u32[]{:S(2)}) collective-permute-start(bf16[128,256]{1,0:T(8,128)(2,1)} %refs_0_.1), channel_id=1, source_target_pairs={{0,1},{1,0},{2,3},{3,2},{4,5},{5,4},{6,7},{7,6},{8,9},{9,8},{10,11... | collective-permute-start | bytes 196616 | tf_op jit(solution)/shard_map/ppermute | solution.py:163
  20.2 2.7 %copy-start.9 = (bf16[128,256]{1,0:T(8,128)(2,1)}, bf16[128,256]{1,0:T(8,128)(2,1)S(1)}, u32[]{:S(2)}) copy-start(bf16[128,256]{1,0:T(8,128)(2,1)S(1)} %collective-permute-done.refs_1_) | copy-start | bytes 196612
  20.2 2.7 %copy-start.5 = (bf16[2,128,256]{2,1,0:T(8,128)(2,1)}, bf16[2,128,256]{2,1,0:T(8,128)(2,1)S(1)}, u32[]{:S(2)}) copy-start(bf16[2,128,256]{2,1,0:T(8,128)(2,1)S(1)} %collective-permute-done.5.refs_6_) | copy-start | bytes 393220
  20.3 2.7 %copy-start.6 = (bf16[2,128,256]{2,1,0:T(8,128)(2,1)}, bf16[2,128,256]{2,1,0:T(8,128)(2,1)S(1)}, u32[]{:S(2)}) copy-start(bf16[2,128,256]{2,1,0:T(8,128)(2,1)S(1)} %collective-permute-done.8.refs_9_) | copy-start | bytes 393220
  22.9 0.7 copy-start.7
  22.9 0.7 copy-start.8

commit v17 on v12

--- a/solution.py
+++ b/solution.py
@@ -9,7 +9,7 @@
 
 FF = 16384
 Y_LO = 2
-CHUNKS = 8
+CHUNKS = 2
 
 
 def ffn_kernel(layout, cnt_ref, gu_ref, dn_ref, me_ref, table_ref, *refs):

time: 80.7 us -> 79.3 us (0.983)
  Pallas kernels: 8.32 us -> 6.91 us
    pallas_call x1, Pallas kernels: 8.32 us -> 6.91 us  [ffn(): pl.pallas_call(functools.partial(ffn_kernel, tuple(layout)), out_shape=ja...]
where the time goes in v17:
time: 79.3 us; the launch traced here: 79.1 us
  blocking collectives  47.8 us (60%)
  starting transfers between devices  15.4 us (19%)
  waiting for transfers between devices  7.39 us (9%)
  Pallas kernels  6.91 us (9%)
  local copies, waits for them, and re-layouts  1.3 us (2%)
    all_to_all x1, blocking collectives, per_device(): lax.all_to_all(outgoing.reshape(ctx_count * tp_count, share, feat_width /...  47.8 us
    pallas_call x1, Pallas kernels, ffn(): pl.pallas_call(functools.partial(ffn_kernel, tuple(layout)), out_shape=ja...  6.91 us
    ppermute x2, starting transfers between devices, per_device(): other = lax.ppermute(tokens, 'tp', ring_pairs(z_count, step, 1))  5.88 us
    ppermute x4, starting transfers between devices, per_device(): pair = lax.ppermute(near[step], 'tp', ring_pairs(z_count, step * hops))  5.87 us
    ppermute x4, waiting for transfers between devices, per_device(): pair = lax.ppermute(near[step], 'tp', ring_pairs(z_count, step * hops))  3.47 us
    ppermute x2, starting transfers between devices, per_device(): same = lax.ppermute(tokens, 'tp', ring_pairs(z_count, step))  3.01 us
    ppermute x1, waiting for transfers between devices, per_device(): arrays = [tokens, lax.ppermute(tokens, 'tp', swap)]  2.97 us
  transfers between devices with their start and end apart: 10, of which 5 were waited for; matrix products, arithmetic and copies ran while one was open for 0% of the time, Pallas kernels for 0%

profile of v17, /device:TPU:1, one launch (start us, length us, event | category | flops | bytes accessed | tf_op | source)
XLA Modules:
  0.0 79.1 jit_solution(4135369397303317984)
XLA Ops:
  0.0 3.5 %collective-permute-start.2 = (bf16[128,256]{1,0:T(8,128)(2,1)}, bf16[128,256]{1,0:T(8,128)(2,1)S(1)}, u32[]{:S(2)}, u32[]{:S(2)}) collective-permute-start(bf16[128,256]{1,0:T(8,128)(2,1)} %refs_0_.1), channel_id=1, source_target_pairs={{0,3},{1,2},{2,5},{3,4},{4,7},{5,6},{6,9},{7,8},{8,11},{9,10},{10,... | collective-permute-start | bytes 196616 | tf_op jit(solution)/shard_map/ppermute | solution.py:157
  3.5 1.6 %collective-permute-start.1 = (bf16[128,256]{1,0:T(8,128)(2,1)}, bf16[128,256]{1,0:T(8,128)(2,1)S(1)}, u32[]{:S(2)}, u32[]{:S(2)}) collective-permute-start(bf16[128,256]{1,0:T(8,128)(2,1)} %refs_0_.1), channel_id=1, source_target_pairs={{0,2},{1,3},{2,4},{3,5},{4,6},{5,7},{6,8},{7,9},{8,10},{9,11},{10,... | collective-permute-start | bytes 196616 | tf_op jit(solution)/shard_map/ppermute | solution.py:156
  5.1 1.4 %collective-permute-start.3 = (bf16[128,256]{1,0:T(8,128)(2,1)}, bf16[128,256]{1,0:T(8,128)(2,1)S(1)}, u32[]{:S(2)}, u32[]{:S(2)}) collective-permute-start(bf16[128,256]{1,0:T(8,128)(2,1)} %refs_0_.1), channel_id=1, source_target_pairs={{0,14},{1,15},{2,0},{3,1},{4,2},{5,3},{6,4},{7,5},{8,6},{9,7},{10,... | collective-permute-start | bytes 196616 | tf_op jit(solution)/shard_map/ppermute | solution.py:156
  6.5 2.4 %collective-permute-start.4 = (bf16[128,256]{1,0:T(8,128)(2,1)}, bf16[128,256]{1,0:T(8,128)(2,1)S(1)}, u32[]{:S(2)}, u32[]{:S(2)}) collective-permute-start(bf16[128,256]{1,0:T(8,128)(2,1)} %refs_0_.1), channel_id=1, source_target_pairs={{0,15},{1,14},{2,1},{3,0},{4,3},{5,2},{6,5},{7,4},{8,7},{9,6},{10,... | collective-permute-start | bytes 196616 | tf_op jit(solution)/shard_map/ppermute | solution.py:157
  8.9 0.4 collective-permute-done.2.refs_3_
  9.3 0.6 collective-permute-done.1.refs_2_
  9.9 1.2 %collective-permute-start.6 = (bf16[2,128,256]{2,1,0:T(8,128)(2,1)S(1)}, bf16[2,128,256]{2,1,0:T(8,128)(2,1)S(1)}, u32[]{:S(2)}, u32[]{:S(2)}) collective-permute-start(bf16[2,128,256]{2,1,0:T(8,128)(2,1)S(1)} %pad_maximum_fusion), channel_id=1, source_target_pairs={{0,4},{1,5},{2,6},{3,7},{4,8},{5,9},{6,10},{7,11},{8,12},{9,13},{1... | collective-permute-start | bytes 393224 | tf_op jit(solution)/shard_map/ppermute | solution.py:164
  11.1 1.7 %collective-permute-start.5 = (bf16[2,128,256]{2,1,0:T(8,128)(2,1)S(1)}, bf16[2,128,256]{2,1,0:T(8,128)(2,1)S(1)}, u32[]{:S(2)}, u32[]{:S(2)}) collective-permute-start(bf16[2,128,256]{2,1,0:T(8,128)(2,1)S(1)} %pad_maximum_fusion), channel_id=1, source_target_pairs={{0,2},{1,3},{2,4},{3,5},{4,6},{5,7},{6,8},{7,9},{8,10},{9,11},{10,... | collective-permute-start | bytes 393224 | tf_op jit(solution)/shard_map/ppermute | solution.py:164
  12.7 0.0 collective-permute-done.3.refs_4_
  12.7 0.0 collective-permute-done.4.refs_5_
  12.8 0.0 copy-start.3
  12.8 1.6 %collective-permute-start.8 = (bf16[2,128,256]{2,1,0:T(8,128)(2,1)S(1)}, bf16[2,128,256]{2,1,0:T(8,128)(2,1)S(1)}, u32[]{:S(2)}, u32[]{:S(2)}) collective-permute-start(bf16[2,128,256]{2,1,0:T(8,128)(2,1)S(1)} %pad_maximum_fusion.1), channel_id=1, source_target_pairs={{0,12},{1,13},{2,14},{3,15},{4,0},{5,1},{6,2},{7,3},{8,4},{9,5},{1... | collective-permute-start | bytes 393224 | tf_op jit(solution)/shard_map/ppermute | solution.py:164
  14.4 1.4 %collective-permute-start.7 = (bf16[2,128,256]{2,1,0:T(8,128)(2,1)S(1)}, bf16[2,128,256]{2,1,0:T(8,128)(2,1)S(1)}, u32[]{:S(2)}, u32[]{:S(2)}) collective-permute-start(bf16[2,128,256]{2,1,0:T(8,128)(2,1)S(1)} %pad_maximum_fusion.1), channel_id=1, source_target_pairs={{0,14},{1,15},{2,0},{3,1},{4,2},{5,3},{6,4},{7,5},{8,6},{9,7},{10,... | collective-permute-start | bytes 393224 | tf_op jit(solution)/shard_map/ppermute | solution.py:164
  15.8 0.8 %collective-permute-done.6.refs_7_ = bf16[2,128,256]{2,1,0:T(8,128)(2,1)S(1)} collective-permute-done((bf16[2,128,256]{2,1,0:T(8,128)(2,1)S(1)}, bf16[2,128,256]{2,1,0:T(8,128)(2,1)S(1)}, u32[]{:S(2)}, u32[]{:S(2)}) %collective-permute-start.6) | collective-permute-done | bytes 131104 | tf_op jit(solution)/shard_map/ppermute | solution.py:164
  16.6 0.0 collective-permute-start.9
  16.6 0.7 collective-permute-start
  17.3 3.0 %collective-permute-done.refs_1_ = bf16[128,256]{1,0:T(8,128)(2,1)S(1)} collective-permute-done((bf16[128,256]{1,0:T(8,128)(2,1)}, bf16[128,256]{1,0:T(8,128)(2,1)S(1)}, u32[]{:S(2)}, u32[]{:S(2)}) %collective-permute-start) | collective-permute-done | bytes 65568 | tf_op jit(solution)/shard_map/ppermute | solution.py:152
  20.2 0.0 collective-permute-done.5.refs_6_
  20.2 0.0 collective-permute-done.8.refs_9_
  20.3 0.0 copy-start.6
  20.3 2.6 %collective-permute-done.7.refs_8_ = bf16[2,128,256]{2,1,0:T(8,128)(2,1)S(1)} collective-permute-done((bf16[2,128,256]{2,1,0:T(8,128)(2,1)S(1)}, bf16[2,128,256]{2,1,0:T(8,128)(2,1)S(1)}, u32[]{:S(2)}, u32[]{:S(2)}) %collective-permute-start.7) | collective-permute-done | bytes 131104 | tf_op jit(solution)/shard_map/ppermute | solution.py:164
  22.9 0.0 collective-permute-done.9.refs_10_
  22.9 0.0 copy-done
  22.9 0.0 copy-done.1
  22.9 0.0 copy-done.2
  22.9 0.0 copy-done.3
  23.0 0.6 copy-done.7
  23.5 0.1 copy-done.8
  23.6 6.9 %shard_map.82 = bf16[16,16,8,256]{3,2,1,0:T(8,128)(2,1)} custom-call(s32[2]{0:T(128)} %bitcast.16, s32[2,64]{1,0:T(2,128)} %gu_ref.1, s32[2,64]{1,0:T(2,128)} %dn_ref.1, s32[1]{0:T(128)} %bitcast.1.me_ref, s32[16]{0:T(128)} %constant.10.table_ref, bf16[128,256]{1,0:T(8,128)(2,1)} %refs_0_.1, bf16[128,256]{1,0:T(8,128)(2,1)} %copy-done.9, ...), custom_call_target="tpu_custom_call" | custom-call | tf_op jit(solution)/shard_map/pallas_call | solution.py:118
  30.5 47.8 %all_to_all.5 = bf16[256,8,256]{2,1,0:T(8,128)(2,1)S(1)} all-to-all(bf16[256,8,256]{2,1,0:T(8,128)(2,1)} %bitcast.10), channel_id=1, replica_groups=mesh['ctx'=16,'tp'=16] {'ctx','tp'}, dimensions={0} | all-to-all | bytes 2097152 | tf_op jit(solution)/shard_map/all_to_all | solution.py:180
  78.3 0.1 bitcast_reduce_fusion
  78.5 0.6 copy.9
  (14 shorter events, 0.1 us)
Async XLA Ops:
  0.0 9.3 %collective-permute-start.2 = (bf16[128,256]{1,0:T(8,128)(2,1)}, bf16[128,256]{1,0:T(8,128)(2,1)S(1)}, u32[]{:S(2)}, u32[]{:S(2)}) collective-permute-start(bf16[128,256]{1,0:T(8,128)(2,1)} %refs_0_.1), channel_id=1, source_target_pairs={{0,3},{1,2},{2,5},{3,4},{4,7},{5,6},{6,9},{7,8},{8,11},{9,10},{10,... | collective-permute-start | bytes 196616 | tf_op jit(solution)/shard_map/ppermute | solution.py:157
  3.5 6.4 %collective-permute-start.1 = (bf16[128,256]{1,0:T(8,128)(2,1)}, bf16[128,256]{1,0:T(8,128)(2,1)S(1)}, u32[]{:S(2)}, u32[]{:S(2)}) collective-permute-start(bf16[128,256]{1,0:T(8,128)(2,1)} %refs_0_.1), channel_id=1, source_target_pairs={{0,2},{1,3},{2,4},{3,5},{4,6},{5,7},{6,8},{7,9},{8,10},{9,11},{10,... | collective-permute-start | bytes 196616 | tf_op jit(solution)/shard_map/ppermute | solution.py:156
  5.1 7.6 %collective-permute-start.3 = (bf16[128,256]{1,0:T(8,128)(2,1)}, bf16[128,256]{1,0:T(8,128)(2,1)S(1)}, u32[]{:S(2)}, u32[]{:S(2)}) collective-permute-start(bf16[128,256]{1,0:T(8,128)(2,1)} %refs_0_.1), channel_id=1, source_target_pairs={{0,14},{1,15},{2,0},{3,1},{4,2},{5,3},{6,4},{7,5},{8,6},{9,7},{10,... | collective-permute-start | bytes 196616 | tf_op jit(solution)/shard_map/ppermute | solution.py:156
  6.5 6.3 %collective-permute-start.4 = (bf16[128,256]{1,0:T(8,128)(2,1)}, bf16[128,256]{1,0:T(8,128)(2,1)S(1)}, u32[]{:S(2)}, u32[]{:S(2)}) collective-permute-start(bf16[128,256]{1,0:T(8,128)(2,1)} %refs_0_.1), channel_id=1, source_target_pairs={{0,15},{1,14},{2,1},{3,0},{4,3},{5,2},{6,5},{7,4},{8,7},{9,6},{10,... | collective-permute-start | bytes 196616 | tf_op jit(solution)/shard_map/ppermute | solution.py:157
  9.3 13.6 %copy-start = (bf16[128,256]{1,0:T(8,128)(2,1)}, bf16[128,256]{1,0:T(8,128)(2,1)S(1)}, u32[]{:S(2)}) copy-start(bf16[128,256]{1,0:T(8,128)(2,1)S(1)} %collective-permute-done.2.refs_3_) | copy-start | bytes 196612
  9.8 13.1 %copy-start.1 = (bf16[128,256]{1,0:T(8,128)(2,1)}, bf16[128,256]{1,0:T(8,128)(2,1)S(1)}, u32[]{:S(2)}) copy-start(bf16[128,256]{1,0:T(8,128)(2,1)S(1)} %collective-permute-done.1.refs_2_) | copy-start | bytes 196612
  9.9 6.8 %collective-permute-start.6 = (bf16[2,128,256]{2,1,0:T(8,128)(2,1)S(1)}, bf16[2,128,256]{2,1,0:T(8,128)(2,1)S(1)}, u32[]{:S(2)}, u32[]{:S(2)}) collective-permute-start(bf16[2,128,256]{2,1,0:T(8,128)(2,1)S(1)} %pad_maximum_fusion), channel_id=1, source_target_pairs={{0,4},{1,5},{2,6},{3,7},{4,8},{5,9},{6,10},{7,11},{8,12},{9,13},{1... | collective-permute-start | bytes 393224 | tf_op jit(solution)/shard_map/ppermute | solution.py:164
  11.1 9.2 %collective-permute-start.5 = (bf16[2,128,256]{2,1,0:T(8,128)(2,1)S(1)}, bf16[2,128,256]{2,1,0:T(8,128)(2,1)S(1)}, u32[]{:S(2)}, u32[]{:S(2)}) collective-permute-start(bf16[2,128,256]{2,1,0:T(8,128)(2,1)S(1)} %pad_maximum_fusion), channel_id=1, source_target_pairs={{0,2},{1,3},{2,4},{3,5},{4,6},{5,7},{6,8},{7,9},{8,10},{9,11},{10,... | collective-permute-start | bytes 393224 | tf_op jit(solution)/shard_map/ppermute | solution.py:164
  12.7 10.2 %copy-start.2 = (bf16[128,256]{1,0:T(8,128)(2,1)}, bf16[128,256]{1,0:T(8,128)(2,1)S(1)}, u32[]{:S(2)}) copy-start(bf16[128,256]{1,0:T(8,128)(2,1)S(1)} %collective-permute-done.3.refs_4_) | copy-start | bytes 196612
  12.8 10.2 %copy-start.3 = (bf16[128,256]{1,0:T(8,128)(2,1)}, bf16[128,256]{1,0:T(8,128)(2,1)S(1)}, u32[]{:S(2)}) copy-start(bf16[128,256]{1,0:T(8,128)(2,1)S(1)} %collective-permute-done.4.refs_5_) | copy-start | bytes 196612
  12.8 7.5 %collective-permute-start.8 = (bf16[2,128,256]{2,1,0:T(8,128)(2,1)S(1)}, bf16[2,128,256]{2,1,0:T(8,128)(2,1)S(1)}, u32[]{:S(2)}, u32[]{:S(2)}) collective-permute-start(bf16[2,128,256]{2,1,0:T(8,128)(2,1)S(1)} %pad_maximum_fusion.1), channel_id=1, source_target_pairs={{0,12},{1,13},{2,14},{3,15},{4,0},{5,1},{6,2},{7,3},{8,4},{9,5},{1... | collective-permute-start | bytes 393224 | tf_op jit(solution)/shard_map/ppermute | solution.py:164
  14.4 8.5 %collective-permute-start.7 = (bf16[2,128,256]{2,1,0:T(8,128)(2,1)S(1)}, bf16[2,128,256]{2,1,0:T(8,128)(2,1)S(1)}, u32[]{:S(2)}, u32[]{:S(2)}) collective-permute-start(bf16[2,128,256]{2,1,0:T(8,128)(2,1)S(1)} %pad_maximum_fusion.1), channel_id=1, source_target_pairs={{0,14},{1,15},{2,0},{3,1},{4,2},{5,3},{6,4},{7,5},{8,6},{9,7},{10,... | collective-permute-start | bytes 393224 | tf_op jit(solution)/shard_map/ppermute | solution.py:164
  16.6 6.3 %copy-start.4 = (bf16[2,128,256]{2,1,0:T(8,128)(2,1)}, bf16[2,128,256]{2,1,0:T(8,128)(2,1)S(1)}, u32[]{:S(2)}) copy-start(bf16[2,128,256]{2,1,0:T(8,128)(2,1)S(1)} %collective-permute-done.6.refs_7_) | copy-start | bytes 393220
  16.6 6.3 %collective-permute-start.9 = (bf16[2,128,256]{2,1,0:T(8,128)(2,1)S(1)}, bf16[2,128,256]{2,1,0:T(8,128)(2,1)S(1)}, u32[]{:S(2)}, u32[]{:S(2)}) collective-permute-start(bf16[2,128,256]{2,1,0:T(8,128)(2,1)S(1)} %collective-permute-done.6.refs_7_), channel_id=1, source_target_pairs={{0,2},{1,3},{2,4},{3,5},{4,6},{5,7},{6,8},{7,9},{8,10},{9,11},{10,... | collective-permute-start | bytes 393224 | tf_op jit(solution)/shard_map/ppermute | solution.py:168
  16.6 3.6 %collective-permute-start = (bf16[128,256]{1,0:T(8,128)(2,1)}, bf16[128,256]{1,0:T(8,128)(2,1)S(1)}, u32[]{:S(2)}, u32[]{:S(2)}) collective-permute-start(bf16[128,256]{1,0:T(8,128)(2,1)} %refs_0_.1), channel_id=1, source_target_pairs={{0,1},{1,0},{2,3},{3,2},{4,5},{5,4},{6,7},{7,6},{8,9},{9,8},{10,11... | collective-permute-start | bytes 196616 | tf_op jit(solution)/shard_map/ppermute | solution.py:152
  20.2 2.7 %copy-start.9 = (bf16[128,256]{1,0:T(8,128)(2,1)}, bf16[128,256]{1,0:T(8,128)(2,1)S(1)}, u32[]{:S(2)}) copy-start(bf16[128,256]{1,0:T(8,128)(2,1)S(1)} %collective-permute-done.refs_1_) | copy-start | bytes 196612
  20.2 2.7 %copy-start.5 = (bf16[2,128,256]{2,1,0:T(8,128)(2,1)}, bf16[2,128,256]{2,1,0:T(8,128)(2,1)S(1)}, u32[]{:S(2)}) copy-start(bf16[2,128,256]{2,1,0:T(8,128)(2,1)S(1)} %collective-permute-done.5.refs_6_) | copy-start | bytes 393220
  20.3 2.7 %copy-start.6 = (bf16[2,128,256]{2,1,0:T(8,128)(2,1)}, bf16[2,128,256]{2,1,0:T(8,128)(2,1)S(1)}, u32[]{:S(2)}) copy-start(bf16[2,128,256]{2,1,0:T(8,128)(2,1)S(1)} %collective-permute-done.8.refs_9_) | copy-start | bytes 393220
  22.9 0.7 copy-start.7
  22.9 0.7 copy-start.8

commit v18 on v17

--- a/solution.py
+++ b/solution.py
@@ -34,11 +34,7 @@
             pltpu.make_async_copy(g_hbm.at[part], gu_v.at[part, :, 0:tile], sems.at[0, k]),
             pltpu.make_async_copy(u_hbm.at[part], gu_v.at[part, :, tile:2 * tile], sems.at[1, k]),
         ))
-    down_copies = [
-        pltpu.make_async_copy(d_hbm.at[pl.ds(k * step, step)], d_v.at[pl.ds(k * step, step)],
-                              sems.at[2, k])
-        for k in range(CHUNKS)
-    ]
+    down_copies = [pltpu.make_async_copy(d_hbm, d_v, sems.at[2, 0])]
     for gate_copy, up_copy in copies:
         gate_copy.start()
         up_copy.start()
@@ -91,7 +87,7 @@
 
     for k, down_copy in enumerate(down_copies):
         down_copy.wait()
-        lax.fori_loop(k * step, (k + 1) * step, dn_body, 0, unroll=True)
+        lax.fori_loop(0, slots, dn_body, 0, unroll=True)
     groups, dests, share, group_width = out_ref.shape
     for h in range(per_src):
         acco_s[me_ref[0] * per_src + h] += piece(0, slice(h * tile, (h + 1) * tile)).astype(jnp.float32)

time: 79.3 us -> 79.1 us (level)
  no operation moved by 1% of the time
where the time goes in v18:
time: 79.1 us; the launch traced here: 79 us
  blocking collectives  47.8 us (60%)
  starting transfers between devices  15.4 us (19%)
  waiting for transfers between devices  7.39 us (9%)
  Pallas kernels  6.79 us (9%)
  local copies, waits for them, and re-layouts  1.3 us (2%)
    all_to_all x1, blocking collectives, per_device(): lax.all_to_all(outgoing.reshape(ctx_count * tp_count, share, feat_width /...  47.8 us
    pallas_call x1, Pallas kernels, ffn(): pl.pallas_call(functools.partial(ffn_kernel, tuple(layout)), out_shape=ja...  6.79 us
    ppermute x2, starting transfers between devices, per_device(): other = lax.ppermute(tokens, 'tp', ring_pairs(z_count, step, 1))  5.88 us
    ppermute x4, starting transfers between devices, per_device(): pair = lax.ppermute(near[step], 'tp', ring_pairs(z_count, step * hops))  5.87 us
    ppermute x4, waiting for transfers between devices, per_device(): pair = lax.ppermute(near[step], 'tp', ring_pairs(z_count, step * hops))  3.47 us
    ppermute x2, starting transfers between devices, per_device(): same = lax.ppermute(tokens, 'tp', ring_pairs(z_count, step))  3.01 us
    ppermute x1, waiting for transfers between devices, per_device(): arrays = [tokens, lax.ppermute(tokens, 'tp', swap)]  2.97 us
  transfers between devices with their start and end apart: 10, of which 5 were waited for; matrix products, arithmetic and copies ran while one was open for 0% of the time, Pallas kernels for 0%

profile of v18, /device:TPU:1, one launch (start us, length us, event | category | flops | bytes accessed | tf_op | source)
XLA Modules:
  0.0 79.0 jit_solution(13355218110045079200)
XLA Ops:
  0.0 3.5 %collective-permute-start.2 = (bf16[128,256]{1,0:T(8,128)(2,1)}, bf16[128,256]{1,0:T(8,128)(2,1)S(1)}, u32[]{:S(2)}, u32[]{:S(2)}) collective-permute-start(bf16[128,256]{1,0:T(8,128)(2,1)} %refs_0_.1), channel_id=1, source_target_pairs={{0,3},{1,2},{2,5},{3,4},{4,7},{5,6},{6,9},{7,8},{8,11},{9,10},{10,... | collective-permute-start | bytes 196616 | tf_op jit(solution)/shard_map/ppermute | solution.py:153
  3.5 1.6 %collective-permute-start.1 = (bf16[128,256]{1,0:T(8,128)(2,1)}, bf16[128,256]{1,0:T(8,128)(2,1)S(1)}, u32[]{:S(2)}, u32[]{:S(2)}) collective-permute-start(bf16[128,256]{1,0:T(8,128)(2,1)} %refs_0_.1), channel_id=1, source_target_pairs={{0,2},{1,3},{2,4},{3,5},{4,6},{5,7},{6,8},{7,9},{8,10},{9,11},{10,... | collective-permute-start | bytes 196616 | tf_op jit(solution)/shard_map/ppermute | solution.py:152
  5.1 1.4 %collective-permute-start.3 = (bf16[128,256]{1,0:T(8,128)(2,1)}, bf16[128,256]{1,0:T(8,128)(2,1)S(1)}, u32[]{:S(2)}, u32[]{:S(2)}) collective-permute-start(bf16[128,256]{1,0:T(8,128)(2,1)} %refs_0_.1), channel_id=1, source_target_pairs={{0,14},{1,15},{2,0},{3,1},{4,2},{5,3},{6,4},{7,5},{8,6},{9,7},{10,... | collective-permute-start | bytes 196616 | tf_op jit(solution)/shard_map/ppermute | solution.py:152
  6.5 2.4 %collective-permute-start.4 = (bf16[128,256]{1,0:T(8,128)(2,1)}, bf16[128,256]{1,0:T(8,128)(2,1)S(1)}, u32[]{:S(2)}, u32[]{:S(2)}) collective-permute-start(bf16[128,256]{1,0:T(8,128)(2,1)} %refs_0_.1), channel_id=1, source_target_pairs={{0,15},{1,14},{2,1},{3,0},{4,3},{5,2},{6,5},{7,4},{8,7},{9,6},{10,... | collective-permute-start | bytes 196616 | tf_op jit(solution)/shard_map/ppermute | solution.py:153
  8.9 0.4 collective-permute-done.2.refs_3_
  9.3 0.6 collective-permute-done.1.refs_2_
  9.9 1.2 %collective-permute-start.6 = (bf16[2,128,256]{2,1,0:T(8,128)(2,1)S(1)}, bf16[2,128,256]{2,1,0:T(8,128)(2,1)S(1)}, u32[]{:S(2)}, u32[]{:S(2)}) collective-permute-start(bf16[2,128,256]{2,1,0:T(8,128)(2,1)S(1)} %pad_maximum_fusion), channel_id=1, source_target_pairs={{0,4},{1,5},{2,6},{3,7},{4,8},{5,9},{6,10},{7,11},{8,12},{9,13},{1... | collective-permute-start | bytes 393224 | tf_op jit(solution)/shard_map/ppermute | solution.py:160
  11.1 1.7 %collective-permute-start.5 = (bf16[2,128,256]{2,1,0:T(8,128)(2,1)S(1)}, bf16[2,128,256]{2,1,0:T(8,128)(2,1)S(1)}, u32[]{:S(2)}, u32[]{:S(2)}) collective-permute-start(bf16[2,128,256]{2,1,0:T(8,128)(2,1)S(1)} %pad_maximum_fusion), channel_id=1, source_target_pairs={{0,2},{1,3},{2,4},{3,5},{4,6},{5,7},{6,8},{7,9},{8,10},{9,11},{10,... | collective-permute-start | bytes 393224 | tf_op jit(solution)/shard_map/ppermute | solution.py:160
  12.7 0.0 collective-permute-done.3.refs_4_
  12.7 0.0 collective-permute-done.4.refs_5_
  12.8 0.0 copy-start.3
  12.8 1.6 %collective-permute-start.8 = (bf16[2,128,256]{2,1,0:T(8,128)(2,1)S(1)}, bf16[2,128,256]{2,1,0:T(8,128)(2,1)S(1)}, u32[]{:S(2)}, u32[]{:S(2)}) collective-permute-start(bf16[2,128,256]{2,1,0:T(8,128)(2,1)S(1)} %pad_maximum_fusion.1), channel_id=1, source_target_pairs={{0,12},{1,13},{2,14},{3,15},{4,0},{5,1},{6,2},{7,3},{8,4},{9,5},{1... | collective-permute-start | bytes 393224 | tf_op jit(solution)/shard_map/ppermute | solution.py:160
  14.4 1.4 %collective-permute-start.7 = (bf16[2,128,256]{2,1,0:T(8,128)(2,1)S(1)}, bf16[2,128,256]{2,1,0:T(8,128)(2,1)S(1)}, u32[]{:S(2)}, u32[]{:S(2)}) collective-permute-start(bf16[2,128,256]{2,1,0:T(8,128)(2,1)S(1)} %pad_maximum_fusion.1), channel_id=1, source_target_pairs={{0,14},{1,15},{2,0},{3,1},{4,2},{5,3},{6,4},{7,5},{8,6},{9,7},{10,... | collective-permute-start | bytes 393224 | tf_op jit(solution)/shard_map/ppermute | solution.py:160
  15.8 0.8 %collective-permute-done.6.refs_7_ = bf16[2,128,256]{2,1,0:T(8,128)(2,1)S(1)} collective-permute-done((bf16[2,128,256]{2,1,0:T(8,128)(2,1)S(1)}, bf16[2,128,256]{2,1,0:T(8,128)(2,1)S(1)}, u32[]{:S(2)}, u32[]{:S(2)}) %collective-permute-start.6) | collective-permute-done | bytes 131104 | tf_op jit(solution)/shard_map/ppermute | solution.py:160
  16.6 0.0 collective-permute-start.9
  16.6 0.7 collective-permute-start
  17.3 3.0 %collective-permute-done.refs_1_ = bf16[128,256]{1,0:T(8,128)(2,1)S(1)} collective-permute-done((bf16[128,256]{1,0:T(8,128)(2,1)}, bf16[128,256]{1,0:T(8,128)(2,1)S(1)}, u32[]{:S(2)}, u32[]{:S(2)}) %collective-permute-start) | collective-permute-done | bytes 65568 | tf_op jit(solution)/shard_map/ppermute | solution.py:148
  20.2 0.0 collective-permute-done.5.refs_6_
  20.2 0.0 collective-permute-done.8.refs_9_
  20.3 0.0 copy-start.6
  20.3 2.6 %collective-permute-done.7.refs_8_ = bf16[2,128,256]{2,1,0:T(8,128)(2,1)S(1)} collective-permute-done((bf16[2,128,256]{2,1,0:T(8,128)(2,1)S(1)}, bf16[2,128,256]{2,1,0:T(8,128)(2,1)S(1)}, u32[]{:S(2)}, u32[]{:S(2)}) %collective-permute-start.7) | collective-permute-done | bytes 131104 | tf_op jit(solution)/shard_map/ppermute | solution.py:160
  22.9 0.0 collective-permute-done.9.refs_10_
  22.9 0.0 copy-done
  22.9 0.0 copy-done.1
  22.9 0.0 copy-done.2
  22.9 0.0 copy-done.3
  23.0 0.6 copy-done.7
  23.5 0.1 copy-done.8
  23.6 6.8 %shard_map.82 = bf16[16,16,8,256]{3,2,1,0:T(8,128)(2,1)} custom-call(s32[2]{0:T(128)} %bitcast.16, s32[2,64]{1,0:T(2,128)} %gu_ref.1, s32[2,64]{1,0:T(2,128)} %dn_ref.1, s32[1]{0:T(128)} %bitcast.1.me_ref, s32[16]{0:T(128)} %constant.10.table_ref, bf16[128,256]{1,0:T(8,128)(2,1)} %refs_0_.1, bf16[128,256]{1,0:T(8,128)(2,1)} %copy-done.9, ...), custom_call_target="tpu_custom_call" | custom-call | tf_op jit(solution)/shard_map/pallas_call | solution.py:114
  30.4 47.8 %all_to_all.5 = bf16[256,8,256]{2,1,0:T(8,128)(2,1)S(1)} all-to-all(bf16[256,8,256]{2,1,0:T(8,128)(2,1)} %bitcast.10), channel_id=1, replica_groups=mesh['ctx'=16,'tp'=16] {'ctx','tp'}, dimensions={0} | all-to-all | bytes 2097152 | tf_op jit(solution)/shard_map/all_to_all | solution.py:176
  78.2 0.1 bitcast_reduce_fusion
  78.3 0.6 copy.9
  (14 shorter events, 0.1 us)
Async XLA Ops:
  0.0 9.3 %collective-permute-start.2 = (bf16[128,256]{1,0:T(8,128)(2,1)}, bf16[128,256]{1,0:T(8,128)(2,1)S(1)}, u32[]{:S(2)}, u32[]{:S(2)}) collective-permute-start(bf16[128,256]{1,0:T(8,128)(2,1)} %refs_0_.1), channel_id=1, source_target_pairs={{0,3},{1,2},{2,5},{3,4},{4,7},{5,6},{6,9},{7,8},{8,11},{9,10},{10,... | collective-permute-start | bytes 196616 | tf_op jit(solution)/shard_map/ppermute | solution.py:153
  3.5 6.4 %collective-permute-start.1 = (bf16[128,256]{1,0:T(8,128)(2,1)}, bf16[128,256]{1,0:T(8,128)(2,1)S(1)}, u32[]{:S(2)}, u32[]{:S(2)}) collective-permute-start(bf16[128,256]{1,0:T(8,128)(2,1)} %refs_0_.1), channel_id=1, source_target_pairs={{0,2},{1,3},{2,4},{3,5},{4,6},{5,7},{6,8},{7,9},{8,10},{9,11},{10,... | collective-permute-start | bytes 196616 | tf_op jit(solution)/shard_map/ppermute | solution.py:152
  5.1 7.6 %collective-permute-start.3 = (bf16[128,256]{1,0:T(8,128)(2,1)}, bf16[128,256]{1,0:T(8,128)(2,1)S(1)}, u32[]{:S(2)}, u32[]{:S(2)}) collective-permute-start(bf16[128,256]{1,0:T(8,128)(2,1)} %refs_0_.1), channel_id=1, source_target_pairs={{0,14},{1,15},{2,0},{3,1},{4,2},{5,3},{6,4},{7,5},{8,6},{9,7},{10,... | collective-permute-start | bytes 196616 | tf_op jit(solution)/shard_map/ppermute | solution.py:152
  6.5 6.3 %collective-permute-start.4 = (bf16[128,256]{1,0:T(8,128)(2,1)}, bf16[128,256]{1,0:T(8,128)(2,1)S(1)}, u32[]{:S(2)}, u32[]{:S(2)}) collective-permute-start(bf16[128,256]{1,0:T(8,128)(2,1)} %refs_0_.1), channel_id=1, source_target_pairs={{0,15},{1,14},{2,1},{3,0},{4,3},{5,2},{6,5},{7,4},{8,7},{9,6},{10,... | collective-permute-start | bytes 196616 | tf_op jit(solution)/shard_map/ppermute | solution.py:153
  9.3 13.6 %copy-start = (bf16[128,256]{1,0:T(8,128)(2,1)}, bf16[128,256]{1,0:T(8,128)(2,1)S(1)}, u32[]{:S(2)}) copy-start(bf16[128,256]{1,0:T(8,128)(2,1)S(1)} %collective-permute-done.2.refs_3_) | copy-start | bytes 196612
  9.8 13.1 %copy-start.1 = (bf16[128,256]{1,0:T(8,128)(2,1)}, bf16[128,256]{1,0:T(8,128)(2,1)S(1)}, u32[]{:S(2)}) copy-start(bf16[128,256]{1,0:T(8,128)(2,1)S(1)} %collective-permute-done.1.refs_2_) | copy-start | bytes 196612
  9.9 6.8 %collective-permute-start.6 = (bf16[2,128,256]{2,1,0:T(8,128)(2,1)S(1)}, bf16[2,128,256]{2,1,0:T(8,128)(2,1)S(1)}, u32[]{:S(2)}, u32[]{:S(2)}) collective-permute-start(bf16[2,128,256]{2,1,0:T(8,128)(2,1)S(1)} %pad_maximum_fusion), channel_id=1, source_target_pairs={{0,4},{1,5},{2,6},{3,7},{4,8},{5,9},{6,10},{7,11},{8,12},{9,13},{1... | collective-permute-start | bytes 393224 | tf_op jit(solution)/shard_map/ppermute | solution.py:160
  11.1 9.2 %collective-permute-start.5 = (bf16[2,128,256]{2,1,0:T(8,128)(2,1)S(1)}, bf16[2,128,256]{2,1,0:T(8,128)(2,1)S(1)}, u32[]{:S(2)}, u32[]{:S(2)}) collective-permute-start(bf16[2,128,256]{2,1,0:T(8,128)(2,1)S(1)} %pad_maximum_fusion), channel_id=1, source_target_pairs={{0,2},{1,3},{2,4},{3,5},{4,6},{5,7},{6,8},{7,9},{8,10},{9,11},{10,... | collective-permute-start | bytes 393224 | tf_op jit(solution)/shard_map/ppermute | solution.py:160
  12.7 10.2 %copy-start.2 = (bf16[128,256]{1,0:T(8,128)(2,1)}, bf16[128,256]{1,0:T(8,128)(2,1)S(1)}, u32[]{:S(2)}) copy-start(bf16[128,256]{1,0:T(8,128)(2,1)S(1)} %collective-permute-done.3.refs_4_) | copy-start | bytes 196612
  12.8 10.2 %copy-start.3 = (bf16[128,256]{1,0:T(8,128)(2,1)}, bf16[128,256]{1,0:T(8,128)(2,1)S(1)}, u32[]{:S(2)}) copy-start(bf16[128,256]{1,0:T(8,128)(2,1)S(1)} %collective-permute-done.4.refs_5_) | copy-start | bytes 196612
  12.8 7.5 %collective-permute-start.8 = (bf16[2,128,256]{2,1,0:T(8,128)(2,1)S(1)}, bf16[2,128,256]{2,1,0:T(8,128)(2,1)S(1)}, u32[]{:S(2)}, u32[]{:S(2)}) collective-permute-start(bf16[2,128,256]{2,1,0:T(8,128)(2,1)S(1)} %pad_maximum_fusion.1), channel_id=1, source_target_pairs={{0,12},{1,13},{2,14},{3,15},{4,0},{5,1},{6,2},{7,3},{8,4},{9,5},{1... | collective-permute-start | bytes 393224 | tf_op jit(solution)/shard_map/ppermute | solution.py:160
  14.4 8.5 %collective-permute-start.7 = (bf16[2,128,256]{2,1,0:T(8,128)(2,1)S(1)}, bf16[2,128,256]{2,1,0:T(8,128)(2,1)S(1)}, u32[]{:S(2)}, u32[]{:S(2)}) collective-permute-start(bf16[2,128,256]{2,1,0:T(8,128)(2,1)S(1)} %pad_maximum_fusion.1), channel_id=1, source_target_pairs={{0,14},{1,15},{2,0},{3,1},{4,2},{5,3},{6,4},{7,5},{8,6},{9,7},{10,... | collective-permute-start | bytes 393224 | tf_op jit(solution)/shard_map/ppermute | solution.py:160
  16.6 6.3 %copy-start.4 = (bf16[2,128,256]{2,1,0:T(8,128)(2,1)}, bf16[2,128,256]{2,1,0:T(8,128)(2,1)S(1)}, u32[]{:S(2)}) copy-start(bf16[2,128,256]{2,1,0:T(8,128)(2,1)S(1)} %collective-permute-done.6.refs_7_) | copy-start | bytes 393220
  16.6 6.3 %collective-permute-start.9 = (bf16[2,128,256]{2,1,0:T(8,128)(2,1)S(1)}, bf16[2,128,256]{2,1,0:T(8,128)(2,1)S(1)}, u32[]{:S(2)}, u32[]{:S(2)}) collective-permute-start(bf16[2,128,256]{2,1,0:T(8,128)(2,1)S(1)} %collective-permute-done.6.refs_7_), channel_id=1, source_target_pairs={{0,2},{1,3},{2,4},{3,5},{4,6},{5,7},{6,8},{7,9},{8,10},{9,11},{10,... | collective-permute-start | bytes 393224 | tf_op jit(solution)/shard_map/ppermute | solution.py:164
  16.6 3.6 %collective-permute-start = (bf16[128,256]{1,0:T(8,128)(2,1)}, bf16[128,256]{1,0:T(8,128)(2,1)S(1)}, u32[]{:S(2)}, u32[]{:S(2)}) collective-permute-start(bf16[128,256]{1,0:T(8,128)(2,1)} %refs_0_.1), channel_id=1, source_target_pairs={{0,1},{1,0},{2,3},{3,2},{4,5},{5,4},{6,7},{7,6},{8,9},{9,8},{10,11... | collective-permute-start | bytes 196616 | tf_op jit(solution)/shard_map/ppermute | solution.py:148
  20.2 2.7 %copy-start.9 = (bf16[128,256]{1,0:T(8,128)(2,1)}, bf16[128,256]{1,0:T(8,128)(2,1)S(1)}, u32[]{:S(2)}) copy-start(bf16[128,256]{1,0:T(8,128)(2,1)S(1)} %collective-permute-done.refs_1_) | copy-start | bytes 196612
  20.2 2.7 %copy-start.5 = (bf16[2,128,256]{2,1,0:T(8,128)(2,1)}, bf16[2,128,256]{2,1,0:T(8,128)(2,1)S(1)}, u32[]{:S(2)}) copy-start(bf16[2,128,256]{2,1,0:T(8,128)(2,1)S(1)} %collective-permute-done.5.refs_6_) | copy-start | bytes 393220
  20.3 2.7 %copy-start.6 = (bf16[2,128,256]{2,1,0:T(8,128)(2,1)}, bf16[2,128,256]{2,1,0:T(8,128)(2,1)S(1)}, u32[]{:S(2)}) copy-start(bf16[2,128,256]{2,1,0:T(8,128)(2,1)S(1)} %collective-permute-done.8.refs_9_) | copy-start | bytes 393220
  22.9 0.7 copy-start.7
  22.9 0.7 copy-start.8

commit v19 on v17

--- a/solution.py
+++ b/solution.py
@@ -80,7 +80,7 @@
         up_copy.wait()
         lax.fori_loop(k * step, (k + 1) * step, gu_body, 0, unroll=True)
     g = accg_s[...]
-    hid_s[...] = (g / (1.0 + jnp.exp(-g)) * accu_s[...]).astype(jnp.bfloat16)
+    hid_s[...] = (g * jax.nn.sigmoid(g) * accu_s[...]).astype(jnp.bfloat16)
     acco_s[...] = jnp.zeros(acco_s.shape, jnp.float32)
 
     def dn_body(m, carry):

time: 79.3 us -> 79.2 us (level)
  no operation moved by 1% of the time
where the time goes in v19:
time: 79.2 us; the launch traced here: 79 us
  blocking collectives  47.8 us (60%)
  starting transfers between devices  15.4 us (19%)
  waiting for transfers between devices  7.39 us (9%)
  Pallas kernels  6.85 us (9%)
  local copies, waits for them, and re-layouts  1.3 us (2%)
    all_to_all x1, blocking collectives, per_device(): lax.all_to_all(outgoing.reshape(ctx_count * tp_count, share, feat_width /...  47.8 us
    pallas_call x1, Pallas kernels, ffn(): pl.pallas_call(functools.partial(ffn_kernel, tuple(layout)), out_shape=ja...  6.85 us
    ppermute x2, starting transfers between devices, per_device(): other = lax.ppermute(tokens, 'tp', ring_pairs(z_count, step, 1))  5.88 us
    ppermute x4, starting transfers between devices, per_device(): pair = lax.ppermute(near[step], 'tp', ring_pairs(z_count, step * hops))  5.87 us
    ppermute x4, waiting for transfers between devices, per_device(): pair = lax.ppermute(near[step], 'tp', ring_pairs(z_count, step * hops))  3.47 us
    ppermute x2, starting transfers between devices, per_device(): same = lax.ppermute(tokens, 'tp', ring_pairs(z_count, step))  3.01 us
    ppermute x1, waiting for transfers between devices, per_device(): arrays = [tokens, lax.ppermute(tokens, 'tp', swap)]  2.97 us
  transfers between devices with their start and end apart: 10, of which 5 were waited for; matrix products, arithmetic and copies ran while one was open for 0% of the time, Pallas kernels for 0%

profile of v19, /device:TPU:1, one launch (start us, length us, event | category | flops | bytes accessed | tf_op | source)
XLA Modules:
  0.0 79.0 jit_solution(7167597670046239865)
XLA Ops:
  0.0 3.5 %collective-permute-start.2 = (bf16[128,256]{1,0:T(8,128)(2,1)}, bf16[128,256]{1,0:T(8,128)(2,1)S(1)}, u32[]{:S(2)}, u32[]{:S(2)}) collective-permute-start(bf16[128,256]{1,0:T(8,128)(2,1)} %refs_0_.1), channel_id=1, source_target_pairs={{0,3},{1,2},{2,5},{3,4},{4,7},{5,6},{6,9},{7,8},{8,11},{9,10},{10,... | collective-permute-start | bytes 196616 | tf_op jit(solution)/shard_map/ppermute | solution.py:157
  3.5 1.6 %collective-permute-start.1 = (bf16[128,256]{1,0:T(8,128)(2,1)}, bf16[128,256]{1,0:T(8,128)(2,1)S(1)}, u32[]{:S(2)}, u32[]{:S(2)}) collective-permute-start(bf16[128,256]{1,0:T(8,128)(2,1)} %refs_0_.1), channel_id=1, source_target_pairs={{0,2},{1,3},{2,4},{3,5},{4,6},{5,7},{6,8},{7,9},{8,10},{9,11},{10,... | collective-permute-start | bytes 196616 | tf_op jit(solution)/shard_map/ppermute | solution.py:156
  5.1 1.4 %collective-permute-start.3 = (bf16[128,256]{1,0:T(8,128)(2,1)}, bf16[128,256]{1,0:T(8,128)(2,1)S(1)}, u32[]{:S(2)}, u32[]{:S(2)}) collective-permute-start(bf16[128,256]{1,0:T(8,128)(2,1)} %refs_0_.1), channel_id=1, source_target_pairs={{0,14},{1,15},{2,0},{3,1},{4,2},{5,3},{6,4},{7,5},{8,6},{9,7},{10,... | collective-permute-start | bytes 196616 | tf_op jit(solution)/shard_map/ppermute | solution.py:156
  6.5 2.4 %collective-permute-start.4 = (bf16[128,256]{1,0:T(8,128)(2,1)}, bf16[128,256]{1,0:T(8,128)(2,1)S(1)}, u32[]{:S(2)}, u32[]{:S(2)}) collective-permute-start(bf16[128,256]{1,0:T(8,128)(2,1)} %refs_0_.1), channel_id=1, source_target_pairs={{0,15},{1,14},{2,1},{3,0},{4,3},{5,2},{6,5},{7,4},{8,7},{9,6},{10,... | collective-permute-start | bytes 196616 | tf_op jit(solution)/shard_map/ppermute | solution.py:157
  8.9 0.4 collective-permute-done.2.refs_3_
  9.3 0.6 collective-permute-done.1.refs_2_
  9.9 1.2 %collective-permute-start.6 = (bf16[2,128,256]{2,1,0:T(8,128)(2,1)S(1)}, bf16[2,128,256]{2,1,0:T(8,128)(2,1)S(1)}, u32[]{:S(2)}, u32[]{:S(2)}) collective-permute-start(bf16[2,128,256]{2,1,0:T(8,128)(2,1)S(1)} %pad_maximum_fusion), channel_id=1, source_target_pairs={{0,4},{1,5},{2,6},{3,7},{4,8},{5,9},{6,10},{7,11},{8,12},{9,13},{1... | collective-permute-start | bytes 393224 | tf_op jit(solution)/shard_map/ppermute | solution.py:164
  11.1 1.7 %collective-permute-start.5 = (bf16[2,128,256]{2,1,0:T(8,128)(2,1)S(1)}, bf16[2,128,256]{2,1,0:T(8,128)(2,1)S(1)}, u32[]{:S(2)}, u32[]{:S(2)}) collective-permute-start(bf16[2,128,256]{2,1,0:T(8,128)(2,1)S(1)} %pad_maximum_fusion), channel_id=1, source_target_pairs={{0,2},{1,3},{2,4},{3,5},{4,6},{5,7},{6,8},{7,9},{8,10},{9,11},{10,... | collective-permute-start | bytes 393224 | tf_op jit(solution)/shard_map/ppermute | solution.py:164
  12.7 0.0 collective-permute-done.3.refs_4_
  12.7 0.0 collective-permute-done.4.refs_5_
  12.8 0.0 copy-start.3
  12.8 1.6 %collective-permute-start.8 = (bf16[2,128,256]{2,1,0:T(8,128)(2,1)S(1)}, bf16[2,128,256]{2,1,0:T(8,128)(2,1)S(1)}, u32[]{:S(2)}, u32[]{:S(2)}) collective-permute-start(bf16[2,128,256]{2,1,0:T(8,128)(2,1)S(1)} %pad_maximum_fusion.1), channel_id=1, source_target_pairs={{0,12},{1,13},{2,14},{3,15},{4,0},{5,1},{6,2},{7,3},{8,4},{9,5},{1... | collective-permute-start | bytes 393224 | tf_op jit(solution)/shard_map/ppermute | solution.py:164
  14.4 1.4 %collective-permute-start.7 = (bf16[2,128,256]{2,1,0:T(8,128)(2,1)S(1)}, bf16[2,128,256]{2,1,0:T(8,128)(2,1)S(1)}, u32[]{:S(2)}, u32[]{:S(2)}) collective-permute-start(bf16[2,128,256]{2,1,0:T(8,128)(2,1)S(1)} %pad_maximum_fusion.1), channel_id=1, source_target_pairs={{0,14},{1,15},{2,0},{3,1},{4,2},{5,3},{6,4},{7,5},{8,6},{9,7},{10,... | collective-permute-start | bytes 393224 | tf_op jit(solution)/shard_map/ppermute | solution.py:164
  15.8 0.8 %collective-permute-done.6.refs_7_ = bf16[2,128,256]{2,1,0:T(8,128)(2,1)S(1)} collective-permute-done((bf16[2,128,256]{2,1,0:T(8,128)(2,1)S(1)}, bf16[2,128,256]{2,1,0:T(8,128)(2,1)S(1)}, u32[]{:S(2)}, u32[]{:S(2)}) %collective-permute-start.6) | collective-permute-done | bytes 131104 | tf_op jit(solution)/shard_map/ppermute | solution.py:164
  16.6 0.0 collective-permute-start.9
  16.6 0.7 collective-permute-start
  17.3 3.0 %collective-permute-done.refs_1_ = bf16[128,256]{1,0:T(8,128)(2,1)S(1)} collective-permute-done((bf16[128,256]{1,0:T(8,128)(2,1)}, bf16[128,256]{1,0:T(8,128)(2,1)S(1)}, u32[]{:S(2)}, u32[]{:S(2)}) %collective-permute-start) | collective-permute-done | bytes 65568 | tf_op jit(solution)/shard_map/ppermute | solution.py:152
  20.2 0.0 collective-permute-done.5.refs_6_
  20.2 0.0 collective-permute-done.8.refs_9_
  20.3 0.0 copy-start.6
  20.3 2.6 %collective-permute-done.7.refs_8_ = bf16[2,128,256]{2,1,0:T(8,128)(2,1)S(1)} collective-permute-done((bf16[2,128,256]{2,1,0:T(8,128)(2,1)S(1)}, bf16[2,128,256]{2,1,0:T(8,128)(2,1)S(1)}, u32[]{:S(2)}, u32[]{:S(2)}) %collective-permute-start.7) | collective-permute-done | bytes 131104 | tf_op jit(solution)/shard_map/ppermute | solution.py:164
  22.9 0.0 collective-permute-done.9.refs_10_
  22.9 0.0 copy-done
  22.9 0.0 copy-done.1
  22.9 0.0 copy-done.2
  22.9 0.0 copy-done.3
  23.0 0.6 copy-done.7
  23.5 0.1 copy-done.8
  23.6 6.8 %shard_map.82 = bf16[16,16,8,256]{3,2,1,0:T(8,128)(2,1)} custom-call(s32[2]{0:T(128)} %bitcast.16, s32[2,64]{1,0:T(2,128)} %gu_ref.1, s32[2,64]{1,0:T(2,128)} %dn_ref.1, s32[1]{0:T(128)} %bitcast.1.me_ref, s32[16]{0:T(128)} %constant.10.table_ref, bf16[128,256]{1,0:T(8,128)(2,1)} %refs_0_.1, bf16[128,256]{1,0:T(8,128)(2,1)} %copy-done.9, ...), custom_call_target="tpu_custom_call" | custom-call | tf_op jit(solution)/shard_map/pallas_call | solution.py:118
  30.5 47.8 %all_to_all.5 = bf16[256,8,256]{2,1,0:T(8,128)(2,1)S(1)} all-to-all(bf16[256,8,256]{2,1,0:T(8,128)(2,1)} %bitcast.10), channel_id=1, replica_groups=mesh['ctx'=16,'tp'=16] {'ctx','tp'}, dimensions={0} | all-to-all | bytes 2097152 | tf_op jit(solution)/shard_map/all_to_all | solution.py:180
  78.3 0.1 bitcast_reduce_fusion
  78.4 0.6 copy.9
  (14 shorter events, 0.1 us)
Async XLA Ops:
  0.0 9.3 %collective-permute-start.2 = (bf16[128,256]{1,0:T(8,128)(2,1)}, bf16[128,256]{1,0:T(8,128)(2,1)S(1)}, u32[]{:S(2)}, u32[]{:S(2)}) collective-permute-start(bf16[128,256]{1,0:T(8,128)(2,1)} %refs_0_.1), channel_id=1, source_target_pairs={{0,3},{1,2},{2,5},{3,4},{4,7},{5,6},{6,9},{7,8},{8,11},{9,10},{10,... | collective-permute-start | bytes 196616 | tf_op jit(solution)/shard_map/ppermute | solution.py:157
  3.5 6.4 %collective-permute-start.1 = (bf16[128,256]{1,0:T(8,128)(2,1)}, bf16[128,256]{1,0:T(8,128)(2,1)S(1)}, u32[]{:S(2)}, u32[]{:S(2)}) collective-permute-start(bf16[128,256]{1,0:T(8,128)(2,1)} %refs_0_.1), channel_id=1, source_target_pairs={{0,2},{1,3},{2,4},{3,5},{4,6},{5,7},{6,8},{7,9},{8,10},{9,11},{10,... | collective-permute-start | bytes 196616 | tf_op jit(solution)/shard_map/ppermute | solution.py:156
  5.1 7.6 %collective-permute-start.3 = (bf16[128,256]{1,0:T(8,128)(2,1)}, bf16[128,256]{1,0:T(8,128)(2,1)S(1)}, u32[]{:S(2)}, u32[]{:S(2)}) collective-permute-start(bf16[128,256]{1,0:T(8,128)(2,1)} %refs_0_.1), channel_id=1, source_target_pairs={{0,14},{1,15},{2,0},{3,1},{4,2},{5,3},{6,4},{7,5},{8,6},{9,7},{10,... | collective-permute-start | bytes 196616 | tf_op jit(solution)/shard_map/ppermute | solution.py:156
  6.5 6.3 %collective-permute-start.4 = (bf16[128,256]{1,0:T(8,128)(2,1)}, bf16[128,256]{1,0:T(8,128)(2,1)S(1)}, u32[]{:S(2)}, u32[]{:S(2)}) collective-permute-start(bf16[128,256]{1,0:T(8,128)(2,1)} %refs_0_.1), channel_id=1, source_target_pairs={{0,15},{1,14},{2,1},{3,0},{4,3},{5,2},{6,5},{7,4},{8,7},{9,6},{10,... | collective-permute-start | bytes 196616 | tf_op jit(solution)/shard_map/ppermute | solution.py:157
  9.3 13.6 %copy-start = (bf16[128,256]{1,0:T(8,128)(2,1)}, bf16[128,256]{1,0:T(8,128)(2,1)S(1)}, u32[]{:S(2)}) copy-start(bf16[128,256]{1,0:T(8,128)(2,1)S(1)} %collective-permute-done.2.refs_3_) | copy-start | bytes 196612
  9.8 13.1 %copy-start.1 = (bf16[128,256]{1,0:T(8,128)(2,1)}, bf16[128,256]{1,0:T(8,128)(2,1)S(1)}, u32[]{:S(2)}) copy-start(bf16[128,256]{1,0:T(8,128)(2,1)S(1)} %collective-permute-done.1.refs_2_) | copy-start | bytes 196612
  9.9 6.8 %collective-permute-start.6 = (bf16[2,128,256]{2,1,0:T(8,128)(2,1)S(1)}, bf16[2,128,256]{2,1,0:T(8,128)(2,1)S(1)}, u32[]{:S(2)}, u32[]{:S(2)}) collective-permute-start(bf16[2,128,256]{2,1,0:T(8,128)(2,1)S(1)} %pad_maximum_fusion), channel_id=1, source_target_pairs={{0,4},{1,5},{2,6},{3,7},{4,8},{5,9},{6,10},{7,11},{8,12},{9,13},{1... | collective-permute-start | bytes 393224 | tf_op jit(solution)/shard_map/ppermute | solution.py:164
  11.1 9.2 %collective-permute-start.5 = (bf16[2,128,256]{2,1,0:T(8,128)(2,1)S(1)}, bf16[2,128,256]{2,1,0:T(8,128)(2,1)S(1)}, u32[]{:S(2)}, u32[]{:S(2)}) collective-permute-start(bf16[2,128,256]{2,1,0:T(8,128)(2,1)S(1)} %pad_maximum_fusion), channel_id=1, source_target_pairs={{0,2},{1,3},{2,4},{3,5},{4,6},{5,7},{6,8},{7,9},{8,10},{9,11},{10,... | collective-permute-start | bytes 393224 | tf_op jit(solution)/shard_map/ppermute | solution.py:164
  12.7 10.2 %copy-start.2 = (bf16[128,256]{1,0:T(8,128)(2,1)}, bf16[128,256]{1,0:T(8,128)(2,1)S(1)}, u32[]{:S(2)}) copy-start(bf16[128,256]{1,0:T(8,128)(2,1)S(1)} %collective-permute-done.3.refs_4_) | copy-start | bytes 196612
  12.8 10.2 %copy-start.3 = (bf16[128,256]{1,0:T(8,128)(2,1)}, bf16[128,256]{1,0:T(8,128)(2,1)S(1)}, u32[]{:S(2)}) copy-start(bf16[128,256]{1,0:T(8,128)(2,1)S(1)} %collective-permute-done.4.refs_5_) | copy-start | bytes 196612
  12.8 7.5 %collective-permute-start.8 = (bf16[2,128,256]{2,1,0:T(8,128)(2,1)S(1)}, bf16[2,128,256]{2,1,0:T(8,128)(2,1)S(1)}, u32[]{:S(2)}, u32[]{:S(2)}) collective-permute-start(bf16[2,128,256]{2,1,0:T(8,128)(2,1)S(1)} %pad_maximum_fusion.1), channel_id=1, source_target_pairs={{0,12},{1,13},{2,14},{3,15},{4,0},{5,1},{6,2},{7,3},{8,4},{9,5},{1... | collective-permute-start | bytes 393224 | tf_op jit(solution)/shard_map/ppermute | solution.py:164
  14.4 8.5 %collective-permute-start.7 = (bf16[2,128,256]{2,1,0:T(8,128)(2,1)S(1)}, bf16[2,128,256]{2,1,0:T(8,128)(2,1)S(1)}, u32[]{:S(2)}, u32[]{:S(2)}) collective-permute-start(bf16[2,128,256]{2,1,0:T(8,128)(2,1)S(1)} %pad_maximum_fusion.1), channel_id=1, source_target_pairs={{0,14},{1,15},{2,0},{3,1},{4,2},{5,3},{6,4},{7,5},{8,6},{9,7},{10,... | collective-permute-start | bytes 393224 | tf_op jit(solution)/shard_map/ppermute | solution.py:164
  16.6 6.3 %copy-start.4 = (bf16[2,128,256]{2,1,0:T(8,128)(2,1)}, bf16[2,128,256]{2,1,0:T(8,128)(2,1)S(1)}, u32[]{:S(2)}) copy-start(bf16[2,128,256]{2,1,0:T(8,128)(2,1)S(1)} %collective-permute-done.6.refs_7_) | copy-start | bytes 393220
  16.6 6.3 %collective-permute-start.9 = (bf16[2,128,256]{2,1,0:T(8,128)(2,1)S(1)}, bf16[2,128,256]{2,1,0:T(8,128)(2,1)S(1)}, u32[]{:S(2)}, u32[]{:S(2)}) collective-permute-start(bf16[2,128,256]{2,1,0:T(8,128)(2,1)S(1)} %collective-permute-done.6.refs_7_), channel_id=1, source_target_pairs={{0,2},{1,3},{2,4},{3,5},{4,6},{5,7},{6,8},{7,9},{8,10},{9,11},{10,... | collective-permute-start | bytes 393224 | tf_op jit(solution)/shard_map/ppermute | solution.py:168
  16.6 3.6 %collective-permute-start = (bf16[128,256]{1,0:T(8,128)(2,1)}, bf16[128,256]{1,0:T(8,128)(2,1)S(1)}, u32[]{:S(2)}, u32[]{:S(2)}) collective-permute-start(bf16[128,256]{1,0:T(8,128)(2,1)} %refs_0_.1), channel_id=1, source_target_pairs={{0,1},{1,0},{2,3},{3,2},{4,5},{5,4},{6,7},{7,6},{8,9},{9,8},{10,11... | collective-permute-start | bytes 196616 | tf_op jit(solution)/shard_map/ppermute | solution.py:152
  20.2 2.7 %copy-start.9 = (bf16[128,256]{1,0:T(8,128)(2,1)}, bf16[128,256]{1,0:T(8,128)(2,1)S(1)}, u32[]{:S(2)}) copy-start(bf16[128,256]{1,0:T(8,128)(2,1)S(1)} %collective-permute-done.refs_1_) | copy-start | bytes 196612
  20.2 2.7 %copy-start.5 = (bf16[2,128,256]{2,1,0:T(8,128)(2,1)}, bf16[2,128,256]{2,1,0:T(8,128)(2,1)S(1)}, u32[]{:S(2)}) copy-start(bf16[2,128,256]{2,1,0:T(8,128)(2,1)S(1)} %collective-permute-done.5.refs_6_) | copy-start | bytes 393220
  20.3 2.7 %copy-start.6 = (bf16[2,128,256]{2,1,0:T(8,128)(2,1)}, bf16[2,128,256]{2,1,0:T(8,128)(2,1)S(1)}, u32[]{:S(2)}) copy-start(bf16[2,128,256]{2,1,0:T(8,128)(2,1)S(1)} %collective-permute-done.8.refs_9_) | copy-start | bytes 393220
  22.9 0.7 copy-start.7
  22.9 0.7 copy-start.8
